TPU v7x, 128 devices: a whole 4x4x4 slice. The times are simulated.
128 devices in a mesh: px: 8 (over x, core), py: 16 (over z, y).
Axes of the slice: x: 4, y: 4, z: 4, core: 2. Of those that a mesh axis runs over, the one named last changes fastest.
Arguments:
- displacement: float32 [6, 128, 2048], P(None, 'px', 'py'), may hold values from -4 to 4
- velocity: float32 [6, 128, 2048], P(None, 'px', 'py'), may hold values from -6 to 6
- load: float32 [6, 128, 2048], P(None, 'px', 'py'), may hold values from -24 to 24
- inv_mass: float32 [6, 128, 2048], P(None, 'px', 'py'), may hold values from 0.2 to 1
- history: float32 [128, 128, 2048], P(None, 'px', 'py'), may hold values from -6 to 6
- contact_home: float32 [128, 128, 2048], P(None, 'px', 'py'), may hold values from 0.25 to 4
- recv_contact: float32 [8, 16, 128, 1152], P('px', 'py'), may hold values from 0.25 to 4
- stiff_base: float32 [24, 24], replicated, as said below
- strain_map: float32 [128, 24], replicated, may hold values from -1.25 to 1.25
- slot_table: int32 [8, 16, 1152], P('px', 'py'), may hold values from 0 to 2048, as said below
Outputs:
- springback: float32 [6, 128, 2048], P(None, 'px', 'py')
- velocity_out: float32 [6, 128, 2048], P(None, 'px', 'py')
- history_out: float32 [128, 128, 2048], P(None, 'px', 'py')
- residual: float32 [6, 128, 2048], P(None, 'px', 'py')
Inputs may be any that keep to these rules, and one draw needn't show every extreme that they name: `slot_table`: for each source block and destination device d, the slots d * 9 .. d * 9 + 8 hold distinct local shell indices first and then 16 * 128; no shell appears twice in one source block; no block sends to itself; every source block fills all 9 slots toward some destination, and about half of the source blocks fill all slots toward every other device. `stiff_base`: Symmetric, with diagonal entries of 5 to 7 and off-diagonal entries of magnitude at most 0.2.
All inputs are finite; a program needn't handle non-finite values.
Results may differ from a plain program's by a relative error of at most 0.0003.
Values sent between devices are 32-bit elements; how exact they have to be, the bound alone decides.
No kernel may reach another device: no remote copies, remote signals or barrier semaphores. Data moves between devices by JAX's collectives and lax.ppermute only.
A program may use at most 128 MiB of HBM per device.

v0:
```python
import jax
import jax.numpy as jnp
from jax import lax
from jax.sharding import PartitionSpec as P

ITERS = 2


HIGH = lax.Precision.HIGHEST
STEP = 0.2
CORNERS = ((0, 0), (1, 0), (0, 1), (1, 1))


def with_halo(shard, sides, width):
    for axis, dim in sides:
        devices, length = (lax.axis_size(axis), shard.shape[dim])
        up = [(i, (i + 1) % devices) for i in range(devices - 1)]
        down = [(j, i) for i, j in up]
        last = lax.slice_in_dim(shard, length - width, length, axis=dim)
        leading = lax.slice_in_dim(shard, 0, width, axis=dim)
        before = lax.ppermute(last, axis, up)
        after = lax.ppermute(leading, axis, down)
        shard = jnp.concatenate([before, shard, after], axis=dim)
    return shard


def shifted(shard, axis, by):
    devices = lax.axis_size(axis)
    pairs = [(i, i + by) for i in range(devices) if 0 <= i + by < devices]
    return lax.ppermute(shard, axis, pairs)


def apply_field(field, multiply):
    rows, cols = (field.shape[1], field.shape[2])
    padded = with_halo(field, (("px", 1), ("py", 2)), 1)
    shells = jnp.concatenate(
        [padded[:, dx : dx + rows + 1, dy : dy + cols + 1] for dx, dy in CORNERS], axis=0
    )
    forces = multiply(shells)
    row_keep = (jnp.arange(rows + 1) > 0) | (lax.axis_index("px") > 0)
    col_keep = (jnp.arange(cols + 1) > 0) | (lax.axis_index("py") > 0)
    keep = (row_keep[:, None] & col_keep[None, :]).astype(jnp.float32)
    forces = forces * keep[None, :, :]
    total = jnp.zeros((6, rows, cols), jnp.float32)
    for index, (dx, dy) in enumerate(CORNERS):
        total = (
            total
            + forces[6 * index : 6 * index + 6, 1 - dx : 1 - dx + rows, 1 - dy : 1 - dy + cols]
        )
    return (total, shells)


def global_sum(value):
    return lax.psum(value, ("px", "py"))


def shards(
    displacement,
    velocity,
    load,
    inv_mass,
    history,
    contact_home,
    recv_contact,
    stiff_base,
    strain_map,
    slot_table,
):
    hist = history.shape[0]
    rows, cols = (displacement.shape[1], displacement.shape[2])
    cells = rows * cols

    def with_base(shells):
        return jnp.einsum("ab,bxy->axy", stiff_base, shells, precision=HIGH)

    force_start, start_shells = apply_field(displacement, with_base)
    velocity_out = velocity + STEP * inv_mass * (load - force_start)
    moved = displacement + STEP * velocity_out
    own = start_shells[:, 1:, 1:].reshape(24, cells)
    history_new = history.reshape(hist, cells) + jnp.dot(strain_map, own, precision=HIGH)
    pairs = (strain_map[:, :, None] * strain_map[:, None, :]).reshape(hist, 576)

    def form(states, contact):
        weights = jax.nn.softplus(states) * contact
        return stiff_base.reshape(576, 1) + jnp.dot(pairs.T, weights, precision=HIGH)

    targets = slot_table.reshape(-1)
    devices = lax.axis_size("px") * lax.axis_size("py")
    width = targets.shape[0] // devices
    held = recv_contact.reshape(hist, devices, width)
    contact_flat = contact_home.reshape(hist, cells)
    outgoing = jnp.take(history_new, targets, axis=1, mode="fill", fill_value=0.0).reshape(
        hist, devices, width
    )
    arrived = lax.all_to_all(outgoing, ("px", "py"), split_axis=1, concat_axis=1, tiled=True)
    formed = form(arrived.reshape(hist, devices * width), held.reshape(hist, devices * width))
    returned = lax.all_to_all(
        formed.reshape(576, devices, width), ("px", "py"), split_axis=1, concat_axis=1, tiled=True
    )
    tangent = (
        form(history_new, contact_flat)
        .at[:, targets]
        .set(returned.reshape(576, devices * width), mode="drop")
    )
    tangent = tangent.reshape(576, rows, cols)
    lower_row = shifted(tangent[:, -1:, :], "px", 1)
    tall = jnp.concatenate([lower_row, tangent], axis=1)
    lower_col = shifted(tall[:, :, -1:], "py", 1)
    extended = jnp.concatenate([lower_col, tall], axis=2).reshape(24, 24, rows + 1, cols + 1)

    def with_tangent(shells):
        return jnp.einsum("abxy,bxy->axy", extended, shells, precision=HIGH)

    rhs = load - force_start
    solution = jnp.zeros_like(rhs)
    residual = rhs
    direction = rhs
    norm_now = global_sum(jnp.sum(residual * residual))
    for step in range(ITERS):
        image = apply_field(direction, with_tangent)[0]
        alpha = norm_now / global_sum(jnp.sum(direction * image))
        solution = solution + alpha * direction
        residual = residual - alpha * image
        if step + 1 < ITERS:
            norm_next = global_sum(jnp.sum(residual * residual))
            direction = residual + norm_next / norm_now * direction
            norm_now = norm_next
    return (moved + solution, velocity_out, history_new.reshape(hist, rows, cols), residual)


def solution(mesh):
    return jax.shard_map(
        shards,
        mesh=mesh,
        in_specs=(
            P(None, "px", "py"),
            P(None, "px", "py"),
            P(None, "px", "py"),
            P(None, "px", "py"),
            P(None, "px", "py"),
            P(None, "px", "py"),
            P("px", "py", None, None),
            P(),
            P(),
            P("px", "py", None),
        ),
        out_specs=(
            P(None, "px", "py"),
            P(None, "px", "py"),
            P(None, "px", "py"),
            P(None, "px", "py"),
        ),
        check_vma=False,
    )
```

profile of v0, /device:TPU:0, one launch (start us, length us, event | category | flops | bytes accessed | tf_op | source)
XLA Modules:
  0.0 429.2 jit_solution(3479435247296395445)
XLA Ops:
  9.0 4.5 %collective-permute-start.2 = (f32[6,18,1]{2,0,1:T(8,128)S(1)}, f32[6,18,1]{2,0,1:T(8,128)S(1)}, u32[]{:S(2)}, u32[]{:S(2)}) collective-permute-start(f32[6,18,1]{2,0,1:T(8,128)S(1)} %get-tuple-element.43), channel_id=1, source_target_pairs={{0,1},{1,2},{2,3},{3,4},{4,5},{5,6},{6,7},{7,8},{8,9},{9,10},{10,1... | collective-permute-start | bytes 1304 | tf_op jit(solution)/shard_map/ppermute | solution.py:21
  22.1 15.8 %all-to-all-start = ((f32[128,128,9]{0,2,1:T(8,128)}), f32[128,128,9]{0,2,1:T(8,128)S(1)}, u32[]{:S(2)}, u32[]{:S(2)}) async-start(f32[128,128,9]{0,2,1:T(8,128)} %broadcast_select_fusion), calls=%async_computation | async-start | bytes 2097152 | tf_op jit(solution)/shard_map/all_to_all | solution.py:95
  40.1 16.8 %all-to-all-done = f32[128,128,9]{0,2,1:T(8,128)S(1)} async-done(((f32[128,128,9]{0,2,1:T(8,128)}), f32[128,128,9]{0,2,1:T(8,128)S(1)}, u32[]{:S(2)}, u32[]{:S(2)}) %all-to-all-start) | async-done | bytes 589856 | tf_op jit(solution)/shard_map/all_to_all | solution.py:95
  57.0 5.0 %convolution_add_fusion = f32[576,1152]{1,0:T(8,128)} fusion(f32[128,576]{0,1:T(8,128)S(1)} %bitcast.60, f32[576]{0:T(1024)S(1)} %add.115, f32[1,1,128,1152]{2,3,1,0:T(8,128)} %copy.61, f32[1,1,128,1152]{2,3,1,0:T(8,128)S(1)} %reshape.193), kind=kOutput, calls=%fused_computation.6 | convolution fusion | flops 1020911616 | bytes 4131072 | tf_op jit(solution)/shard_map/dot_general | solution.py:85
  62.0 3.5 copy.62
  65.5 4.6 %reshape.194 = f32[576,128,9]{0,2,1:T(8,128)} reshape(f32[576,1152]{0,1:T(8,128)} %copy.62) | data formatting | bytes 5308416 | tf_op jit(solution)/shard_map/reshape | solution.py:98
  70.2 5.9 %all-to-all-start.1 = ((f32[576,128,9]{0,2,1:T(8,128)}), f32[576,128,9]{0,2,1:T(8,128)}, u32[]{:S(2)}, u32[]{:S(2)}) async-start(f32[576,128,9]{0,2,1:T(8,128)} %reshape.194), calls=%async_computation.1 | async-start | bytes 10485760 | tf_op jit(solution)/shard_map/all_to_all | solution.py:97
  79.8 3.2 collective-permute-start.4
  83.0 5.9 %convolution_add_fusion.1 = f32[576,2048]{1,0:T(8,128)} fusion(f32[128,576]{0,1:T(8,128)S(1)} %bitcast.61, f32[576]{0:T(1024)S(1)} %add.115, f32[128,2048]{0,1:T(8,128)S(1)} %bitcast.58, f32[128,2048]{0,1:T(8,128)S(1)} %fusion.2), kind=kOutput, calls=%fused_computation.7 | convolution fusion | flops 1814953984 | bytes 7112960 | tf_op jit(solution)/shard_map/dot_general | solution.py:85
  88.9 5.8 %copy.63 = f32[576,2048]{0,1:T(8,128)} copy(f32[576,2048]{1,0:T(8,128)} %convolution_add_fusion.1) | data formatting | bytes 9437184 | tf_op jit(solution)/shard_map/add | solution.py:85
  98.8 40.9 %all-to-all-done.1 = f32[576,128,9]{0,2,1:T(8,128)} async-done(((f32[576,128,9]{0,2,1:T(8,128)}), f32[576,128,9]{0,2,1:T(8,128)}, u32[]{:S(2)}, u32[]{:S(2)}) %all-to-all-start.1) | async-done | bytes 2654240 | tf_op jit(solution)/shard_map/all_to_all | solution.py:97
  139.8 5.0 %reshape.208 = f32[576,1152]{0,1:T(8,128)} reshape(f32[576,128,9]{0,2,1:T(8,128)} %all-to-all-done.1) | data formatting | bytes 5308416 | tf_op jit(solution)/shard_map/reshape | solution.py:103
  144.8 13.4 %scatter_custom_fusion = f32[576,2048]{0,1:T(8,128)} fusion(f32[576,2048]{0,1:T(8,128)} %copy.63, s32[1152]{0:T(1024)} %copy-done.6, f32[576,1152]{0,1:T(8,128)} %reshape.208), kind=kCustom, calls=%fused_computation.9 | custom fusion | bytes 7667712 | tf_op jit(solution)/shard_map/scatter | solution.py:103
  158.1 5.8 %copy.64 = f32[576,16,128]{2,0,1:T(8,128)} copy(f32[576,16,128]{0,2,1:T(8,128)} %bitcast.57) | data formatting | bytes 9437184 | tf_op jit(solution)/shard_map/reshape | solution.py:105
  167.4 5.9 %pad_maximum_fusion = f32[576,17,1]{2,0,1:T(8,128)} fusion(f32[576,16,128]{2,0,1:T(8,128)} %copy.64, f32[576,1,128]{2,0,1:T(8,128)S(1)} %collective-permute-done.8), kind=kLoop, calls=%fused_computation.5 | loop fusion | flops 9792 | bytes 5052672 | tf_op jit(solution)/shard_map/concatenate | solution.py:107
  173.3 3.5 copy.66
  176.8 3.1 collective-permute-start.9
  181.4 3.0 copy.67
  184.4 6.5 %maximum_maximum_fusion = f32[576,17,129]{2,0,1:T(8,128)S(1)} fusion(f32[576,16,128]{2,0,1:T(8,128)} %copy.64, f32[576,1,128]{2,0,1:T(8,128)S(1)} %collective-permute-done.8, f32[576,17,1]{2,0,1:T(8,128)} %copy.67), kind=kLoop, calls=%fused_computation.2 | loop fusion | flops 2526336 | bytes 10105344 | tf_op jit(solution)/shard_map/concatenate | solution.py:109
  195.5 74.2 %all-reduce = (f32[]{:T(128)}, f32[]{:T(128)}) all-reduce(f32[]{:T(128)} %get-tuple-element.17, f32[]{:T(128)} %get-tuple-element.16), channel_id=1, replica_groups=mesh['px'=8,'py'=16] {'px','py'}, use_global_device_ids=true, to_apply=%region_1.2 | all-reduce | flops 2 | bytes 16 | tf_op jit(solution)/shard_map/psum | solution.py:54
  271.7 64.9 %psum.30 = f32[]{:T(128)} all-reduce(f32[]{:T(128)} %multiply_reduce_fusion.3), channel_id=1, replica_groups=mesh['px'=8,'py'=16] {'px','py'}, use_global_device_ids=true, to_apply=%region_6.7 | all-reduce | flops 1 | bytes 8 | tf_op jit(solution)/shard_map/psum | solution.py:54
  347.1 4.2 collective-permute-done.13
  351.6 5.9 %multiply_reduce_fusion = f32[17,129,24]{1,2,0:T(8,128)S(1)} fusion(f32[17,129,24,24]{1,2,3,0:T(8,128)} %bitcast.55, f32[17,129,24]{1,2,0:T(8,128)S(1)} %maximum_bitcast_fusion.1), kind=kLoop, calls=%fused_computation.3 | loop fusion | flops 2473704 | bytes 5473728 | tf_op jit(solution)/shard_map/abxy,bxy->axy/dot_general | solution.py:112
  358.3 67.6 %psum.31 = f32[]{:T(128)} all-reduce(f32[]{:T(128)} %get-tuple-element.22), channel_id=1, replica_groups=mesh['px'=8,'py'=16] {'px','py'}, use_global_device_ids=true, to_apply=%region_8.9 | all-reduce | flops 1 | bytes 8 | tf_op jit(solution)/shard_map/psum | solution.py:54
  (96 shorter events, 49.1 us)
Async XLA Ops:
  1.4 4.3 collective-permute-start
  2.7 4.9 %collective-permute-start.1 = (f32[6,1,128]{2,0,1:T(8,128)S(1)}, f32[6,1,128]{2,0,1:T(8,128)S(1)}, u32[]{:S(2)}, u32[]{:S(2)}) collective-permute-start(f32[6,1,128]{2,0,1:T(8,128)S(1)} %copy.103), channel_id=1, source_target_pairs={{16,0},{32,16},{48,32},{64,48},{80,64},{96,80},{112,96},{17,1},{33... | collective-permute-start | bytes 9224 | tf_op jit(solution)/shard_map/ppermute | solution.py:22
  5.7 9.5 %copy-start.6 = (s32[1152]{0:T(1024)}, s32[1152]{0:T(1024)S(1)}, u32[]{:S(2)}) copy-start(s32[1152]{0:T(1024)S(1)} %fusion.39) | copy-start | bytes 13828
  7.7 7.5 %collective-permute-start.3 = (f32[6,18,1]{2,0,1:T(8,128)S(1)}, f32[6,18,1]{2,0,1:T(8,128)S(1)}, u32[]{:S(2)}, u32[]{:S(2)}) collective-permute-start(f32[6,18,1]{2,0,1:T(8,128)S(1)} %get-tuple-element.44), channel_id=1, source_target_pairs={{1,0},{2,1},{3,2},{4,3},{5,4},{6,5},{7,6},{8,7},{9,8},{10,9},{11,1... | collective-permute-start | bytes 1304 | tf_op jit(solution)/shard_map/ppermute | solution.py:22
  9.0 6.5 %collective-permute-start.2 = (f32[6,18,1]{2,0,1:T(8,128)S(1)}, f32[6,18,1]{2,0,1:T(8,128)S(1)}, u32[]{:S(2)}, u32[]{:S(2)}) collective-permute-start(f32[6,18,1]{2,0,1:T(8,128)S(1)} %get-tuple-element.43), channel_id=1, source_target_pairs={{0,1},{1,2},{2,3},{3,4},{4,5},{5,6},{6,7},{7,8},{8,9},{9,10},{10,1... | collective-permute-start | bytes 1304 | tf_op jit(solution)/shard_map/ppermute | solution.py:21
  18.3 19.6 %copy-start.7 = (f32[24,24]{1,0:T(8,128)S(1)}, f32[24,24]{1,0:T(8,128)}, u32[]{:S(2)}) copy-start(f32[24,24]{1,0:T(8,128)} %param.17) | copy-start | bytes 6916
  18.3 21.8 %copy-start.2 = (f32[128,24]{0,1:T(8,128)S(1)}, f32[128,24]{0,1:T(8,128)}, u32[]{:S(2)}) copy-start(f32[128,24]{0,1:T(8,128)} %param.18) | copy-start | bytes 36868
  22.1 34.8 %all-to-all-start = ((f32[128,128,9]{0,2,1:T(8,128)}), f32[128,128,9]{0,2,1:T(8,128)S(1)}, u32[]{:S(2)}, u32[]{:S(2)}) async-start(f32[128,128,9]{0,2,1:T(8,128)} %broadcast_select_fusion), calls=%async_computation | async-start | bytes 2097152 | tf_op jit(solution)/shard_map/all_to_all | solution.py:95
  70.2 7.6 %copy-start.8 = (f32[24,24]{1,0:T(8,128)S(1)}, f32[24,24]{1,0:T(8,128)}, u32[]{:S(2)}) copy-start(f32[24,24]{1,0:T(8,128)} %param.17) | copy-start | bytes 6916
  70.2 8.2 %copy-start.5 = (f32[6,16,128]{2,1,0:T(8,128)S(1)}, f32[6,16,128]{2,1,0:T(8,128)}, u32[]{:S(2)}) copy-start(f32[6,16,128]{2,1,0:T(8,128)} %param.12) | copy-start | bytes 147460
  70.2 69.6 %all-to-all-start.1 = ((f32[576,128,9]{0,2,1:T(8,128)}), f32[576,128,9]{0,2,1:T(8,128)}, u32[]{:S(2)}, u32[]{:S(2)}) async-start(f32[576,128,9]{0,2,1:T(8,128)} %reshape.194), calls=%async_computation.1 | async-start | bytes 10485760 | tf_op jit(solution)/shard_map/all_to_all | solution.py:97
  78.5 16.2 %collective-permute-start.5 = (f32[6,1,128]{2,0,1:T(8,128)S(1)}, f32[6,1,128]{2,0,1:T(8,128)S(1)}, u32[]{:S(2)}, u32[]{:S(2)}) collective-permute-start(f32[6,1,128]{2,0,1:T(8,128)S(1)} %get-tuple-element.49), channel_id=1, source_target_pairs={{16,0},{32,16},{48,32},{64,48},{80,64},{96,80},{112,96},{17,1},{33... | collective-permute-start | bytes 9224 | tf_op jit(solution)/shard_map/ppermute | solution.py:22
  79.8 14.9 %collective-permute-start.4 = (f32[6,1,128]{2,0,1:T(8,128)S(1)}, f32[6,1,128]{2,0,1:T(8,128)S(1)}, u32[]{:S(2)}, u32[]{:S(2)}) collective-permute-start(f32[6,1,128]{2,0,1:T(8,128)S(1)} %get-tuple-element.48), channel_id=1, source_target_pairs={{0,16},{16,32},{32,48},{48,64},{64,80},{80,96},{96,112},{1,17},{17... | collective-permute-start | bytes 9224 | tf_op jit(solution)/shard_map/ppermute | solution.py:21
  94.8 71.4 %collective-permute-start.6 = (f32[6,18,1]{2,0,1:T(8,128)S(1)}, f32[6,18,1]{2,0,1:T(8,128)S(1)}, u32[]{:S(2)}, u32[]{:S(2)}) collective-permute-start(f32[6,18,1]{2,0,1:T(8,128)S(1)} %get-tuple-element.39), channel_id=1, source_target_pairs={{0,1},{1,2},{2,3},{3,4},{4,5},{5,6},{6,7},{7,8},{8,9},{9,10},{10,1... | collective-permute-start | bytes 1304 | tf_op jit(solution)/shard_map/ppermute | solution.py:21
  97.5 68.7 %collective-permute-start.7 = (f32[6,18,1]{2,0,1:T(8,128)S(1)}, f32[6,18,1]{2,0,1:T(8,128)S(1)}, u32[]{:S(2)}, u32[]{:S(2)}) collective-permute-start(f32[6,18,1]{2,0,1:T(8,128)S(1)} %get-tuple-element.40), channel_id=1, source_target_pairs={{1,0},{2,1},{3,2},{4,3},{5,4},{6,5},{7,6},{8,7},{9,8},{10,9},{11,1... | collective-permute-start | bytes 1304 | tf_op jit(solution)/shard_map/ppermute | solution.py:22
  164.9 2.5 collective-permute-start.8
  176.8 4.6 %collective-permute-start.9 = (f32[576,17,1]{0,2,1:T(1,128)S(1)}, f32[576,17,1]{0,2,1:T(1,128)S(1)}, u32[]{:S(2)}, u32[]{:S(2)}) collective-permute-start(f32[576,17,1]{0,2,1:T(1,128)S(1)} %copy.66), channel_id=1, source_target_pairs={{0,1},{1,2},{2,3},{3,4},{4,5},{5,6},{6,7},{7,8},{8,9},{9,10},{10,1... | collective-permute-start | bytes 117512 | tf_op jit(solution)/shard_map/ppermute | solution.py:30
  337.9 4.3 %collective-permute-start.11 = (f32[6,1,128]{2,0,1:T(8,128)S(1)}, f32[6,1,128]{2,0,1:T(8,128)S(1)}, u32[]{:S(2)}, u32[]{:S(2)}) collective-permute-start(f32[6,1,128]{2,0,1:T(8,128)S(1)} %get-tuple-element.47), channel_id=1, source_target_pairs={{16,0},{32,16},{48,32},{64,48},{80,64},{96,80},{112,96},{17,1},{33... | collective-permute-start | bytes 9224 | tf_op jit(solution)/shard_map/ppermute | solution.py:22
  339.2 3.8 collective-permute-start.10
  343.2 4.0 collective-permute-start.12
  344.5 6.8 %collective-permute-start.13 = (f32[6,18,1]{2,0,1:T(8,128)S(1)}, f32[6,18,1]{2,0,1:T(8,128)S(1)}, u32[]{:S(2)}, u32[]{:S(2)}) collective-permute-start(f32[6,18,1]{2,0,1:T(8,128)S(1)} %get-tuple-element.36), channel_id=1, source_target_pairs={{1,0},{2,1},{3,2},{4,3},{5,4},{6,5},{7,6},{8,7},{9,8},{10,9},{11,1... | collective-permute-start | bytes 1304 | tf_op jit(solution)/shard_map/ppermute | solution.py:22
  351.6 75.7 %copy-start.1 = (f32[6,16,128]{2,1,0:T(8,128)S(1)}, f32[6,16,128]{2,1,0:T(8,128)}, u32[]{:S(2)}) copy-start(f32[6,16,128]{2,1,0:T(8,128)} %param.10) | copy-start | bytes 147460
  351.6 75.7 %copy-start.3 = (f32[6,16,128]{2,1,0:T(8,128)S(1)}, f32[6,16,128]{2,1,0:T(8,128)}, u32[]{:S(2)}) copy-start(f32[6,16,128]{2,1,0:T(8,128)} %param.13) | copy-start | bytes 147460
  351.6 75.7 %copy-start.4 = (f32[6,16,128]{2,1,0:T(8,128)S(1)}, f32[6,16,128]{2,1,0:T(8,128)}, u32[]{:S(2)}) copy-start(f32[6,16,128]{2,1,0:T(8,128)} %param.11) | copy-start | bytes 147460
  (1 other events, 3.8 us)
where the time goes:
time: 432 us; the launch traced here: 429 us
  blocking collectives  207 us (48%)
  waiting for transfers between devices  66.5 us (15%)
  local copies, waits for them, and re-layouts  60.6 us (14%)
  starting transfers between devices  49.9 us (12%)
  other arithmetic  26.2 us (6%)
  matrix products  14.2 us (3%)
  between operations  5.17 us (1%)
    psum x3, blocking collectives, global_sum(): return lax.psum(value, ('px', 'py'))  207 us
    all_to_all x1, waiting for transfers between devices, shards(): lax.all_to_all(formed.reshape(576, devices, width), ('px', 'py'), split_a...  40.9 us
    all_to_all x1, waiting for transfers between devices, shards(): lax.all_to_all(outgoing, ('px', 'py'), split_axis=1, concat_axis=1, tiled...  16.8 us
    ppermute x6, starting transfers between devices, with_halo(): before = lax.ppermute(last, axis, up)  16.1 us
    all_to_all x1, starting transfers between devices, shards(): lax.all_to_all(outgoing, ('px', 'py'), split_axis=1, concat_axis=1, tiled...  15.8 us
    scatter x1, local copies, waits for them, and re-layouts, shards(): tangent = form(history_new, contact_flat).at[:, targets].set(returned.res...  13.4 us
    unnamed x29, local copies, waits for them, and re-layouts  11.1 us
    dot_general x2, matrix products, form(): jnp.dot(pairs.T, weights, precision=HIGH)  10.9 us
  transfers between devices with their start and end apart: 16, of which 8 were waited for; matrix products, arithmetic and copies ran while one was open for 11% of the time, Pallas kernels for 0%

commit v1 on v0

v1 whole, which is shorter than its diff:
```python
import jax
import jax.numpy as jnp
from jax import lax
from jax.sharding import PartitionSpec as P

ITERS = 2


HIGH = lax.Precision.HIGHEST
STEP = 0.2
CORNERS = ((0, 0), (1, 0), (0, 1), (1, 1))


def with_halo(shard, sides, width):
    for axis, dim in sides:
        devices, length = (lax.axis_size(axis), shard.shape[dim])
        up = [(i, (i + 1) % devices) for i in range(devices - 1)]
        down = [(j, i) for i, j in up]
        last = lax.slice_in_dim(shard, length - width, length, axis=dim)
        leading = lax.slice_in_dim(shard, 0, width, axis=dim)
        before = lax.ppermute(last, axis, up)
        after = lax.ppermute(leading, axis, down)
        shard = jnp.concatenate([before, shard, after], axis=dim)
    return shard


def shifted(shard, axis, by):
    devices = lax.axis_size(axis)
    pairs = [(i, i + by) for i in range(devices) if 0 <= i + by < devices]
    return lax.ppermute(shard, axis, pairs)


def all_sum(value):
    for axis in ("px", "py"):
        devices = lax.axis_size(axis)
        stride = 1
        while stride < devices:
            radix = min(4, devices // stride)
            total = value
            for k in range(1, radix):
                pairs = []
                for i in range(devices):
                    digit = (i // stride) % radix
                    pairs.append((i, i + (((digit + k) % radix) - digit) * stride))
                total = total + lax.ppermute(value, axis, pairs)
            value = total
            stride *= radix
    return value


def gather_shells(field):
    rows, cols = (field.shape[1] - 2, field.shape[2] - 2)
    return jnp.concatenate(
        [field[:, dx : dx + rows + 1, dy : dy + cols + 1] for dx, dy in CORNERS], axis=0
    )


def scatter_nodes(forces):
    rows, cols = (forces.shape[1] - 1, forces.shape[2] - 1)
    row_keep = (jnp.arange(rows + 1) > 0) | (lax.axis_index("px") > 0)
    col_keep = (jnp.arange(cols + 1) > 0) | (lax.axis_index("py") > 0)
    keep = (row_keep[:, None] & col_keep[None, :]).astype(jnp.float32)
    forces = forces * keep[None, :, :]
    total = jnp.zeros((6, rows, cols), jnp.float32)
    for index, (dx, dy) in enumerate(CORNERS):
        total = (
            total
            + forces[6 * index : 6 * index + 6, 1 - dx : 1 - dx + rows, 1 - dy : 1 - dy + cols]
        )
    return total


def shards(
    displacement,
    velocity,
    load,
    inv_mass,
    history,
    contact_home,
    recv_contact,
    stiff_base,
    strain_map,
    slot_table,
):
    hist = history.shape[0]
    rows, cols = (displacement.shape[1], displacement.shape[2])
    cells = rows * cols

    targets = slot_table.reshape(-1)
    devices = lax.axis_size("px") * lax.axis_size("py")
    width = targets.shape[0] // devices
    held = recv_contact.reshape(hist, devices, width)
    arrived = lax.all_to_all(held, ("px", "py"), split_axis=1, concat_axis=1, tiled=True)

    def with_base(shells):
        return jnp.einsum("ab,bxy->axy", stiff_base, shells, precision=HIGH)

    start_shells = gather_shells(with_halo(displacement, (("px", 1), ("py", 2)), 1))
    force_start = scatter_nodes(with_base(start_shells))
    velocity_out = velocity + STEP * inv_mass * (load - force_start)
    moved = displacement + STEP * velocity_out
    own = start_shells[:, 1:, 1:].reshape(24, cells)
    history_new = history.reshape(hist, cells) + jnp.dot(strain_map, own, precision=HIGH)

    contact = (
        contact_home.reshape(hist, cells)
        .at[:, targets]
        .set(arrived.reshape(hist, devices * width), mode="drop")
    )
    weights = (jax.nn.softplus(history_new) * contact).reshape(hist, rows, cols)
    lower_row = shifted(weights[:, -1:, :], "px", 1)
    tall = jnp.concatenate([lower_row, weights], axis=1)
    lower_col = shifted(tall[:, :, -1:], "py", 1)
    extended = jnp.concatenate([lower_col, tall], axis=2)

    def operate(field):
        shells = gather_shells(with_halo(field, (("px", 1), ("py", 2)), 1))
        strains = jnp.einsum("hb,bxy->hxy", strain_map, shells, precision=HIGH)
        forces = jnp.einsum("hb,hxy->bxy", strain_map, extended * strains, precision=HIGH)
        return scatter_nodes(forces + with_base(shells))

    rhs = load - force_start
    solution = jnp.zeros_like(rhs)
    residual = rhs
    direction = rhs
    norm_now = all_sum(jnp.sum(residual * residual).reshape(1))[0]
    for step in range(ITERS):
        image = operate(direction)
        alpha = norm_now / all_sum(jnp.sum(direction * image).reshape(1))[0]
        solution = solution + alpha * direction
        residual = residual - alpha * image
        if step + 1 < ITERS:
            norm_next = all_sum(jnp.sum(residual * residual).reshape(1))[0]
            direction = residual + norm_next / norm_now * direction
            norm_now = norm_next
    return (moved + solution, velocity_out, history_new.reshape(hist, rows, cols), residual)


def solution(mesh):
    return jax.shard_map(
        shards,
        mesh=mesh,
        in_specs=(
            P(None, "px", "py"),
            P(None, "px", "py"),
            P(None, "px", "py"),
            P(None, "px", "py"),
            P(None, "px", "py"),
            P(None, "px", "py"),
            P("px", "py", None, None),
            P(),
            P(),
            P("px", "py", None),
        ),
        out_specs=(
            P(None, "px", "py"),
            P(None, "px", "py"),
            P(None, "px", "py"),
            P(None, "px", "py"),
        ),
        check_vma=False,
    )
```

time: 432 us -> 241 us (0.56)
  blocking collectives: 207 us -> 0 us
  starting transfers between devices: 49.9 us -> 149 us
  local copies, waits for them, and re-layouts: 60.6 us -> 18.1 us
  waiting for transfers between devices: 66.5 us -> 25.6 us
  between operations: 5.17 us -> 28.8 us
  other arithmetic: 26.2 us -> 4.26 us
    psum x3 -> x0, blocking collectives: 207 us -> none  [global_sum(): return lax.psum(value, ('px', 'py'))]
    ppermute x0 -> x40, starting transfers between devices: none -> 107 us  [all_sum(): total = total + lax.ppermute(value, axis, pairs)]
    all_to_all x2 -> x1, waiting for transfers between devices: 57.7 us -> 0.01 us  [shards(): lax.all_to_all(held, ('px', 'py'), split_axis=1, concat_axis=1, tiled=True)]
    reshape x4 -> x1, local copies, waits for them, and re-layouts: 15.6 us -> 1.04 us  [shards(): held = recv_contact.reshape(hist, devices, width)]
    concatenate x2 -> x1, other arithmetic: 12.4 us -> 0.01 us  [shards(): tall = jnp.concatenate([lower_row, weights], axis=1)]
    ppermute x6, waiting for transfers between devices: 5.26 us -> 17 us  [with_halo(): after = lax.ppermute(leading, axis, down)]
    add x3 -> x0, local copies, waits for them, and re-layouts: 9.35 us -> none  [form(): stiff_base.reshape(576, 1) + jnp.dot(pairs.T, weights, precision=HIGH)]
    dot_general x2 -> x0, other arithmetic: 8.07 us -> none  [with_tangent(): return jnp.einsum('abxy,bxy->axy', extended, shells, precision=HIGH)]
  transfers between devices with their start and end apart: 16 -> 55, of which waited for: 8 -> 11; matrix products, arithmetic and copies ran while one was open for 11% -> 4% of each run, Pallas kernels for 0% -> 0%
where the time goes in v1:
time: 241 us; the launch traced here: 240 us
  starting transfers between devices  149 us (62%)
  between operations  28.8 us (12%)
  waiting for transfers between devices  25.6 us (11%)
  local copies, waits for them, and re-layouts  18.1 us (8%)
  matrix products  14 us (6%)
  other arithmetic  4.26 us (2%)
    ppermute x40, starting transfers between devices, all_sum(): total = total + lax.ppermute(value, axis, pairs)  107 us
    ppermute x6, waiting for transfers between devices, with_halo(): after = lax.ppermute(leading, axis, down)  17 us
    all_to_all x1, starting transfers between devices, shards(): lax.all_to_all(held, ('px', 'py'), split_axis=1, concat_axis=1, tiled=True)  14.2 us
    ppermute x6, starting transfers between devices, with_halo(): before = lax.ppermute(last, axis, up)  14.1 us
    ppermute x6, starting transfers between devices, with_halo(): after = lax.ppermute(leading, axis, down)  7.74 us
    unnamed x45, local copies, waits for them, and re-layouts  7.66 us
    scatter x1, local copies, waits for them, and re-layouts, shards(): contact = contact_home.reshape(hist, cells).at[:, targets].set(arrived.re...  6.8 us
    ppermute x2, starting transfers between devices, shifted(): return lax.ppermute(shard, axis, pairs)  6.15 us
  transfers between devices with their start and end apart: 55, of which 11 were waited for; matrix products, arithmetic and copies ran while one was open for 4% of the time, Pallas kernels for 0%

profile of v1, /device:TPU:0, one launch (start us, length us, event | category | flops | bytes accessed | tf_op | source)
XLA Modules:
  0.0 239.8 jit_solution(18399872455715493709)
XLA Ops:
  6.4 14.2 %all-to-all-start = ((f32[128,128,9]{0,2,1:T(8,128)}), f32[128,128,9]{0,2,1:T(8,128)S(1)}, u32[]{:S(2)}, u32[]{:S(2)}) async-start(f32[128,128,9]{0,2,1:T(8,128)} %reshape.118), calls=%async_computation | async-start | bytes 2097152 | tf_op jit(solution)/shard_map/all_to_all | solution.py:93
  25.0 5.6 %collective-permute-done.2 = f32[6,18,1]{2,0,1:T(8,128)S(1)} collective-permute-done((f32[6,18,1]{2,0,1:T(8,128)S(1)}, f32[6,18,1]{2,0,1:T(8,128)S(1)}, u32[]{:S(2)}, u32[]{:S(2)}) %collective-permute-start.2) | collective-permute-done | bytes 464 | tf_op jit(solution)/shard_map/ppermute | solution.py:21
  37.4 4.1 %collective-permute-done.17 = f32[6,1,128]{2,0,1:T(8,128)S(1)} collective-permute-done((f32[6,1,128]{2,0,1:T(8,128)S(1)}, f32[6,1,128]{2,0,1:T(8,128)S(1)}, u32[]{:S(2)}, u32[]{:S(2)}) %collective-permute-start.17) | collective-permute-done | bytes 3104 | tf_op jit(solution)/shard_map/ppermute | solution.py:22
  42.3 4.1 %collective-permute-start.18 = (f32[6,18,1]{2,0,1:T(8,128)}, f32[6,18,1]{2,0,1:T(8,128)}, u32[]{:S(2)}, u32[]{:S(2)}) collective-permute-start(f32[6,18,1]{2,0,1:T(8,128)} %get-tuple-element.33), channel_id=1, source_target_pairs={{0,1},{1,2},{2,3},{3,4},{4,5},{5,6},{6,7},{7,8},{8,9},{9,10},{10,1... | collective-permute-start | bytes 1304 | tf_op jit(solution)/shard_map/ppermute | solution.py:21
  54.9 6.8 %scatter_custom_fusion = f32[128,2048]{0,1:T(8,128)S(1)} fusion(f32[128,2048]{0,1:T(8,128)S(1)} %bitcast.74, s32[1152]{0:T(1024)} %fusion.35, f32[128,1152]{0,1:T(8,128)} %reshape.126), kind=kCustom, calls=%fused_computation.18 | custom fusion | bytes 1638400 | tf_op jit(solution)/shard_map/scatter | solution.py:108
  62.6 3.8 %fusion.8 = (f32[128,2048]{0,1:T(8,128)S(1)}, f32[128,2048]{0,1:T(8,128)S(1)}) fusion(f32[128,2048]{0,1:T(8,128)} %copy-done.1, f32[128,2048]{0,1:T(8,128)S(1)} %bitcast.73, f32[128,24]{0,1:T(8,128)S(1)} %copy-done, f32[6,18,1]{2,0,1:T(8,128)} %copy-done.7, f32[6,18,128]{2,0,1:T(8,128)} %copy-done.2, f32[6,17,129]{2,0,1:T(8,128)} %copy-done.5, ...), kind=kOutput, calls=%fused_computation.17 | convolution fusion | flops 77840384 | bytes 4368016 | tf_op jit(solution)/shard_map/dot_general | solution.py:103
  70.2 3.3 %collective-permute-start.15 = (f32[128,17,1]{0,2,1:T(1,128)S(1)}, f32[128,17,1]{0,2,1:T(1,128)S(1)}, u32[]{:S(2)}, u32[]{:S(2)}) collective-permute-start(f32[128,17,1]{0,2,1:T(1,128)S(1)} %pad_maximum_fusion.12), channel_id=1, source_target_pairs={{0,1},{1,2},{2,3},{3,4},{4,5},{5,6},{6,7},{7,8},{8,9},{9,10},{10,1... | collective-permute-start | bytes 26120 | tf_op jit(solution)/shard_map/ppermute | solution.py:30
  89.9 4.2 %collective-permute-start.23 = (f32[1]{0:T(128)}, f32[1]{0:T(128)}, u32[]{:S(2)}, u32[]{:S(2)}) collective-permute-start(f32[1]{0:T(128)} %add.215), channel_id=1, source_target_pairs={{0,64},{16,80},{32,96},{48,112},{64,0},{80,16},{96,32},{112,48},{1... | collective-permute-start | bytes 20 | tf_op jit(solution)/shard_map/ppermute | solution.py:45
  99.3 3.7 %collective-permute-start.24 = (f32[1]{0:T(128)}, f32[1]{0:T(128)}, u32[]{:S(2)}, u32[]{:S(2)}) collective-permute-start(f32[1]{0:T(128)} %add.216), channel_id=1, source_target_pairs={{0,1},{1,2},{2,3},{3,0},{4,5},{5,6},{6,7},{7,4},{8,9},{9,10},{10,1... | collective-permute-start | bytes 20 | tf_op jit(solution)/shard_map/ppermute | solution.py:45
  102.9 7.0 %collective-permute-start.25 = (f32[1]{0:T(128)}, f32[1]{0:T(128)}, u32[]{:S(2)}, u32[]{:S(2)}) collective-permute-start(f32[1]{0:T(128)} %add.216), channel_id=1, source_target_pairs={{0,2},{1,3},{2,0},{3,1},{4,6},{5,7},{6,4},{7,5},{8,10},{9,11},{10,... | collective-permute-start | bytes 20 | tf_op jit(solution)/shard_map/ppermute | solution.py:45
  116.6 4.0 %collective-permute-start.10 = (f32[1]{0:T(128)}, f32[1]{0:T(128)}, u32[]{:S(2)}, u32[]{:S(2)}) collective-permute-start(f32[1]{0:T(128)} %add.198), channel_id=1, source_target_pairs={{0,3},{1,0},{2,1},{3,2},{4,7},{5,4},{6,5},{7,6},{8,11},{9,8},{10,9... | collective-permute-start | bytes 20 | tf_op jit(solution)/shard_map/ppermute | solution.py:45
  122.4 3.4 %collective-permute-start.27 = (f32[1]{0:T(128)}, f32[1]{0:T(128)}, u32[]{:S(2)}, u32[]{:S(2)}) collective-permute-start(f32[1]{0:T(128)} %add.219), channel_id=1, source_target_pairs={{0,4},{1,5},{2,6},{3,7},{4,8},{5,9},{6,10},{7,11},{8,12},{9,13},{1... | collective-permute-start | bytes 20 | tf_op jit(solution)/shard_map/ppermute | solution.py:45
  125.8 4.9 %collective-permute-start.28 = (f32[1]{0:T(128)}, f32[1]{0:T(128)}, u32[]{:S(2)}, u32[]{:S(2)}) collective-permute-start(f32[1]{0:T(128)} %add.219), channel_id=1, source_target_pairs={{0,8},{1,9},{2,10},{3,11},{4,12},{5,13},{6,14},{7,15},{8,0},{9,1},... | collective-permute-start | bytes 20 | tf_op jit(solution)/shard_map/ppermute | solution.py:45
  138.9 3.7 %collective-permute-start.13 = (f32[1]{0:T(128)}, f32[1]{0:T(128)}, u32[]{:S(2)}, u32[]{:S(2)}) collective-permute-start(f32[1]{0:T(128)} %add.201), channel_id=1, source_target_pairs={{0,12},{1,13},{2,14},{3,15},{4,0},{5,1},{6,2},{7,3},{8,4},{9,5},{1... | collective-permute-start | bytes 20 | tf_op jit(solution)/shard_map/ppermute | solution.py:45
  152.8 4.8 %collective-permute-start.33 = (f32[1]{0:T(128)}, f32[1]{0:T(128)}, u32[]{:S(2)}, u32[]{:S(2)}) collective-permute-start(f32[1]{0:T(128)} %add.225), channel_id=1, source_target_pairs={{0,64},{16,80},{32,96},{48,112},{64,0},{80,16},{96,32},{112,48},{1... | collective-permute-start | bytes 20 | tf_op jit(solution)/shard_map/ppermute | solution.py:45
  160.0 3.3 %collective-permute-start.35 = (f32[1]{0:T(128)}, f32[1]{0:T(128)}, u32[]{:S(2)}, u32[]{:S(2)}) collective-permute-start(f32[1]{0:T(128)} %add.226), channel_id=1, source_target_pairs={{0,2},{1,3},{2,0},{3,1},{4,6},{5,7},{6,4},{7,5},{8,10},{9,11},{10,... | collective-permute-start | bytes 20 | tf_op jit(solution)/shard_map/ppermute | solution.py:45
  170.2 3.4 %collective-permute-start.38 = (f32[1]{0:T(128)}, f32[1]{0:T(128)}, u32[]{:S(2)}, u32[]{:S(2)}) collective-permute-start(f32[1]{0:T(128)} %add.229), channel_id=1, source_target_pairs={{0,8},{1,9},{2,10},{3,11},{4,12},{5,13},{6,14},{7,15},{8,0},{9,1},... | collective-permute-start | bytes 20 | tf_op jit(solution)/shard_map/ppermute | solution.py:45
  173.6 3.9 %collective-permute-start.39 = (f32[1]{0:T(128)}, f32[1]{0:T(128)}, u32[]{:S(2)}, u32[]{:S(2)}) collective-permute-start(f32[1]{0:T(128)} %add.229), channel_id=1, source_target_pairs={{0,12},{1,13},{2,14},{3,15},{4,0},{5,1},{6,2},{7,3},{8,4},{9,5},{1... | collective-permute-start | bytes 20 | tf_op jit(solution)/shard_map/ppermute | solution.py:45
  182.1 3.7 %collective-permute-done.41 = f32[6,1,128]{2,0,1:T(8,128)S(1)} collective-permute-done((f32[6,1,128]{2,0,1:T(8,128)S(1)}, f32[6,1,128]{2,0,1:T(8,128)S(1)}, u32[]{:S(2)}, u32[]{:S(2)}) %collective-permute-start.41) | collective-permute-done | bytes 3104 | tf_op jit(solution)/shard_map/ppermute | solution.py:22
  191.5 3.6 %collective-permute-done.43 = f32[6,18,1]{2,0,1:T(8,128)S(1)} collective-permute-done((f32[6,18,1]{2,0,1:T(8,128)S(1)}, f32[6,18,1]{2,0,1:T(8,128)S(1)}, u32[]{:S(2)}, u32[]{:S(2)}) %collective-permute-start.43) | collective-permute-done | bytes 464 | tf_op jit(solution)/shard_map/ppermute | solution.py:22
  207.3 4.8 %collective-permute-start.47 = (f32[1]{0:T(128)}, f32[1]{0:T(128)}, u32[]{:S(2)}, u32[]{:S(2)}) collective-permute-start(f32[1]{0:T(128)} %add.240), channel_id=1, source_target_pairs={{0,64},{16,80},{32,96},{48,112},{64,0},{80,16},{96,32},{112,48},{1... | collective-permute-start | bytes 20 | tf_op jit(solution)/shard_map/ppermute | solution.py:45
  215.5 5.3 %collective-permute-start.49 = (f32[1]{0:T(128)}, f32[1]{0:T(128)}, u32[]{:S(2)}, u32[]{:S(2)}) collective-permute-start(f32[1]{0:T(128)} %add.241), channel_id=1, source_target_pairs={{0,2},{1,3},{2,0},{3,1},{4,6},{5,7},{6,4},{7,5},{8,10},{9,11},{10,... | collective-permute-start | bytes 20 | tf_op jit(solution)/shard_map/ppermute | solution.py:45
  227.4 4.5 %collective-permute-start.52 = (f32[1]{0:T(128)}, f32[1]{0:T(128)}, u32[]{:S(2)}, u32[]{:S(2)}) collective-permute-start(f32[1]{0:T(128)} %add.244), channel_id=1, source_target_pairs={{0,8},{1,9},{2,10},{3,11},{4,12},{5,13},{6,14},{7,15},{8,0},{9,1},... | collective-permute-start | bytes 20 | tf_op jit(solution)/shard_map/ppermute | solution.py:45
  232.0 3.9 %collective-permute-start.53 = (f32[1]{0:T(128)}, f32[1]{0:T(128)}, u32[]{:S(2)}, u32[]{:S(2)}) collective-permute-start(f32[1]{0:T(128)} %add.244), channel_id=1, source_target_pairs={{0,12},{1,13},{2,14},{3,15},{4,0},{5,1},{6,2},{7,3},{8,4},{9,5},{1... | collective-permute-start | bytes 20 | tf_op jit(solution)/shard_map/ppermute | solution.py:45
  (169 shorter events, 97.2 us)
Async XLA Ops:
  1.4 19.2 %collective-permute-start = (f32[6,1,128]{2,0,1:T(8,128)S(1)}, f32[6,1,128]{2,0,1:T(8,128)S(1)}, u32[]{:S(2)}, u32[]{:S(2)}) collective-permute-start(f32[6,1,128]{2,0,1:T(8,128)S(1)} %copy.57), channel_id=1, source_target_pairs={{0,16},{16,32},{32,48},{48,64},{64,80},{80,96},{96,112},{1,17},{17... | collective-permute-start | bytes 9224 | tf_op jit(solution)/shard_map/ppermute | solution.py:21
  2.7 17.9 %collective-permute-start.1 = (f32[6,1,128]{2,0,1:T(8,128)S(1)}, f32[6,1,128]{2,0,1:T(8,128)S(1)}, u32[]{:S(2)}, u32[]{:S(2)}) collective-permute-start(f32[6,1,128]{2,0,1:T(8,128)S(1)} %copy.58), channel_id=1, source_target_pairs={{16,0},{32,16},{48,32},{64,48},{80,64},{96,80},{112,96},{17,1},{33... | collective-permute-start | bytes 9224 | tf_op jit(solution)/shard_map/ppermute | solution.py:22
  6.4 47.6 %all-to-all-start = ((f32[128,128,9]{0,2,1:T(8,128)}), f32[128,128,9]{0,2,1:T(8,128)S(1)}, u32[]{:S(2)}, u32[]{:S(2)}) async-start(f32[128,128,9]{0,2,1:T(8,128)} %reshape.118), calls=%async_computation | async-start | bytes 2097152 | tf_op jit(solution)/shard_map/all_to_all | solution.py:93
  20.7 9.8 %collective-permute-start.2 = (f32[6,18,1]{2,0,1:T(8,128)S(1)}, f32[6,18,1]{2,0,1:T(8,128)S(1)}, u32[]{:S(2)}, u32[]{:S(2)}) collective-permute-start(f32[6,18,1]{2,0,1:T(8,128)S(1)} %get-tuple-element.37), channel_id=1, source_target_pairs={{0,1},{1,2},{2,3},{3,4},{4,5},{5,6},{6,7},{7,8},{8,9},{9,10},{10,1... | collective-permute-start | bytes 1304 | tf_op jit(solution)/shard_map/ppermute | solution.py:21
  23.6 10.0 %collective-permute-start.3 = (f32[6,18,1]{2,0,1:T(8,128)S(1)}, f32[6,18,1]{2,0,1:T(8,128)S(1)}, u32[]{:S(2)}, u32[]{:S(2)}) collective-permute-start(f32[6,18,1]{2,0,1:T(8,128)S(1)} %get-tuple-element.38), channel_id=1, source_target_pairs={{1,0},{2,1},{3,2},{4,3},{5,4},{6,5},{7,6},{8,7},{9,8},{10,9},{11,1... | collective-permute-start | bytes 1304 | tf_op jit(solution)/shard_map/ppermute | solution.py:22
  85.6 8.5 %collective-permute-start.4 = (f32[1]{0:T(128)}, f32[1]{0:T(128)}, u32[]{:S(2)}, u32[]{:S(2)}) collective-permute-start(f32[1]{0:T(128)} %bitcast.2), channel_id=1, source_target_pairs={{0,16},{16,32},{32,48},{48,0},{64,80},{80,96},{96,112},{112,64},{1... | collective-permute-start | bytes 20 | tf_op jit(solution)/shard_map/ppermute | solution.py:45
  85.6 9.7 %collective-permute-start.5 = (f32[1]{0:T(128)}, f32[1]{0:T(128)}, u32[]{:S(2)}, u32[]{:S(2)}) collective-permute-start(f32[1]{0:T(128)} %bitcast.2), channel_id=1, source_target_pairs={{0,32},{16,48},{32,0},{48,16},{64,96},{80,112},{96,64},{112,80},{1... | collective-permute-start | bytes 20 | tf_op jit(solution)/shard_map/ppermute | solution.py:45
  86.0 10.0 %collective-permute-start.6 = (f32[1]{0:T(128)}, f32[1]{0:T(128)}, u32[]{:S(2)}, u32[]{:S(2)}) collective-permute-start(f32[1]{0:T(128)} %bitcast.2), channel_id=1, source_target_pairs={{0,48},{16,0},{32,16},{48,32},{64,112},{80,64},{96,80},{112,96},{1... | collective-permute-start | bytes 20 | tf_op jit(solution)/shard_map/ppermute | solution.py:45
  89.9 8.8 %collective-permute-start.23 = (f32[1]{0:T(128)}, f32[1]{0:T(128)}, u32[]{:S(2)}, u32[]{:S(2)}) collective-permute-start(f32[1]{0:T(128)} %add.215), channel_id=1, source_target_pairs={{0,64},{16,80},{32,96},{48,112},{64,0},{80,16},{96,32},{112,48},{1... | collective-permute-start | bytes 20 | tf_op jit(solution)/shard_map/ppermute | solution.py:45
  96.6 15.0 %collective-permute-start.7 = (f32[1]{0:T(128)}, f32[1]{0:T(128)}, u32[]{:S(2)}, u32[]{:S(2)}) collective-permute-start(f32[1]{0:T(128)} %add.197), channel_id=1, source_target_pairs={{0,64},{16,80},{32,96},{48,112},{64,0},{80,16},{96,32},{112,48},{1... | collective-permute-start | bytes 20 | tf_op jit(solution)/shard_map/ppermute | solution.py:45
  99.3 17.3 %collective-permute-start.24 = (f32[1]{0:T(128)}, f32[1]{0:T(128)}, u32[]{:S(2)}, u32[]{:S(2)}) collective-permute-start(f32[1]{0:T(128)} %add.216), channel_id=1, source_target_pairs={{0,1},{1,2},{2,3},{3,0},{4,5},{5,6},{6,7},{7,4},{8,9},{9,10},{10,1... | collective-permute-start | bytes 20 | tf_op jit(solution)/shard_map/ppermute | solution.py:45
  102.9 18.3 %collective-permute-start.25 = (f32[1]{0:T(128)}, f32[1]{0:T(128)}, u32[]{:S(2)}, u32[]{:S(2)}) collective-permute-start(f32[1]{0:T(128)} %add.216), channel_id=1, source_target_pairs={{0,2},{1,3},{2,0},{3,1},{4,6},{5,7},{6,4},{7,5},{8,10},{9,11},{10,... | collective-permute-start | bytes 20 | tf_op jit(solution)/shard_map/ppermute | solution.py:45
  110.0 11.8 %collective-permute-start.26 = (f32[1]{0:T(128)}, f32[1]{0:T(128)}, u32[]{:S(2)}, u32[]{:S(2)}) collective-permute-start(f32[1]{0:T(128)} %add.216), channel_id=1, source_target_pairs={{0,3},{1,0},{2,1},{3,2},{4,7},{5,4},{6,5},{7,6},{8,11},{9,8},{10,9... | collective-permute-start | bytes 20 | tf_op jit(solution)/shard_map/ppermute | solution.py:45
  112.3 18.5 %collective-permute-start.8 = (f32[1]{0:T(128)}, f32[1]{0:T(128)}, u32[]{:S(2)}, u32[]{:S(2)}) collective-permute-start(f32[1]{0:T(128)} %add.198), channel_id=1, source_target_pairs={{0,1},{1,2},{2,3},{3,0},{4,5},{5,6},{6,7},{7,4},{8,9},{9,10},{10,1... | collective-permute-start | bytes 20 | tf_op jit(solution)/shard_map/ppermute | solution.py:45
  115.3 18.2 %collective-permute-start.9 = (f32[1]{0:T(128)}, f32[1]{0:T(128)}, u32[]{:S(2)}, u32[]{:S(2)}) collective-permute-start(f32[1]{0:T(128)} %add.198), channel_id=1, source_target_pairs={{0,2},{1,3},{2,0},{3,1},{4,6},{5,7},{6,4},{7,5},{8,10},{9,11},{10,... | collective-permute-start | bytes 20 | tf_op jit(solution)/shard_map/ppermute | solution.py:45
  116.6 17.4 %collective-permute-start.10 = (f32[1]{0:T(128)}, f32[1]{0:T(128)}, u32[]{:S(2)}, u32[]{:S(2)}) collective-permute-start(f32[1]{0:T(128)} %add.198), channel_id=1, source_target_pairs={{0,3},{1,0},{2,1},{3,2},{4,7},{5,4},{6,5},{7,6},{8,11},{9,8},{10,9... | collective-permute-start | bytes 20 | tf_op jit(solution)/shard_map/ppermute | solution.py:45
  122.4 16.5 %collective-permute-start.27 = (f32[1]{0:T(128)}, f32[1]{0:T(128)}, u32[]{:S(2)}, u32[]{:S(2)}) collective-permute-start(f32[1]{0:T(128)} %add.219), channel_id=1, source_target_pairs={{0,4},{1,5},{2,6},{3,7},{4,8},{5,9},{6,10},{7,11},{8,12},{9,13},{1... | collective-permute-start | bytes 20 | tf_op jit(solution)/shard_map/ppermute | solution.py:45
  125.8 18.0 %collective-permute-start.28 = (f32[1]{0:T(128)}, f32[1]{0:T(128)}, u32[]{:S(2)}, u32[]{:S(2)}) collective-permute-start(f32[1]{0:T(128)} %add.219), channel_id=1, source_target_pairs={{0,8},{1,9},{2,10},{3,11},{4,12},{5,13},{6,14},{7,15},{8,0},{9,1},... | collective-permute-start | bytes 20 | tf_op jit(solution)/shard_map/ppermute | solution.py:45
  130.7 13.8 %collective-permute-start.29 = (f32[1]{0:T(128)}, f32[1]{0:T(128)}, u32[]{:S(2)}, u32[]{:S(2)}) collective-permute-start(f32[1]{0:T(128)} %add.219), channel_id=1, source_target_pairs={{0,12},{1,13},{2,14},{3,15},{4,0},{5,1},{6,2},{7,3},{8,4},{9,5},{1... | collective-permute-start | bytes 20 | tf_op jit(solution)/shard_map/ppermute | solution.py:45
  134.7 8.4 %collective-permute-start.11 = (f32[1]{0:T(128)}, f32[1]{0:T(128)}, u32[]{:S(2)}, u32[]{:S(2)}) collective-permute-start(f32[1]{0:T(128)} %add.201), channel_id=1, source_target_pairs={{0,4},{1,5},{2,6},{3,7},{4,8},{5,9},{6,10},{7,11},{8,12},{9,13},{1... | collective-permute-start | bytes 20 | tf_op jit(solution)/shard_map/ppermute | solution.py:45
  168.0 9.5 %collective-permute-start.37 = (f32[1]{0:T(128)}, f32[1]{0:T(128)}, u32[]{:S(2)}, u32[]{:S(2)}) collective-permute-start(f32[1]{0:T(128)} %add.229), channel_id=1, source_target_pairs={{0,4},{1,5},{2,6},{3,7},{4,8},{5,9},{6,10},{7,11},{8,12},{9,13},{1... | collective-permute-start | bytes 20 | tf_op jit(solution)/shard_map/ppermute | solution.py:45
  213.2 9.4 %collective-permute-start.48 = (f32[1]{0:T(128)}, f32[1]{0:T(128)}, u32[]{:S(2)}, u32[]{:S(2)}) collective-permute-start(f32[1]{0:T(128)} %add.241), channel_id=1, source_target_pairs={{0,1},{1,2},{2,3},{3,0},{4,5},{5,6},{6,7},{7,4},{8,9},{9,10},{10,1... | collective-permute-start | bytes 20 | tf_op jit(solution)/shard_map/ppermute | solution.py:45
  225.1 10.8 %collective-permute-start.51 = (f32[1]{0:T(128)}, f32[1]{0:T(128)}, u32[]{:S(2)}, u32[]{:S(2)}) collective-permute-start(f32[1]{0:T(128)} %add.244), channel_id=1, source_target_pairs={{0,4},{1,5},{2,6},{3,7},{4,8},{5,9},{6,10},{7,11},{8,12},{9,13},{1... | collective-permute-start | bytes 20 | tf_op jit(solution)/shard_map/ppermute | solution.py:45
  227.4 9.1 %collective-permute-start.52 = (f32[1]{0:T(128)}, f32[1]{0:T(128)}, u32[]{:S(2)}, u32[]{:S(2)}) collective-permute-start(f32[1]{0:T(128)} %add.244), channel_id=1, source_target_pairs={{0,8},{1,9},{2,10},{3,11},{4,12},{5,13},{6,14},{7,15},{8,0},{9,1},... | collective-permute-start | bytes 20 | tf_op jit(solution)/shard_map/ppermute | solution.py:45
  (48 other events, 528.5 us)

commit v2 on v1

--- a/solution.py
+++ b/solution.py
@@ -120,19 +120,31 @@
         return scatter_nodes(forces + with_base(shells))
 
     rhs = load - force_start
-    solution = jnp.zeros_like(rhs)
-    residual = rhs
-    direction = rhs
-    norm_now = all_sum(jnp.sum(residual * residual).reshape(1))[0]
-    for step in range(ITERS):
-        image = operate(direction)
-        alpha = norm_now / all_sum(jnp.sum(direction * image).reshape(1))[0]
-        solution = solution + alpha * direction
-        residual = residual - alpha * image
-        if step + 1 < ITERS:
-            norm_next = all_sum(jnp.sum(residual * residual).reshape(1))[0]
-            direction = residual + norm_next / norm_now * direction
-            norm_now = norm_next
+    image = operate(rhs)
+    again = operate(image)
+    first = all_sum(jnp.stack([jnp.sum(rhs * rhs), jnp.sum(rhs * image)]))
+    norm_now, curvature = first[0], first[1]
+    alpha = norm_now / curvature
+    residual = rhs - alpha * image
+    bent = image - alpha * again
+    second = all_sum(
+        jnp.stack(
+            [
+                jnp.sum(residual * residual),
+                jnp.sum(residual * bent),
+                jnp.sum(residual * image),
+                jnp.sum(rhs * bent),
+            ]
+        )
+    )
+    norm_next = second[0]
+    beta = norm_next / norm_now
+    direction = residual + beta * rhs
+    turned = bent + beta * image
+    curvature_next = second[1] + beta * (second[2] + second[3]) + beta * beta * curvature
+    alpha_next = norm_next / curvature_next
+    solution = alpha * rhs + alpha_next * direction
+    residual = residual - alpha_next * turned
     return (moved + solution, velocity_out, history_new.reshape(hist, rows, cols), residual)
 
 

time: 241 us -> 172 us (0.71)
  starting transfers between devices: 149 us -> 86.6 us
  between operations: 28.8 us -> 6.97 us
  other arithmetic: 4.26 us -> 11.5 us
  waiting for transfers between devices: 25.6 us -> 32 us
    ppermute x40 -> x20, starting transfers between devices: 107 us -> 43.3 us  [all_sum(): total = total + lax.ppermute(value, axis, pairs)]
    ppermute x40 -> x20, waiting for transfers between devices: 1.57 us -> 13.9 us  [all_sum(): total = total + lax.ppermute(value, axis, pairs)]
    ppermute x6, waiting for transfers between devices: 17 us -> 11.7 us  [with_halo(): after = lax.ppermute(leading, axis, down)]
    add x1 -> x8, other arithmetic: 0.01 us -> 3.93 us  [all_sum(): total = total + lax.ppermute(value, axis, pairs)]
    another operation x0 -> x2, other arithmetic: none -> 3.9 us  [the longest x1 2.53 us: shards(): jnp.stack([jnp.sum(residual * residual), jnp.sum(residual * bent), jnp.su...]
    unnamed x45 -> x51, local copies, waits for them, and re-layouts: 7.66 us -> 8.83 us
  transfers between devices with their start and end apart: 55 -> 35, of which waited for: 11 -> 19; matrix products, arithmetic and copies ran while one was open for 4% -> 7% of each run, Pallas kernels for 0% -> 0%
where the time goes in v2:
time: 172 us; the launch traced here: 171 us
  starting transfers between devices  86.6 us (50%)
  waiting for transfers between devices  32 us (19%)
  local copies, waits for them, and re-layouts  19.9 us (12%)
  matrix products  13.9 us (8%)
  other arithmetic  11.5 us (7%)
  between operations  6.97 us (4%)
    ppermute x20, starting transfers between devices, all_sum(): total = total + lax.ppermute(value, axis, pairs)  43.3 us
    ppermute x6, starting transfers between devices, with_halo(): before = lax.ppermute(last, axis, up)  14.4 us
    all_to_all x1, starting transfers between devices, shards(): lax.all_to_all(held, ('px', 'py'), split_axis=1, concat_axis=1, tiled=True)  14.2 us
    ppermute x20, waiting for transfers between devices, all_sum(): total = total + lax.ppermute(value, axis, pairs)  13.9 us
    ppermute x6, waiting for transfers between devices, with_halo(): after = lax.ppermute(leading, axis, down)  11.7 us
    unnamed x51, local copies, waits for them, and re-layouts  8.83 us
    ppermute x6, starting transfers between devices, with_halo(): after = lax.ppermute(leading, axis, down)  7.97 us
    scatter x1, local copies, waits for them, and re-layouts, shards(): contact = contact_home.reshape(hist, cells).at[:, targets].set(arrived.re...  6.8 us
  transfers between devices with their start and end apart: 35, of which 19 were waited for; matrix products, arithmetic and copies ran while one was open for 7% of the time, Pallas kernels for 0%

profile of v2, /device:TPU:0, one launch (start us, length us, event | category | flops | bytes accessed | tf_op | source)
XLA Modules:
  0.0 170.9 jit_solution(14650446645190759067)
XLA Ops:
  6.4 14.2 %all-to-all-start = ((f32[128,128,9]{0,2,1:T(8,128)}), f32[128,128,9]{0,2,1:T(8,128)S(1)}, u32[]{:S(2)}, u32[]{:S(2)}) async-start(f32[128,128,9]{0,2,1:T(8,128)} %reshape.103), calls=%async_computation | async-start | bytes 2097152 | tf_op jit(solution)/shard_map/all_to_all | solution.py:93
  20.7 2.9 %collective-permute-start.2 = (f32[6,18,1]{2,0,1:T(8,128)S(1)}, f32[6,18,1]{2,0,1:T(8,128)S(1)}, u32[]{:S(2)}, u32[]{:S(2)}) collective-permute-start(f32[6,18,1]{2,0,1:T(8,128)S(1)} %get-tuple-element.41), channel_id=1, source_target_pairs={{0,1},{1,2},{2,3},{3,4},{4,5},{5,6},{6,7},{7,8},{8,9},{9,10},{10,1... | collective-permute-start | bytes 1304 | tf_op jit(solution)/shard_map/ppermute | solution.py:21
  25.0 5.6 %collective-permute-done.2 = f32[6,18,1]{2,0,1:T(8,128)S(1)} collective-permute-done((f32[6,18,1]{2,0,1:T(8,128)S(1)}, f32[6,18,1]{2,0,1:T(8,128)S(1)}, u32[]{:S(2)}, u32[]{:S(2)}) %collective-permute-start.2) | collective-permute-done | bytes 464 | tf_op jit(solution)/shard_map/ppermute | solution.py:21
  30.6 3.1 %collective-permute-done.3 = f32[6,18,1]{2,0,1:T(8,128)S(1)} collective-permute-done((f32[6,18,1]{2,0,1:T(8,128)S(1)}, f32[6,18,1]{2,0,1:T(8,128)S(1)}, u32[]{:S(2)}, u32[]{:S(2)}) %collective-permute-start.3) | collective-permute-done | bytes 464 | tf_op jit(solution)/shard_map/ppermute | solution.py:22
  37.4 4.1 %collective-permute-done.7 = f32[6,1,128]{2,0,1:T(8,128)S(1)} collective-permute-done((f32[6,1,128]{2,0,1:T(8,128)S(1)}, f32[6,1,128]{2,0,1:T(8,128)S(1)}, u32[]{:S(2)}, u32[]{:S(2)}) %collective-permute-start.7) | collective-permute-done | bytes 3104 | tf_op jit(solution)/shard_map/ppermute | solution.py:22
  42.1 3.4 %collective-permute-start.8 = (f32[6,18,1]{2,0,1:T(8,128)S(1)}, f32[6,18,1]{2,0,1:T(8,128)S(1)}, u32[]{:S(2)}, u32[]{:S(2)}) collective-permute-start(f32[6,18,1]{2,0,1:T(8,128)S(1)} %get-tuple-element.37), channel_id=1, source_target_pairs={{0,1},{1,2},{2,3},{3,4},{4,5},{5,6},{6,7},{7,8},{8,9},{9,10},{10,1... | collective-permute-start | bytes 1304 | tf_op jit(solution)/shard_map/ppermute | solution.py:21
  53.9 6.8 %scatter_custom_fusion = f32[128,2048]{0,1:T(8,128)S(1)} fusion(f32[128,2048]{0,1:T(8,128)S(1)} %bitcast.78, s32[1152]{0:T(1024)} %fusion.37, f32[128,1152]{0,1:T(8,128)} %reshape.108), kind=kCustom, calls=%fused_computation.18 | custom fusion | bytes 1638400 | tf_op jit(solution)/shard_map/scatter | solution.py:108
  61.7 3.8 %fusion.8 = (f32[128,2048]{0,1:T(8,128)S(1)}, f32[128,2048]{0,1:T(8,128)S(1)}) fusion(f32[128,2048]{0,1:T(8,128)} %copy-done.1, f32[128,2048]{0,1:T(8,128)S(1)} %bitcast.76, f32[128,24]{0,1:T(8,128)S(1)} %copy-done, f32[6,18,1]{2,0,1:T(8,128)} %copy-done.7, f32[6,18,128]{2,0,1:T(8,128)} %copy-done.2, f32[6,17,129]{2,0,1:T(8,128)} %copy-done.5, ...), kind=kOutput, calls=%fused_computation.17 | convolution fusion | flops 77840384 | bytes 4368016 | tf_op jit(solution)/shard_map/dot_general | solution.py:103
  65.5 2.8 %collective-permute-start.4 = (f32[128,1,128]{0,2,1:T(8,128)S(1)}, f32[128,1,128]{0,2,1:T(8,128)S(1)}, u32[]{:S(2)}, u32[]{:S(2)}) collective-permute-start(f32[128,1,128]{0,2,1:T(8,128)S(1)} %slice.204), channel_id=1, source_target_pairs={{0,16},{16,32},{32,48},{48,64},{64,80},{80,96},{96,112},{1,17},{17... | collective-permute-start | bytes 196616 | tf_op jit(solution)/shard_map/ppermute | solution.py:30
  69.2 3.9 %collective-permute-start.5 = (f32[128,17,1]{0,2,1:T(1,128)S(1)}, f32[128,17,1]{0,2,1:T(1,128)S(1)}, u32[]{:S(2)}, u32[]{:S(2)}) collective-permute-start(f32[128,17,1]{0,2,1:T(1,128)S(1)} %pad_maximum_fusion.12), channel_id=1, source_target_pairs={{0,1},{1,2},{2,3},{3,4},{4,5},{5,6},{6,7},{7,8},{8,9},{9,10},{10,1... | collective-permute-start | bytes 26120 | tf_op jit(solution)/shard_map/ppermute | solution.py:30
  75.1 2.3 %fusion.2 = f32[128,17,129]{0,2,1:T(8,128)S(1)} fusion(f32[128,16,128]{0,2,1:T(8,128)S(1)} %bitcast.74, f32[128,1,128]{0,2,1:T(8,128)S(1)} %collective-permute-done.4, f32[128,17,1]{0,2,1:T(1,128)S(1)} %collective-permute-done.5, f32[6,17,129]{2,0,1:T(8,128)S(1)} %get-tuple-element.57, f32[6,17,129]{2,0,1:T(8,128)S(1)} %get-tuple-element.58, ...), kind=kOutput, calls=%fused_computation.7 | convolution fusion | flops 81842760 | bytes 2468448 | tf_op jit(solution)/shard_map/hb,bxy->hxy/dot_general | solution.py:118
  83.4 2.6 %collective-permute-start.11 = (f32[2]{0:T(128)S(1)}, f32[2]{0:T(128)S(1)}, u32[]{:S(2)}, u32[]{:S(2)}) collective-permute-start(f32[2]{0:T(128)S(1)} %pad_maximum_fusion.13), channel_id=1, source_target_pairs={{0,32},{16,48},{32,0},{48,16},{64,96},{80,112},{96,64},{112,80},{1... | collective-permute-start | bytes 32 | tf_op jit(solution)/shard_map/ppermute | solution.py:45
  91.4 4.7 %collective-permute-start.13 = (f32[2]{0:T(128)S(1)}, f32[2]{0:T(128)S(1)}, u32[]{:S(2)}, u32[]{:S(2)}) collective-permute-start(f32[2]{0:T(128)S(1)} %add_add_fusion.6), channel_id=1, source_target_pairs={{0,64},{16,80},{32,96},{48,112},{64,0},{80,16},{96,32},{112,48},{1... | collective-permute-start | bytes 32 | tf_op jit(solution)/shard_map/ppermute | solution.py:45
  99.7 5.7 %collective-permute-start.15 = (f32[2]{0:T(128)S(1)}, f32[2]{0:T(128)S(1)}, u32[]{:S(2)}, u32[]{:S(2)}) collective-permute-start(f32[2]{0:T(128)S(1)} %add.161), channel_id=1, source_target_pairs={{0,2},{1,3},{2,0},{3,1},{4,6},{5,7},{6,4},{7,5},{8,10},{9,11},{10,... | collective-permute-start | bytes 32 | tf_op jit(solution)/shard_map/ppermute | solution.py:45
  110.7 2.8 %collective-permute-start.18 = (f32[2]{0:T(128)S(1)}, f32[2]{0:T(128)S(1)}, u32[]{:S(2)}, u32[]{:S(2)}) collective-permute-start(f32[2]{0:T(128)S(1)} %add_add_fusion.5), channel_id=1, source_target_pairs={{0,8},{1,9},{2,10},{3,11},{4,12},{5,13},{6,14},{7,15},{8,0},{9,1},... | collective-permute-start | bytes 32 | tf_op jit(solution)/shard_map/ppermute | solution.py:45
  117.1 3.9 %collective-permute-start.22 = (f32[6,18,1]{2,0,1:T(8,128)S(1)}, f32[6,18,1]{2,0,1:T(8,128)S(1)}, u32[]{:S(2)}, u32[]{:S(2)}) collective-permute-start(f32[6,18,1]{2,0,1:T(8,128)S(1)} %get-tuple-element.33), channel_id=1, source_target_pairs={{0,1},{1,2},{2,3},{3,4},{4,5},{5,6},{6,7},{7,8},{8,9},{9,10},{10,1... | collective-permute-start | bytes 1304 | tf_op jit(solution)/shard_map/ppermute | solution.py:21
  124.5 2.8 %collective-permute-done.23 = f32[6,18,1]{2,0,1:T(8,128)S(1)} collective-permute-done((f32[6,18,1]{2,0,1:T(8,128)S(1)}, f32[6,18,1]{2,0,1:T(8,128)S(1)}, u32[]{:S(2)}, u32[]{:S(2)}) %collective-permute-start.23) | collective-permute-done | bytes 464 | tf_op jit(solution)/shard_map/ppermute | solution.py:22
  128.1 2.3 %fusion.1 = f32[128,17,129]{0,2,1:T(8,128)S(1)} fusion(f32[128,16,128]{0,2,1:T(8,128)S(1)} %bitcast.75, f32[128,1,128]{0,2,1:T(8,128)S(1)} %collective-permute-done.4, f32[128,17,1]{0,2,1:T(1,128)S(1)} %copy-done.16, f32[6,17,129]{2,0,1:T(8,128)S(1)} %get-tuple-element.25, f32[6,17,129]{2,0,1:T(8,128)S(1)} %get-tuple-element.24, ...), kind=kOutput, calls=%fused_computation.5 | convolution fusion | flops 81842760 | bytes 2468448 | tf_op jit(solution)/shard_map/hb,bxy->hxy/dot_general | solution.py:118
  133.1 2.5 %pad_maximum_fusion.14 = f32[4]{0:T(128)S(1)} fusion(f32[1]{0:T(128)} %bitcast.20, f32[1]{0:T(128)} %bitcast.19, f32[1]{0:T(128)} %bitcast.18, f32[1]{0:T(128)} %bitcast.15), kind=kLoop, calls=%fused_computation.89 | loop fusion | flops 12 | bytes 32 | tf_op jit(solution)/shard_map/stack | solution.py:131
  139.7 2.5 %add_add_fusion.3 = f32[4]{0:T(128)S(1)} fusion(f32[4]{0:T(128)S(1)} %collective-permute-done.26, f32[4]{0:T(128)S(1)} %collective-permute-done.25, f32[4]{0:T(128)S(1)} %collective-permute-done.24, f32[1]{0:T(128)} %bitcast.20, f32[1]{0:T(128)} %bitcast.19, f32[1]{0:T(128)} %bitcast.18, f32[1]{0:T(128)} %bitcast.15), kind=kLoop, calls=%fused_computation.92 | loop fusion | flops 24 | bytes 80 | tf_op jit(solution)/shard_map/add | solution.py:45
  142.2 3.3 %collective-permute-start.27 = (f32[4]{0:T(128)S(1)}, f32[4]{0:T(128)S(1)}, u32[]{:S(2)}, u32[]{:S(2)}) collective-permute-start(f32[4]{0:T(128)S(1)} %add_add_fusion.3), channel_id=1, source_target_pairs={{0,64},{16,80},{32,96},{48,112},{64,0},{80,16},{96,32},{112,48},{1... | collective-permute-start | bytes 56 | tf_op jit(solution)/shard_map/ppermute | solution.py:45
  147.4 5.1 %collective-permute-start.29 = (f32[4]{0:T(128)S(1)}, f32[4]{0:T(128)S(1)}, u32[]{:S(2)}, u32[]{:S(2)}) collective-permute-start(f32[4]{0:T(128)S(1)} %add.175), channel_id=1, source_target_pairs={{0,2},{1,3},{2,0},{3,1},{4,6},{5,7},{6,4},{7,5},{8,10},{9,11},{10,... | collective-permute-start | bytes 56 | tf_op jit(solution)/shard_map/ppermute | solution.py:45
  156.6 3.4 %collective-permute-start.32 = (f32[4]{0:T(128)S(1)}, f32[4]{0:T(128)S(1)}, u32[]{:S(2)}, u32[]{:S(2)}) collective-permute-start(f32[4]{0:T(128)S(1)} %add_add_fusion.2), channel_id=1, source_target_pairs={{0,8},{1,9},{2,10},{3,11},{4,12},{5,13},{6,14},{7,15},{8,0},{9,1},... | collective-permute-start | bytes 56 | tf_op jit(solution)/shard_map/ppermute | solution.py:45
  160.0 2.5 %collective-permute-start.33 = (f32[4]{0:T(128)S(1)}, f32[4]{0:T(128)S(1)}, u32[]{:S(2)}, u32[]{:S(2)}) collective-permute-start(f32[4]{0:T(128)S(1)} %add_add_fusion.2), channel_id=1, source_target_pairs={{0,12},{1,13},{2,14},{3,15},{4,0},{5,1},{6,2},{7,3},{8,4},{9,5},{1... | collective-permute-start | bytes 56 | tf_op jit(solution)/shard_map/ppermute | solution.py:45
  (145 shorter events, 67.1 us)
Async XLA Ops:
  1.4 19.2 %collective-permute-start = (f32[6,1,128]{2,0,1:T(8,128)S(1)}, f32[6,1,128]{2,0,1:T(8,128)S(1)}, u32[]{:S(2)}, u32[]{:S(2)}) collective-permute-start(f32[6,1,128]{2,0,1:T(8,128)S(1)} %copy.57), channel_id=1, source_target_pairs={{0,16},{16,32},{32,48},{48,64},{64,80},{80,96},{96,112},{1,17},{17... | collective-permute-start | bytes 9224 | tf_op jit(solution)/shard_map/ppermute | solution.py:21
  2.7 17.9 %collective-permute-start.1 = (f32[6,1,128]{2,0,1:T(8,128)S(1)}, f32[6,1,128]{2,0,1:T(8,128)S(1)}, u32[]{:S(2)}, u32[]{:S(2)}) collective-permute-start(f32[6,1,128]{2,0,1:T(8,128)S(1)} %copy.58), channel_id=1, source_target_pairs={{16,0},{32,16},{48,32},{64,48},{80,64},{96,80},{112,96},{17,1},{33... | collective-permute-start | bytes 9224 | tf_op jit(solution)/shard_map/ppermute | solution.py:22
  6.4 46.6 %all-to-all-start = ((f32[128,128,9]{0,2,1:T(8,128)}), f32[128,128,9]{0,2,1:T(8,128)S(1)}, u32[]{:S(2)}, u32[]{:S(2)}) async-start(f32[128,128,9]{0,2,1:T(8,128)} %reshape.103), calls=%async_computation | async-start | bytes 2097152 | tf_op jit(solution)/shard_map/all_to_all | solution.py:93
  20.7 9.8 %collective-permute-start.2 = (f32[6,18,1]{2,0,1:T(8,128)S(1)}, f32[6,18,1]{2,0,1:T(8,128)S(1)}, u32[]{:S(2)}, u32[]{:S(2)}) collective-permute-start(f32[6,18,1]{2,0,1:T(8,128)S(1)} %get-tuple-element.41), channel_id=1, source_target_pairs={{0,1},{1,2},{2,3},{3,4},{4,5},{5,6},{6,7},{7,8},{8,9},{9,10},{10,1... | collective-permute-start | bytes 1304 | tf_op jit(solution)/shard_map/ppermute | solution.py:21
  23.6 10.0 %collective-permute-start.3 = (f32[6,18,1]{2,0,1:T(8,128)S(1)}, f32[6,18,1]{2,0,1:T(8,128)S(1)}, u32[]{:S(2)}, u32[]{:S(2)}) collective-permute-start(f32[6,18,1]{2,0,1:T(8,128)S(1)} %get-tuple-element.42), channel_id=1, source_target_pairs={{1,0},{2,1},{3,2},{4,3},{5,4},{6,5},{7,6},{8,7},{9,8},{10,9},{11,1... | collective-permute-start | bytes 1304 | tf_op jit(solution)/shard_map/ppermute | solution.py:22
  36.1 5.4 %collective-permute-start.7 = (f32[6,1,128]{2,0,1:T(8,128)S(1)}, f32[6,1,128]{2,0,1:T(8,128)S(1)}, u32[]{:S(2)}, u32[]{:S(2)}) collective-permute-start(f32[6,1,128]{2,0,1:T(8,128)S(1)} %get-tuple-element.46), channel_id=1, source_target_pairs={{16,0},{32,16},{48,32},{64,48},{80,64},{96,80},{112,96},{17,1},{33... | collective-permute-start | bytes 9224 | tf_op jit(solution)/shard_map/ppermute | solution.py:22
  42.1 7.4 %collective-permute-start.8 = (f32[6,18,1]{2,0,1:T(8,128)S(1)}, f32[6,18,1]{2,0,1:T(8,128)S(1)}, u32[]{:S(2)}, u32[]{:S(2)}) collective-permute-start(f32[6,18,1]{2,0,1:T(8,128)S(1)} %get-tuple-element.37), channel_id=1, source_target_pairs={{0,1},{1,2},{2,3},{3,4},{4,5},{5,6},{6,7},{7,8},{8,9},{9,10},{10,1... | collective-permute-start | bytes 1304 | tf_op jit(solution)/shard_map/ppermute | solution.py:21
  45.5 6.4 %collective-permute-start.9 = (f32[6,18,1]{2,0,1:T(8,128)S(1)}, f32[6,18,1]{2,0,1:T(8,128)}, u32[]{:S(2)}, u32[]{:S(2)}) collective-permute-start(f32[6,18,1]{2,0,1:T(8,128)S(1)} %get-tuple-element.38), channel_id=1, source_target_pairs={{1,0},{2,1},{3,2},{4,3},{5,4},{6,5},{7,6},{8,7},{9,8},{10,9},{11,1... | collective-permute-start | bytes 1304 | tf_op jit(solution)/shard_map/ppermute | solution.py:22
  69.2 5.9 %collective-permute-start.5 = (f32[128,17,1]{0,2,1:T(1,128)S(1)}, f32[128,17,1]{0,2,1:T(1,128)S(1)}, u32[]{:S(2)}, u32[]{:S(2)}) collective-permute-start(f32[128,17,1]{0,2,1:T(1,128)S(1)} %pad_maximum_fusion.12), channel_id=1, source_target_pairs={{0,1},{1,2},{2,3},{3,4},{4,5},{5,6},{6,7},{7,8},{8,9},{9,10},{10,1... | collective-permute-start | bytes 26120 | tf_op jit(solution)/shard_map/ppermute | solution.py:30
  81.4 8.6 %collective-permute-start.10 = (f32[2]{0:T(128)S(1)}, f32[2]{0:T(128)S(1)}, u32[]{:S(2)}, u32[]{:S(2)}) collective-permute-start(f32[2]{0:T(128)S(1)} %pad_maximum_fusion.13), channel_id=1, source_target_pairs={{0,16},{16,32},{32,48},{48,0},{64,80},{80,96},{96,112},{112,64},{1... | collective-permute-start | bytes 32 | tf_op jit(solution)/shard_map/ppermute | solution.py:45
  83.4 6.6 %collective-permute-start.11 = (f32[2]{0:T(128)S(1)}, f32[2]{0:T(128)S(1)}, u32[]{:S(2)}, u32[]{:S(2)}) collective-permute-start(f32[2]{0:T(128)S(1)} %pad_maximum_fusion.13), channel_id=1, source_target_pairs={{0,32},{16,48},{32,0},{48,16},{64,96},{80,112},{96,64},{112,80},{1... | collective-permute-start | bytes 32 | tf_op jit(solution)/shard_map/ppermute | solution.py:45
  87.4 29.6 %collective-permute-start.20 = (f32[6,1,128]{2,0,1:T(8,128)S(1)}, f32[6,1,128]{2,0,1:T(8,128)S(1)}, u32[]{:S(2)}, u32[]{:S(2)}) collective-permute-start(f32[6,1,128]{2,0,1:T(8,128)S(1)} %get-tuple-element.43), channel_id=1, source_target_pairs={{0,16},{16,32},{32,48},{48,64},{64,80},{80,96},{96,112},{1,17},{17... | collective-permute-start | bytes 9224 | tf_op jit(solution)/shard_map/ppermute | solution.py:21
  88.7 28.3 %collective-permute-start.21 = (f32[6,1,128]{2,0,1:T(8,128)S(1)}, f32[6,1,128]{2,0,1:T(8,128)S(1)}, u32[]{:S(2)}, u32[]{:S(2)}) collective-permute-start(f32[6,1,128]{2,0,1:T(8,128)S(1)} %get-tuple-element.44), channel_id=1, source_target_pairs={{16,0},{32,16},{48,32},{64,48},{80,64},{96,80},{112,96},{17,1},{33... | collective-permute-start | bytes 9224 | tf_op jit(solution)/shard_map/ppermute | solution.py:22
  91.4 6.2 %collective-permute-start.13 = (f32[2]{0:T(128)S(1)}, f32[2]{0:T(128)S(1)}, u32[]{:S(2)}, u32[]{:S(2)}) collective-permute-start(f32[2]{0:T(128)S(1)} %add_add_fusion.6), channel_id=1, source_target_pairs={{0,64},{16,80},{32,96},{48,112},{64,0},{80,16},{96,32},{112,48},{1... | collective-permute-start | bytes 32 | tf_op jit(solution)/shard_map/ppermute | solution.py:45
  97.6 8.9 %collective-permute-start.14 = (f32[2]{0:T(128)S(1)}, f32[2]{0:T(128)S(1)}, u32[]{:S(2)}, u32[]{:S(2)}) collective-permute-start(f32[2]{0:T(128)S(1)} %add.161), channel_id=1, source_target_pairs={{0,1},{1,2},{2,3},{3,0},{4,5},{5,6},{6,7},{7,4},{8,9},{9,10},{10,1... | collective-permute-start | bytes 32 | tf_op jit(solution)/shard_map/ppermute | solution.py:45
  99.7 7.2 %collective-permute-start.15 = (f32[2]{0:T(128)S(1)}, f32[2]{0:T(128)S(1)}, u32[]{:S(2)}, u32[]{:S(2)}) collective-permute-start(f32[2]{0:T(128)S(1)} %add.161), channel_id=1, source_target_pairs={{0,2},{1,3},{2,0},{3,1},{4,6},{5,7},{6,4},{7,5},{8,10},{9,11},{10,... | collective-permute-start | bytes 32 | tf_op jit(solution)/shard_map/ppermute | solution.py:45
  109.0 6.1 %collective-permute-start.17 = (f32[2]{0:T(128)S(1)}, f32[2]{0:T(128)S(1)}, u32[]{:S(2)}, u32[]{:S(2)}) collective-permute-start(f32[2]{0:T(128)S(1)} %add_add_fusion.5), channel_id=1, source_target_pairs={{0,4},{1,5},{2,6},{3,7},{4,8},{5,9},{6,10},{7,11},{8,12},{9,13},{1... | collective-permute-start | bytes 32 | tf_op jit(solution)/shard_map/ppermute | solution.py:45
  117.1 7.4 %collective-permute-start.22 = (f32[6,18,1]{2,0,1:T(8,128)S(1)}, f32[6,18,1]{2,0,1:T(8,128)S(1)}, u32[]{:S(2)}, u32[]{:S(2)}) collective-permute-start(f32[6,18,1]{2,0,1:T(8,128)S(1)} %get-tuple-element.33), channel_id=1, source_target_pairs={{0,1},{1,2},{2,3},{3,4},{4,5},{5,6},{6,7},{7,8},{8,9},{9,10},{10,1... | collective-permute-start | bytes 1304 | tf_op jit(solution)/shard_map/ppermute | solution.py:21
  121.1 6.2 %collective-permute-start.23 = (f32[6,18,1]{2,0,1:T(8,128)S(1)}, f32[6,18,1]{2,0,1:T(8,128)S(1)}, u32[]{:S(2)}, u32[]{:S(2)}) collective-permute-start(f32[6,18,1]{2,0,1:T(8,128)S(1)} %get-tuple-element.34), channel_id=1, source_target_pairs={{1,0},{2,1},{3,2},{4,3},{5,4},{6,5},{7,6},{8,7},{9,8},{10,9},{11,1... | collective-permute-start | bytes 1304 | tf_op jit(solution)/shard_map/ppermute | solution.py:22
  142.2 5.1 %collective-permute-start.27 = (f32[4]{0:T(128)S(1)}, f32[4]{0:T(128)S(1)}, u32[]{:S(2)}, u32[]{:S(2)}) collective-permute-start(f32[4]{0:T(128)S(1)} %add_add_fusion.3), channel_id=1, source_target_pairs={{0,64},{16,80},{32,96},{48,112},{64,0},{80,16},{96,32},{112,48},{1... | collective-permute-start | bytes 56 | tf_op jit(solution)/shard_map/ppermute | solution.py:45
  147.3 5.3 %collective-permute-start.28 = (f32[4]{0:T(128)S(1)}, f32[4]{0:T(128)S(1)}, u32[]{:S(2)}, u32[]{:S(2)}) collective-permute-start(f32[4]{0:T(128)S(1)} %add.175), channel_id=1, source_target_pairs={{0,1},{1,2},{2,3},{3,0},{4,5},{5,6},{6,7},{7,4},{8,9},{9,10},{10,1... | collective-permute-start | bytes 56 | tf_op jit(solution)/shard_map/ppermute | solution.py:45
  147.4 6.6 %collective-permute-start.29 = (f32[4]{0:T(128)S(1)}, f32[4]{0:T(128)S(1)}, u32[]{:S(2)}, u32[]{:S(2)}) collective-permute-start(f32[4]{0:T(128)S(1)} %add.175), channel_id=1, source_target_pairs={{0,2},{1,3},{2,0},{3,1},{4,6},{5,7},{6,4},{7,5},{8,10},{9,11},{10,... | collective-permute-start | bytes 56 | tf_op jit(solution)/shard_map/ppermute | solution.py:45
  156.1 6.5 %collective-permute-start.31 = (f32[4]{0:T(128)S(1)}, f32[4]{0:T(128)S(1)}, u32[]{:S(2)}, u32[]{:S(2)}) collective-permute-start(f32[4]{0:T(128)S(1)} %add_add_fusion.2), channel_id=1, source_target_pairs={{0,4},{1,5},{2,6},{3,7},{4,8},{5,9},{6,10},{7,11},{8,12},{9,13},{1... | collective-permute-start | bytes 56 | tf_op jit(solution)/shard_map/ppermute | solution.py:45
  156.6 5.9 %collective-permute-start.32 = (f32[4]{0:T(128)S(1)}, f32[4]{0:T(128)S(1)}, u32[]{:S(2)}, u32[]{:S(2)}) collective-permute-start(f32[4]{0:T(128)S(1)} %add_add_fusion.2), channel_id=1, source_target_pairs={{0,8},{1,9},{2,10},{3,11},{4,12},{5,13},{6,14},{7,15},{8,0},{9,1},... | collective-permute-start | bytes 56 | tf_op jit(solution)/shard_map/ppermute | solution.py:45
  (31 other events, 387.4 us)

commit v3 on v2

--- a/solution.py
+++ b/solution.py
@@ -11,23 +11,20 @@
 CORNERS = ((0, 0), (1, 0), (0, 1), (1, 1))
 
 
-def with_halo(shard, sides, width):
-    for axis, dim in sides:
+def with_halo(shard, before, after):
+    for axis, dim in (("px", 1), ("py", 2)):
         devices, length = (lax.axis_size(axis), shard.shape[dim])
-        up = [(i, (i + 1) % devices) for i in range(devices - 1)]
+        up = [(i, i + 1) for i in range(devices - 1)]
         down = [(j, i) for i, j in up]
-        last = lax.slice_in_dim(shard, length - width, length, axis=dim)
-        leading = lax.slice_in_dim(shard, 0, width, axis=dim)
-        before = lax.ppermute(last, axis, up)
-        after = lax.ppermute(leading, axis, down)
-        shard = jnp.concatenate([before, shard, after], axis=dim)
+        parts = [shard]
+        if before:
+            last = lax.slice_in_dim(shard, length - before, length, axis=dim)
+            parts.insert(0, lax.ppermute(last, axis, up))
+        if after:
+            leading = lax.slice_in_dim(shard, 0, after, axis=dim)
+            parts.append(lax.ppermute(leading, axis, down))
+        shard = jnp.concatenate(parts, axis=dim)
     return shard
-
-
-def shifted(shard, axis, by):
-    devices = lax.axis_size(axis)
-    pairs = [(i, i + by) for i in range(devices) if 0 <= i + by < devices]
-    return lax.ppermute(shard, axis, pairs)
 
 
 def all_sum(value):
@@ -49,18 +46,14 @@
 
 
 def gather_shells(field):
-    rows, cols = (field.shape[1] - 2, field.shape[2] - 2)
+    rows, cols = (field.shape[1] - 1, field.shape[2] - 1)
     return jnp.concatenate(
-        [field[:, dx : dx + rows + 1, dy : dy + cols + 1] for dx, dy in CORNERS], axis=0
+        [field[:, dx : dx + rows, dy : dy + cols] for dx, dy in CORNERS], axis=0
     )
 
 
 def scatter_nodes(forces):
     rows, cols = (forces.shape[1] - 1, forces.shape[2] - 1)
-    row_keep = (jnp.arange(rows + 1) > 0) | (lax.axis_index("px") > 0)
-    col_keep = (jnp.arange(cols + 1) > 0) | (lax.axis_index("py") > 0)
-    keep = (row_keep[:, None] & col_keep[None, :]).astype(jnp.float32)
-    forces = forces * keep[None, :, :]
     total = jnp.zeros((6, rows, cols), jnp.float32)
     for index, (dx, dy) in enumerate(CORNERS):
         total = (
@@ -68,6 +61,18 @@
             + forces[6 * index : 6 * index + 6, 1 - dx : 1 - dx + rows, 1 - dy : 1 - dy + cols]
         )
     return total
+
+
+def inside(shape, row_from, col_from, rows_total, cols_total, low_only):
+    rows, cols = shape
+    row = lax.axis_index("px") * rows_total + row_from + jnp.arange(rows)
+    col = lax.axis_index("py") * cols_total + col_from + jnp.arange(cols)
+    row_ok = row >= 0
+    col_ok = col >= 0
+    if not low_only:
+        row_ok = row_ok & (row < rows_total * lax.axis_size("px"))
+        col_ok = col_ok & (col < cols_total * lax.axis_size("py"))
+    return (row_ok[:, None] & col_ok[None, :]).astype(jnp.float32)
 
 
 def shards(
@@ -95,12 +100,21 @@
     def with_base(shells):
         return jnp.einsum("ab,bxy->axy", stiff_base, shells, precision=HIGH)
 
-    start_shells = gather_shells(with_halo(displacement, (("px", 1), ("py", 2)), 1))
-    force_start = scatter_nodes(with_base(start_shells))
+    def shell_keep(forces, offset):
+        return forces * inside(forces.shape[1:], offset, offset, rows, cols, True)[None]
+
+    def node_keep(field, offset):
+        return field * inside(field.shape[1:], offset, offset, rows, cols, False)[None]
+
+    both = with_halo(jnp.concatenate([displacement, load], axis=0), 3, 3)
+    start_shells = gather_shells(both[:6])
+    force_wide = scatter_nodes(shell_keep(with_base(start_shells), -3))
+    force_start = force_wide[:, 2 : rows + 2, 2 : cols + 2]
     velocity_out = velocity + STEP * inv_mass * (load - force_start)
     moved = displacement + STEP * velocity_out
-    own = start_shells[:, 1:, 1:].reshape(24, cells)
+    own = start_shells[:, 3 : rows + 3, 3 : cols + 3].reshape(24, cells)
     history_new = history.reshape(hist, cells) + jnp.dot(strain_map, own, precision=HIGH)
+    rhs_wide = node_keep(both[6:, 1 : rows + 5, 1 : cols + 5] - force_wide, -2)
 
     contact = (
         contact_home.reshape(hist, cells)
@@ -108,20 +122,18 @@
         .set(arrived.reshape(hist, devices * width), mode="drop")
     )
     weights = (jax.nn.softplus(history_new) * contact).reshape(hist, rows, cols)
-    lower_row = shifted(weights[:, -1:, :], "px", 1)
-    tall = jnp.concatenate([lower_row, weights], axis=1)
-    lower_col = shifted(tall[:, :, -1:], "py", 1)
-    extended = jnp.concatenate([lower_col, tall], axis=2)
+    weights_wide = with_halo(weights, 2, 1)
 
-    def operate(field):
-        shells = gather_shells(with_halo(field, (("px", 1), ("py", 2)), 1))
+    def operate(field, weights_of, offset):
+        shells = gather_shells(field)
         strains = jnp.einsum("hb,bxy->hxy", strain_map, shells, precision=HIGH)
-        forces = jnp.einsum("hb,hxy->bxy", strain_map, extended * strains, precision=HIGH)
-        return scatter_nodes(forces + with_base(shells))
+        forces = jnp.einsum("hb,hxy->bxy", strain_map, weights_of * strains, precision=HIGH)
+        return scatter_nodes(shell_keep(forces + with_base(shells), offset))
 
-    rhs = load - force_start
-    image = operate(rhs)
-    again = operate(image)
+    rhs = rhs_wide[:, 2 : rows + 2, 2 : cols + 2]
+    image_wide = node_keep(operate(rhs_wide, weights_wide, -2), -1)
+    image = image_wide[:, 1 : rows + 1, 1 : cols + 1]
+    again = operate(image_wide, weights_wide[:, 1 : rows + 2, 1 : cols + 2], -1)
     first = all_sum(jnp.stack([jnp.sum(rhs * rhs), jnp.sum(rhs * image)]))
     norm_now, curvature = first[0], first[1]
     alpha = norm_now / curvature

time: 172 us -> 149 us (0.87)
  starting transfers between devices: 86.6 us -> 63.5 us
  waiting for transfers between devices: 32 us -> 26.3 us
  other arithmetic: 11.5 us -> 14 us
  local copies, waits for them, and re-layouts: 19.9 us -> 22.3 us
    ppermute x14 -> x8, starting transfers between devices: 29.1 us -> 15.6 us  [the longest x4 10.2 us: with_halo(): parts.insert(0, lax.ppermute(last, axis, up))]
    ppermute x20, starting transfers between devices: 43.3 us -> 33.8 us  [all_sum(): total = total + lax.ppermute(value, axis, pairs)]
    ppermute x14 -> x8, waiting for transfers between devices: 18.1 us -> 9.09 us  [the longest x4 5.47 us: with_halo(): parts.insert(0, lax.ppermute(last, axis, up))]
    ppermute x20, waiting for transfers between devices: 13.9 us -> 17.2 us  [all_sum(): total = total + lax.ppermute(value, axis, pairs)]
    unnamed x51 -> x43, local copies, waits for them, and re-layouts: 8.83 us -> 10.4 us
  transfers between devices with their start and end apart: 35 -> 29, of which waited for: 19 -> 18; matrix products, arithmetic and copies ran while one was open for 7% -> 14% of each run, Pallas kernels for 0% -> 0%
where the time goes in v3:
time: 149 us; the launch traced here: 148 us
  starting transfers between devices  63.5 us (43%)
  waiting for transfers between devices  26.3 us (18%)
  local copies, waits for them, and re-layouts  22.3 us (15%)
  matrix products  15.2 us (10%)
  other arithmetic  14 us (9%)
  between operations  7.02 us (5%)
    ppermute x20, starting transfers between devices, all_sum(): total = total + lax.ppermute(value, axis, pairs)  33.8 us
    ppermute x20, waiting for transfers between devices, all_sum(): total = total + lax.ppermute(value, axis, pairs)  17.2 us
    all_to_all x1, starting transfers between devices, shards(): lax.all_to_all(held, ('px', 'py'), split_axis=1, concat_axis=1, tiled=True)  14.2 us
    unnamed x43, local copies, waits for them, and re-layouts  10.4 us
    ppermute x4, starting transfers between devices, with_halo(): parts.insert(0, lax.ppermute(last, axis, up))  10.2 us
    scatter x1, local copies, waits for them, and re-layouts, shards(): contact = contact_home.reshape(hist, cells).at[:, targets].set(arrived.re...  6.8 us
    ppermute x4, waiting for transfers between devices, with_halo(): parts.insert(0, lax.ppermute(last, axis, up))  5.47 us
    ppermute x4, starting transfers between devices, with_halo(): parts.append(lax.ppermute(leading, axis, down))  5.34 us
  transfers between devices with their start and end apart: 29, of which 18 were waited for; matrix products, arithmetic and copies ran while one was open for 14% of the time, Pallas kernels for 0%

profile of v3, /device:TPU:0, one launch (start us, length us, event | category | flops | bytes accessed | tf_op | source)
XLA Modules:
  0.0 148.4 jit_solution(10859325919997757100)
XLA Ops:
  7.3 14.2 %all-to-all-start = ((f32[128,128,9]{0,2,1:T(8,128)}), f32[128,128,9]{0,2,1:T(8,128)S(1)}, u32[]{:S(2)}, u32[]{:S(2)}) async-start(f32[128,128,9]{0,2,1:T(8,128)} %reshape.263), calls=%async_computation | async-start | bytes 2097152 | tf_op jit(solution)/shard_map/all_to_all | solution.py:98
  23.4 3.5 %collective-permute-start.2 = (f32[12,22,3]{2,0,1:T(8,128)}, f32[12,22,3]{2,0,1:T(8,128)}, u32[]{:S(2)}, u32[]{:S(2)}) collective-permute-start(f32[12,22,3]{2,0,1:T(8,128)} %get-tuple-element.28), channel_id=1, source_target_pairs={{0,1},{1,2},{2,3},{3,4},{4,5},{5,6},{6,7},{7,8},{8,9},{9,10},{10,1... | collective-permute-start | bytes 9512 | tf_op jit(solution)/shard_map/ppermute | solution.py:22
  30.3 5.5 %collective-permute-done.2 = f32[12,22,3]{2,0,1:T(8,128)} collective-permute-done((f32[12,22,3]{2,0,1:T(8,128)}, f32[12,22,3]{2,0,1:T(8,128)}, u32[]{:S(2)}, u32[]{:S(2)}) %collective-permute-start.2) | collective-permute-done | bytes 3200 | tf_op jit(solution)/shard_map/ppermute | solution.py:22
  35.8 2.7 %collective-permute-done.3 = f32[12,22,3]{2,0,1:T(8,128)} collective-permute-done((f32[12,22,3]{2,0,1:T(8,128)}, f32[12,22,3]{2,0,1:T(8,128)}, u32[]{:S(2)}, u32[]{:S(2)}) %collective-permute-start.3) | collective-permute-done | bytes 3200 | tf_op jit(solution)/shard_map/ppermute | solution.py:25
  44.2 6.8 %scatter_custom_fusion = f32[128,2048]{0,1:T(8,128)S(1)} fusion(f32[128,2048]{0,1:T(8,128)S(1)} %bitcast.73, s32[1152]{0:T(1024)S(1)} %fusion.46, f32[128,1152]{0,1:T(8,128)} %reshape.268), kind=kCustom, calls=%fused_computation.30 | custom fusion | bytes 1638400 | tf_op jit(solution)/shard_map/scatter | solution.py:122
  51.0 4.4 %fusion.19 = (f32[128,2048]{0,1:T(8,128)S(1)}, f32[128,2048]{0,1:T(8,128)}) fusion(f32[128,2048]{0,1:T(8,128)S(1)} %scatter_custom_fusion, f32[128,2048]{0,1:T(8,128)S(1)} %bitcast.72, f32[128,24]{0,1:T(8,128)S(1)} %copy-done, f32[6,21,133]{2,0,1:T(8,128)} %copy-done.2, f32[6,21,133]{2,0,1:T(8,128)} %copy-done.3, f32[6,21,133]{2,0,1:T(8,128)} %copy-done.4, ...), kind=kOutput, calls=%fused_computation.29 | convolution fusion | flops 77742080 | bytes 4474720 | tf_op jit(solution)/shard_map/dot_general | solution.py:116
  58.8 2.5 %convolution_bitcast_fusion.1 = f32[128,19,131]{0,2,1:T(8,128)S(1)} fusion(f32[6,19,131]{2,0,1:T(8,128)S(1)} %copy-done.6, f32[6,19,131]{2,0,1:T(8,128)S(1)} %copy-done.7, f32[6,19,131]{2,0,1:T(8,128)S(1)} %copy-done.8, f32[6,19,131]{2,0,1:T(8,128)S(1)} %copy-done.5, f32[128,24]{0,1:T(8,128)S(1)} %copy-done), kind=kOutput, calls=%fused_computation.4 | convolution fusion | flops 91933704 | bytes 1525600 | tf_op jit(solution)/shard_map/hb,bxy->hxy/dot_general | solution.py:129
  61.3 3.4 %collective-permute-start.6 = (f32[128,19,2]{0,2,1:T(2,128)S(1)}, f32[128,19,2]{0,2,1:T(2,128)S(1)}, u32[]{:S(2)}, u32[]{:S(2)}) collective-permute-start(f32[128,19,2]{0,2,1:T(2,128)S(1)} %pad_maximum_fusion.15), channel_id=1, source_target_pairs={{0,1},{1,2},{2,3},{3,4},{4,5},{5,6},{6,7},{7,8},{8,9},{9,10},{10,1... | collective-permute-start | bytes 58376 | tf_op jit(solution)/shard_map/ppermute | solution.py:22
  66.9 2.6 %copy.39 = f32[128,16,128]{2,1,0:T(8,128)} copy(f32[128,16,128]{0,2,1:T(8,128)} %bitcast.74) | data formatting | bytes 2097152
  70.3 2.2 %fusion.13 = f32[24,19,131]{2,0,1:T(8,128)S(1)} fusion(f32[19,131,24]{1,2,0:T(8,128)S(1)} %fusion.31, f32[128,19,131]{0,2,1:T(8,128)S(1)} %convolution_bitcast_fusion.1, f32[128,19,1]{0,2,1:T(1,128)S(1)} %collective-permute-done.7, f32[128,1,128]{0,2,1:T(8,128)S(1)} %collective-permute-done.5, f32[128,16,128]{0,2,1:T(8,128)S(1)} %bitcast.70, ...), kind=kOutput, calls=%fused_computation.20 | convolution fusion | flops 93466928 | bytes 3048868 | tf_op jit(solution)/shard_map/hb,hxy->bxy/dot_general | solution.py:130
  74.8 2.4 %collective-permute-start.10 = (f32[2]{0:T(128)S(1)}, f32[2]{0:T(128)S(1)}, u32[]{:S(2)}, u32[]{:S(2)}) collective-permute-start(f32[2]{0:T(128)S(1)} %pad_maximum_fusion.18), channel_id=1, source_target_pairs={{0,48},{16,0},{32,16},{48,32},{64,112},{80,64},{96,80},{112,96},{1... | collective-permute-start | bytes 32 | tf_op jit(solution)/shard_map/ppermute | solution.py:42
  78.7 2.3 %convolution_bitcast_fusion.2 = f32[128,17,129]{0,2,1:T(8,128)S(1)} fusion(f32[6,17,129]{2,0,1:T(8,128)S(1)} %get-tuple-element.35, f32[6,17,129]{2,0,1:T(8,128)S(1)} %get-tuple-element.36, f32[6,17,129]{2,0,1:T(8,128)S(1)} %get-tuple-element.37, f32[6,17,129]{2,0,1:T(8,128)S(1)} %get-tuple-element.34, f32[128,24]{0,1:T(8,128)S(1)} %copy-done), kind=kOutput, calls=%fused_computation.5 | convolution fusion | flops 81000648 | bytes 1345632 | tf_op jit(solution)/shard_map/hb,bxy->hxy/dot_general | solution.py:129
  85.0 2.6 %collective-permute-start.11 = (f32[2]{0:T(128)S(1)}, f32[2]{0:T(128)S(1)}, u32[]{:S(2)}, u32[]{:S(2)}) collective-permute-start(f32[2]{0:T(128)S(1)} %add_add_fusion.6), channel_id=1, source_target_pairs={{0,64},{16,80},{32,96},{48,112},{64,0},{80,16},{96,32},{112,48},{1... | collective-permute-start | bytes 32 | tf_op jit(solution)/shard_map/ppermute | solution.py:42
  87.6 2.5 %collective-permute-done.11 = f32[2]{0:T(128)S(1)} collective-permute-done((f32[2]{0:T(128)S(1)}, f32[2]{0:T(128)S(1)}, u32[]{:S(2)}, u32[]{:S(2)}) %collective-permute-start.11) | collective-permute-done | bytes 40 | tf_op jit(solution)/shard_map/ppermute | solution.py:42
  91.9 5.5 %collective-permute-start.13 = (f32[2]{0:T(128)S(1)}, f32[2]{0:T(128)S(1)}, u32[]{:S(2)}, u32[]{:S(2)}) collective-permute-start(f32[2]{0:T(128)S(1)} %add.305), channel_id=1, source_target_pairs={{0,2},{1,3},{2,0},{3,1},{4,6},{5,7},{6,4},{7,5},{8,10},{9,11},{10,... | collective-permute-start | bytes 32 | tf_op jit(solution)/shard_map/ppermute | solution.py:42
  98.9 2.0 %collective-permute-done.14 = f32[2]{0:T(128)S(1)} collective-permute-done((f32[2]{0:T(128)S(1)}, f32[2]{0:T(128)S(1)}, u32[]{:S(2)}, u32[]{:S(2)}) %collective-permute-start.14) | collective-permute-done | bytes 40 | tf_op jit(solution)/shard_map/ppermute | solution.py:42
  104.6 2.5 %collective-permute-start.17 = (f32[2]{0:T(128)S(1)}, f32[2]{0:T(128)S(1)}, u32[]{:S(2)}, u32[]{:S(2)}) collective-permute-start(f32[2]{0:T(128)S(1)} %add_add_fusion.5), channel_id=1, source_target_pairs={{0,12},{1,13},{2,14},{3,15},{4,0},{5,1},{6,2},{7,3},{8,4},{9,5},{1... | collective-permute-start | bytes 32 | tf_op jit(solution)/shard_map/ppermute | solution.py:42
  111.2 2.6 %pad_maximum_fusion.19 = f32[4]{0:T(128)S(1)} fusion(f32[1]{0:T(128)} %bitcast.20, f32[1]{0:T(128)} %bitcast.19, f32[1]{0:T(128)} %bitcast.18, f32[1]{0:T(128)} %bitcast.15), kind=kLoop, calls=%fused_computation.102 | loop fusion | flops 12 | bytes 32 | tf_op jit(solution)/shard_map/stack | solution.py:143
  117.5 2.6 %add_add_fusion.3 = f32[4]{0:T(128)S(1)} fusion(f32[4]{0:T(128)S(1)} %collective-permute-done.20, f32[4]{0:T(128)S(1)} %collective-permute-done.19, f32[4]{0:T(128)S(1)} %collective-permute-done.18, f32[1]{0:T(128)} %bitcast.20, f32[1]{0:T(128)} %bitcast.19, f32[1]{0:T(128)} %bitcast.18, f32[1]{0:T(128)} %bitcast.15), kind=kLoop, calls=%fused_computation.105 | loop fusion | flops 24 | bytes 80 | tf_op jit(solution)/shard_map/add | solution.py:42
  120.2 2.9 %collective-permute-start.21 = (f32[4]{0:T(128)S(1)}, f32[4]{0:T(128)S(1)}, u32[]{:S(2)}, u32[]{:S(2)}) collective-permute-start(f32[4]{0:T(128)S(1)} %add_add_fusion.3), channel_id=1, source_target_pairs={{0,64},{16,80},{32,96},{48,112},{64,0},{80,16},{96,32},{112,48},{1... | collective-permute-start | bytes 56 | tf_op jit(solution)/shard_map/ppermute | solution.py:42
  123.0 2.4 %collective-permute-done.21 = f32[4]{0:T(128)S(1)} collective-permute-done((f32[4]{0:T(128)S(1)}, f32[4]{0:T(128)S(1)}, u32[]{:S(2)}, u32[]{:S(2)}) %collective-permute-start.21) | collective-permute-done | bytes 48 | tf_op jit(solution)/shard_map/ppermute | solution.py:42
  127.5 2.2 %collective-permute-start.23 = (f32[4]{0:T(128)S(1)}, f32[4]{0:T(128)S(1)}, u32[]{:S(2)}, u32[]{:S(2)}) collective-permute-start(f32[4]{0:T(128)S(1)} %add.323), channel_id=1, source_target_pairs={{0,2},{1,3},{2,0},{3,1},{4,6},{5,7},{6,4},{7,5},{8,10},{9,11},{10,... | collective-permute-start | bytes 56 | tf_op jit(solution)/shard_map/ppermute | solution.py:42
  130.3 2.3 %collective-permute-done.23 = f32[4]{0:T(128)S(1)} collective-permute-done((f32[4]{0:T(128)S(1)}, f32[4]{0:T(128)S(1)}, u32[]{:S(2)}, u32[]{:S(2)}) %collective-permute-start.23) | collective-permute-done | bytes 48 | tf_op jit(solution)/shard_map/ppermute | solution.py:42
  133.2 3.5 %collective-permute-start.26 = (f32[4]{0:T(128)S(1)}, f32[4]{0:T(128)S(1)}, u32[]{:S(2)}, u32[]{:S(2)}) collective-permute-start(f32[4]{0:T(128)S(1)} %add_add_fusion.2), channel_id=1, source_target_pairs={{0,8},{1,9},{2,10},{3,11},{4,12},{5,13},{6,14},{7,15},{8,0},{9,1},... | collective-permute-start | bytes 56 | tf_op jit(solution)/shard_map/ppermute | solution.py:42
  (132 shorter events, 55.2 us)
Async XLA Ops:
  2.3 20.3 %collective-permute-start = (f32[12,3,128]{2,0,1:T(8,128)S(1)}, f32[12,3,128]{2,0,1:T(8,128)S(1)}, u32[]{:S(2)}, u32[]{:S(2)}) collective-permute-start(f32[12,3,128]{2,0,1:T(8,128)S(1)} %get-tuple-element.38), channel_id=1, source_target_pairs={{0,16},{16,32},{32,48},{48,64},{64,80},{80,96},{96,112},{1,17},{17... | collective-permute-start | bytes 55304 | tf_op jit(solution)/shard_map/ppermute | solution.py:22
  3.6 19.0 %collective-permute-start.1 = (f32[12,3,128]{2,0,1:T(8,128)S(1)}, f32[12,3,128]{2,0,1:T(8,128)S(1)}, u32[]{:S(2)}, u32[]{:S(2)}) collective-permute-start(f32[12,3,128]{2,0,1:T(8,128)S(1)} %get-tuple-element.39), channel_id=1, source_target_pairs={{16,0},{32,16},{48,32},{64,48},{80,64},{96,80},{112,96},{17,1},{33... | collective-permute-start | bytes 55304 | tf_op jit(solution)/shard_map/ppermute | solution.py:25
  7.3 36.0 %all-to-all-start = ((f32[128,128,9]{0,2,1:T(8,128)}), f32[128,128,9]{0,2,1:T(8,128)S(1)}, u32[]{:S(2)}, u32[]{:S(2)}) async-start(f32[128,128,9]{0,2,1:T(8,128)} %reshape.263), calls=%async_computation | async-start | bytes 2097152 | tf_op jit(solution)/shard_map/all_to_all | solution.py:98
  23.4 12.4 %collective-permute-start.2 = (f32[12,22,3]{2,0,1:T(8,128)}, f32[12,22,3]{2,0,1:T(8,128)}, u32[]{:S(2)}, u32[]{:S(2)}) collective-permute-start(f32[12,22,3]{2,0,1:T(8,128)} %get-tuple-element.28), channel_id=1, source_target_pairs={{0,1},{1,2},{2,3},{3,4},{4,5},{5,6},{6,7},{7,8},{8,9},{9,10},{10,1... | collective-permute-start | bytes 9512 | tf_op jit(solution)/shard_map/ppermute | solution.py:22
  26.9 11.6 %collective-permute-start.3 = (f32[12,22,3]{2,0,1:T(8,128)}, f32[12,22,3]{2,0,1:T(8,128)}, u32[]{:S(2)}, u32[]{:S(2)}) collective-permute-start(f32[12,22,3]{2,0,1:T(8,128)} %get-tuple-element.29), channel_id=1, source_target_pairs={{1,0},{2,1},{3,2},{4,3},{5,4},{6,5},{7,6},{8,7},{9,8},{10,9},{11,1... | collective-permute-start | bytes 9512 | tf_op jit(solution)/shard_map/ppermute | solution.py:25
  55.4 5.9 %collective-permute-start.4 = (f32[128,2,128]{0,2,1:T(8,128)S(1)}, f32[128,2,128]{0,2,1:T(8,128)S(1)}, u32[]{:S(2)}, u32[]{:S(2)}) collective-permute-start(f32[128,2,128]{0,2,1:T(8,128)S(1)} %slice.195), channel_id=1, source_target_pairs={{0,16},{16,32},{32,48},{48,64},{64,80},{80,96},{96,112},{1,17},{17... | collective-permute-start | bytes 393224 | tf_op jit(solution)/shard_map/ppermute | solution.py:22
  57.5 3.9 %collective-permute-start.5 = (f32[128,1,128]{0,2,1:T(8,128)S(1)}, f32[128,1,128]{0,2,1:T(8,128)S(1)}, u32[]{:S(2)}, u32[]{:S(2)}) collective-permute-start(f32[128,1,128]{0,2,1:T(8,128)S(1)} %slice.196), channel_id=1, source_target_pairs={{16,0},{32,16},{48,32},{64,48},{80,64},{96,80},{112,96},{17,1},{33... | collective-permute-start | bytes 196616 | tf_op jit(solution)/shard_map/ppermute | solution.py:25
  61.3 9.0 %collective-permute-start.6 = (f32[128,19,2]{0,2,1:T(2,128)S(1)}, f32[128,19,2]{0,2,1:T(2,128)S(1)}, u32[]{:S(2)}, u32[]{:S(2)}) collective-permute-start(f32[128,19,2]{0,2,1:T(2,128)S(1)} %pad_maximum_fusion.15), channel_id=1, source_target_pairs={{0,1},{1,2},{2,3},{3,4},{4,5},{5,6},{6,7},{7,8},{8,9},{9,10},{10,1... | collective-permute-start | bytes 58376 | tf_op jit(solution)/shard_map/ppermute | solution.py:22
  64.8 5.6 %collective-permute-start.7 = (f32[128,19,1]{0,2,1:T(1,128)S(1)}, f32[128,19,1]{0,2,1:T(1,128)S(1)}, u32[]{:S(2)}, u32[]{:S(2)}) collective-permute-start(f32[128,19,1]{0,2,1:T(1,128)S(1)} %pad_maximum_fusion.16), channel_id=1, source_target_pairs={{1,0},{2,1},{3,2},{4,3},{5,4},{6,5},{7,6},{8,7},{9,8},{10,9},{11,1... | collective-permute-start | bytes 29192 | tf_op jit(solution)/shard_map/ppermute | solution.py:25
  74.8 8.8 %collective-permute-start.10 = (f32[2]{0:T(128)S(1)}, f32[2]{0:T(128)S(1)}, u32[]{:S(2)}, u32[]{:S(2)}) collective-permute-start(f32[2]{0:T(128)S(1)} %pad_maximum_fusion.18), channel_id=1, source_target_pairs={{0,48},{16,0},{32,16},{48,32},{64,112},{80,64},{96,80},{112,96},{1... | collective-permute-start | bytes 32 | tf_op jit(solution)/shard_map/ppermute | solution.py:42
  77.2 6.4 %collective-permute-start.8 = (f32[2]{0:T(128)S(1)}, f32[2]{0:T(128)S(1)}, u32[]{:S(2)}, u32[]{:S(2)}) collective-permute-start(f32[2]{0:T(128)S(1)} %pad_maximum_fusion.18), channel_id=1, source_target_pairs={{0,16},{16,32},{32,48},{48,0},{64,80},{80,96},{96,112},{112,64},{1... | collective-permute-start | bytes 32 | tf_op jit(solution)/shard_map/ppermute | solution.py:42
  77.2 6.4 %collective-permute-start.9 = (f32[2]{0:T(128)S(1)}, f32[2]{0:T(128)S(1)}, u32[]{:S(2)}, u32[]{:S(2)}) collective-permute-start(f32[2]{0:T(128)S(1)} %pad_maximum_fusion.18), channel_id=1, source_target_pairs={{0,32},{16,48},{32,0},{48,16},{64,96},{80,112},{96,64},{112,80},{1... | collective-permute-start | bytes 32 | tf_op jit(solution)/shard_map/ppermute | solution.py:42
  85.0 5.1 %collective-permute-start.11 = (f32[2]{0:T(128)S(1)}, f32[2]{0:T(128)S(1)}, u32[]{:S(2)}, u32[]{:S(2)}) collective-permute-start(f32[2]{0:T(128)S(1)} %add_add_fusion.6), channel_id=1, source_target_pairs={{0,64},{16,80},{32,96},{48,112},{64,0},{80,16},{96,32},{112,48},{1... | collective-permute-start | bytes 32 | tf_op jit(solution)/shard_map/ppermute | solution.py:42
  90.1 7.4 %collective-permute-start.12 = (f32[2]{0:T(128)S(1)}, f32[2]{0:T(128)S(1)}, u32[]{:S(2)}, u32[]{:S(2)}) collective-permute-start(f32[2]{0:T(128)S(1)} %add.305), channel_id=1, source_target_pairs={{0,1},{1,2},{2,3},{3,0},{4,5},{5,6},{6,7},{7,4},{8,9},{9,10},{10,1... | collective-permute-start | bytes 32 | tf_op jit(solution)/shard_map/ppermute | solution.py:42
  91.9 7.1 %collective-permute-start.13 = (f32[2]{0:T(128)S(1)}, f32[2]{0:T(128)S(1)}, u32[]{:S(2)}, u32[]{:S(2)}) collective-permute-start(f32[2]{0:T(128)S(1)} %add.305), channel_id=1, source_target_pairs={{0,2},{1,3},{2,0},{3,1},{4,6},{5,7},{6,4},{7,5},{8,10},{9,11},{10,... | collective-permute-start | bytes 32 | tf_op jit(solution)/shard_map/ppermute | solution.py:42
  101.0 6.2 %collective-permute-start.15 = (f32[2]{0:T(128)S(1)}, f32[2]{0:T(128)S(1)}, u32[]{:S(2)}, u32[]{:S(2)}) collective-permute-start(f32[2]{0:T(128)S(1)} %add_add_fusion.5), channel_id=1, source_target_pairs={{0,4},{1,5},{2,6},{3,7},{4,8},{5,9},{6,10},{7,11},{8,12},{9,13},{1... | collective-permute-start | bytes 32 | tf_op jit(solution)/shard_map/ppermute | solution.py:42
  102.7 5.1 %collective-permute-start.16 = (f32[2]{0:T(128)S(1)}, f32[2]{0:T(128)S(1)}, u32[]{:S(2)}, u32[]{:S(2)}) collective-permute-start(f32[2]{0:T(128)S(1)} %add_add_fusion.5), channel_id=1, source_target_pairs={{0,8},{1,9},{2,10},{3,11},{4,12},{5,13},{6,14},{7,15},{8,0},{9,1},... | collective-permute-start | bytes 32 | tf_op jit(solution)/shard_map/ppermute | solution.py:42
  104.6 3.8 %collective-permute-start.17 = (f32[2]{0:T(128)S(1)}, f32[2]{0:T(128)S(1)}, u32[]{:S(2)}, u32[]{:S(2)}) collective-permute-start(f32[2]{0:T(128)S(1)} %add_add_fusion.5), channel_id=1, source_target_pairs={{0,12},{1,13},{2,14},{3,15},{4,0},{5,1},{6,2},{7,3},{8,4},{9,5},{1... | collective-permute-start | bytes 32 | tf_op jit(solution)/shard_map/ppermute | solution.py:42
  113.9 3.6 %collective-permute-start.19 = (f32[4]{0:T(128)S(1)}, f32[4]{0:T(128)S(1)}, u32[]{:S(2)}, u32[]{:S(2)}) collective-permute-start(f32[4]{0:T(128)S(1)} %pad_maximum_fusion.19), channel_id=1, source_target_pairs={{0,32},{16,48},{32,0},{48,16},{64,96},{80,112},{96,64},{112,80},{1... | collective-permute-start | bytes 56 | tf_op jit(solution)/shard_map/ppermute | solution.py:42
  120.2 5.3 %collective-permute-start.21 = (f32[4]{0:T(128)S(1)}, f32[4]{0:T(128)S(1)}, u32[]{:S(2)}, u32[]{:S(2)}) collective-permute-start(f32[4]{0:T(128)S(1)} %add_add_fusion.3), channel_id=1, source_target_pairs={{0,64},{16,80},{32,96},{48,112},{64,0},{80,16},{96,32},{112,48},{1... | collective-permute-start | bytes 56 | tf_op jit(solution)/shard_map/ppermute | solution.py:42
  125.5 4.8 %collective-permute-start.22 = (f32[4]{0:T(128)S(1)}, f32[4]{0:T(128)S(1)}, u32[]{:S(2)}, u32[]{:S(2)}) collective-permute-start(f32[4]{0:T(128)S(1)} %add.323), channel_id=1, source_target_pairs={{0,1},{1,2},{2,3},{3,0},{4,5},{5,6},{6,7},{7,4},{8,9},{9,10},{10,1... | collective-permute-start | bytes 56 | tf_op jit(solution)/shard_map/ppermute | solution.py:42
  127.5 5.1 %collective-permute-start.23 = (f32[4]{0:T(128)S(1)}, f32[4]{0:T(128)S(1)}, u32[]{:S(2)}, u32[]{:S(2)}) collective-permute-start(f32[4]{0:T(128)S(1)} %add.323), channel_id=1, source_target_pairs={{0,2},{1,3},{2,0},{3,1},{4,6},{5,7},{6,4},{7,5},{8,10},{9,11},{10,... | collective-permute-start | bytes 56 | tf_op jit(solution)/shard_map/ppermute | solution.py:42
  133.2 4.8 %collective-permute-start.25 = (f32[4]{0:T(128)S(1)}, f32[4]{0:T(128)S(1)}, u32[]{:S(2)}, u32[]{:S(2)}) collective-permute-start(f32[4]{0:T(128)S(1)} %add_add_fusion.2), channel_id=1, source_target_pairs={{0,4},{1,5},{2,6},{3,7},{4,8},{5,9},{6,10},{7,11},{8,12},{9,13},{1... | collective-permute-start | bytes 56 | tf_op jit(solution)/shard_map/ppermute | solution.py:42
  133.2 5.2 %collective-permute-start.26 = (f32[4]{0:T(128)S(1)}, f32[4]{0:T(128)S(1)}, u32[]{:S(2)}, u32[]{:S(2)}) collective-permute-start(f32[4]{0:T(128)S(1)} %add_add_fusion.2), channel_id=1, source_target_pairs={{0,8},{1,9},{2,10},{3,11},{4,12},{5,13},{6,14},{7,15},{8,0},{9,1},... | collective-permute-start | bytes 56 | tf_op jit(solution)/shard_map/ppermute | solution.py:42
  (22 other events, 410.8 us)

commit v4 on v3

--- a/solution.py
+++ b/solution.py
@@ -131,29 +131,45 @@
         return scatter_nodes(shell_keep(forces + with_base(shells), offset))
 
     rhs = rhs_wide[:, 2 : rows + 2, 2 : cols + 2]
+    own_rhs = gather_shells(rhs_wide[:, 2 : rows + 3, 2 : cols + 3])
+    own_rhs_base = with_base(own_rhs)
+    own_rhs_strain = jnp.einsum("hb,bxy->hxy", strain_map, own_rhs, precision=HIGH)
+    first = all_sum(
+        jnp.stack(
+            [
+                jnp.sum(rhs * rhs),
+                jnp.sum(own_rhs * own_rhs_base) + jnp.sum(weights * own_rhs_strain * own_rhs_strain),
+            ]
+        )
+    )
     image_wide = node_keep(operate(rhs_wide, weights_wide, -2), -1)
     image = image_wide[:, 1 : rows + 1, 1 : cols + 1]
     again = operate(image_wide, weights_wide[:, 1 : rows + 2, 1 : cols + 2], -1)
-    first = all_sum(jnp.stack([jnp.sum(rhs * rhs), jnp.sum(rhs * image)]))
+    own_image = gather_shells(image_wide[:, 1 : rows + 2, 1 : cols + 2])
+    own_image_base = with_base(own_image)
+    own_image_strain = jnp.einsum("hb,bxy->hxy", strain_map, own_image, precision=HIGH)
     norm_now, curvature = first[0], first[1]
     alpha = norm_now / curvature
     residual = rhs - alpha * image
-    bent = image - alpha * again
+    own_res = own_rhs - alpha * own_image
+    own_res_base = own_rhs_base - alpha * own_image_base
+    own_res_strain = own_rhs_strain - alpha * own_image_strain
     second = all_sum(
         jnp.stack(
             [
                 jnp.sum(residual * residual),
-                jnp.sum(residual * bent),
-                jnp.sum(residual * image),
-                jnp.sum(rhs * bent),
+                jnp.sum(own_res * own_res_base)
+                + jnp.sum(weights * own_res_strain * own_res_strain),
+                jnp.sum(own_res * own_rhs_base)
+                + jnp.sum(weights * own_res_strain * own_rhs_strain),
             ]
         )
     )
     norm_next = second[0]
     beta = norm_next / norm_now
     direction = residual + beta * rhs
-    turned = bent + beta * image
-    curvature_next = second[1] + beta * (second[2] + second[3]) + beta * beta * curvature
+    turned = image - alpha * again + beta * image
+    curvature_next = second[1] + 2.0 * beta * second[2] + beta * beta * curvature
     alpha_next = norm_next / curvature_next
     solution = alpha * rhs + alpha_next * direction
     residual = residual - alpha_next * turned

time: 149 us -> 161 us (1.081)
  matrix products: 15.2 us -> 26.9 us
  waiting for transfers between devices: 26.3 us -> 22.5 us
  between operations: 7.02 us -> 10.2 us
  other arithmetic: 14 us -> 11.9 us
  starting transfers between devices: 63.5 us -> 65.3 us
    dot_general x0 -> x2, matrix products: none -> 5.89 us  [the longest x1 3.39 us: shards(): jnp.einsum('hb,bxy->hxy', strain_map, own_rhs, precision=HIGH)]
    dot_general x3 -> x5, matrix products: 1.83 us -> 6.21 us  [with_base(): return jnp.einsum('ab,bxy->axy', stiff_base, shells, precision=HIGH)]
    ppermute x20, starting transfers between devices: 33.8 us -> 37.9 us  [all_sum(): total = total + lax.ppermute(value, axis, pairs)]
    ppermute x20, waiting for transfers between devices: 17.2 us -> 14.6 us  [all_sum(): total = total + lax.ppermute(value, axis, pairs)]
    another operation x2, other arithmetic: 4 us -> 1.44 us  [the longest x1 0.72 us: shards(): jnp.stack([jnp.sum(residual * residual), jnp.sum(own_res * own_res_base)...]
    add x8, other arithmetic: 4.04 us -> 1.53 us  [all_sum(): total = total + lax.ppermute(value, axis, pairs)]
    ppermute x4, starting transfers between devices: 10.2 us -> 7.85 us  [with_halo(): parts.insert(0, lax.ppermute(last, axis, up))]
    convert_element_type x5, other arithmetic: 0.98 us -> 2.8 us  [inside(): return (row_ok[:, None] & col_ok[None, :]).astype(jnp.float32)]
  transfers between devices with their start and end apart: 29 -> 29, of which waited for: 18 -> 12; matrix products, arithmetic and copies ran while one was open for 14% -> 17% of each run, Pallas kernels for 0% -> 0%
where the time goes in v4:
time: 161 us; the launch traced here: 160 us
  starting transfers between devices  65.3 us (41%)
  matrix products  26.9 us (17%)
  local copies, waits for them, and re-layouts  23.7 us (15%)
  waiting for transfers between devices  22.5 us (14%)
  other arithmetic  11.9 us (7%)
  between operations  10.2 us (6%)
    ppermute x20, starting transfers between devices, all_sum(): total = total + lax.ppermute(value, axis, pairs)  37.9 us
    ppermute x20, waiting for transfers between devices, all_sum(): total = total + lax.ppermute(value, axis, pairs)  14.6 us
    all_to_all x1, starting transfers between devices, shards(): lax.all_to_all(held, ('px', 'py'), split_axis=1, concat_axis=1, tiled=True)  14.2 us
    unnamed x59, local copies, waits for them, and re-layouts  11 us
    scatter x1, local copies, waits for them, and re-layouts, shards(): contact = contact_home.reshape(hist, cells).at[:, targets].set(arrived.re...  8.41 us
    ppermute x4, starting transfers between devices, with_halo(): parts.insert(0, lax.ppermute(last, axis, up))  7.85 us
    dot_general x5, matrix products, with_base(): return jnp.einsum('ab,bxy->axy', stiff_base, shells, precision=HIGH)  6.21 us
    ppermute x4, starting transfers between devices, with_halo(): parts.append(lax.ppermute(leading, axis, down))  5.39 us
  transfers between devices with their start and end apart: 29, of which 12 were waited for; matrix products, arithmetic and copies ran while one was open for 17% of the time, Pallas kernels for 0%

profile of v4, /device:TPU:0, one launch (start us, length us, event | category | flops | bytes accessed | tf_op | source)
XLA Modules:
  0.0 160.5 jit_solution(17939144555492882985)
XLA Ops:
  7.3 14.2 %all-to-all-start = ((f32[128,128,9]{0,2,1:T(8,128)}), f32[128,128,9]{0,2,1:T(8,128)S(1)}, u32[]{:S(2)}, u32[]{:S(2)}) async-start(f32[128,128,9]{0,2,1:T(8,128)} %reshape.262), calls=%async_computation | async-start | bytes 2097152 | tf_op jit(solution)/shard_map/all_to_all | solution.py:98
  25.3 2.9 %collective-permute-start.2 = (f32[12,22,3]{2,0,1:T(8,128)}, f32[12,22,3]{2,0,1:T(8,128)S(1)}, u32[]{:S(2)}, u32[]{:S(2)}) collective-permute-start(f32[12,22,3]{2,0,1:T(8,128)} %get-tuple-element.23), channel_id=1, source_target_pairs={{0,1},{1,2},{2,3},{3,4},{4,5},{5,6},{6,7},{7,8},{8,9},{9,10},{10,1... | collective-permute-start | bytes 9512 | tf_op jit(solution)/shard_map/ppermute | solution.py:22
  32.9 3.7 %collective-permute-done.2 = f32[12,22,3]{2,0,1:T(8,128)S(1)} collective-permute-done((f32[12,22,3]{2,0,1:T(8,128)}, f32[12,22,3]{2,0,1:T(8,128)S(1)}, u32[]{:S(2)}, u32[]{:S(2)}) %collective-permute-start.2) | collective-permute-done | bytes 3200 | tf_op jit(solution)/shard_map/ppermute | solution.py:22
  47.6 2.5 %convolution_bitcast_fusion.1 = f32[128,19,131]{0,2,1:T(8,128)S(1)} fusion(f32[6,19,131]{2,0,1:T(8,128)S(1)} %get-tuple-element.26, f32[6,19,131]{2,0,1:T(8,128)S(1)} %get-tuple-element.27, f32[6,19,131]{2,0,1:T(8,128)S(1)} %get-tuple-element.28, f32[6,19,131]{2,0,1:T(8,128)S(1)} %get-tuple-element.25, f32[128,24]{0,1:T(8,128)S(1)} %copy-done), kind=kOutput, calls=%fused_computation.5 | convolution fusion | flops 91933704 | bytes 1525600 | tf_op jit(solution)/shard_map/hb,bxy->hxy/dot_general | solution.py:129
  50.3 8.4 %scatter_custom_fusion = f32[128,2048]{0,1:T(8,128)} fusion(f32[128,2048]{0,1:T(8,128)} %bitcast.106, s32[1152]{0:T(1024)} %fusion.60, f32[128,1152]{0,1:T(8,128)S(1)} %reshape.267), kind=kCustom, calls=%fused_computation.37 | custom fusion | bytes 1638400 | tf_op jit(solution)/shard_map/scatter | solution.py:122
  58.7 5.0 %fusion.20 = (f32[128,2048]{0,1:T(8,128)S(1)}, f32[128,2048]{0,1:T(8,128)}) fusion(f32[128,2048]{0,1:T(8,128)} %scatter_custom_fusion, f32[128,2048]{0,1:T(8,128)} %bitcast.105, f32[128,24]{0,1:T(8,128)S(1)} %copy-done, f32[6,21,133]{2,0,1:T(8,128)S(1)} %get-tuple-element.19, f32[6,21,133]{2,0,1:T(8,128)} %get-tuple-element.20, ...), kind=kOutput, calls=%fused_computation.33 | convolution fusion | flops 77742080 | bytes 4474720 | tf_op jit(solution)/shard_map/dot_general | solution.py:116
  63.7 3.4 %fusion.19 = (f32[]{:T(128)}, f32[128,16,128]{0,2,1:T(8,128)}) fusion(f32[128,16,128]{0,2,1:T(8,128)S(1)} %bitcast.99, f32[128,24]{0,1:T(8,128)S(1)} %copy-done, f32[6,16,128]{2,0,1:T(8,128)S(1)} %get-tuple-element.30, f32[6,16,128]{2,0,1:T(8,128)S(1)} %copy-done.8, f32[6,16,128]{2,0,1:T(8,128)S(1)} %copy-done.11, f32[6,16,128]{2,0,1:T(8,128)S(1)} %copy-done.14), kind=kOutput, calls=%fused_computation.32 | convolution fusion | flops 76431360 | bytes 2306052 | tf_op jit(solution)/shard_map/hb,bxy->hxy/dot_general | solution.py:136
  74.3 2.6 %copy.39 = f32[128,16,128]{2,1,0:T(8,128)} copy(f32[128,16,128]{0,2,1:T(8,128)} %bitcast.107) | data formatting | bytes 2097152
  77.7 5.4 %collective-permute-start.7 = (f32[2]{0:T(128)S(1)}, f32[2]{0:T(128)S(1)}, u32[]{:S(2)}, u32[]{:S(2)}) collective-permute-start(f32[2]{0:T(128)S(1)} %add_add_fusion.6), channel_id=1, source_target_pairs={{0,64},{16,80},{32,96},{48,112},{64,0},{80,16},{96,32},{112,48},{1... | collective-permute-start | bytes 32 | tf_op jit(solution)/shard_map/ppermute | solution.py:42
  84.7 3.9 %collective-permute-start.10 = (f32[2]{0:T(128)S(1)}, f32[2]{0:T(128)S(1)}, u32[]{:S(2)}, u32[]{:S(2)}) collective-permute-start(f32[2]{0:T(128)S(1)} %add.295), channel_id=1, source_target_pairs={{0,3},{1,0},{2,1},{3,2},{4,7},{5,4},{6,5},{7,6},{8,11},{9,8},{10,9... | collective-permute-start | bytes 32 | tf_op jit(solution)/shard_map/ppermute | solution.py:42
  90.1 3.3 %collective-permute-done.8 = f32[2]{0:T(128)S(1)} collective-permute-done((f32[2]{0:T(128)S(1)}, f32[2]{0:T(128)S(1)}, u32[]{:S(2)}, u32[]{:S(2)}) %collective-permute-start.8) | collective-permute-done | bytes 40 | tf_op jit(solution)/shard_map/ppermute | solution.py:42
  95.7 2.2 %collective-permute-start.12 = (f32[2]{0:T(128)S(1)}, f32[2]{0:T(128)S(1)}, u32[]{:S(2)}, u32[]{:S(2)}) collective-permute-start(f32[2]{0:T(128)S(1)} %add_add_fusion.5), channel_id=1, source_target_pairs={{0,8},{1,9},{2,10},{3,11},{4,12},{5,13},{6,14},{7,15},{8,0},{9,1},... | collective-permute-start | bytes 32 | tf_op jit(solution)/shard_map/ppermute | solution.py:42
  101.5 2.3 %collective-permute-start.16 = (f32[128,19,2]{0,2,1:T(2,128)S(1)}, f32[128,19,2]{0,2,1:T(2,128)S(1)}, u32[]{:S(2)}, u32[]{:S(2)}) collective-permute-start(f32[128,19,2]{0,2,1:T(2,128)S(1)} %pad_maximum_fusion.17), channel_id=1, source_target_pairs={{0,1},{1,2},{2,3},{3,4},{4,5},{5,6},{6,7},{7,8},{8,9},{9,10},{10,1... | collective-permute-start | bytes 58376 | tf_op jit(solution)/shard_map/ppermute | solution.py:22
  107.3 2.1 %collective-permute-done.17 = f32[128,19,1]{0,2,1:T(1,128)S(1)} collective-permute-done((f32[128,19,1]{0,2,1:T(1,128)S(1)}, f32[128,19,1]{0,2,1:T(1,128)S(1)}, u32[]{:S(2)}, u32[]{:S(2)}) %collective-permute-start.17) | collective-permute-done | bytes 9760 | tf_op jit(solution)/shard_map/ppermute | solution.py:25
  109.5 2.2 %fusion.13 = f32[24,19,131]{2,0,1:T(8,128)S(1)} fusion(f32[19,131,24]{1,2,0:T(8,128)S(1)} %copy-done.2, f32[128,19,131]{0,2,1:T(8,128)S(1)} %convolution_bitcast_fusion.1, f32[128,19,1]{0,2,1:T(1,128)S(1)} %collective-permute-done.17, f32[128,1,128]{0,2,1:T(8,128)S(1)} %collective-permute-done.15, f32[128,16,128]{0,2,1:T(8,128)S(1)} %bitcast.102, ...), kind=kOutput, calls=%fused_computation.22 | convolution fusion | flops 93466928 | bytes 3048868 | tf_op jit(solution)/shard_map/hb,hxy->bxy/dot_general | solution.py:130
  112.1 2.2 %convolution_bitcast_fusion.2 = f32[128,17,129]{0,2,1:T(8,128)S(1)} fusion(f32[6,17,129]{2,0,1:T(8,128)S(1)} %get-tuple-element.35, f32[6,17,129]{2,0,1:T(8,128)S(1)} %get-tuple-element.36, f32[6,17,129]{2,0,1:T(8,128)S(1)} %get-tuple-element.37, f32[6,17,129]{2,0,1:T(8,128)S(1)} %get-tuple-element.34, f32[128,24]{0,1:T(8,128)S(1)} %copy-done), kind=kOutput, calls=%fused_computation.6 | convolution fusion | flops 81000648 | bytes 1345632 | tf_op jit(solution)/shard_map/hb,bxy->hxy/dot_general | solution.py:129
  117.3 2.5 %multiply_reduce_fusion.1 = (f32[]{:T(128)}, f32[]{:T(128)}) fusion(f32[128,16,128]{0,2,1:T(8,128)S(1)} %bitcast.103, f32[128,16,128]{0,2,1:T(8,128)S(1)} %copy-done.1, f32[]{:T(128)S(6)} %div.9, f32[128,24]{0,1:T(8,128)S(1)} %copy-done, f32[6,16,128]{2,0,1:T(8,128)S(1)} %get-tuple-element.39, f32[6,16,128]{2,0,1:T(8,128)S(1)} %get-tuple-element.40, ...), kind=kOutput, calls=%fused_computation.36 | convolution fusion | flops 77479936 | bytes 2306060 | tf_op jit(solution)/shard_map/hb,bxy->hxy/dot_general | solution.py:150
  123.0 2.6 %collective-permute-start.19 = (f32[3]{0:T(128)S(1)}, f32[3]{0:T(128)S(1)}, u32[]{:S(2)}, u32[]{:S(2)}) collective-permute-start(f32[3]{0:T(128)S(1)} %pad_maximum_fusion.21), channel_id=1, source_target_pairs={{0,32},{16,48},{32,0},{48,16},{64,96},{80,112},{96,64},{112,80},{1... | collective-permute-start | bytes 44 | tf_op jit(solution)/shard_map/ppermute | solution.py:42
  127.0 2.9 %fusion.15 = f32[24,17,129]{2,0,1:T(8,128)S(1)} fusion(f32[17,129,24]{1,2,0:T(8,128)S(1)} %fusion.35, f32[128,17,129]{0,2,1:T(8,128)S(1)} %convolution_bitcast_fusion.2, f32[128,19,2]{0,2,1:T(2,128)} %copy-done.23, f32[128,1,128]{0,2,1:T(8,128)} %copy-done.4, f32[128,16,128]{0,2,1:T(8,128)S(1)} %bitcast.104, ...), kind=kOutput, calls=%fused_computation.25 | convolution fusion | flops 82070832 | bytes 2829572 | tf_op jit(solution)/shard_map/hb,hxy->bxy/dot_general | solution.py:130
  130.6 2.2 %collective-permute-start.21 = (f32[3]{0:T(128)S(1)}, f32[3]{0:T(128)S(1)}, u32[]{:S(2)}, u32[]{:S(2)}) collective-permute-start(f32[3]{0:T(128)S(1)} %add_add_fusion.3), channel_id=1, source_target_pairs={{0,64},{16,80},{32,96},{48,112},{64,0},{80,16},{96,32},{112,48},{1... | collective-permute-start | bytes 44 | tf_op jit(solution)/shard_map/ppermute | solution.py:42
  132.7 2.9 %collective-permute-done.21 = f32[3]{0:T(128)S(1)} collective-permute-done((f32[3]{0:T(128)S(1)}, f32[3]{0:T(128)S(1)}, u32[]{:S(2)}, u32[]{:S(2)}) %collective-permute-start.21) | collective-permute-done | bytes 44 | tf_op jit(solution)/shard_map/ppermute | solution.py:42
  137.1 4.5 %collective-permute-start.23 = (f32[3]{0:T(128)S(1)}, f32[3]{0:T(128)S(1)}, u32[]{:S(2)}, u32[]{:S(2)}) collective-permute-start(f32[3]{0:T(128)S(1)} %add.321), channel_id=1, source_target_pairs={{0,2},{1,3},{2,0},{3,1},{4,6},{5,7},{6,4},{7,5},{8,10},{9,11},{10,... | collective-permute-start | bytes 44 | tf_op jit(solution)/shard_map/ppermute | solution.py:42
  146.3 2.8 %collective-permute-start.26 = (f32[3]{0:T(128)S(1)}, f32[3]{0:T(128)S(1)}, u32[]{:S(2)}, u32[]{:S(2)}) collective-permute-start(f32[3]{0:T(128)S(1)} %add_add_fusion.2), channel_id=1, source_target_pairs={{0,8},{1,9},{2,10},{3,11},{4,12},{5,13},{6,14},{7,15},{8,0},{9,1},... | collective-permute-start | bytes 44 | tf_op jit(solution)/shard_map/ppermute | solution.py:42
  149.1 2.5 %collective-permute-start.27 = (f32[3]{0:T(128)S(1)}, f32[3]{0:T(128)S(1)}, u32[]{:S(2)}, u32[]{:S(2)}) collective-permute-start(f32[3]{0:T(128)S(1)} %add_add_fusion.2), channel_id=1, source_target_pairs={{0,12},{1,13},{2,14},{3,15},{4,0},{5,1},{6,2},{7,3},{8,4},{9,5},{1... | collective-permute-start | bytes 44 | tf_op jit(solution)/shard_map/ppermute | solution.py:42
  (153 shorter events, 60.9 us)
Async XLA Ops:
  2.3 22.1 %collective-permute-start = (f32[12,3,128]{2,0,1:T(8,128)S(1)}, f32[12,3,128]{2,0,1:T(8,128)S(1)}, u32[]{:S(2)}, u32[]{:S(2)}) collective-permute-start(f32[12,3,128]{2,0,1:T(8,128)S(1)} %get-tuple-element.43), channel_id=1, source_target_pairs={{0,16},{16,32},{32,48},{48,64},{64,80},{80,96},{96,112},{1,17},{17... | collective-permute-start | bytes 55304 | tf_op jit(solution)/shard_map/ppermute | solution.py:22
  3.6 20.8 %collective-permute-start.1 = (f32[12,3,128]{2,0,1:T(8,128)S(1)}, f32[12,3,128]{2,0,1:T(8,128)S(1)}, u32[]{:S(2)}, u32[]{:S(2)}) collective-permute-start(f32[12,3,128]{2,0,1:T(8,128)S(1)} %get-tuple-element.44), channel_id=1, source_target_pairs={{16,0},{32,16},{48,32},{64,48},{80,64},{96,80},{112,96},{17,1},{33... | collective-permute-start | bytes 55304 | tf_op jit(solution)/shard_map/ppermute | solution.py:25
  7.3 42.9 %all-to-all-start = ((f32[128,128,9]{0,2,1:T(8,128)}), f32[128,128,9]{0,2,1:T(8,128)S(1)}, u32[]{:S(2)}, u32[]{:S(2)}) async-start(f32[128,128,9]{0,2,1:T(8,128)} %reshape.262), calls=%async_computation | async-start | bytes 2097152 | tf_op jit(solution)/shard_map/all_to_all | solution.py:98
  25.3 11.3 %collective-permute-start.2 = (f32[12,22,3]{2,0,1:T(8,128)}, f32[12,22,3]{2,0,1:T(8,128)S(1)}, u32[]{:S(2)}, u32[]{:S(2)}) collective-permute-start(f32[12,22,3]{2,0,1:T(8,128)} %get-tuple-element.23), channel_id=1, source_target_pairs={{0,1},{1,2},{2,3},{3,4},{4,5},{5,6},{6,7},{7,8},{8,9},{9,10},{10,1... | collective-permute-start | bytes 9512 | tf_op jit(solution)/shard_map/ppermute | solution.py:22
  28.2 10.4 %collective-permute-start.3 = (f32[12,22,3]{2,0,1:T(8,128)}, f32[12,22,3]{2,0,1:T(8,128)}, u32[]{:S(2)}, u32[]{:S(2)}) collective-permute-start(f32[12,22,3]{2,0,1:T(8,128)} %get-tuple-element.24), channel_id=1, source_target_pairs={{1,0},{2,1},{3,2},{4,3},{5,4},{6,5},{7,6},{8,7},{9,8},{10,9},{11,1... | collective-permute-start | bytes 9512 | tf_op jit(solution)/shard_map/ppermute | solution.py:25
  69.2 7.7 %collective-permute-start.4 = (f32[2]{0:T(128)S(1)}, f32[2]{0:T(128)S(1)}, u32[]{:S(2)}, u32[]{:S(2)}) collective-permute-start(f32[2]{0:T(128)S(1)} %pad_maximum_fusion.20), channel_id=1, source_target_pairs={{0,16},{16,32},{32,48},{48,0},{64,80},{80,96},{96,112},{112,64},{1... | collective-permute-start | bytes 32 | tf_op jit(solution)/shard_map/ppermute | solution.py:42
  69.2 7.7 %collective-permute-start.5 = (f32[2]{0:T(128)S(1)}, f32[2]{0:T(128)S(1)}, u32[]{:S(2)}, u32[]{:S(2)}) collective-permute-start(f32[2]{0:T(128)S(1)} %pad_maximum_fusion.20), channel_id=1, source_target_pairs={{0,32},{16,48},{32,0},{48,16},{64,96},{80,112},{96,64},{112,80},{1... | collective-permute-start | bytes 32 | tf_op jit(solution)/shard_map/ppermute | solution.py:42
  70.2 6.7 %collective-permute-start.6 = (f32[2]{0:T(128)S(1)}, f32[2]{0:T(128)S(1)}, u32[]{:S(2)}, u32[]{:S(2)}) collective-permute-start(f32[2]{0:T(128)S(1)} %pad_maximum_fusion.20), channel_id=1, source_target_pairs={{0,48},{16,0},{32,16},{48,32},{64,112},{80,64},{96,80},{112,96},{1... | collective-permute-start | bytes 32 | tf_op jit(solution)/shard_map/ppermute | solution.py:42
  71.6 29.9 %collective-permute-start.14 = (f32[128,2,128]{0,2,1:T(8,128)S(1)}, f32[128,2,128]{0,2,1:T(8,128)S(1)}, u32[]{:S(2)}, u32[]{:S(2)}) collective-permute-start(f32[128,2,128]{0,2,1:T(8,128)S(1)} %slice.230), channel_id=1, source_target_pairs={{0,16},{16,32},{32,48},{48,64},{64,80},{80,96},{96,112},{1,17},{17... | collective-permute-start | bytes 393224 | tf_op jit(solution)/shard_map/ppermute | solution.py:22
  73.0 28.5 %collective-permute-start.15 = (f32[128,1,128]{0,2,1:T(8,128)S(1)}, f32[128,1,128]{0,2,1:T(8,128)S(1)}, u32[]{:S(2)}, u32[]{:S(2)}) collective-permute-start(f32[128,1,128]{0,2,1:T(8,128)S(1)} %slice.231), channel_id=1, source_target_pairs={{16,0},{32,16},{48,32},{64,48},{80,64},{96,80},{112,96},{17,1},{33... | collective-permute-start | bytes 196616 | tf_op jit(solution)/shard_map/ppermute | solution.py:25
  77.7 7.0 %collective-permute-start.7 = (f32[2]{0:T(128)S(1)}, f32[2]{0:T(128)S(1)}, u32[]{:S(2)}, u32[]{:S(2)}) collective-permute-start(f32[2]{0:T(128)S(1)} %add_add_fusion.6), channel_id=1, source_target_pairs={{0,64},{16,80},{32,96},{48,112},{64,0},{80,16},{96,32},{112,48},{1... | collective-permute-start | bytes 32 | tf_op jit(solution)/shard_map/ppermute | solution.py:42
  84.7 5.4 %collective-permute-start.10 = (f32[2]{0:T(128)S(1)}, f32[2]{0:T(128)S(1)}, u32[]{:S(2)}, u32[]{:S(2)}) collective-permute-start(f32[2]{0:T(128)S(1)} %add.295), channel_id=1, source_target_pairs={{0,3},{1,0},{2,1},{3,2},{4,7},{5,4},{6,5},{7,6},{8,11},{9,8},{10,9... | collective-permute-start | bytes 32 | tf_op jit(solution)/shard_map/ppermute | solution.py:42
  88.6 5.1 %collective-permute-start.9 = (f32[2]{0:T(128)S(1)}, f32[2]{0:T(128)S(1)}, u32[]{:S(2)}, u32[]{:S(2)}) collective-permute-start(f32[2]{0:T(128)S(1)} %add.295), channel_id=1, source_target_pairs={{0,2},{1,3},{2,0},{3,1},{4,6},{5,7},{6,4},{7,5},{8,10},{9,11},{10,... | collective-permute-start | bytes 32 | tf_op jit(solution)/shard_map/ppermute | solution.py:42
  93.7 5.9 %collective-permute-start.11 = (f32[2]{0:T(128)S(1)}, f32[2]{0:T(128)S(1)}, u32[]{:S(2)}, u32[]{:S(2)}) collective-permute-start(f32[2]{0:T(128)S(1)} %add_add_fusion.5), channel_id=1, source_target_pairs={{0,4},{1,5},{2,6},{3,7},{4,8},{5,9},{6,10},{7,11},{8,12},{9,13},{1... | collective-permute-start | bytes 32 | tf_op jit(solution)/shard_map/ppermute | solution.py:42
  95.7 5.1 %collective-permute-start.12 = (f32[2]{0:T(128)S(1)}, f32[2]{0:T(128)S(1)}, u32[]{:S(2)}, u32[]{:S(2)}) collective-permute-start(f32[2]{0:T(128)S(1)} %add_add_fusion.5), channel_id=1, source_target_pairs={{0,8},{1,9},{2,10},{3,11},{4,12},{5,13},{6,14},{7,15},{8,0},{9,1},... | collective-permute-start | bytes 32 | tf_op jit(solution)/shard_map/ppermute | solution.py:42
  101.5 7.9 %collective-permute-start.16 = (f32[128,19,2]{0,2,1:T(2,128)S(1)}, f32[128,19,2]{0,2,1:T(2,128)S(1)}, u32[]{:S(2)}, u32[]{:S(2)}) collective-permute-start(f32[128,19,2]{0,2,1:T(2,128)S(1)} %pad_maximum_fusion.17), channel_id=1, source_target_pairs={{0,1},{1,2},{2,3},{3,4},{4,5},{5,6},{6,7},{7,8},{8,9},{9,10},{10,1... | collective-permute-start | bytes 58376 | tf_op jit(solution)/shard_map/ppermute | solution.py:22
  103.9 5.6 %collective-permute-start.17 = (f32[128,19,1]{0,2,1:T(1,128)S(1)}, f32[128,19,1]{0,2,1:T(1,128)S(1)}, u32[]{:S(2)}, u32[]{:S(2)}) collective-permute-start(f32[128,19,1]{0,2,1:T(1,128)S(1)} %pad_maximum_fusion.18), channel_id=1, source_target_pairs={{1,0},{2,1},{3,2},{4,3},{5,4},{6,5},{7,6},{8,7},{9,8},{10,9},{11,1... | collective-permute-start | bytes 29192 | tf_op jit(solution)/shard_map/ppermute | solution.py:25
  123.0 6.8 %collective-permute-start.18 = (f32[3]{0:T(128)S(1)}, f32[3]{0:T(128)S(1)}, u32[]{:S(2)}, u32[]{:S(2)}) collective-permute-start(f32[3]{0:T(128)S(1)} %pad_maximum_fusion.21), channel_id=1, source_target_pairs={{0,16},{16,32},{32,48},{48,0},{64,80},{80,96},{96,112},{112,64},{1... | collective-permute-start | bytes 44 | tf_op jit(solution)/shard_map/ppermute | solution.py:42
  123.0 6.8 %collective-permute-start.19 = (f32[3]{0:T(128)S(1)}, f32[3]{0:T(128)S(1)}, u32[]{:S(2)}, u32[]{:S(2)}) collective-permute-start(f32[3]{0:T(128)S(1)} %pad_maximum_fusion.21), channel_id=1, source_target_pairs={{0,32},{16,48},{32,0},{48,16},{64,96},{80,112},{96,64},{112,80},{1... | collective-permute-start | bytes 44 | tf_op jit(solution)/shard_map/ppermute | solution.py:42
  130.6 5.1 %collective-permute-start.21 = (f32[3]{0:T(128)S(1)}, f32[3]{0:T(128)S(1)}, u32[]{:S(2)}, u32[]{:S(2)}) collective-permute-start(f32[3]{0:T(128)S(1)} %add_add_fusion.3), channel_id=1, source_target_pairs={{0,64},{16,80},{32,96},{48,112},{64,0},{80,16},{96,32},{112,48},{1... | collective-permute-start | bytes 44 | tf_op jit(solution)/shard_map/ppermute | solution.py:42
  135.7 6.1 %collective-permute-start.22 = (f32[3]{0:T(128)S(1)}, f32[3]{0:T(128)S(1)}, u32[]{:S(2)}, u32[]{:S(2)}) collective-permute-start(f32[3]{0:T(128)S(1)} %add.321), channel_id=1, source_target_pairs={{0,1},{1,2},{2,3},{3,0},{4,5},{5,6},{6,7},{7,4},{8,9},{9,10},{10,1... | collective-permute-start | bytes 44 | tf_op jit(solution)/shard_map/ppermute | solution.py:42
  137.1 6.0 %collective-permute-start.23 = (f32[3]{0:T(128)S(1)}, f32[3]{0:T(128)S(1)}, u32[]{:S(2)}, u32[]{:S(2)}) collective-permute-start(f32[3]{0:T(128)S(1)} %add.321), channel_id=1, source_target_pairs={{0,2},{1,3},{2,0},{3,1},{4,6},{5,7},{6,4},{7,5},{8,10},{9,11},{10,... | collective-permute-start | bytes 44 | tf_op jit(solution)/shard_map/ppermute | solution.py:42
  145.2 6.5 %collective-permute-start.25 = (f32[3]{0:T(128)S(1)}, f32[3]{0:T(128)S(1)}, u32[]{:S(2)}, u32[]{:S(2)}) collective-permute-start(f32[3]{0:T(128)S(1)} %add_add_fusion.2), channel_id=1, source_target_pairs={{0,4},{1,5},{2,6},{3,7},{4,8},{5,9},{6,10},{7,11},{8,12},{9,13},{1... | collective-permute-start | bytes 44 | tf_op jit(solution)/shard_map/ppermute | solution.py:42
  146.3 5.4 %collective-permute-start.26 = (f32[3]{0:T(128)S(1)}, f32[3]{0:T(128)S(1)}, u32[]{:S(2)}, u32[]{:S(2)}) collective-permute-start(f32[3]{0:T(128)S(1)} %add_add_fusion.2), channel_id=1, source_target_pairs={{0,8},{1,9},{2,10},{3,11},{4,12},{5,13},{6,14},{7,15},{8,0},{9,1},... | collective-permute-start | bytes 44 | tf_op jit(solution)/shard_map/ppermute | solution.py:42
  (30 other events, 271.3 us)

commit v5 on v3

--- a/solution.py
+++ b/solution.py
@@ -116,12 +116,16 @@
     history_new = history.reshape(hist, cells) + jnp.dot(strain_map, own, precision=HIGH)
     rhs_wide = node_keep(both[6:, 1 : rows + 5, 1 : cols + 5] - force_wide, -2)
 
-    contact = (
-        contact_home.reshape(hist, cells)
-        .at[:, targets]
-        .set(arrived.reshape(hist, devices * width), mode="drop")
+    soft = jax.nn.softplus(history_new)
+    soft_relaid = jnp.take(soft, targets, axis=1, mode="fill", fill_value=0.0)
+    weights_home, soft_relaid = lax.optimization_barrier(
+        (soft * contact_home.reshape(hist, cells), soft_relaid)
     )
-    weights = (jax.nn.softplus(history_new) * contact).reshape(hist, rows, cols)
+    weights = (
+        weights_home.at[:, targets]
+        .set(soft_relaid * arrived.reshape(hist, devices * width), mode="drop")
+        .reshape(hist, rows, cols)
+    )
     weights_wide = with_halo(weights, 2, 1)
 
     def operate(field, weights_of, offset):

time: 149 us -> 152 us (1.020)
  other arithmetic: 14 us -> 23.9 us
  local copies, waits for them, and re-layouts: 22.3 us -> 18 us
    scatter x1 -> x0, local copies, waits for them, and re-layouts: 6.8 us -> none  [shards(): contact = contact_home.reshape(hist, cells).at[:, targets].set(arrived.re...]
    scatter x0 -> x1, other arithmetic: none -> 6.69 us  [shards(): weights = weights_home.at[:, targets].set(soft_relaid * arrived.reshape(h...]
    gather x0 -> x1, local copies, waits for them, and re-layouts: none -> 2.44 us  [shards(): soft_relaid = jnp.take(soft, targets, axis=1, mode='fill', fill_value=0.0)]
    convert_element_type x5, other arithmetic: 0.98 us -> 2.8 us  [inside(): return (row_ok[:, None] & col_ok[None, :]).astype(jnp.float32)]
    unnamed x43 -> x69, local copies, waits for them, and re-layouts: 10.4 us -> 10.6 us
  transfers between devices with their start and end apart: 29 -> 29, of which waited for: 18 -> 19; matrix products, arithmetic and copies ran while one was open for 14% -> 20% of each run, Pallas kernels for 0% -> 0%
where the time goes in v5:
time: 152 us; the launch traced here: 151 us
  starting transfers between devices  62.7 us (41%)
  waiting for transfers between devices  24.8 us (16%)
  other arithmetic  23.9 us (16%)
  local copies, waits for them, and re-layouts  18 us (12%)
  matrix products  15 us (10%)
  between operations  6.99 us (5%)
    ppermute x20, starting transfers between devices, all_sum(): total = total + lax.ppermute(value, axis, pairs)  33.7 us
    ppermute x20, waiting for transfers between devices, all_sum(): total = total + lax.ppermute(value, axis, pairs)  17.2 us
    all_to_all x1, starting transfers between devices, shards(): lax.all_to_all(held, ('px', 'py'), split_axis=1, concat_axis=1, tiled=True)  14.7 us
    unnamed x69, local copies, waits for them, and re-layouts  10.6 us
    ppermute x4, starting transfers between devices, with_halo(): parts.insert(0, lax.ppermute(last, axis, up))  9.01 us
    scatter x1, other arithmetic, shards(): weights = weights_home.at[:, targets].set(soft_relaid * arrived.reshape(h...  6.69 us
    ppermute x4, starting transfers between devices, with_halo(): parts.append(lax.ppermute(leading, axis, down))  5.35 us
    dot_general x2, matrix products, operate(): strains = jnp.einsum('hb,bxy->hxy', strain_map, shells, precision=HIGH)  4.77 us
  transfers between devices with their start and end apart: 29, of which 19 were waited for; matrix products, arithmetic and copies ran while one was open for 20% of the time, Pallas kernels for 0%

profile of v5, /device:TPU:0, one launch (start us, length us, event | category | flops | bytes accessed | tf_op | source)
XLA Modules:
  0.0 151.3 jit_solution(15609212413515863383)
XLA Ops:
  7.3 14.7 %all-to-all-start = ((f32[128,128,9]{0,2,1:T(8,128)}), f32[128,128,9]{0,2,1:T(8,128)}, u32[]{:S(2)}, u32[]{:S(2)}) async-start(f32[128,128,9]{0,2,1:T(8,128)} %reshape.272), calls=%async_computation | async-start | bytes 2097152 | tf_op jit(solution)/shard_map/all_to_all | solution.py:98
  25.9 2.8 %collective-permute-start.2 = (f32[12,22,3]{2,0,1:T(8,128)}, f32[12,22,3]{2,0,1:T(8,128)S(1)}, u32[]{:S(2)}, u32[]{:S(2)}) collective-permute-start(f32[12,22,3]{2,0,1:T(8,128)} %get-tuple-element.34), channel_id=1, source_target_pairs={{0,1},{1,2},{2,3},{3,4},{4,5},{5,6},{6,7},{7,8},{8,9},{9,10},{10,1... | collective-permute-start | bytes 9512 | tf_op jit(solution)/shard_map/ppermute | solution.py:22
  32.5 4.1 %collective-permute-done.2 = f32[12,22,3]{2,0,1:T(8,128)S(1)} collective-permute-done((f32[12,22,3]{2,0,1:T(8,128)}, f32[12,22,3]{2,0,1:T(8,128)S(1)}, u32[]{:S(2)}, u32[]{:S(2)}) %collective-permute-start.2) | collective-permute-done | bytes 3200 | tf_op jit(solution)/shard_map/ppermute | solution.py:22
  36.6 2.2 %collective-permute-done.3 = f32[12,22,3]{2,0,1:T(8,128)} collective-permute-done((f32[12,22,3]{2,0,1:T(8,128)}, f32[12,22,3]{2,0,1:T(8,128)}, u32[]{:S(2)}, u32[]{:S(2)}) %collective-permute-start.3) | collective-permute-done | bytes 3200 | tf_op jit(solution)/shard_map/ppermute | solution.py:25
  40.7 3.2 %compare_select_fusion = (f32[128,2048]{0,1:T(8,128)S(1)}, f32[128,2048]{0,1:T(8,128)S(1)}, f32[128,2048]{0,1:T(8,128)}) fusion(f32[128,16,128]{0,2,1:T(8,128)S(1)} %copy-done.1, f32[128,2048]{0,1:T(8,128)S(1)} %bitcast.76, f32[128,24]{0,1:T(8,128)S(1)} %copy-done, f32[6,21,133]{2,0,1:T(8,128)S(1)} %get-tuple-element.31, ...), kind=kOutput, calls=%fused_computation.2 | convolution fusion | flops 77742080 | bytes 5523296 | tf_op jit(solution)/shard_map/dot_general | solution.py:116
  43.9 2.4 %gather_fusion = f32[1152,128]{1,0:T(8,128)S(1)} fusion(f32[128,2048]{0,1:T(8,128)S(1)} %get-tuple-element.28, s32[2048]{0:T(1024)S(1)} %copy-done.27), kind=kCustom, calls=%fused_computation | custom fusion | bytes 1184256 | tf_op jit(solution)/shard_map/jit(_take)/gather | solution.py:120
  51.7 6.7 %scatter_custom_fusion = f32[128,2048]{0,1:T(8,128)S(1)} fusion(f32[128,2048]{0,1:T(8,128)S(1)} %get-tuple-element.6, s32[1152]{0:T(1024)} %copy-done.28, f32[128,1152]{0,1:T(8,128)S(1)} %select_bitcast_fusion, f32[128,1152]{0,1:T(8,128)S(1)} %reshape.273), kind=kCustom, calls=%fused_computation.31 | custom fusion | flops 147456 | bytes 2228224 | tf_op jit(solution)/shard_map/scatter | solution.py:126
  61.1 2.5 %convolution_bitcast_fusion.1 = f32[128,19,131]{0,2,1:T(8,128)S(1)} fusion(f32[6,19,131]{2,0,1:T(8,128)S(1)} %get-tuple-element.37, f32[6,19,131]{2,0,1:T(8,128)S(1)} %get-tuple-element.38, f32[6,19,131]{2,0,1:T(8,128)S(1)} %get-tuple-element.39, f32[6,19,131]{2,0,1:T(8,128)S(1)} %get-tuple-element.36, f32[128,24]{0,1:T(8,128)S(1)} %copy-done), kind=kOutput, calls=%fused_computation.5 | convolution fusion | flops 91933704 | bytes 1525600 | tf_op jit(solution)/shard_map/hb,bxy->hxy/dot_general | solution.py:133
  64.2 3.6 %collective-permute-start.6 = (f32[128,19,2]{0,2,1:T(2,128)S(1)}, f32[128,19,2]{0,2,1:T(2,128)S(1)}, u32[]{:S(2)}, u32[]{:S(2)}) collective-permute-start(f32[128,19,2]{0,2,1:T(2,128)S(1)} %pad_maximum_fusion.15), channel_id=1, source_target_pairs={{0,1},{1,2},{2,3},{3,4},{4,5},{5,6},{6,7},{7,8},{8,9},{9,10},{10,1... | collective-permute-start | bytes 58376 | tf_op jit(solution)/shard_map/ppermute | solution.py:22
  69.9 2.6 %copy.39 = f32[128,16,128]{2,1,0:T(8,128)} copy(f32[128,16,128]{0,2,1:T(8,128)} %bitcast.75) | data formatting | bytes 2097152
  74.0 2.2 %fusion.13 = f32[24,19,131]{2,0,1:T(8,128)S(1)} fusion(f32[19,131,24]{1,2,0:T(8,128)S(1)} %fusion.31, f32[128,19,131]{0,2,1:T(8,128)S(1)} %convolution_bitcast_fusion.1, f32[128,19,1]{0,2,1:T(1,128)S(1)} %collective-permute-done.7, f32[128,1,128]{0,2,1:T(8,128)S(1)} %collective-permute-done.5, f32[128,16,128]{0,2,1:T(8,128)S(1)} %bitcast.73, ...), kind=kOutput, calls=%fused_computation.21 | convolution fusion | flops 93466928 | bytes 3048868 | tf_op jit(solution)/shard_map/hb,hxy->bxy/dot_general | solution.py:134
  78.4 2.5 %collective-permute-start.10 = (f32[2]{0:T(128)S(1)}, f32[2]{0:T(128)S(1)}, u32[]{:S(2)}, u32[]{:S(2)}) collective-permute-start(f32[2]{0:T(128)S(1)} %pad_maximum_fusion.18), channel_id=1, source_target_pairs={{0,48},{16,0},{32,16},{48,32},{64,112},{80,64},{96,80},{112,96},{1... | collective-permute-start | bytes 32 | tf_op jit(solution)/shard_map/ppermute | solution.py:42
  82.6 2.2 %convolution_bitcast_fusion.2 = f32[128,17,129]{0,2,1:T(8,128)S(1)} fusion(f32[6,17,129]{2,0,1:T(8,128)S(1)} %get-tuple-element.41, f32[6,17,129]{2,0,1:T(8,128)S(1)} %get-tuple-element.42, f32[6,17,129]{2,0,1:T(8,128)S(1)} %get-tuple-element.43, f32[6,17,129]{2,0,1:T(8,128)S(1)} %get-tuple-element.40, f32[128,24]{0,1:T(8,128)S(1)} %copy-done), kind=kOutput, calls=%fused_computation.6 | convolution fusion | flops 81000648 | bytes 1345632 | tf_op jit(solution)/shard_map/hb,bxy->hxy/dot_general | solution.py:133
  88.9 2.7 %collective-permute-start.11 = (f32[2]{0:T(128)S(1)}, f32[2]{0:T(128)S(1)}, u32[]{:S(2)}, u32[]{:S(2)}) collective-permute-start(f32[2]{0:T(128)S(1)} %add_add_fusion.6), channel_id=1, source_target_pairs={{0,64},{16,80},{32,96},{48,112},{64,0},{80,16},{96,32},{112,48},{1... | collective-permute-start | bytes 32 | tf_op jit(solution)/shard_map/ppermute | solution.py:42
  91.6 2.3 %collective-permute-done.11 = f32[2]{0:T(128)S(1)} collective-permute-done((f32[2]{0:T(128)S(1)}, f32[2]{0:T(128)S(1)}, u32[]{:S(2)}, u32[]{:S(2)}) %collective-permute-start.11) | collective-permute-done | bytes 40 | tf_op jit(solution)/shard_map/ppermute | solution.py:42
  95.9 5.1 %collective-permute-start.13 = (f32[2]{0:T(128)S(1)}, f32[2]{0:T(128)S(1)}, u32[]{:S(2)}, u32[]{:S(2)}) collective-permute-start(f32[2]{0:T(128)S(1)} %add.317), channel_id=1, source_target_pairs={{0,2},{1,3},{2,0},{3,1},{4,6},{5,7},{6,4},{7,5},{8,10},{9,11},{10,... | collective-permute-start | bytes 32 | tf_op jit(solution)/shard_map/ppermute | solution.py:42
  108.1 2.5 %collective-permute-start.17 = (f32[2]{0:T(128)S(1)}, f32[2]{0:T(128)S(1)}, u32[]{:S(2)}, u32[]{:S(2)}) collective-permute-start(f32[2]{0:T(128)S(1)} %add_add_fusion.5), channel_id=1, source_target_pairs={{0,12},{1,13},{2,14},{3,15},{4,0},{5,1},{6,2},{7,3},{8,4},{9,5},{1... | collective-permute-start | bytes 32 | tf_op jit(solution)/shard_map/ppermute | solution.py:42
  114.7 2.4 %pad_maximum_fusion.19 = f32[4]{0:T(128)S(1)} fusion(f32[1]{0:T(128)} %bitcast.21, f32[1]{0:T(128)} %bitcast.20, f32[1]{0:T(128)} %bitcast.19, f32[1]{0:T(128)} %bitcast.16), kind=kLoop, calls=%fused_computation.108 | loop fusion | flops 12 | bytes 32 | tf_op jit(solution)/shard_map/stack | solution.py:147
  120.9 2.4 %add_add_fusion.3 = f32[4]{0:T(128)S(1)} fusion(f32[4]{0:T(128)S(1)} %collective-permute-done.20, f32[4]{0:T(128)S(1)} %collective-permute-done.19, f32[4]{0:T(128)S(1)} %collective-permute-done.18, f32[1]{0:T(128)} %bitcast.21, f32[1]{0:T(128)} %bitcast.20, f32[1]{0:T(128)} %bitcast.19, f32[1]{0:T(128)} %bitcast.16), kind=kLoop, calls=%fused_computation.111 | loop fusion | flops 24 | bytes 80 | tf_op jit(solution)/shard_map/add | solution.py:42
  123.3 2.9 %collective-permute-start.21 = (f32[4]{0:T(128)S(1)}, f32[4]{0:T(128)S(1)}, u32[]{:S(2)}, u32[]{:S(2)}) collective-permute-start(f32[4]{0:T(128)S(1)} %add_add_fusion.3), channel_id=1, source_target_pairs={{0,64},{16,80},{32,96},{48,112},{64,0},{80,16},{96,32},{112,48},{1... | collective-permute-start | bytes 56 | tf_op jit(solution)/shard_map/ppermute | solution.py:42
  126.2 2.4 %collective-permute-done.21 = f32[4]{0:T(128)S(1)} collective-permute-done((f32[4]{0:T(128)S(1)}, f32[4]{0:T(128)S(1)}, u32[]{:S(2)}, u32[]{:S(2)}) %collective-permute-start.21) | collective-permute-done | bytes 48 | tf_op jit(solution)/shard_map/ppermute | solution.py:42
  130.5 2.2 %collective-permute-start.23 = (f32[4]{0:T(128)S(1)}, f32[4]{0:T(128)S(1)}, u32[]{:S(2)}, u32[]{:S(2)}) collective-permute-start(f32[4]{0:T(128)S(1)} %add.335), channel_id=1, source_target_pairs={{0,2},{1,3},{2,0},{3,1},{4,6},{5,7},{6,4},{7,5},{8,10},{9,11},{10,... | collective-permute-start | bytes 56 | tf_op jit(solution)/shard_map/ppermute | solution.py:42
  133.4 2.2 %collective-permute-done.23 = f32[4]{0:T(128)S(1)} collective-permute-done((f32[4]{0:T(128)S(1)}, f32[4]{0:T(128)S(1)}, u32[]{:S(2)}, u32[]{:S(2)}) %collective-permute-start.23) | collective-permute-done | bytes 48 | tf_op jit(solution)/shard_map/ppermute | solution.py:42
  136.3 3.6 %collective-permute-start.26 = (f32[4]{0:T(128)S(1)}, f32[4]{0:T(128)S(1)}, u32[]{:S(2)}, u32[]{:S(2)}) collective-permute-start(f32[4]{0:T(128)S(1)} %add_add_fusion.2), channel_id=1, source_target_pairs={{0,8},{1,9},{2,10},{3,11},{4,12},{5,13},{6,14},{7,15},{8,0},{9,1},... | collective-permute-start | bytes 56 | tf_op jit(solution)/shard_map/ppermute | solution.py:42
  (163 shorter events, 61.6 us)
Async XLA Ops:
  2.3 22.7 %collective-permute-start = (f32[12,3,128]{2,0,1:T(8,128)S(1)}, f32[12,3,128]{2,0,1:T(8,128)S(1)}, u32[]{:S(2)}, u32[]{:S(2)}) collective-permute-start(f32[12,3,128]{2,0,1:T(8,128)S(1)} %get-tuple-element.44), channel_id=1, source_target_pairs={{0,16},{16,32},{32,48},{48,64},{64,80},{80,96},{96,112},{1,17},{17... | collective-permute-start | bytes 55304 | tf_op jit(solution)/shard_map/ppermute | solution.py:22
  3.6 21.4 %collective-permute-start.1 = (f32[12,3,128]{2,0,1:T(8,128)S(1)}, f32[12,3,128]{2,0,1:T(8,128)S(1)}, u32[]{:S(2)}, u32[]{:S(2)}) collective-permute-start(f32[12,3,128]{2,0,1:T(8,128)S(1)} %get-tuple-element.45), channel_id=1, source_target_pairs={{16,0},{32,16},{48,32},{64,48},{80,64},{96,80},{112,96},{17,1},{33... | collective-permute-start | bytes 55304 | tf_op jit(solution)/shard_map/ppermute | solution.py:25
  7.3 43.0 %all-to-all-start = ((f32[128,128,9]{0,2,1:T(8,128)}), f32[128,128,9]{0,2,1:T(8,128)}, u32[]{:S(2)}, u32[]{:S(2)}) async-start(f32[128,128,9]{0,2,1:T(8,128)} %reshape.272), calls=%async_computation | async-start | bytes 2097152 | tf_op jit(solution)/shard_map/all_to_all | solution.py:98
  25.9 10.7 %collective-permute-start.2 = (f32[12,22,3]{2,0,1:T(8,128)}, f32[12,22,3]{2,0,1:T(8,128)S(1)}, u32[]{:S(2)}, u32[]{:S(2)}) collective-permute-start(f32[12,22,3]{2,0,1:T(8,128)} %get-tuple-element.34), channel_id=1, source_target_pairs={{0,1},{1,2},{2,3},{3,4},{4,5},{5,6},{6,7},{7,8},{8,9},{9,10},{10,1... | collective-permute-start | bytes 9512 | tf_op jit(solution)/shard_map/ppermute | solution.py:22
  28.7 10.1 %collective-permute-start.3 = (f32[12,22,3]{2,0,1:T(8,128)}, f32[12,22,3]{2,0,1:T(8,128)}, u32[]{:S(2)}, u32[]{:S(2)}) collective-permute-start(f32[12,22,3]{2,0,1:T(8,128)} %get-tuple-element.35), channel_id=1, source_target_pairs={{1,0},{2,1},{3,2},{4,3},{5,4},{6,5},{7,6},{8,7},{9,8},{10,9},{11,1... | collective-permute-start | bytes 9512 | tf_op jit(solution)/shard_map/ppermute | solution.py:25
  58.5 5.7 %collective-permute-start.4 = (f32[128,2,128]{0,2,1:T(8,128)S(1)}, f32[128,2,128]{0,2,1:T(8,128)S(1)}, u32[]{:S(2)}, u32[]{:S(2)}) collective-permute-start(f32[128,2,128]{0,2,1:T(8,128)S(1)} %slice.197), channel_id=1, source_target_pairs={{0,16},{16,32},{32,48},{48,64},{64,80},{80,96},{96,112},{1,17},{17... | collective-permute-start | bytes 393224 | tf_op jit(solution)/shard_map/ppermute | solution.py:22
  59.8 4.3 %collective-permute-start.5 = (f32[128,1,128]{0,2,1:T(8,128)S(1)}, f32[128,1,128]{0,2,1:T(8,128)S(1)}, u32[]{:S(2)}, u32[]{:S(2)}) collective-permute-start(f32[128,1,128]{0,2,1:T(8,128)S(1)} %slice.198), channel_id=1, source_target_pairs={{16,0},{32,16},{48,32},{64,48},{80,64},{96,80},{112,96},{17,1},{33... | collective-permute-start | bytes 196616 | tf_op jit(solution)/shard_map/ppermute | solution.py:25
  64.2 9.2 %collective-permute-start.6 = (f32[128,19,2]{0,2,1:T(2,128)S(1)}, f32[128,19,2]{0,2,1:T(2,128)S(1)}, u32[]{:S(2)}, u32[]{:S(2)}) collective-permute-start(f32[128,19,2]{0,2,1:T(2,128)S(1)} %pad_maximum_fusion.15), channel_id=1, source_target_pairs={{0,1},{1,2},{2,3},{3,4},{4,5},{5,6},{6,7},{7,8},{8,9},{9,10},{10,1... | collective-permute-start | bytes 58376 | tf_op jit(solution)/shard_map/ppermute | solution.py:22
  67.8 5.6 %collective-permute-start.7 = (f32[128,19,1]{0,2,1:T(1,128)S(1)}, f32[128,19,1]{0,2,1:T(1,128)S(1)}, u32[]{:S(2)}, u32[]{:S(2)}) collective-permute-start(f32[128,19,1]{0,2,1:T(1,128)S(1)} %pad_maximum_fusion.16), channel_id=1, source_target_pairs={{1,0},{2,1},{3,2},{4,3},{5,4},{6,5},{7,6},{8,7},{9,8},{10,9},{11,1... | collective-permute-start | bytes 29192 | tf_op jit(solution)/shard_map/ppermute | solution.py:25
  78.4 9.0 %collective-permute-start.10 = (f32[2]{0:T(128)S(1)}, f32[2]{0:T(128)S(1)}, u32[]{:S(2)}, u32[]{:S(2)}) collective-permute-start(f32[2]{0:T(128)S(1)} %pad_maximum_fusion.18), channel_id=1, source_target_pairs={{0,48},{16,0},{32,16},{48,32},{64,112},{80,64},{96,80},{112,96},{1... | collective-permute-start | bytes 32 | tf_op jit(solution)/shard_map/ppermute | solution.py:42
  81.0 6.5 %collective-permute-start.8 = (f32[2]{0:T(128)S(1)}, f32[2]{0:T(128)S(1)}, u32[]{:S(2)}, u32[]{:S(2)}) collective-permute-start(f32[2]{0:T(128)S(1)} %pad_maximum_fusion.18), channel_id=1, source_target_pairs={{0,16},{16,32},{32,48},{48,0},{64,80},{80,96},{96,112},{112,64},{1... | collective-permute-start | bytes 32 | tf_op jit(solution)/shard_map/ppermute | solution.py:42
  81.0 6.5 %collective-permute-start.9 = (f32[2]{0:T(128)S(1)}, f32[2]{0:T(128)S(1)}, u32[]{:S(2)}, u32[]{:S(2)}) collective-permute-start(f32[2]{0:T(128)S(1)} %pad_maximum_fusion.18), channel_id=1, source_target_pairs={{0,32},{16,48},{32,0},{48,16},{64,96},{80,112},{96,64},{112,80},{1... | collective-permute-start | bytes 32 | tf_op jit(solution)/shard_map/ppermute | solution.py:42
  88.9 5.1 %collective-permute-start.11 = (f32[2]{0:T(128)S(1)}, f32[2]{0:T(128)S(1)}, u32[]{:S(2)}, u32[]{:S(2)}) collective-permute-start(f32[2]{0:T(128)S(1)} %add_add_fusion.6), channel_id=1, source_target_pairs={{0,64},{16,80},{32,96},{48,112},{64,0},{80,16},{96,32},{112,48},{1... | collective-permute-start | bytes 32 | tf_op jit(solution)/shard_map/ppermute | solution.py:42
  94.0 7.1 %collective-permute-start.12 = (f32[2]{0:T(128)S(1)}, f32[2]{0:T(128)S(1)}, u32[]{:S(2)}, u32[]{:S(2)}) collective-permute-start(f32[2]{0:T(128)S(1)} %add.317), channel_id=1, source_target_pairs={{0,1},{1,2},{2,3},{3,0},{4,5},{5,6},{6,7},{7,4},{8,9},{9,10},{10,1... | collective-permute-start | bytes 32 | tf_op jit(solution)/shard_map/ppermute | solution.py:42
  95.9 6.6 %collective-permute-start.13 = (f32[2]{0:T(128)S(1)}, f32[2]{0:T(128)S(1)}, u32[]{:S(2)}, u32[]{:S(2)}) collective-permute-start(f32[2]{0:T(128)S(1)} %add.317), channel_id=1, source_target_pairs={{0,2},{1,3},{2,0},{3,1},{4,6},{5,7},{6,4},{7,5},{8,10},{9,11},{10,... | collective-permute-start | bytes 32 | tf_op jit(solution)/shard_map/ppermute | solution.py:42
  104.5 6.2 %collective-permute-start.15 = (f32[2]{0:T(128)S(1)}, f32[2]{0:T(128)S(1)}, u32[]{:S(2)}, u32[]{:S(2)}) collective-permute-start(f32[2]{0:T(128)S(1)} %add_add_fusion.5), channel_id=1, source_target_pairs={{0,4},{1,5},{2,6},{3,7},{4,8},{5,9},{6,10},{7,11},{8,12},{9,13},{1... | collective-permute-start | bytes 32 | tf_op jit(solution)/shard_map/ppermute | solution.py:42
  106.3 5.1 %collective-permute-start.16 = (f32[2]{0:T(128)S(1)}, f32[2]{0:T(128)S(1)}, u32[]{:S(2)}, u32[]{:S(2)}) collective-permute-start(f32[2]{0:T(128)S(1)} %add_add_fusion.5), channel_id=1, source_target_pairs={{0,8},{1,9},{2,10},{3,11},{4,12},{5,13},{6,14},{7,15},{8,0},{9,1},... | collective-permute-start | bytes 32 | tf_op jit(solution)/shard_map/ppermute | solution.py:42
  108.1 3.8 %collective-permute-start.17 = (f32[2]{0:T(128)S(1)}, f32[2]{0:T(128)S(1)}, u32[]{:S(2)}, u32[]{:S(2)}) collective-permute-start(f32[2]{0:T(128)S(1)} %add_add_fusion.5), channel_id=1, source_target_pairs={{0,12},{1,13},{2,14},{3,15},{4,0},{5,1},{6,2},{7,3},{8,4},{9,5},{1... | collective-permute-start | bytes 32 | tf_op jit(solution)/shard_map/ppermute | solution.py:42
  117.2 3.6 %collective-permute-start.19 = (f32[4]{0:T(128)S(1)}, f32[4]{0:T(128)S(1)}, u32[]{:S(2)}, u32[]{:S(2)}) collective-permute-start(f32[4]{0:T(128)S(1)} %pad_maximum_fusion.19), channel_id=1, source_target_pairs={{0,32},{16,48},{32,0},{48,16},{64,96},{80,112},{96,64},{112,80},{1... | collective-permute-start | bytes 56 | tf_op jit(solution)/shard_map/ppermute | solution.py:42
  123.3 5.3 %collective-permute-start.21 = (f32[4]{0:T(128)S(1)}, f32[4]{0:T(128)S(1)}, u32[]{:S(2)}, u32[]{:S(2)}) collective-permute-start(f32[4]{0:T(128)S(1)} %add_add_fusion.3), channel_id=1, source_target_pairs={{0,64},{16,80},{32,96},{48,112},{64,0},{80,16},{96,32},{112,48},{1... | collective-permute-start | bytes 56 | tf_op jit(solution)/shard_map/ppermute | solution.py:42
  128.6 4.8 %collective-permute-start.22 = (f32[4]{0:T(128)S(1)}, f32[4]{0:T(128)S(1)}, u32[]{:S(2)}, u32[]{:S(2)}) collective-permute-start(f32[4]{0:T(128)S(1)} %add.335), channel_id=1, source_target_pairs={{0,1},{1,2},{2,3},{3,0},{4,5},{5,6},{6,7},{7,4},{8,9},{9,10},{10,1... | collective-permute-start | bytes 56 | tf_op jit(solution)/shard_map/ppermute | solution.py:42
  130.5 5.1 %collective-permute-start.23 = (f32[4]{0:T(128)S(1)}, f32[4]{0:T(128)S(1)}, u32[]{:S(2)}, u32[]{:S(2)}) collective-permute-start(f32[4]{0:T(128)S(1)} %add.335), channel_id=1, source_target_pairs={{0,2},{1,3},{2,0},{3,1},{4,6},{5,7},{6,4},{7,5},{8,10},{9,11},{10,... | collective-permute-start | bytes 56 | tf_op jit(solution)/shard_map/ppermute | solution.py:42
  136.2 4.8 %collective-permute-start.25 = (f32[4]{0:T(128)S(1)}, f32[4]{0:T(128)S(1)}, u32[]{:S(2)}, u32[]{:S(2)}) collective-permute-start(f32[4]{0:T(128)S(1)} %add_add_fusion.2), channel_id=1, source_target_pairs={{0,4},{1,5},{2,6},{3,7},{4,8},{5,9},{6,10},{7,11},{8,12},{9,13},{1... | collective-permute-start | bytes 56 | tf_op jit(solution)/shard_map/ppermute | solution.py:42
  136.3 5.2 %collective-permute-start.26 = (f32[4]{0:T(128)S(1)}, f32[4]{0:T(128)S(1)}, u32[]{:S(2)}, u32[]{:S(2)}) collective-permute-start(f32[4]{0:T(128)S(1)} %add_add_fusion.2), channel_id=1, source_target_pairs={{0,8},{1,9},{2,10},{3,11},{4,12},{5,13},{6,14},{7,15},{8,0},{9,1},... | collective-permute-start | bytes 56 | tf_op jit(solution)/shard_map/ppermute | solution.py:42
  (35 other events, 455.3 us)

commit v6 on v3

--- a/solution.py
+++ b/solution.py
@@ -94,8 +94,9 @@
     targets = slot_table.reshape(-1)
     devices = lax.axis_size("px") * lax.axis_size("py")
     width = targets.shape[0] // devices
-    held = recv_contact.reshape(hist, devices, width)
-    arrived = lax.all_to_all(held, ("px", "py"), split_axis=1, concat_axis=1, tiled=True)
+    held = recv_contact.reshape(hist, lax.axis_size("px"), lax.axis_size("py"), width)
+    held = lax.all_to_all(held, "py", split_axis=2, concat_axis=2, tiled=True)
+    arrived = lax.all_to_all(held, "px", split_axis=1, concat_axis=1, tiled=True)
 
     def with_base(shells):
         return jnp.einsum("ab,bxy->axy", stiff_base, shells, precision=HIGH)

time: 149 us -> 156 us (1.047)
  waiting for transfers between devices: 26.3 us -> 32.7 us
  starting transfers between devices: 63.5 us -> 61.1 us
  local copies, waits for them, and re-layouts: 22.3 us -> 24 us
    all_to_all x1 -> x2, waiting for transfers between devices: 0.01 us -> 7.58 us  [the longest x1 7.58 us: shards(): lax.all_to_all(held, 'px', split_axis=1, concat_axis=1, tiled=True)]
    ppermute x4, waiting for transfers between devices: 5.47 us -> 1.53 us  [with_halo(): parts.insert(0, lax.ppermute(last, axis, up))]
    ppermute x20, starting transfers between devices: 33.8 us -> 31.5 us  [all_sum(): total = total + lax.ppermute(value, axis, pairs)]
    all_to_all x0 -> x2, local copies, waits for them, and re-layouts: none -> 2.21 us  [the longest x1 1.29 us: shards(): lax.all_to_all(held, 'px', split_axis=1, concat_axis=1, tiled=True)]
    ppermute x20, waiting for transfers between devices: 17.2 us -> 18.8 us  [all_sum(): total = total + lax.ppermute(value, axis, pairs)]
    unnamed x43 -> x37, local copies, waits for them, and re-layouts: 10.4 us -> 9.53 us
    all_to_all x1 -> x2, starting transfers between devices: 14.2 us -> 14.2 us  [the longest x1 8.74 us: shards(): held = lax.all_to_all(held, 'py', split_axis=2, concat_axis=2, tiled=True)]
  transfers between devices with their start and end apart: 29 -> 30, of which waited for: 18 -> 18; matrix products, arithmetic and copies ran while one was open for 14% -> 14% of each run, Pallas kernels for 0% -> 0%
where the time goes in v6:
time: 156 us; the launch traced here: 155 us
  starting transfers between devices  61.1 us (39%)
  waiting for transfers between devices  32.7 us (21%)
  local copies, waits for them, and re-layouts  24 us (15%)
  matrix products  16.3 us (10%)
  other arithmetic  13.9 us (9%)
  between operations  7.11 us (5%)
    ppermute x20, starting transfers between devices, all_sum(): total = total + lax.ppermute(value, axis, pairs)  31.5 us
    ppermute x20, waiting for transfers between devices, all_sum(): total = total + lax.ppermute(value, axis, pairs)  18.8 us
    ppermute x4, starting transfers between devices, with_halo(): parts.insert(0, lax.ppermute(last, axis, up))  10 us
    unnamed x37, local copies, waits for them, and re-layouts  9.53 us
    all_to_all x1, starting transfers between devices, shards(): held = lax.all_to_all(held, 'py', split_axis=2, concat_axis=2, tiled=True)  8.74 us
    all_to_all x1, waiting for transfers between devices, shards(): lax.all_to_all(held, 'px', split_axis=1, concat_axis=1, tiled=True)  7.58 us
    scatter x1, local copies, waits for them, and re-layouts, shards(): contact = contact_home.reshape(hist, cells).at[:, targets].set(arrived.re...  6.8 us
    all_to_all x1, starting transfers between devices, shards(): lax.all_to_all(held, 'px', split_axis=1, concat_axis=1, tiled=True)  5.5 us
  transfers between devices with their start and end apart: 30, of which 18 were waited for; matrix products, arithmetic and copies ran while one was open for 14% of the time, Pallas kernels for 0%

profile of v6, /device:TPU:0, one launch (start us, length us, event | category | flops | bytes accessed | tf_op | source)
XLA Modules:
  0.0 155.1 jit_solution(8097743102972657028)
XLA Ops:
  7.4 8.7 %all-to-all-start = ((f32[128,8,16,9]{0,1,3,2:T(8,128)}), f32[128,8,16,9]{0,1,3,2:T(8,128)S(1)}, u32[]{:S(2)}, u32[]{:S(2)}) async-start(f32[128,8,16,9]{0,1,3,2:T(8,128)} %copy.51), calls=%async_computation | async-start | bytes 1179648 | tf_op jit(solution)/shard_map/all_to_all | solution.py:98
  17.5 3.8 %collective-permute-start.2 = (f32[12,22,3]{2,0,1:T(8,128)S(1)}, f32[12,22,3]{2,0,1:T(8,128)S(1)}, u32[]{:S(2)}, u32[]{:S(2)}) collective-permute-start(f32[12,22,3]{2,0,1:T(8,128)S(1)} %get-tuple-element.32), channel_id=1, source_target_pairs={{0,1},{1,2},{2,3},{3,4},{4,5},{5,6},{6,7},{7,8},{8,9},{9,10},{10,1... | collective-permute-start | bytes 9512 | tf_op jit(solution)/shard_map/ppermute | solution.py:22
  26.3 3.9 %collective-permute-done.3 = f32[12,22,3]{2,0,1:T(8,128)} collective-permute-done((f32[12,22,3]{2,0,1:T(8,128)S(1)}, f32[12,22,3]{2,0,1:T(8,128)}, u32[]{:S(2)}, u32[]{:S(2)}) %collective-permute-start.3) | collective-permute-done | bytes 3200 | tf_op jit(solution)/shard_map/ppermute | solution.py:25
  33.2 5.5 %all-to-all-start.1 = ((f32[128,8,16,9]{0,2,3,1:T(8,128)}), f32[128,8,16,9]{0,2,3,1:T(8,128)}, u32[]{:S(2)}, u32[]{:S(2)}) async-start(f32[128,8,16,9]{0,2,3,1:T(8,128)} %copy.52), calls=%async_computation.1 | async-start | bytes 1179648 | tf_op jit(solution)/shard_map/all_to_all | solution.py:99
  42.3 7.6 %all-to-all-done.1 = f32[128,8,16,9]{0,2,3,1:T(8,128)} async-done(((f32[128,8,16,9]{0,2,3,1:T(8,128)}), f32[128,8,16,9]{0,2,3,1:T(8,128)}, u32[]{:S(2)}, u32[]{:S(2)}) %all-to-all-start.1) | async-done | bytes 589856 | tf_op jit(solution)/shard_map/all_to_all | solution.py:99
  52.0 6.8 %scatter_custom_fusion = f32[128,2048]{0,1:T(8,128)S(1)} fusion(f32[128,2048]{0,1:T(8,128)S(1)} %bitcast.73, s32[1152]{0:T(1024)S(1)} %fusion.46, f32[128,1152]{0,1:T(8,128)} %reshape.268), kind=kCustom, calls=%fused_computation.30 | custom fusion | bytes 1638400 | tf_op jit(solution)/shard_map/scatter | solution.py:123
  58.9 4.4 %fusion.19 = (f32[128,2048]{0,1:T(8,128)S(1)}, f32[128,2048]{0,1:T(8,128)}) fusion(f32[128,2048]{0,1:T(8,128)S(1)} %scatter_custom_fusion, f32[128,2048]{0,1:T(8,128)S(1)} %bitcast.72, f32[128,24]{0,1:T(8,128)S(1)} %copy-done, f32[6,21,133]{2,0,1:T(8,128)} %get-tuple-element.29, f32[6,21,133]{2,0,1:T(8,128)} %get-tuple-element.30, ...), kind=kOutput, calls=%fused_computation.29 | convolution fusion | flops 77742080 | bytes 4474720 | tf_op jit(solution)/shard_map/dot_general | solution.py:117
  66.1 2.5 %convolution_bitcast_fusion.1 = f32[128,19,131]{0,2,1:T(8,128)S(1)} fusion(f32[6,19,131]{2,0,1:T(8,128)S(1)} %copy-done.3, f32[6,19,131]{2,0,1:T(8,128)S(1)} %copy-done.4, f32[6,19,131]{2,0,1:T(8,128)S(1)} %copy-done.5, f32[6,19,131]{2,0,1:T(8,128)S(1)} %copy-done.2, f32[128,24]{0,1:T(8,128)S(1)} %copy-done), kind=kOutput, calls=%fused_computation.4 | convolution fusion | flops 91933704 | bytes 1525600 | tf_op jit(solution)/shard_map/hb,bxy->hxy/dot_general | solution.py:130
  68.6 3.5 %collective-permute-start.6 = (f32[128,19,2]{0,2,1:T(2,128)S(1)}, f32[128,19,2]{0,2,1:T(2,128)S(1)}, u32[]{:S(2)}, u32[]{:S(2)}) collective-permute-start(f32[128,19,2]{0,2,1:T(2,128)S(1)} %pad_maximum_fusion.15), channel_id=1, source_target_pairs={{0,1},{1,2},{2,3},{3,4},{4,5},{5,6},{6,7},{7,8},{8,9},{9,10},{10,1... | collective-permute-start | bytes 58376 | tf_op jit(solution)/shard_map/ppermute | solution.py:22
  74.2 2.6 %copy.56 = f32[128,16,128]{2,1,0:T(8,128)} copy(f32[128,16,128]{0,2,1:T(8,128)} %bitcast.74) | data formatting | bytes 2097152
  77.7 2.2 %fusion.13 = f32[24,19,131]{2,0,1:T(8,128)S(1)} fusion(f32[19,131,24]{1,2,0:T(8,128)S(1)} %fusion.31, f32[128,19,131]{0,2,1:T(8,128)S(1)} %convolution_bitcast_fusion.1, f32[128,19,1]{0,2,1:T(1,128)S(1)} %collective-permute-done.7, f32[128,1,128]{0,2,1:T(8,128)S(1)} %collective-permute-done.5, f32[128,16,128]{0,2,1:T(8,128)S(1)} %bitcast.70, ...), kind=kOutput, calls=%fused_computation.20 | convolution fusion | flops 93466928 | bytes 3048868 | tf_op jit(solution)/shard_map/hb,hxy->bxy/dot_general | solution.py:131
  84.0 2.1 %collective-permute-start.9 = (f32[2]{0:T(128)S(1)}, f32[2]{0:T(128)S(1)}, u32[]{:S(2)}, u32[]{:S(2)}) collective-permute-start(f32[2]{0:T(128)S(1)} %pad_maximum_fusion.18), channel_id=1, source_target_pairs={{0,32},{16,48},{32,0},{48,16},{64,96},{80,112},{96,64},{112,80},{1... | collective-permute-start | bytes 32 | tf_op jit(solution)/shard_map/ppermute | solution.py:42
  86.2 2.3 %convolution_bitcast_fusion.2 = f32[128,17,129]{0,2,1:T(8,128)S(1)} fusion(f32[6,17,129]{2,0,1:T(8,128)S(1)} %get-tuple-element.39, f32[6,17,129]{2,0,1:T(8,128)S(1)} %get-tuple-element.40, f32[6,17,129]{2,0,1:T(8,128)S(1)} %get-tuple-element.41, f32[6,17,129]{2,0,1:T(8,128)S(1)} %get-tuple-element.38, f32[128,24]{0,1:T(8,128)S(1)} %copy-done), kind=kOutput, calls=%fused_computation.5 | convolution fusion | flops 81000648 | bytes 1345632 | tf_op jit(solution)/shard_map/hb,bxy->hxy/dot_general | solution.py:130
  92.5 2.1 %collective-permute-start.11 = (f32[2]{0:T(128)S(1)}, f32[2]{0:T(128)S(1)}, u32[]{:S(2)}, u32[]{:S(2)}) collective-permute-start(f32[2]{0:T(128)S(1)} %add_add_fusion.6), channel_id=1, source_target_pairs={{0,64},{16,80},{32,96},{48,112},{64,0},{80,16},{96,32},{112,48},{1... | collective-permute-start | bytes 32 | tf_op jit(solution)/shard_map/ppermute | solution.py:42
  94.6 3.0 %collective-permute-done.11 = f32[2]{0:T(128)S(1)} collective-permute-done((f32[2]{0:T(128)S(1)}, f32[2]{0:T(128)S(1)}, u32[]{:S(2)}, u32[]{:S(2)}) %collective-permute-start.11) | collective-permute-done | bytes 40 | tf_op jit(solution)/shard_map/ppermute | solution.py:42
  97.6 2.6 %collective-permute-start.12 = (f32[2]{0:T(128)S(1)}, f32[2]{0:T(128)S(1)}, u32[]{:S(2)}, u32[]{:S(2)}) collective-permute-start(f32[2]{0:T(128)S(1)} %add.305), channel_id=1, source_target_pairs={{0,1},{1,2},{2,3},{3,0},{4,5},{5,6},{6,7},{7,4},{8,9},{9,10},{10,1... | collective-permute-start | bytes 32 | tf_op jit(solution)/shard_map/ppermute | solution.py:42
  100.2 4.3 %collective-permute-start.13 = (f32[2]{0:T(128)S(1)}, f32[2]{0:T(128)S(1)}, u32[]{:S(2)}, u32[]{:S(2)}) collective-permute-start(f32[2]{0:T(128)S(1)} %add.305), channel_id=1, source_target_pairs={{0,2},{1,3},{2,0},{3,1},{4,6},{5,7},{6,4},{7,5},{8,10},{9,11},{10,... | collective-permute-start | bytes 32 | tf_op jit(solution)/shard_map/ppermute | solution.py:42
  111.1 2.5 %collective-permute-start.17 = (f32[2]{0:T(128)S(1)}, f32[2]{0:T(128)S(1)}, u32[]{:S(2)}, u32[]{:S(2)}) collective-permute-start(f32[2]{0:T(128)S(1)} %add_add_fusion.5), channel_id=1, source_target_pairs={{0,12},{1,13},{2,14},{3,15},{4,0},{5,1},{6,2},{7,3},{8,4},{9,5},{1... | collective-permute-start | bytes 32 | tf_op jit(solution)/shard_map/ppermute | solution.py:42
  117.7 2.6 %pad_maximum_fusion.19 = f32[4]{0:T(128)S(1)} fusion(f32[1]{0:T(128)} %bitcast.20, f32[1]{0:T(128)} %bitcast.19, f32[1]{0:T(128)} %bitcast.18, f32[1]{0:T(128)} %bitcast.15), kind=kLoop, calls=%fused_computation.102 | loop fusion | flops 12 | bytes 32 | tf_op jit(solution)/shard_map/stack | solution.py:144
  124.0 2.6 %add_add_fusion.3 = f32[4]{0:T(128)S(1)} fusion(f32[4]{0:T(128)S(1)} %collective-permute-done.20, f32[4]{0:T(128)S(1)} %collective-permute-done.19, f32[4]{0:T(128)S(1)} %collective-permute-done.18, f32[1]{0:T(128)} %bitcast.20, f32[1]{0:T(128)} %bitcast.19, f32[1]{0:T(128)} %bitcast.18, f32[1]{0:T(128)} %bitcast.15), kind=kLoop, calls=%fused_computation.105 | loop fusion | flops 24 | bytes 80 | tf_op jit(solution)/shard_map/add | solution.py:42
  126.7 2.3 %collective-permute-start.21 = (f32[4]{0:T(128)S(1)}, f32[4]{0:T(128)S(1)}, u32[]{:S(2)}, u32[]{:S(2)}) collective-permute-start(f32[4]{0:T(128)S(1)} %add_add_fusion.3), channel_id=1, source_target_pairs={{0,64},{16,80},{32,96},{48,112},{64,0},{80,16},{96,32},{112,48},{1... | collective-permute-start | bytes 56 | tf_op jit(solution)/shard_map/ppermute | solution.py:42
  129.0 3.0 %collective-permute-done.21 = f32[4]{0:T(128)S(1)} collective-permute-done((f32[4]{0:T(128)S(1)}, f32[4]{0:T(128)S(1)}, u32[]{:S(2)}, u32[]{:S(2)}) %collective-permute-start.21) | collective-permute-done | bytes 48 | tf_op jit(solution)/shard_map/ppermute | solution.py:42
  133.4 2.2 %collective-permute-start.23 = (f32[4]{0:T(128)S(1)}, f32[4]{0:T(128)S(1)}, u32[]{:S(2)}, u32[]{:S(2)}) collective-permute-start(f32[4]{0:T(128)S(1)} %add.323), channel_id=1, source_target_pairs={{0,2},{1,3},{2,0},{3,1},{4,6},{5,7},{6,4},{7,5},{8,10},{9,11},{10,... | collective-permute-start | bytes 56 | tf_op jit(solution)/shard_map/ppermute | solution.py:42
  139.5 3.8 %collective-permute-start.26 = (f32[4]{0:T(128)S(1)}, f32[4]{0:T(128)S(1)}, u32[]{:S(2)}, u32[]{:S(2)}) collective-permute-start(f32[4]{0:T(128)S(1)} %add_add_fusion.2), channel_id=1, source_target_pairs={{0,8},{1,9},{2,10},{3,11},{4,12},{5,13},{6,14},{7,15},{8,0},{9,1},... | collective-permute-start | bytes 56 | tf_op jit(solution)/shard_map/ppermute | solution.py:42
  (131 shorter events, 61.0 us)
Async XLA Ops:
  2.3 15.0 %collective-permute-start = (f32[12,3,128]{2,0,1:T(8,128)S(1)}, f32[12,3,128]{2,0,1:T(8,128)S(1)}, u32[]{:S(2)}, u32[]{:S(2)}) collective-permute-start(f32[12,3,128]{2,0,1:T(8,128)S(1)} %get-tuple-element.42), channel_id=1, source_target_pairs={{0,16},{16,32},{32,48},{48,64},{64,80},{80,96},{96,112},{1,17},{17... | collective-permute-start | bytes 55304 | tf_op jit(solution)/shard_map/ppermute | solution.py:22
  3.6 13.7 %collective-permute-start.1 = (f32[12,3,128]{2,0,1:T(8,128)S(1)}, f32[12,3,128]{2,0,1:T(8,128)S(1)}, u32[]{:S(2)}, u32[]{:S(2)}) collective-permute-start(f32[12,3,128]{2,0,1:T(8,128)S(1)} %get-tuple-element.43), channel_id=1, source_target_pairs={{16,0},{32,16},{48,32},{64,48},{80,64},{96,80},{112,96},{17,1},{33... | collective-permute-start | bytes 55304 | tf_op jit(solution)/shard_map/ppermute | solution.py:25
  7.4 24.8 %all-to-all-start = ((f32[128,8,16,9]{0,1,3,2:T(8,128)}), f32[128,8,16,9]{0,1,3,2:T(8,128)S(1)}, u32[]{:S(2)}, u32[]{:S(2)}) async-start(f32[128,8,16,9]{0,1,3,2:T(8,128)} %copy.51), calls=%async_computation | async-start | bytes 1179648 | tf_op jit(solution)/shard_map/all_to_all | solution.py:98
  17.5 8.8 %collective-permute-start.2 = (f32[12,22,3]{2,0,1:T(8,128)S(1)}, f32[12,22,3]{2,0,1:T(8,128)S(1)}, u32[]{:S(2)}, u32[]{:S(2)}) collective-permute-start(f32[12,22,3]{2,0,1:T(8,128)S(1)} %get-tuple-element.32), channel_id=1, source_target_pairs={{0,1},{1,2},{2,3},{3,4},{4,5},{5,6},{6,7},{7,8},{8,9},{9,10},{10,1... | collective-permute-start | bytes 9512 | tf_op jit(solution)/shard_map/ppermute | solution.py:22
  21.3 8.8 %collective-permute-start.3 = (f32[12,22,3]{2,0,1:T(8,128)S(1)}, f32[12,22,3]{2,0,1:T(8,128)}, u32[]{:S(2)}, u32[]{:S(2)}) collective-permute-start(f32[12,22,3]{2,0,1:T(8,128)S(1)} %get-tuple-element.33), channel_id=1, source_target_pairs={{1,0},{2,1},{3,2},{4,3},{5,4},{6,5},{7,6},{8,7},{9,8},{10,9},{11,1... | collective-permute-start | bytes 9512 | tf_op jit(solution)/shard_map/ppermute | solution.py:25
  33.2 16.6 %all-to-all-start.1 = ((f32[128,8,16,9]{0,2,3,1:T(8,128)}), f32[128,8,16,9]{0,2,3,1:T(8,128)}, u32[]{:S(2)}, u32[]{:S(2)}) async-start(f32[128,8,16,9]{0,2,3,1:T(8,128)} %copy.52), calls=%async_computation.1 | async-start | bytes 1179648 | tf_op jit(solution)/shard_map/all_to_all | solution.py:99
  63.3 5.3 %collective-permute-start.4 = (f32[128,2,128]{0,2,1:T(8,128)S(1)}, f32[128,2,128]{0,2,1:T(8,128)S(1)}, u32[]{:S(2)}, u32[]{:S(2)}) collective-permute-start(f32[128,2,128]{0,2,1:T(8,128)S(1)} %slice.195), channel_id=1, source_target_pairs={{0,16},{16,32},{32,48},{48,64},{64,80},{80,96},{96,112},{1,17},{17... | collective-permute-start | bytes 393224 | tf_op jit(solution)/shard_map/ppermute | solution.py:22
  64.8 3.9 %collective-permute-start.5 = (f32[128,1,128]{0,2,1:T(8,128)S(1)}, f32[128,1,128]{0,2,1:T(8,128)S(1)}, u32[]{:S(2)}, u32[]{:S(2)}) collective-permute-start(f32[128,1,128]{0,2,1:T(8,128)S(1)} %slice.196), channel_id=1, source_target_pairs={{16,0},{32,16},{48,32},{64,48},{80,64},{96,80},{112,96},{17,1},{33... | collective-permute-start | bytes 196616 | tf_op jit(solution)/shard_map/ppermute | solution.py:25
  68.6 9.1 %collective-permute-start.6 = (f32[128,19,2]{0,2,1:T(2,128)S(1)}, f32[128,19,2]{0,2,1:T(2,128)S(1)}, u32[]{:S(2)}, u32[]{:S(2)}) collective-permute-start(f32[128,19,2]{0,2,1:T(2,128)S(1)} %pad_maximum_fusion.15), channel_id=1, source_target_pairs={{0,1},{1,2},{2,3},{3,4},{4,5},{5,6},{6,7},{7,8},{8,9},{9,10},{10,1... | collective-permute-start | bytes 58376 | tf_op jit(solution)/shard_map/ppermute | solution.py:22
  72.1 5.6 %collective-permute-start.7 = (f32[128,19,1]{0,2,1:T(1,128)S(1)}, f32[128,19,1]{0,2,1:T(1,128)S(1)}, u32[]{:S(2)}, u32[]{:S(2)}) collective-permute-start(f32[128,19,1]{0,2,1:T(1,128)S(1)} %pad_maximum_fusion.16), channel_id=1, source_target_pairs={{1,0},{2,1},{3,2},{4,3},{5,4},{6,5},{7,6},{8,7},{9,8},{10,9},{11,1... | collective-permute-start | bytes 29192 | tf_op jit(solution)/shard_map/ppermute | solution.py:25
  82.2 8.9 %collective-permute-start.10 = (f32[2]{0:T(128)S(1)}, f32[2]{0:T(128)S(1)}, u32[]{:S(2)}, u32[]{:S(2)}) collective-permute-start(f32[2]{0:T(128)S(1)} %pad_maximum_fusion.18), channel_id=1, source_target_pairs={{0,48},{16,0},{32,16},{48,32},{64,112},{80,64},{96,80},{112,96},{1... | collective-permute-start | bytes 32 | tf_op jit(solution)/shard_map/ppermute | solution.py:42
  83.3 7.8 %collective-permute-start.8 = (f32[2]{0:T(128)S(1)}, f32[2]{0:T(128)S(1)}, u32[]{:S(2)}, u32[]{:S(2)}) collective-permute-start(f32[2]{0:T(128)S(1)} %pad_maximum_fusion.18), channel_id=1, source_target_pairs={{0,16},{16,32},{32,48},{48,0},{64,80},{80,96},{96,112},{112,64},{1... | collective-permute-start | bytes 32 | tf_op jit(solution)/shard_map/ppermute | solution.py:42
  84.0 7.1 %collective-permute-start.9 = (f32[2]{0:T(128)S(1)}, f32[2]{0:T(128)S(1)}, u32[]{:S(2)}, u32[]{:S(2)}) collective-permute-start(f32[2]{0:T(128)S(1)} %pad_maximum_fusion.18), channel_id=1, source_target_pairs={{0,32},{16,48},{32,0},{48,16},{64,96},{80,112},{96,64},{112,80},{1... | collective-permute-start | bytes 32 | tf_op jit(solution)/shard_map/ppermute | solution.py:42
  92.5 5.1 %collective-permute-start.11 = (f32[2]{0:T(128)S(1)}, f32[2]{0:T(128)S(1)}, u32[]{:S(2)}, u32[]{:S(2)}) collective-permute-start(f32[2]{0:T(128)S(1)} %add_add_fusion.6), channel_id=1, source_target_pairs={{0,64},{16,80},{32,96},{48,112},{64,0},{80,16},{96,32},{112,48},{1... | collective-permute-start | bytes 32 | tf_op jit(solution)/shard_map/ppermute | solution.py:42
  97.6 7.4 %collective-permute-start.12 = (f32[2]{0:T(128)S(1)}, f32[2]{0:T(128)S(1)}, u32[]{:S(2)}, u32[]{:S(2)}) collective-permute-start(f32[2]{0:T(128)S(1)} %add.305), channel_id=1, source_target_pairs={{0,1},{1,2},{2,3},{3,0},{4,5},{5,6},{6,7},{7,4},{8,9},{9,10},{10,1... | collective-permute-start | bytes 32 | tf_op jit(solution)/shard_map/ppermute | solution.py:42
  100.2 5.8 %collective-permute-start.13 = (f32[2]{0:T(128)S(1)}, f32[2]{0:T(128)S(1)}, u32[]{:S(2)}, u32[]{:S(2)}) collective-permute-start(f32[2]{0:T(128)S(1)} %add.305), channel_id=1, source_target_pairs={{0,2},{1,3},{2,0},{3,1},{4,6},{5,7},{6,4},{7,5},{8,10},{9,11},{10,... | collective-permute-start | bytes 32 | tf_op jit(solution)/shard_map/ppermute | solution.py:42
  108.1 5.6 %collective-permute-start.15 = (f32[2]{0:T(128)S(1)}, f32[2]{0:T(128)S(1)}, u32[]{:S(2)}, u32[]{:S(2)}) collective-permute-start(f32[2]{0:T(128)S(1)} %add_add_fusion.5), channel_id=1, source_target_pairs={{0,4},{1,5},{2,6},{3,7},{4,8},{5,9},{6,10},{7,11},{8,12},{9,13},{1... | collective-permute-start | bytes 32 | tf_op jit(solution)/shard_map/ppermute | solution.py:42
  109.5 5.1 %collective-permute-start.16 = (f32[2]{0:T(128)S(1)}, f32[2]{0:T(128)S(1)}, u32[]{:S(2)}, u32[]{:S(2)}) collective-permute-start(f32[2]{0:T(128)S(1)} %add_add_fusion.5), channel_id=1, source_target_pairs={{0,8},{1,9},{2,10},{3,11},{4,12},{5,13},{6,14},{7,15},{8,0},{9,1},... | collective-permute-start | bytes 32 | tf_op jit(solution)/shard_map/ppermute | solution.py:42
  111.1 3.8 %collective-permute-start.17 = (f32[2]{0:T(128)S(1)}, f32[2]{0:T(128)S(1)}, u32[]{:S(2)}, u32[]{:S(2)}) collective-permute-start(f32[2]{0:T(128)S(1)} %add_add_fusion.5), channel_id=1, source_target_pairs={{0,12},{1,13},{2,14},{3,15},{4,0},{5,1},{6,2},{7,3},{8,4},{9,5},{1... | collective-permute-start | bytes 32 | tf_op jit(solution)/shard_map/ppermute | solution.py:42
  126.7 5.3 %collective-permute-start.21 = (f32[4]{0:T(128)S(1)}, f32[4]{0:T(128)S(1)}, u32[]{:S(2)}, u32[]{:S(2)}) collective-permute-start(f32[4]{0:T(128)S(1)} %add_add_fusion.3), channel_id=1, source_target_pairs={{0,64},{16,80},{32,96},{48,112},{64,0},{80,16},{96,32},{112,48},{1... | collective-permute-start | bytes 56 | tf_op jit(solution)/shard_map/ppermute | solution.py:42
  132.0 4.8 %collective-permute-start.22 = (f32[4]{0:T(128)S(1)}, f32[4]{0:T(128)S(1)}, u32[]{:S(2)}, u32[]{:S(2)}) collective-permute-start(f32[4]{0:T(128)S(1)} %add.323), channel_id=1, source_target_pairs={{0,1},{1,2},{2,3},{3,0},{4,5},{5,6},{6,7},{7,4},{8,9},{9,10},{10,1... | collective-permute-start | bytes 56 | tf_op jit(solution)/shard_map/ppermute | solution.py:42
  133.4 5.1 %collective-permute-start.23 = (f32[4]{0:T(128)S(1)}, f32[4]{0:T(128)S(1)}, u32[]{:S(2)}, u32[]{:S(2)}) collective-permute-start(f32[4]{0:T(128)S(1)} %add.323), channel_id=1, source_target_pairs={{0,2},{1,3},{2,0},{3,1},{4,6},{5,7},{6,4},{7,5},{8,10},{9,11},{10,... | collective-permute-start | bytes 56 | tf_op jit(solution)/shard_map/ppermute | solution.py:42
  139.1 4.8 %collective-permute-start.25 = (f32[4]{0:T(128)S(1)}, f32[4]{0:T(128)S(1)}, u32[]{:S(2)}, u32[]{:S(2)}) collective-permute-start(f32[4]{0:T(128)S(1)} %add_add_fusion.2), channel_id=1, source_target_pairs={{0,4},{1,5},{2,6},{3,7},{4,8},{5,9},{6,10},{7,11},{8,12},{9,13},{1... | collective-permute-start | bytes 56 | tf_op jit(solution)/shard_map/ppermute | solution.py:42
  139.5 5.4 %collective-permute-start.26 = (f32[4]{0:T(128)S(1)}, f32[4]{0:T(128)S(1)}, u32[]{:S(2)}, u32[]{:S(2)}) collective-permute-start(f32[4]{0:T(128)S(1)} %add_add_fusion.2), channel_id=1, source_target_pairs={{0,8},{1,9},{2,10},{3,11},{4,12},{5,13},{6,14},{7,15},{8,0},{9,1},... | collective-permute-start | bytes 56 | tf_op jit(solution)/shard_map/ppermute | solution.py:42
  (20 other events, 408.7 us)

commit v7 on v3

--- a/solution.py
+++ b/solution.py
@@ -134,13 +134,17 @@
     image_wide = node_keep(operate(rhs_wide, weights_wide, -2), -1)
     image = image_wide[:, 1 : rows + 1, 1 : cols + 1]
     again = operate(image_wide, weights_wide[:, 1 : rows + 2, 1 : cols + 2], -1)
-    first = all_sum(jnp.stack([jnp.sum(rhs * rhs), jnp.sum(rhs * image)]))
+    def lanes(values):
+        values = jnp.stack(values)
+        return jnp.broadcast_to(values[:, None], (values.shape[0], cols))
+
+    first = all_sum(lanes([jnp.sum(rhs * rhs), jnp.sum(rhs * image)]))
     norm_now, curvature = first[0], first[1]
     alpha = norm_now / curvature
     residual = rhs - alpha * image
     bent = image - alpha * again
     second = all_sum(
-        jnp.stack(
+        lanes(
             [
                 jnp.sum(residual * residual),
                 jnp.sum(residual * bent),

time: 149 us -> 135 us (0.906)
  between operations: 7.02 us -> 1.25 us
  waiting for transfers between devices: 26.3 us -> 23.5 us
  local copies, waits for them, and re-layouts: 22.3 us -> 20 us
  other arithmetic: 14 us -> 12.5 us
    ppermute x20, waiting for transfers between devices: 17.2 us -> 12.9 us  [all_sum(): total = total + lax.ppermute(value, axis, pairs)]
    add x8, other arithmetic: 4.04 us -> 0.18 us  [all_sum(): total = total + lax.ppermute(value, axis, pairs)]
    ppermute x4, waiting for transfers between devices: 3.62 us -> 6.11 us  [with_halo(): parts.append(lax.ppermute(leading, axis, down))]
    convert_element_type x5, other arithmetic: 0.98 us -> 3.39 us  [inside(): return (row_ok[:, None] & col_ok[None, :]).astype(jnp.float32)]
    unnamed x43 -> x49, local copies, waits for them, and re-layouts: 10.4 us -> 9.1 us
  transfers between devices with their start and end apart: 29 -> 29, of which waited for: 18 -> 17; matrix products, arithmetic and copies ran while one was open for 14% -> 16% of each run, Pallas kernels for 0% -> 0%
where the time goes in v7:
time: 135 us; the launch traced here: 134 us
  starting transfers between devices  62.5 us (46%)
  waiting for transfers between devices  23.5 us (17%)
  local copies, waits for them, and re-layouts  20 us (15%)
  matrix products  14.2 us (11%)
  other arithmetic  12.5 us (9%)
    ppermute x20, starting transfers between devices, all_sum(): total = total + lax.ppermute(value, axis, pairs)  34.1 us
    all_to_all x1, starting transfers between devices, shards(): lax.all_to_all(held, ('px', 'py'), split_axis=1, concat_axis=1, tiled=True)  14.2 us
    ppermute x20, waiting for transfers between devices, all_sum(): total = total + lax.ppermute(value, axis, pairs)  12.9 us
    unnamed x49, local copies, waits for them, and re-layouts  9.1 us
    ppermute x4, starting transfers between devices, with_halo(): parts.insert(0, lax.ppermute(last, axis, up))  8.96 us
    scatter x1, local copies, waits for them, and re-layouts, shards(): contact = contact_home.reshape(hist, cells).at[:, targets].set(arrived.re...  6.8 us
    ppermute x4, waiting for transfers between devices, with_halo(): parts.append(lax.ppermute(leading, axis, down))  6.11 us
    ppermute x4, starting transfers between devices, with_halo(): parts.append(lax.ppermute(leading, axis, down))  5.35 us
  transfers between devices with their start and end apart: 29, of which 17 were waited for; matrix products, arithmetic and copies ran while one was open for 16% of the time, Pallas kernels for 0%

profile of v7, /device:TPU:0, one launch (start us, length us, event | category | flops | bytes accessed | tf_op | source)
XLA Modules:
  0.0 133.8 jit_solution(4337990277809226122)
XLA Ops:
  7.3 14.2 %all-to-all-start = ((f32[128,128,9]{0,2,1:T(8,128)}), f32[128,128,9]{0,2,1:T(8,128)S(1)}, u32[]{:S(2)}, u32[]{:S(2)}) async-start(f32[128,128,9]{0,2,1:T(8,128)} %reshape.315), calls=%async_computation | async-start | bytes 2097152 | tf_op jit(solution)/shard_map/all_to_all | solution.py:98
  25.8 2.9 %collective-permute-start.2 = (f32[12,22,3]{2,0,1:T(8,128)}, f32[12,22,3]{2,0,1:T(8,128)S(1)}, u32[]{:S(2)}, u32[]{:S(2)}) collective-permute-start(f32[12,22,3]{2,0,1:T(8,128)} %get-tuple-element.30), channel_id=1, source_target_pairs={{0,1},{1,2},{2,3},{3,4},{4,5},{5,6},{6,7},{7,8},{8,9},{9,10},{10,1... | collective-permute-start | bytes 9512 | tf_op jit(solution)/shard_map/ppermute | solution.py:22
  32.1 4.5 %collective-permute-done.2 = f32[12,22,3]{2,0,1:T(8,128)S(1)} collective-permute-done((f32[12,22,3]{2,0,1:T(8,128)}, f32[12,22,3]{2,0,1:T(8,128)S(1)}, u32[]{:S(2)}, u32[]{:S(2)}) %collective-permute-start.2) | collective-permute-done | bytes 3200 | tf_op jit(solution)/shard_map/ppermute | solution.py:22
  36.6 2.2 %collective-permute-done.3 = f32[12,22,3]{2,0,1:T(8,128)} collective-permute-done((f32[12,22,3]{2,0,1:T(8,128)}, f32[12,22,3]{2,0,1:T(8,128)}, u32[]{:S(2)}, u32[]{:S(2)}) %collective-permute-start.3) | collective-permute-done | bytes 3200 | tf_op jit(solution)/shard_map/ppermute | solution.py:25
  44.2 6.8 %scatter_custom_fusion = f32[128,2048]{0,1:T(8,128)S(1)} fusion(f32[128,2048]{0,1:T(8,128)S(1)} %bitcast.92, s32[1152]{0:T(1024)S(1)} %fusion.46, f32[128,1152]{0,1:T(8,128)} %reshape.320), kind=kCustom, calls=%fused_computation.30 | custom fusion | bytes 1638400 | tf_op jit(solution)/shard_map/scatter | solution.py:122
  51.1 3.4 %fusion.19 = (f32[128,2048]{0,1:T(8,128)S(1)}, f32[128,2048]{0,1:T(8,128)S(1)}) fusion(f32[128,2048]{0,1:T(8,128)S(1)} %scatter_custom_fusion, f32[128,2048]{0,1:T(8,128)S(1)} %bitcast.91, f32[128,24]{0,1:T(8,128)S(1)} %copy-done, f32[6,21,133]{2,0,1:T(8,128)} %copy-done.1, f32[6,21,133]{2,0,1:T(8,128)} %copy-done.2, f32[6,21,133]{2,0,1:T(8,128)} %copy-done.3, ...), kind=kOutput, calls=%fused_computation.29 | convolution fusion | flops 77742080 | bytes 4474720 | tf_op jit(solution)/shard_map/dot_general | solution.py:116
  57.2 2.5 %convolution_bitcast_fusion.1 = f32[128,19,131]{0,2,1:T(8,128)S(1)} fusion(f32[6,19,131]{2,0,1:T(8,128)S(1)} %copy-done.5, f32[6,19,131]{2,0,1:T(8,128)S(1)} %copy-done.6, f32[6,19,131]{2,0,1:T(8,128)S(1)} %copy-done.7, f32[6,19,131]{2,0,1:T(8,128)S(1)} %copy-done.4, f32[128,24]{0,1:T(8,128)S(1)} %copy-done), kind=kOutput, calls=%fused_computation.4 | convolution fusion | flops 91933704 | bytes 1525600 | tf_op jit(solution)/shard_map/hb,bxy->hxy/dot_general | solution.py:129
  60.2 3.5 %collective-permute-start.6 = (f32[128,19,2]{0,2,1:T(2,128)S(1)}, f32[128,19,2]{0,2,1:T(2,128)S(1)}, u32[]{:S(2)}, u32[]{:S(2)}) collective-permute-start(f32[128,19,2]{0,2,1:T(2,128)S(1)} %pad_maximum_fusion.15), channel_id=1, source_target_pairs={{0,1},{1,2},{2,3},{3,4},{4,5},{5,6},{6,7},{7,8},{8,9},{9,10},{10,1... | collective-permute-start | bytes 58376 | tf_op jit(solution)/shard_map/ppermute | solution.py:22
  65.8 3.5 %collective-permute-done.7 = f32[128,19,1]{0,2,1:T(1,128)S(1)} collective-permute-done((f32[128,19,1]{0,2,1:T(1,128)S(1)}, f32[128,19,1]{0,2,1:T(1,128)S(1)}, u32[]{:S(2)}, u32[]{:S(2)}) %collective-permute-start.7) | collective-permute-done | bytes 9760 | tf_op jit(solution)/shard_map/ppermute | solution.py:25
  69.3 2.2 %fusion.13 = f32[24,19,131]{2,0,1:T(8,128)S(1)} fusion(f32[19,131,24]{1,2,0:T(8,128)S(1)} %fusion.31, f32[128,19,131]{0,2,1:T(8,128)S(1)} %convolution_bitcast_fusion.1, f32[128,19,1]{0,2,1:T(1,128)S(1)} %collective-permute-done.7, f32[128,1,128]{0,2,1:T(8,128)S(1)} %collective-permute-done.5, f32[128,16,128]{0,2,1:T(8,128)S(1)} %bitcast.88, ...), kind=kOutput, calls=%fused_computation.20 | convolution fusion | flops 93466928 | bytes 3048868 | tf_op jit(solution)/shard_map/hb,hxy->bxy/dot_general | solution.py:130
  73.8 2.3 %collective-permute-start.10 = (f32[2,128]{1,0:T(2,128)S(1)}, f32[2,128]{1,0:T(2,128)S(1)}, u32[]{:S(2)}, u32[]{:S(2)}) collective-permute-start(f32[2,128]{1,0:T(2,128)S(1)} %broadcast_in_dim.4), channel_id=1, source_target_pairs={{0,48},{16,0},{32,16},{48,32},{64,112},{80,64},{96,80},{112,96},{1... | collective-permute-start | bytes 3080 | tf_op jit(solution)/shard_map/ppermute | solution.py:42
  79.8 2.9 %collective-permute-start.11 = (f32[2,128]{1,0:T(2,128)S(1)}, f32[2,128]{1,0:T(2,128)S(1)}, u32[]{:S(2)}, u32[]{:S(2)}) collective-permute-start(f32[2,128]{1,0:T(2,128)S(1)} %add_add_fusion.6), channel_id=1, source_target_pairs={{0,64},{16,80},{32,96},{48,112},{64,0},{80,16},{96,32},{112,48},{1... | collective-permute-start | bytes 3080 | tf_op jit(solution)/shard_map/ppermute | solution.py:42
  82.7 2.2 %convolution_bitcast_fusion.2 = f32[128,17,129]{0,2,1:T(8,128)S(1)} fusion(f32[6,17,129]{2,0,1:T(8,128)S(1)} %get-tuple-element.37, f32[6,17,129]{2,0,1:T(8,128)S(1)} %get-tuple-element.38, f32[6,17,129]{2,0,1:T(8,128)S(1)} %get-tuple-element.39, f32[6,17,129]{2,0,1:T(8,128)S(1)} %get-tuple-element.36, f32[128,24]{0,1:T(8,128)S(1)} %copy-done), kind=kOutput, calls=%fused_computation.5 | convolution fusion | flops 81000648 | bytes 1345632 | tf_op jit(solution)/shard_map/hb,bxy->hxy/dot_general | solution.py:129
  85.0 2.2 %collective-permute-start.12 = (f32[2,128]{1,0:T(2,128)S(1)}, f32[2,128]{1,0:T(2,128)S(1)}, u32[]{:S(2)}, u32[]{:S(2)}) collective-permute-start(f32[2,128]{1,0:T(2,128)S(1)} %add.317), channel_id=1, source_target_pairs={{0,1},{1,2},{2,3},{3,0},{4,5},{5,6},{6,7},{7,4},{8,9},{9,10},{10,1... | collective-permute-start | bytes 3080 | tf_op jit(solution)/shard_map/ppermute | solution.py:42
  87.2 5.1 %collective-permute-start.13 = (f32[2,128]{1,0:T(2,128)S(1)}, f32[2,128]{1,0:T(2,128)S(1)}, u32[]{:S(2)}, u32[]{:S(2)}) collective-permute-start(f32[2,128]{1,0:T(2,128)S(1)} %add.317), channel_id=1, source_target_pairs={{0,2},{1,3},{2,0},{3,1},{4,6},{5,7},{6,4},{7,5},{8,10},{9,11},{10,... | collective-permute-start | bytes 3080 | tf_op jit(solution)/shard_map/ppermute | solution.py:42
  93.8 2.0 %collective-permute-done.14 = f32[2,128]{1,0:T(2,128)S(1)} collective-permute-done((f32[2,128]{1,0:T(2,128)S(1)}, f32[2,128]{1,0:T(2,128)S(1)}, u32[]{:S(2)}, u32[]{:S(2)}) %collective-permute-start.14) | collective-permute-done | bytes 1056 | tf_op jit(solution)/shard_map/ppermute | solution.py:42
  99.5 2.5 %collective-permute-start.17 = (f32[2,128]{1,0:T(2,128)S(1)}, f32[2,128]{1,0:T(2,128)S(1)}, u32[]{:S(2)}, u32[]{:S(2)}) collective-permute-start(f32[2,128]{1,0:T(2,128)S(1)} %add_add_fusion.5), channel_id=1, source_target_pairs={{0,12},{1,13},{2,14},{3,15},{4,0},{5,1},{6,2},{7,3},{8,4},{9,5},{1... | collective-permute-start | bytes 3080 | tf_op jit(solution)/shard_map/ppermute | solution.py:42
  102.0 2.0 %fusion.15 = f32[24,17,129]{2,0,1:T(8,128)S(1)} fusion(f32[17,129,24]{1,2,0:T(8,128)S(1)} %fusion.32, f32[128,17,129]{0,2,1:T(8,128)S(1)} %convolution_bitcast_fusion.2, f32[128,19,2]{0,2,1:T(2,128)S(1)} %collective-permute-done.6, f32[128,1,128]{0,2,1:T(8,128)S(1)} %collective-permute-done.5, f32[128,16,128]{0,2,1:T(8,128)S(1)} %bitcast.89, ...), kind=kOutput, calls=%fused_computation.23 | convolution fusion | flops 82070832 | bytes 2829572 | tf_op jit(solution)/shard_map/hb,hxy->bxy/dot_general | solution.py:130
  104.9 2.7 %pad_maximum_fusion.19 = f32[4]{0:T(128)S(1)} fusion(f32[1]{0:T(128)} %bitcast.20, f32[1]{0:T(128)} %bitcast.19, f32[1]{0:T(128)} %bitcast.18, f32[1]{0:T(128)} %bitcast.15), kind=kLoop, calls=%fused_computation.108 | loop fusion | flops 12 | bytes 32 | tf_op jit(solution)/shard_map/stack | solution.py:138
  111.7 2.6 %collective-permute-start.21 = (f32[4,128]{1,0:T(4,128)S(1)}, f32[4,128]{1,0:T(4,128)S(1)}, u32[]{:S(2)}, u32[]{:S(2)}) collective-permute-start(f32[4,128]{1,0:T(4,128)S(1)} %add_add_fusion.3), channel_id=1, source_target_pairs={{0,64},{16,80},{32,96},{48,112},{64,0},{80,16},{96,32},{112,48},{1... | collective-permute-start | bytes 6152 | tf_op jit(solution)/shard_map/ppermute | solution.py:42
  114.3 2.5 %collective-permute-done.21 = f32[4,128]{1,0:T(4,128)S(1)} collective-permute-done((f32[4,128]{1,0:T(4,128)S(1)}, f32[4,128]{1,0:T(4,128)S(1)}, u32[]{:S(2)}, u32[]{:S(2)}) %collective-permute-start.21) | collective-permute-done | bytes 2080 | tf_op jit(solution)/shard_map/ppermute | solution.py:42
  116.8 2.7 %collective-permute-start.23 = (f32[4,128]{1,0:T(4,128)S(1)}, f32[4,128]{1,0:T(4,128)S(1)}, u32[]{:S(2)}, u32[]{:S(2)}) collective-permute-start(f32[4,128]{1,0:T(4,128)S(1)} %add.335), channel_id=1, source_target_pairs={{0,2},{1,3},{2,0},{3,1},{4,6},{5,7},{6,4},{7,5},{8,10},{9,11},{10,... | collective-permute-start | bytes 6152 | tf_op jit(solution)/shard_map/ppermute | solution.py:42
  123.4 3.8 %collective-permute-start.26 = (f32[4,128]{1,0:T(4,128)S(1)}, f32[4,128]{1,0:T(4,128)S(1)}, u32[]{:S(2)}, u32[]{:S(2)}) collective-permute-start(f32[4,128]{1,0:T(4,128)S(1)} %add_add_fusion.2), channel_id=1, source_target_pairs={{0,8},{1,9},{2,10},{3,11},{4,12},{5,13},{6,14},{7,15},{8,0},{9,1},... | collective-permute-start | bytes 6152 | tf_op jit(solution)/shard_map/ppermute | solution.py:42
  128.8 2.0 %collective-permute-done.27 = f32[4,128]{1,0:T(4,128)S(1)} collective-permute-done((f32[4,128]{1,0:T(4,128)S(1)}, f32[4,128]{1,0:T(4,128)S(1)}, u32[]{:S(2)}, u32[]{:S(2)}) %collective-permute-start.27) | collective-permute-done | bytes 2080 | tf_op jit(solution)/shard_map/ppermute | solution.py:42
  (140 shorter events, 49.5 us)
Async XLA Ops:
  2.3 22.7 %collective-permute-start = (f32[12,3,128]{2,0,1:T(8,128)S(1)}, f32[12,3,128]{2,0,1:T(8,128)S(1)}, u32[]{:S(2)}, u32[]{:S(2)}) collective-permute-start(f32[12,3,128]{2,0,1:T(8,128)S(1)} %get-tuple-element.40), channel_id=1, source_target_pairs={{0,16},{16,32},{32,48},{48,64},{64,80},{80,96},{96,112},{1,17},{17... | collective-permute-start | bytes 55304 | tf_op jit(solution)/shard_map/ppermute | solution.py:22
  3.6 21.4 %collective-permute-start.1 = (f32[12,3,128]{2,0,1:T(8,128)S(1)}, f32[12,3,128]{2,0,1:T(8,128)S(1)}, u32[]{:S(2)}, u32[]{:S(2)}) collective-permute-start(f32[12,3,128]{2,0,1:T(8,128)S(1)} %get-tuple-element.41), channel_id=1, source_target_pairs={{16,0},{32,16},{48,32},{64,48},{80,64},{96,80},{112,96},{17,1},{33... | collective-permute-start | bytes 55304 | tf_op jit(solution)/shard_map/ppermute | solution.py:25
  7.3 36.1 %all-to-all-start = ((f32[128,128,9]{0,2,1:T(8,128)}), f32[128,128,9]{0,2,1:T(8,128)S(1)}, u32[]{:S(2)}, u32[]{:S(2)}) async-start(f32[128,128,9]{0,2,1:T(8,128)} %reshape.315), calls=%async_computation | async-start | bytes 2097152 | tf_op jit(solution)/shard_map/all_to_all | solution.py:98
  25.8 10.8 %collective-permute-start.2 = (f32[12,22,3]{2,0,1:T(8,128)}, f32[12,22,3]{2,0,1:T(8,128)S(1)}, u32[]{:S(2)}, u32[]{:S(2)}) collective-permute-start(f32[12,22,3]{2,0,1:T(8,128)} %get-tuple-element.30), channel_id=1, source_target_pairs={{0,1},{1,2},{2,3},{3,4},{4,5},{5,6},{6,7},{7,8},{8,9},{9,10},{10,1... | collective-permute-start | bytes 9512 | tf_op jit(solution)/shard_map/ppermute | solution.py:22
  28.7 10.1 %collective-permute-start.3 = (f32[12,22,3]{2,0,1:T(8,128)}, f32[12,22,3]{2,0,1:T(8,128)}, u32[]{:S(2)}, u32[]{:S(2)}) collective-permute-start(f32[12,22,3]{2,0,1:T(8,128)} %get-tuple-element.31), channel_id=1, source_target_pairs={{1,0},{2,1},{3,2},{4,3},{5,4},{6,5},{7,6},{8,7},{9,8},{10,9},{11,1... | collective-permute-start | bytes 9512 | tf_op jit(solution)/shard_map/ppermute | solution.py:25
  54.5 5.7 %collective-permute-start.4 = (f32[128,2,128]{0,2,1:T(8,128)S(1)}, f32[128,2,128]{0,2,1:T(8,128)S(1)}, u32[]{:S(2)}, u32[]{:S(2)}) collective-permute-start(f32[128,2,128]{0,2,1:T(8,128)S(1)} %slice.195), channel_id=1, source_target_pairs={{0,16},{16,32},{32,48},{48,64},{64,80},{80,96},{96,112},{1,17},{17... | collective-permute-start | bytes 393224 | tf_op jit(solution)/shard_map/ppermute | solution.py:22
  55.9 4.3 %collective-permute-start.5 = (f32[128,1,128]{0,2,1:T(8,128)S(1)}, f32[128,1,128]{0,2,1:T(8,128)S(1)}, u32[]{:S(2)}, u32[]{:S(2)}) collective-permute-start(f32[128,1,128]{0,2,1:T(8,128)S(1)} %slice.196), channel_id=1, source_target_pairs={{16,0},{32,16},{48,32},{64,48},{80,64},{96,80},{112,96},{17,1},{33... | collective-permute-start | bytes 196616 | tf_op jit(solution)/shard_map/ppermute | solution.py:25
  60.2 9.0 %collective-permute-start.6 = (f32[128,19,2]{0,2,1:T(2,128)S(1)}, f32[128,19,2]{0,2,1:T(2,128)S(1)}, u32[]{:S(2)}, u32[]{:S(2)}) collective-permute-start(f32[128,19,2]{0,2,1:T(2,128)S(1)} %pad_maximum_fusion.15), channel_id=1, source_target_pairs={{0,1},{1,2},{2,3},{3,4},{4,5},{5,6},{6,7},{7,8},{8,9},{9,10},{10,1... | collective-permute-start | bytes 58376 | tf_op jit(solution)/shard_map/ppermute | solution.py:22
  63.7 5.6 %collective-permute-start.7 = (f32[128,19,1]{0,2,1:T(1,128)S(1)}, f32[128,19,1]{0,2,1:T(1,128)S(1)}, u32[]{:S(2)}, u32[]{:S(2)}) collective-permute-start(f32[128,19,1]{0,2,1:T(1,128)S(1)} %pad_maximum_fusion.16), channel_id=1, source_target_pairs={{1,0},{2,1},{3,2},{4,3},{5,4},{6,5},{7,6},{8,7},{9,8},{10,9},{11,1... | collective-permute-start | bytes 29192 | tf_op jit(solution)/shard_map/ppermute | solution.py:25
  73.8 4.1 %collective-permute-start.10 = (f32[2,128]{1,0:T(2,128)S(1)}, f32[2,128]{1,0:T(2,128)S(1)}, u32[]{:S(2)}, u32[]{:S(2)}) collective-permute-start(f32[2,128]{1,0:T(2,128)S(1)} %broadcast_in_dim.4), channel_id=1, source_target_pairs={{0,48},{16,0},{32,16},{48,32},{64,112},{80,64},{96,80},{112,96},{1... | collective-permute-start | bytes 3080 | tf_op jit(solution)/shard_map/ppermute | solution.py:42
  79.8 5.2 %collective-permute-start.11 = (f32[2,128]{1,0:T(2,128)S(1)}, f32[2,128]{1,0:T(2,128)S(1)}, u32[]{:S(2)}, u32[]{:S(2)}) collective-permute-start(f32[2,128]{1,0:T(2,128)S(1)} %add_add_fusion.6), channel_id=1, source_target_pairs={{0,64},{16,80},{32,96},{48,112},{64,0},{80,16},{96,32},{112,48},{1... | collective-permute-start | bytes 3080 | tf_op jit(solution)/shard_map/ppermute | solution.py:42
  85.0 7.9 %collective-permute-start.12 = (f32[2,128]{1,0:T(2,128)S(1)}, f32[2,128]{1,0:T(2,128)S(1)}, u32[]{:S(2)}, u32[]{:S(2)}) collective-permute-start(f32[2,128]{1,0:T(2,128)S(1)} %add.317), channel_id=1, source_target_pairs={{0,1},{1,2},{2,3},{3,0},{4,5},{5,6},{6,7},{7,4},{8,9},{9,10},{10,1... | collective-permute-start | bytes 3080 | tf_op jit(solution)/shard_map/ppermute | solution.py:42
  87.2 6.6 %collective-permute-start.13 = (f32[2,128]{1,0:T(2,128)S(1)}, f32[2,128]{1,0:T(2,128)S(1)}, u32[]{:S(2)}, u32[]{:S(2)}) collective-permute-start(f32[2,128]{1,0:T(2,128)S(1)} %add.317), channel_id=1, source_target_pairs={{0,2},{1,3},{2,0},{3,1},{4,6},{5,7},{6,4},{7,5},{8,10},{9,11},{10,... | collective-permute-start | bytes 3080 | tf_op jit(solution)/shard_map/ppermute | solution.py:42
  95.8 8.2 %collective-permute-start.15 = (f32[2,128]{1,0:T(2,128)S(1)}, f32[2,128]{1,0:T(2,128)S(1)}, u32[]{:S(2)}, u32[]{:S(2)}) collective-permute-start(f32[2,128]{1,0:T(2,128)S(1)} %add_add_fusion.5), channel_id=1, source_target_pairs={{0,4},{1,5},{2,6},{3,7},{4,8},{5,9},{6,10},{7,11},{8,12},{9,13},{1... | collective-permute-start | bytes 3080 | tf_op jit(solution)/shard_map/ppermute | solution.py:42
  97.6 6.5 %collective-permute-start.16 = (f32[2,128]{1,0:T(2,128)S(1)}, f32[2,128]{1,0:T(2,128)S(1)}, u32[]{:S(2)}, u32[]{:S(2)}) collective-permute-start(f32[2,128]{1,0:T(2,128)S(1)} %add_add_fusion.5), channel_id=1, source_target_pairs={{0,8},{1,9},{2,10},{3,11},{4,12},{5,13},{6,14},{7,15},{8,0},{9,1},... | collective-permute-start | bytes 3080 | tf_op jit(solution)/shard_map/ppermute | solution.py:42
  99.5 4.6 %collective-permute-start.17 = (f32[2,128]{1,0:T(2,128)S(1)}, f32[2,128]{1,0:T(2,128)S(1)}, u32[]{:S(2)}, u32[]{:S(2)}) collective-permute-start(f32[2,128]{1,0:T(2,128)S(1)} %add_add_fusion.5), channel_id=1, source_target_pairs={{0,12},{1,13},{2,14},{3,15},{4,0},{5,1},{6,2},{7,3},{8,4},{9,5},{1... | collective-permute-start | bytes 3080 | tf_op jit(solution)/shard_map/ppermute | solution.py:42
  107.6 3.6 %collective-permute-start.19 = (f32[4,128]{1,0:T(4,128)S(1)}, f32[4,128]{1,0:T(4,128)S(1)}, u32[]{:S(2)}, u32[]{:S(2)}) collective-permute-start(f32[4,128]{1,0:T(4,128)S(1)} %broadcast_in_dim.5), channel_id=1, source_target_pairs={{0,32},{16,48},{32,0},{48,16},{64,96},{80,112},{96,64},{112,80},{1... | collective-permute-start | bytes 6152 | tf_op jit(solution)/shard_map/ppermute | solution.py:42
  111.7 5.1 %collective-permute-start.21 = (f32[4,128]{1,0:T(4,128)S(1)}, f32[4,128]{1,0:T(4,128)S(1)}, u32[]{:S(2)}, u32[]{:S(2)}) collective-permute-start(f32[4,128]{1,0:T(4,128)S(1)} %add_add_fusion.3), channel_id=1, source_target_pairs={{0,64},{16,80},{32,96},{48,112},{64,0},{80,16},{96,32},{112,48},{1... | collective-permute-start | bytes 6152 | tf_op jit(solution)/shard_map/ppermute | solution.py:42
  116.8 4.8 %collective-permute-start.22 = (f32[4,128]{1,0:T(4,128)S(1)}, f32[4,128]{1,0:T(4,128)S(1)}, u32[]{:S(2)}, u32[]{:S(2)}) collective-permute-start(f32[4,128]{1,0:T(4,128)S(1)} %add.335), channel_id=1, source_target_pairs={{0,1},{1,2},{2,3},{3,0},{4,5},{5,6},{6,7},{7,4},{8,9},{9,10},{10,1... | collective-permute-start | bytes 6152 | tf_op jit(solution)/shard_map/ppermute | solution.py:42
  116.8 5.1 %collective-permute-start.23 = (f32[4,128]{1,0:T(4,128)S(1)}, f32[4,128]{1,0:T(4,128)S(1)}, u32[]{:S(2)}, u32[]{:S(2)}) collective-permute-start(f32[4,128]{1,0:T(4,128)S(1)} %add.335), channel_id=1, source_target_pairs={{0,2},{1,3},{2,0},{3,1},{4,6},{5,7},{6,4},{7,5},{8,10},{9,11},{10,... | collective-permute-start | bytes 6152 | tf_op jit(solution)/shard_map/ppermute | solution.py:42
  119.5 3.6 %collective-permute-start.24 = (f32[4,128]{1,0:T(4,128)S(1)}, f32[4,128]{1,0:T(4,128)S(1)}, u32[]{:S(2)}, u32[]{:S(2)}) collective-permute-start(f32[4,128]{1,0:T(4,128)S(1)} %add.335), channel_id=1, source_target_pairs={{0,3},{1,0},{2,1},{3,2},{4,7},{5,4},{6,5},{7,6},{8,11},{9,8},{10,9... | collective-permute-start | bytes 6152 | tf_op jit(solution)/shard_map/ppermute | solution.py:42
  123.1 5.6 %collective-permute-start.25 = (f32[4,128]{1,0:T(4,128)S(1)}, f32[4,128]{1,0:T(4,128)S(1)}, u32[]{:S(2)}, u32[]{:S(2)}) collective-permute-start(f32[4,128]{1,0:T(4,128)S(1)} %add_add_fusion.2), channel_id=1, source_target_pairs={{0,4},{1,5},{2,6},{3,7},{4,8},{5,9},{6,10},{7,11},{8,12},{9,13},{1... | collective-permute-start | bytes 6152 | tf_op jit(solution)/shard_map/ppermute | solution.py:42
  123.4 5.4 %collective-permute-start.26 = (f32[4,128]{1,0:T(4,128)S(1)}, f32[4,128]{1,0:T(4,128)S(1)}, u32[]{:S(2)}, u32[]{:S(2)}) collective-permute-start(f32[4,128]{1,0:T(4,128)S(1)} %add_add_fusion.2), channel_id=1, source_target_pairs={{0,8},{1,9},{2,10},{3,11},{4,12},{5,13},{6,14},{7,15},{8,0},{9,1},... | collective-permute-start | bytes 6152 | tf_op jit(solution)/shard_map/ppermute | solution.py:42
  127.3 3.6 %collective-permute-start.27 = (f32[4,128]{1,0:T(4,128)S(1)}, f32[4,128]{1,0:T(4,128)S(1)}, u32[]{:S(2)}, u32[]{:S(2)}) collective-permute-start(f32[4,128]{1,0:T(4,128)S(1)} %add_add_fusion.2), channel_id=1, source_target_pairs={{0,12},{1,13},{2,14},{3,15},{4,0},{5,1},{6,2},{7,3},{8,4},{9,5},{1... | collective-permute-start | bytes 6152 | tf_op jit(solution)/shard_map/ppermute | solution.py:42
  (25 other events, 299.0 us)

commit v8 on v7

--- a/solution.py
+++ b/solution.py
@@ -100,11 +100,16 @@
     def with_base(shells):
         return jnp.einsum("ab,bxy->axy", stiff_base, shells, precision=HIGH)
 
+    shell_mask = inside((rows + 5, cols + 5), -3, -3, rows, cols, True)
+    node_mask = inside((rows + 4, cols + 4), -2, -2, rows, cols, False)
+
     def shell_keep(forces, offset):
-        return forces * inside(forces.shape[1:], offset, offset, rows, cols, True)[None]
+        skip = offset + 3
+        return forces * shell_mask[None, skip : skip + forces.shape[1], skip : skip + forces.shape[2]]
 
     def node_keep(field, offset):
-        return field * inside(field.shape[1:], offset, offset, rows, cols, False)[None]
+        skip = offset + 2
+        return field * node_mask[None, skip : skip + field.shape[1], skip : skip + field.shape[2]]
 
     both = with_halo(jnp.concatenate([displacement, load], axis=0), 3, 3)
     start_shells = gather_shells(both[:6])

time: 135 us -> 135 us (level)
  other arithmetic: 12.5 us -> 9.83 us
  local copies, waits for them, and re-layouts: 20 us -> 22 us
  starting transfers between devices: 62.5 us -> 64.1 us
    convert_element_type x5 -> x2, other arithmetic: 3.39 us -> 0.15 us  [inside(): return (row_ok[:, None] & col_ok[None, :]).astype(jnp.float32)]
    slice x0 -> x3, local copies, waits for them, and re-layouts: none -> 2.05 us  [the longest x2 1.37 us: shell_keep(): shell_mask[None, skip:skip + forces.shape[1], skip:skip + forces.shape[2]]]
    unnamed x49 -> x45, local copies, waits for them, and re-layouts: 9.1 us -> 9.09 us
  transfers between devices with their start and end apart: 29 -> 29, of which waited for: 17 -> 16; matrix products, arithmetic and copies ran while one was open for 16% -> 16% of each run, Pallas kernels for 0% -> 0%
where the time goes in v8:
time: 135 us; the launch traced here: 134 us
  starting transfers between devices  64.1 us (47%)
  waiting for transfers between devices  22.7 us (17%)
  local copies, waits for them, and re-layouts  22 us (16%)
  matrix products  14.2 us (11%)
  other arithmetic  9.83 us (7%)
    ppermute x20, starting transfers between devices, all_sum(): total = total + lax.ppermute(value, axis, pairs)  34.4 us
    all_to_all x1, starting transfers between devices, shards(): lax.all_to_all(held, ('px', 'py'), split_axis=1, concat_axis=1, tiled=True)  14.2 us
    ppermute x20, waiting for transfers between devices, all_sum(): total = total + lax.ppermute(value, axis, pairs)  12.9 us
    ppermute x4, starting transfers between devices, with_halo(): parts.insert(0, lax.ppermute(last, axis, up))  10.2 us
    unnamed x45, local copies, waits for them, and re-layouts  9.09 us
    scatter x1, local copies, waits for them, and re-layouts, shards(): contact = contact_home.reshape(hist, cells).at[:, targets].set(arrived.re...  6.8 us
    ppermute x4, waiting for transfers between devices, with_halo(): parts.append(lax.ppermute(leading, axis, down))  6.02 us
    ppermute x4, starting transfers between devices, with_halo(): parts.append(lax.ppermute(leading, axis, down))  5.34 us
  transfers between devices with their start and end apart: 29, of which 16 were waited for; matrix products, arithmetic and copies ran while one was open for 16% of the time, Pallas kernels for 0%

profile of v8, /device:TPU:0, one launch (start us, length us, event | category | flops | bytes accessed | tf_op | source)
XLA Modules:
  0.0 134.0 jit_solution(17022682528582659014)
XLA Ops:
  7.3 14.2 %all-to-all-start = ((f32[128,128,9]{0,2,1:T(8,128)}), f32[128,128,9]{0,2,1:T(8,128)S(1)}, u32[]{:S(2)}, u32[]{:S(2)}) async-start(f32[128,128,9]{0,2,1:T(8,128)} %reshape.200), calls=%async_computation | async-start | bytes 2097152 | tf_op jit(solution)/shard_map/all_to_all | solution.py:98
  22.5 3.5 %collective-permute-start.2 = (f32[12,22,3]{2,0,1:T(8,128)}, f32[12,22,3]{2,0,1:T(8,128)}, u32[]{:S(2)}, u32[]{:S(2)}) collective-permute-start(f32[12,22,3]{2,0,1:T(8,128)} %get-tuple-element.30), channel_id=1, source_target_pairs={{0,1},{1,2},{2,3},{3,4},{4,5},{5,6},{6,7},{7,8},{8,9},{9,10},{10,1... | collective-permute-start | bytes 9512 | tf_op jit(solution)/shard_map/ppermute | solution.py:22
  32.0 3.8 %collective-permute-done.2 = f32[12,22,3]{2,0,1:T(8,128)} collective-permute-done((f32[12,22,3]{2,0,1:T(8,128)}, f32[12,22,3]{2,0,1:T(8,128)}, u32[]{:S(2)}, u32[]{:S(2)}) %collective-permute-start.2) | collective-permute-done | bytes 3200 | tf_op jit(solution)/shard_map/ppermute | solution.py:22
  35.8 2.6 %collective-permute-done.3 = f32[12,22,3]{2,0,1:T(8,128)} collective-permute-done((f32[12,22,3]{2,0,1:T(8,128)}, f32[12,22,3]{2,0,1:T(8,128)}, u32[]{:S(2)}, u32[]{:S(2)}) %collective-permute-start.3) | collective-permute-done | bytes 3200 | tf_op jit(solution)/shard_map/ppermute | solution.py:25
  43.9 6.8 %scatter_custom_fusion = f32[128,2048]{0,1:T(8,128)S(1)} fusion(f32[128,2048]{0,1:T(8,128)S(1)} %bitcast.92, s32[1152]{0:T(1024)} %fusion.46, f32[128,1152]{0,1:T(8,128)} %reshape.205), kind=kCustom, calls=%fused_computation.30 | custom fusion | bytes 1638400 | tf_op jit(solution)/shard_map/scatter | solution.py:127
  50.8 3.4 %fusion.19 = (f32[128,2048]{0,1:T(8,128)S(1)}, f32[128,2048]{0,1:T(8,128)S(1)}) fusion(f32[128,2048]{0,1:T(8,128)S(1)} %scatter_custom_fusion, f32[128,2048]{0,1:T(8,128)S(1)} %bitcast.91, f32[128,24]{0,1:T(8,128)S(1)} %copy-done, f32[6,21,133]{2,0,1:T(8,128)} %copy-done.1, f32[6,21,133]{2,0,1:T(8,128)} %copy-done.2, f32[6,21,133]{2,0,1:T(8,128)} %copy-done.3, ...), kind=kOutput, calls=%fused_computation.29 | convolution fusion | flops 77742080 | bytes 4474720 | tf_op jit(solution)/shard_map/dot_general | solution.py:121
  57.3 2.5 %convolution_bitcast_fusion.1 = f32[128,19,131]{0,2,1:T(8,128)S(1)} fusion(f32[6,19,131]{2,0,1:T(8,128)S(1)} %copy-done.5, f32[6,19,131]{2,0,1:T(8,128)S(1)} %copy-done.6, f32[6,19,131]{2,0,1:T(8,128)S(1)} %copy-done.7, f32[6,19,131]{2,0,1:T(8,128)S(1)} %copy-done.4, f32[128,24]{0,1:T(8,128)S(1)} %copy-done), kind=kOutput, calls=%fused_computation.4 | convolution fusion | flops 91933704 | bytes 1525600 | tf_op jit(solution)/shard_map/hb,bxy->hxy/dot_general | solution.py:134
  59.9 3.5 %collective-permute-start.6 = (f32[128,19,2]{0,2,1:T(2,128)S(1)}, f32[128,19,2]{0,2,1:T(2,128)S(1)}, u32[]{:S(2)}, u32[]{:S(2)}) collective-permute-start(f32[128,19,2]{0,2,1:T(2,128)S(1)} %pad_maximum_fusion.15), channel_id=1, source_target_pairs={{0,1},{1,2},{2,3},{3,4},{4,5},{5,6},{6,7},{7,8},{8,9},{9,10},{10,1... | collective-permute-start | bytes 58376 | tf_op jit(solution)/shard_map/ppermute | solution.py:22
  65.6 3.5 %collective-permute-done.7 = f32[128,19,1]{0,2,1:T(1,128)S(1)} collective-permute-done((f32[128,19,1]{0,2,1:T(1,128)S(1)}, f32[128,19,1]{0,2,1:T(1,128)S(1)}, u32[]{:S(2)}, u32[]{:S(2)}) %collective-permute-start.7) | collective-permute-done | bytes 9760 | tf_op jit(solution)/shard_map/ppermute | solution.py:25
  69.0 2.2 %fusion.13 = f32[24,19,131]{2,0,1:T(8,128)S(1)} fusion(f32[19,131,24]{1,2,0:T(8,128)S(1)} %fusion.31, f32[128,19,131]{0,2,1:T(8,128)S(1)} %convolution_bitcast_fusion.1, f32[128,19,1]{0,2,1:T(1,128)S(1)} %collective-permute-done.7, f32[128,1,128]{0,2,1:T(8,128)S(1)} %collective-permute-done.5, f32[128,16,128]{0,2,1:T(8,128)S(1)} %bitcast.88, ...), kind=kOutput, calls=%fused_computation.20 | convolution fusion | flops 93466928 | bytes 3048868 | tf_op jit(solution)/shard_map/hb,hxy->bxy/dot_general | solution.py:135
  73.6 2.4 %collective-permute-start.10 = (f32[2,128]{1,0:T(2,128)S(1)}, f32[2,128]{1,0:T(2,128)S(1)}, u32[]{:S(2)}, u32[]{:S(2)}) collective-permute-start(f32[2,128]{1,0:T(2,128)S(1)} %broadcast_in_dim.4), channel_id=1, source_target_pairs={{0,48},{16,0},{32,16},{48,32},{64,112},{80,64},{96,80},{112,96},{1... | collective-permute-start | bytes 3080 | tf_op jit(solution)/shard_map/ppermute | solution.py:42
  79.6 2.9 %collective-permute-start.11 = (f32[2,128]{1,0:T(2,128)S(1)}, f32[2,128]{1,0:T(2,128)S(1)}, u32[]{:S(2)}, u32[]{:S(2)}) collective-permute-start(f32[2,128]{1,0:T(2,128)S(1)} %add_add_fusion.6), channel_id=1, source_target_pairs={{0,64},{16,80},{32,96},{48,112},{64,0},{80,16},{96,32},{112,48},{1... | collective-permute-start | bytes 3080 | tf_op jit(solution)/shard_map/ppermute | solution.py:42
  82.5 2.2 %convolution_bitcast_fusion.2 = f32[128,17,129]{0,2,1:T(8,128)S(1)} fusion(f32[6,17,129]{2,0,1:T(8,128)S(1)} %get-tuple-element.37, f32[6,17,129]{2,0,1:T(8,128)S(1)} %get-tuple-element.38, f32[6,17,129]{2,0,1:T(8,128)S(1)} %get-tuple-element.39, f32[6,17,129]{2,0,1:T(8,128)S(1)} %get-tuple-element.36, f32[128,24]{0,1:T(8,128)S(1)} %copy-done), kind=kOutput, calls=%fused_computation.5 | convolution fusion | flops 81000648 | bytes 1345632 | tf_op jit(solution)/shard_map/hb,bxy->hxy/dot_general | solution.py:134
  86.3 6.1 %collective-permute-start.13 = (f32[2,128]{1,0:T(2,128)S(1)}, f32[2,128]{1,0:T(2,128)S(1)}, u32[]{:S(2)}, u32[]{:S(2)}) collective-permute-start(f32[2,128]{1,0:T(2,128)S(1)} %add.237), channel_id=1, source_target_pairs={{0,2},{1,3},{2,0},{3,1},{4,6},{5,7},{6,4},{7,5},{8,10},{9,11},{10,... | collective-permute-start | bytes 3080 | tf_op jit(solution)/shard_map/ppermute | solution.py:42
  94.0 2.0 %collective-permute-done.14 = f32[2,128]{1,0:T(2,128)S(1)} collective-permute-done((f32[2,128]{1,0:T(2,128)S(1)}, f32[2,128]{1,0:T(2,128)S(1)}, u32[]{:S(2)}, u32[]{:S(2)}) %collective-permute-start.14) | collective-permute-done | bytes 1056 | tf_op jit(solution)/shard_map/ppermute | solution.py:42
  97.7 1.9 %collective-permute-start.16 = (f32[2,128]{1,0:T(2,128)S(1)}, f32[2,128]{1,0:T(2,128)S(1)}, u32[]{:S(2)}, u32[]{:S(2)}) collective-permute-start(f32[2,128]{1,0:T(2,128)S(1)} %add_add_fusion.5), channel_id=1, source_target_pairs={{0,8},{1,9},{2,10},{3,11},{4,12},{5,13},{6,14},{7,15},{8,0},{9,1},... | collective-permute-start | bytes 3080 | tf_op jit(solution)/shard_map/ppermute | solution.py:42
  99.6 2.5 %collective-permute-start.17 = (f32[2,128]{1,0:T(2,128)S(1)}, f32[2,128]{1,0:T(2,128)S(1)}, u32[]{:S(2)}, u32[]{:S(2)}) collective-permute-start(f32[2,128]{1,0:T(2,128)S(1)} %add_add_fusion.5), channel_id=1, source_target_pairs={{0,12},{1,13},{2,14},{3,15},{4,0},{5,1},{6,2},{7,3},{8,4},{9,5},{1... | collective-permute-start | bytes 3080 | tf_op jit(solution)/shard_map/ppermute | solution.py:42
  102.2 2.0 %fusion.15 = f32[24,17,129]{2,0,1:T(8,128)S(1)} fusion(f32[17,129,24]{1,2,0:T(8,128)S(1)} %fusion.32, f32[128,17,129]{0,2,1:T(8,128)S(1)} %convolution_bitcast_fusion.2, f32[128,19,2]{0,2,1:T(2,128)S(1)} %collective-permute-done.6, f32[128,1,128]{0,2,1:T(8,128)S(1)} %collective-permute-done.5, f32[128,16,128]{0,2,1:T(8,128)S(1)} %bitcast.89, ...), kind=kOutput, calls=%fused_computation.23 | convolution fusion | flops 82070832 | bytes 2829572 | tf_op jit(solution)/shard_map/hb,hxy->bxy/dot_general | solution.py:135
  105.0 2.7 %pad_maximum_fusion.19 = f32[4]{0:T(128)S(1)} fusion(f32[1]{0:T(128)} %bitcast.20, f32[1]{0:T(128)} %bitcast.19, f32[1]{0:T(128)} %bitcast.18, f32[1]{0:T(128)} %bitcast.15), kind=kLoop, calls=%fused_computation.101 | loop fusion | flops 12 | bytes 32 | tf_op jit(solution)/shard_map/stack | solution.py:143
  111.9 2.6 %collective-permute-start.21 = (f32[4,128]{1,0:T(4,128)S(1)}, f32[4,128]{1,0:T(4,128)S(1)}, u32[]{:S(2)}, u32[]{:S(2)}) collective-permute-start(f32[4,128]{1,0:T(4,128)S(1)} %add_add_fusion.3), channel_id=1, source_target_pairs={{0,64},{16,80},{32,96},{48,112},{64,0},{80,16},{96,32},{112,48},{1... | collective-permute-start | bytes 6152 | tf_op jit(solution)/shard_map/ppermute | solution.py:42
  114.4 2.5 %collective-permute-done.21 = f32[4,128]{1,0:T(4,128)S(1)} collective-permute-done((f32[4,128]{1,0:T(4,128)S(1)}, f32[4,128]{1,0:T(4,128)S(1)}, u32[]{:S(2)}, u32[]{:S(2)}) %collective-permute-start.21) | collective-permute-done | bytes 2080 | tf_op jit(solution)/shard_map/ppermute | solution.py:42
  117.0 2.7 %collective-permute-start.23 = (f32[4,128]{1,0:T(4,128)S(1)}, f32[4,128]{1,0:T(4,128)S(1)}, u32[]{:S(2)}, u32[]{:S(2)}) collective-permute-start(f32[4,128]{1,0:T(4,128)S(1)} %add.251), channel_id=1, source_target_pairs={{0,2},{1,3},{2,0},{3,1},{4,6},{5,7},{6,4},{7,5},{8,10},{9,11},{10,... | collective-permute-start | bytes 6152 | tf_op jit(solution)/shard_map/ppermute | solution.py:42
  123.6 3.8 %collective-permute-start.26 = (f32[4,128]{1,0:T(4,128)S(1)}, f32[4,128]{1,0:T(4,128)S(1)}, u32[]{:S(2)}, u32[]{:S(2)}) collective-permute-start(f32[4,128]{1,0:T(4,128)S(1)} %add_add_fusion.2), channel_id=1, source_target_pairs={{0,8},{1,9},{2,10},{3,11},{4,12},{5,13},{6,14},{7,15},{8,0},{9,1},... | collective-permute-start | bytes 6152 | tf_op jit(solution)/shard_map/ppermute | solution.py:42
  129.0 2.0 %collective-permute-done.27 = f32[4,128]{1,0:T(4,128)S(1)} collective-permute-done((f32[4,128]{1,0:T(4,128)S(1)}, f32[4,128]{1,0:T(4,128)S(1)}, u32[]{:S(2)}, u32[]{:S(2)}) %collective-permute-start.27) | collective-permute-done | bytes 2080 | tf_op jit(solution)/shard_map/ppermute | solution.py:42
  (130 shorter events, 48.6 us)
Async XLA Ops:
  2.3 19.3 %collective-permute-start = (f32[12,3,128]{2,0,1:T(8,128)S(1)}, f32[12,3,128]{2,0,1:T(8,128)S(1)}, u32[]{:S(2)}, u32[]{:S(2)}) collective-permute-start(f32[12,3,128]{2,0,1:T(8,128)S(1)} %get-tuple-element.40), channel_id=1, source_target_pairs={{0,16},{16,32},{32,48},{48,64},{64,80},{80,96},{96,112},{1,17},{17... | collective-permute-start | bytes 55304 | tf_op jit(solution)/shard_map/ppermute | solution.py:22
  3.6 18.0 %collective-permute-start.1 = (f32[12,3,128]{2,0,1:T(8,128)S(1)}, f32[12,3,128]{2,0,1:T(8,128)S(1)}, u32[]{:S(2)}, u32[]{:S(2)}) collective-permute-start(f32[12,3,128]{2,0,1:T(8,128)S(1)} %get-tuple-element.41), channel_id=1, source_target_pairs={{16,0},{32,16},{48,32},{64,48},{80,64},{96,80},{112,96},{17,1},{33... | collective-permute-start | bytes 55304 | tf_op jit(solution)/shard_map/ppermute | solution.py:25
  7.3 35.8 %all-to-all-start = ((f32[128,128,9]{0,2,1:T(8,128)}), f32[128,128,9]{0,2,1:T(8,128)S(1)}, u32[]{:S(2)}, u32[]{:S(2)}) async-start(f32[128,128,9]{0,2,1:T(8,128)} %reshape.200), calls=%async_computation | async-start | bytes 2097152 | tf_op jit(solution)/shard_map/all_to_all | solution.py:98
  22.5 13.3 %collective-permute-start.2 = (f32[12,22,3]{2,0,1:T(8,128)}, f32[12,22,3]{2,0,1:T(8,128)}, u32[]{:S(2)}, u32[]{:S(2)}) collective-permute-start(f32[12,22,3]{2,0,1:T(8,128)} %get-tuple-element.30), channel_id=1, source_target_pairs={{0,1},{1,2},{2,3},{3,4},{4,5},{5,6},{6,7},{7,8},{8,9},{9,10},{10,1... | collective-permute-start | bytes 9512 | tf_op jit(solution)/shard_map/ppermute | solution.py:22
  26.0 12.4 %collective-permute-start.3 = (f32[12,22,3]{2,0,1:T(8,128)}, f32[12,22,3]{2,0,1:T(8,128)}, u32[]{:S(2)}, u32[]{:S(2)}) collective-permute-start(f32[12,22,3]{2,0,1:T(8,128)} %get-tuple-element.31), channel_id=1, source_target_pairs={{1,0},{2,1},{3,2},{4,3},{5,4},{6,5},{7,6},{8,7},{9,8},{10,9},{11,1... | collective-permute-start | bytes 9512 | tf_op jit(solution)/shard_map/ppermute | solution.py:25
  54.2 5.7 %collective-permute-start.4 = (f32[128,2,128]{0,2,1:T(8,128)S(1)}, f32[128,2,128]{0,2,1:T(8,128)S(1)}, u32[]{:S(2)}, u32[]{:S(2)}) collective-permute-start(f32[128,2,128]{0,2,1:T(8,128)S(1)} %slice.207), channel_id=1, source_target_pairs={{0,16},{16,32},{32,48},{48,64},{64,80},{80,96},{96,112},{1,17},{17... | collective-permute-start | bytes 393224 | tf_op jit(solution)/shard_map/ppermute | solution.py:22
  56.0 3.9 %collective-permute-start.5 = (f32[128,1,128]{0,2,1:T(8,128)S(1)}, f32[128,1,128]{0,2,1:T(8,128)S(1)}, u32[]{:S(2)}, u32[]{:S(2)}) collective-permute-start(f32[128,1,128]{0,2,1:T(8,128)S(1)} %slice.208), channel_id=1, source_target_pairs={{16,0},{32,16},{48,32},{64,48},{80,64},{96,80},{112,96},{17,1},{33... | collective-permute-start | bytes 196616 | tf_op jit(solution)/shard_map/ppermute | solution.py:25
  59.9 9.1 %collective-permute-start.6 = (f32[128,19,2]{0,2,1:T(2,128)S(1)}, f32[128,19,2]{0,2,1:T(2,128)S(1)}, u32[]{:S(2)}, u32[]{:S(2)}) collective-permute-start(f32[128,19,2]{0,2,1:T(2,128)S(1)} %pad_maximum_fusion.15), channel_id=1, source_target_pairs={{0,1},{1,2},{2,3},{3,4},{4,5},{5,6},{6,7},{7,8},{8,9},{9,10},{10,1... | collective-permute-start | bytes 58376 | tf_op jit(solution)/shard_map/ppermute | solution.py:22
  63.5 5.6 %collective-permute-start.7 = (f32[128,19,1]{0,2,1:T(1,128)S(1)}, f32[128,19,1]{0,2,1:T(1,128)S(1)}, u32[]{:S(2)}, u32[]{:S(2)}) collective-permute-start(f32[128,19,1]{0,2,1:T(1,128)S(1)} %pad_maximum_fusion.16), channel_id=1, source_target_pairs={{1,0},{2,1},{3,2},{4,3},{5,4},{6,5},{7,6},{8,7},{9,8},{10,9},{11,1... | collective-permute-start | bytes 29192 | tf_op jit(solution)/shard_map/ppermute | solution.py:25
  73.6 4.1 %collective-permute-start.10 = (f32[2,128]{1,0:T(2,128)S(1)}, f32[2,128]{1,0:T(2,128)S(1)}, u32[]{:S(2)}, u32[]{:S(2)}) collective-permute-start(f32[2,128]{1,0:T(2,128)S(1)} %broadcast_in_dim.4), channel_id=1, source_target_pairs={{0,48},{16,0},{32,16},{48,32},{64,112},{80,64},{96,80},{112,96},{1... | collective-permute-start | bytes 3080 | tf_op jit(solution)/shard_map/ppermute | solution.py:42
  79.6 5.2 %collective-permute-start.11 = (f32[2,128]{1,0:T(2,128)S(1)}, f32[2,128]{1,0:T(2,128)S(1)}, u32[]{:S(2)}, u32[]{:S(2)}) collective-permute-start(f32[2,128]{1,0:T(2,128)S(1)} %add_add_fusion.6), channel_id=1, source_target_pairs={{0,64},{16,80},{32,96},{48,112},{64,0},{80,16},{96,32},{112,48},{1... | collective-permute-start | bytes 3080 | tf_op jit(solution)/shard_map/ppermute | solution.py:42
  84.8 8.2 %collective-permute-start.12 = (f32[2,128]{1,0:T(2,128)S(1)}, f32[2,128]{1,0:T(2,128)S(1)}, u32[]{:S(2)}, u32[]{:S(2)}) collective-permute-start(f32[2,128]{1,0:T(2,128)S(1)} %add.237), channel_id=1, source_target_pairs={{0,1},{1,2},{2,3},{3,0},{4,5},{5,6},{6,7},{7,4},{8,9},{9,10},{10,1... | collective-permute-start | bytes 3080 | tf_op jit(solution)/shard_map/ppermute | solution.py:42
  86.3 7.7 %collective-permute-start.13 = (f32[2,128]{1,0:T(2,128)S(1)}, f32[2,128]{1,0:T(2,128)S(1)}, u32[]{:S(2)}, u32[]{:S(2)}) collective-permute-start(f32[2,128]{1,0:T(2,128)S(1)} %add.237), channel_id=1, source_target_pairs={{0,2},{1,3},{2,0},{3,1},{4,6},{5,7},{6,4},{7,5},{8,10},{9,11},{10,... | collective-permute-start | bytes 3080 | tf_op jit(solution)/shard_map/ppermute | solution.py:42
  96.0 8.2 %collective-permute-start.15 = (f32[2,128]{1,0:T(2,128)S(1)}, f32[2,128]{1,0:T(2,128)S(1)}, u32[]{:S(2)}, u32[]{:S(2)}) collective-permute-start(f32[2,128]{1,0:T(2,128)S(1)} %add_add_fusion.5), channel_id=1, source_target_pairs={{0,4},{1,5},{2,6},{3,7},{4,8},{5,9},{6,10},{7,11},{8,12},{9,13},{1... | collective-permute-start | bytes 3080 | tf_op jit(solution)/shard_map/ppermute | solution.py:42
  97.7 6.5 %collective-permute-start.16 = (f32[2,128]{1,0:T(2,128)S(1)}, f32[2,128]{1,0:T(2,128)S(1)}, u32[]{:S(2)}, u32[]{:S(2)}) collective-permute-start(f32[2,128]{1,0:T(2,128)S(1)} %add_add_fusion.5), channel_id=1, source_target_pairs={{0,8},{1,9},{2,10},{3,11},{4,12},{5,13},{6,14},{7,15},{8,0},{9,1},... | collective-permute-start | bytes 3080 | tf_op jit(solution)/shard_map/ppermute | solution.py:42
  99.6 4.6 %collective-permute-start.17 = (f32[2,128]{1,0:T(2,128)S(1)}, f32[2,128]{1,0:T(2,128)S(1)}, u32[]{:S(2)}, u32[]{:S(2)}) collective-permute-start(f32[2,128]{1,0:T(2,128)S(1)} %add_add_fusion.5), channel_id=1, source_target_pairs={{0,12},{1,13},{2,14},{3,15},{4,0},{5,1},{6,2},{7,3},{8,4},{9,5},{1... | collective-permute-start | bytes 3080 | tf_op jit(solution)/shard_map/ppermute | solution.py:42
  107.8 3.6 %collective-permute-start.19 = (f32[4,128]{1,0:T(4,128)S(1)}, f32[4,128]{1,0:T(4,128)S(1)}, u32[]{:S(2)}, u32[]{:S(2)}) collective-permute-start(f32[4,128]{1,0:T(4,128)S(1)} %broadcast_in_dim.5), channel_id=1, source_target_pairs={{0,32},{16,48},{32,0},{48,16},{64,96},{80,112},{96,64},{112,80},{1... | collective-permute-start | bytes 6152 | tf_op jit(solution)/shard_map/ppermute | solution.py:42
  111.9 5.1 %collective-permute-start.21 = (f32[4,128]{1,0:T(4,128)S(1)}, f32[4,128]{1,0:T(4,128)S(1)}, u32[]{:S(2)}, u32[]{:S(2)}) collective-permute-start(f32[4,128]{1,0:T(4,128)S(1)} %add_add_fusion.3), channel_id=1, source_target_pairs={{0,64},{16,80},{32,96},{48,112},{64,0},{80,16},{96,32},{112,48},{1... | collective-permute-start | bytes 6152 | tf_op jit(solution)/shard_map/ppermute | solution.py:42
  116.9 4.8 %collective-permute-start.22 = (f32[4,128]{1,0:T(4,128)S(1)}, f32[4,128]{1,0:T(4,128)S(1)}, u32[]{:S(2)}, u32[]{:S(2)}) collective-permute-start(f32[4,128]{1,0:T(4,128)S(1)} %add.251), channel_id=1, source_target_pairs={{0,1},{1,2},{2,3},{3,0},{4,5},{5,6},{6,7},{7,4},{8,9},{9,10},{10,1... | collective-permute-start | bytes 6152 | tf_op jit(solution)/shard_map/ppermute | solution.py:42
  117.0 5.1 %collective-permute-start.23 = (f32[4,128]{1,0:T(4,128)S(1)}, f32[4,128]{1,0:T(4,128)S(1)}, u32[]{:S(2)}, u32[]{:S(2)}) collective-permute-start(f32[4,128]{1,0:T(4,128)S(1)} %add.251), channel_id=1, source_target_pairs={{0,2},{1,3},{2,0},{3,1},{4,6},{5,7},{6,4},{7,5},{8,10},{9,11},{10,... | collective-permute-start | bytes 6152 | tf_op jit(solution)/shard_map/ppermute | solution.py:42
  119.6 3.6 %collective-permute-start.24 = (f32[4,128]{1,0:T(4,128)S(1)}, f32[4,128]{1,0:T(4,128)S(1)}, u32[]{:S(2)}, u32[]{:S(2)}) collective-permute-start(f32[4,128]{1,0:T(4,128)S(1)} %add.251), channel_id=1, source_target_pairs={{0,3},{1,0},{2,1},{3,2},{4,7},{5,4},{6,5},{7,6},{8,11},{9,8},{10,9... | collective-permute-start | bytes 6152 | tf_op jit(solution)/shard_map/ppermute | solution.py:42
  123.2 5.6 %collective-permute-start.25 = (f32[4,128]{1,0:T(4,128)S(1)}, f32[4,128]{1,0:T(4,128)S(1)}, u32[]{:S(2)}, u32[]{:S(2)}) collective-permute-start(f32[4,128]{1,0:T(4,128)S(1)} %add_add_fusion.2), channel_id=1, source_target_pairs={{0,4},{1,5},{2,6},{3,7},{4,8},{5,9},{6,10},{7,11},{8,12},{9,13},{1... | collective-permute-start | bytes 6152 | tf_op jit(solution)/shard_map/ppermute | solution.py:42
  123.6 5.4 %collective-permute-start.26 = (f32[4,128]{1,0:T(4,128)S(1)}, f32[4,128]{1,0:T(4,128)S(1)}, u32[]{:S(2)}, u32[]{:S(2)}) collective-permute-start(f32[4,128]{1,0:T(4,128)S(1)} %add_add_fusion.2), channel_id=1, source_target_pairs={{0,8},{1,9},{2,10},{3,11},{4,12},{5,13},{6,14},{7,15},{8,0},{9,1},... | collective-permute-start | bytes 6152 | tf_op jit(solution)/shard_map/ppermute | solution.py:42
  127.4 3.6 %collective-permute-start.27 = (f32[4,128]{1,0:T(4,128)S(1)}, f32[4,128]{1,0:T(4,128)S(1)}, u32[]{:S(2)}, u32[]{:S(2)}) collective-permute-start(f32[4,128]{1,0:T(4,128)S(1)} %add_add_fusion.2), channel_id=1, source_target_pairs={{0,12},{1,13},{2,14},{3,15},{4,0},{5,1},{6,2},{7,3},{8,4},{9,5},{1... | collective-permute-start | bytes 6152 | tf_op jit(solution)/shard_map/ppermute | solution.py:42
  (23 other events, 287.5 us)

commit v9 on v7

--- a/solution.py
+++ b/solution.py
@@ -11,8 +11,8 @@
 CORNERS = ((0, 0), (1, 0), (0, 1), (1, 1))
 
 
-def with_halo(shard, before, after):
-    for axis, dim in (("px", 1), ("py", 2)):
+def with_halo(shard, before, after, sides=(("px", 1), ("py", 2))):
+    for axis, dim in sides:
         devices, length = (lax.axis_size(axis), shard.shape[dim])
         up = [(i, i + 1) for i in range(devices - 1)]
         down = [(j, i) for i, j in up]
@@ -106,7 +106,9 @@
     def node_keep(field, offset):
         return field * inside(field.shape[1:], offset, offset, rows, cols, False)[None]
 
-    both = with_halo(jnp.concatenate([displacement, load], axis=0), 3, 3)
+    both = with_halo(jnp.concatenate([displacement, load], axis=0), 3, 3, (("px", 1),))
+    both, arrived = lax.optimization_barrier((both, arrived))
+    both = with_halo(both, 3, 3, (("py", 2),))
     start_shells = gather_shells(both[:6])
     force_wide = scatter_nodes(shell_keep(with_base(start_shells), -3))
     force_start = force_wide[:, 2 : rows + 2, 2 : cols + 2]

time: 135 us -> 138 us (1.022)
  waiting for transfers between devices: 23.5 us -> 33 us
  other arithmetic: 12.5 us -> 9.75 us
  local copies, waits for them, and re-layouts: 20 us -> 18.4 us
    all_to_all x1, waiting for transfers between devices: 0.01 us -> 16.6 us  [shards(): lax.all_to_all(held, ('px', 'py'), split_axis=1, concat_axis=1, tiled=True)]
    ppermute x4, waiting for transfers between devices: 4.49 us -> 0.01 us  [with_halo(): parts.insert(0, lax.ppermute(last, axis, up))]
    ppermute x4, waiting for transfers between devices: 6.11 us -> 3.46 us  [with_halo(): parts.append(lax.ppermute(leading, axis, down))]
    ppermute x20, starting transfers between devices: 34.1 us -> 32.6 us  [all_sum(): total = total + lax.ppermute(value, axis, pairs)]
    unnamed x49 -> x31, local copies, waits for them, and re-layouts: 9.1 us -> 8.3 us
  transfers between devices with their start and end apart: 29 -> 29, of which waited for: 17 -> 16; matrix products, arithmetic and copies ran while one was open for 16% -> 18% of each run, Pallas kernels for 0% -> 0%
where the time goes in v9:
time: 138 us
  starting transfers between devices  62.4 us (45%)
  waiting for transfers between devices  33 us (24%)
  local copies, waits for them, and re-layouts  18.4 us (13%)
  matrix products  13.1 us (9%)
  other arithmetic  9.75 us (7%)
    ppermute x20, starting transfers between devices, all_sum(): total = total + lax.ppermute(value, axis, pairs)  32.6 us
    all_to_all x1, waiting for transfers between devices, shards(): lax.all_to_all(held, ('px', 'py'), split_axis=1, concat_axis=1, tiled=True)  16.6 us
    all_to_all x1, starting transfers between devices, shards(): lax.all_to_all(held, ('px', 'py'), split_axis=1, concat_axis=1, tiled=True)  14.2 us
    ppermute x20, waiting for transfers between devices, all_sum(): total = total + lax.ppermute(value, axis, pairs)  12.9 us
    ppermute x4, starting transfers between devices, with_halo(): parts.insert(0, lax.ppermute(last, axis, up))  10.3 us
    unnamed x31, local copies, waits for them, and re-layouts  8.3 us
    scatter x1, local copies, waits for them, and re-layouts, shards(): contact = contact_home.reshape(hist, cells).at[:, targets].set(arrived.re...  6.8 us
    ppermute x4, starting transfers between devices, with_halo(): parts.append(lax.ppermute(leading, axis, down))  5.34 us
  transfers between devices with their start and end apart: 29, of which 16 were waited for; matrix products, arithmetic and copies ran while one was open for 18% of the time, Pallas kernels for 0%

profile of v9, /device:TPU:0, one launch (start us, length us, event | category | flops | bytes accessed | tf_op | source)
XLA Modules:
  0.0 137.7 jit_solution(6078817847739825746)
XLA Ops:
  7.3 14.2 %all-to-all-start = ((f32[128,128,9]{0,2,1:T(8,128)}), f32[128,128,9]{0,2,1:T(8,128)S(1)}, u32[]{:S(2)}, u32[]{:S(2)}) async-start(f32[128,128,9]{0,2,1:T(8,128)} %reshape.311), calls=%async_computation | async-start | bytes 2097152 | tf_op jit(solution)/shard_map/all_to_all | solution.py:98
  23.8 16.6 %all-to-all-done = f32[128,128,9]{0,2,1:T(8,128)S(1)} async-done(((f32[128,128,9]{0,2,1:T(8,128)}), f32[128,128,9]{0,2,1:T(8,128)S(1)}, u32[]{:S(2)}, u32[]{:S(2)}) %all-to-all-start) | async-done | bytes 589856 | tf_op jit(solution)/shard_map/all_to_all | solution.py:98
  41.2 3.2 %collective-permute-start.2 = (f32[12,22,3]{2,0,1:T(8,128)}, f32[12,22,3]{2,0,1:T(8,128)}, u32[]{:S(2)}, u32[]{:S(2)}) collective-permute-start(f32[12,22,3]{2,0,1:T(8,128)} %get-tuple-element.34), channel_id=1, source_target_pairs={{0,1},{1,2},{2,3},{3,4},{4,5},{5,6},{6,7},{7,8},{8,9},{9,10},{10,1... | collective-permute-start | bytes 9512 | tf_op jit(solution)/shard_map/ppermute | solution.py:22
  46.2 1.6 %copy.34 = f32[128,16,128]{0,2,1:T(8,128)S(1)} copy(f32[128,16,128]{2,1,0:T(8,128)} %param.14) | data formatting | bytes 2097152 | tf_op args[4]
  48.7 6.8 %scatter_custom_fusion = f32[128,2048]{0,1:T(8,128)S(1)} fusion(f32[128,2048]{0,1:T(8,128)S(1)} %bitcast.92, s32[1152]{0:T(1024)S(1)} %fusion.46, f32[128,1152]{0,1:T(8,128)} %reshape.320), kind=kCustom, calls=%fused_computation.30 | custom fusion | bytes 1638400 | tf_op jit(solution)/shard_map/scatter | solution.py:124
  56.9 2.3 %fusion.19 = (f32[128,2048]{0,1:T(8,128)S(1)}, f32[128,2048]{0,1:T(8,128)S(1)}) fusion(f32[128,2048]{0,1:T(8,128)S(1)} %scatter_custom_fusion, f32[128,2048]{0,1:T(8,128)S(1)} %bitcast.91, f32[128,24]{0,1:T(8,128)S(1)} %copy-done, f32[6,21,133]{2,0,1:T(8,128)S(1)} %get-tuple-element.31, f32[6,21,133]{2,0,1:T(8,128)S(1)} %get-tuple-element.32, ...), kind=kOutput, calls=%fused_computation.29 | convolution fusion | flops 77742080 | bytes 4474720 | tf_op jit(solution)/shard_map/dot_general | solution.py:118
  62.9 2.5 %convolution_bitcast_fusion.1 = f32[128,19,131]{0,2,1:T(8,128)S(1)} fusion(f32[6,19,131]{2,0,1:T(8,128)S(1)} %get-tuple-element.37, f32[6,19,131]{2,0,1:T(8,128)S(1)} %get-tuple-element.38, f32[6,19,131]{2,0,1:T(8,128)S(1)} %get-tuple-element.39, f32[6,19,131]{2,0,1:T(8,128)S(1)} %get-tuple-element.36, f32[128,24]{0,1:T(8,128)S(1)} %copy-done), kind=kOutput, calls=%fused_computation.4 | convolution fusion | flops 91933704 | bytes 1525600 | tf_op jit(solution)/shard_map/hb,bxy->hxy/dot_general | solution.py:131
  65.5 4.5 %collective-permute-start.6 = (f32[128,19,2]{0,2,1:T(2,128)S(1)}, f32[128,19,2]{0,2,1:T(2,128)S(1)}, u32[]{:S(2)}, u32[]{:S(2)}) collective-permute-start(f32[128,19,2]{0,2,1:T(2,128)S(1)} %pad_maximum_fusion.15), channel_id=1, source_target_pairs={{0,1},{1,2},{2,3},{3,4},{4,5},{5,6},{6,7},{7,8},{8,9},{9,10},{10,1... | collective-permute-start | bytes 58376 | tf_op jit(solution)/shard_map/ppermute | solution.py:22
  72.2 3.5 %collective-permute-done.7 = f32[128,19,1]{0,2,1:T(1,128)S(1)} collective-permute-done((f32[128,19,1]{0,2,1:T(1,128)S(1)}, f32[128,19,1]{0,2,1:T(1,128)S(1)}, u32[]{:S(2)}, u32[]{:S(2)}) %collective-permute-start.7) | collective-permute-done | bytes 9760 | tf_op jit(solution)/shard_map/ppermute | solution.py:25
  75.6 2.2 %fusion.13 = f32[24,19,131]{2,0,1:T(8,128)S(1)} fusion(f32[19,131,24]{1,2,0:T(8,128)S(1)} %fusion.31, f32[128,19,131]{0,2,1:T(8,128)S(1)} %convolution_bitcast_fusion.1, f32[128,19,1]{0,2,1:T(1,128)S(1)} %collective-permute-done.7, f32[128,1,128]{0,2,1:T(8,128)S(1)} %collective-permute-done.5, f32[128,16,128]{0,2,1:T(8,128)S(1)} %bitcast.88, ...), kind=kOutput, calls=%fused_computation.20 | convolution fusion | flops 93466928 | bytes 3048868 | tf_op jit(solution)/shard_map/hb,hxy->bxy/dot_general | solution.py:132
  80.8 3.5 %collective-permute-start.9 = (f32[2,128]{1,0:T(2,128)S(1)}, f32[2,128]{1,0:T(2,128)S(1)}, u32[]{:S(2)}, u32[]{:S(2)}) collective-permute-start(f32[2,128]{1,0:T(2,128)S(1)} %broadcast_in_dim.4), channel_id=1, source_target_pairs={{0,32},{16,48},{32,0},{48,16},{64,96},{80,112},{96,64},{112,80},{1... | collective-permute-start | bytes 3080 | tf_op jit(solution)/shard_map/ppermute | solution.py:42
  85.9 2.1 %collective-permute-start.11 = (f32[2,128]{1,0:T(2,128)S(1)}, f32[2,128]{1,0:T(2,128)S(1)}, u32[]{:S(2)}, u32[]{:S(2)}) collective-permute-start(f32[2,128]{1,0:T(2,128)S(1)} %add_add_fusion.6), channel_id=1, source_target_pairs={{0,64},{16,80},{32,96},{48,112},{64,0},{80,16},{96,32},{112,48},{1... | collective-permute-start | bytes 3080 | tf_op jit(solution)/shard_map/ppermute | solution.py:42
  88.1 2.2 %convolution_bitcast_fusion.2 = f32[128,17,129]{0,2,1:T(8,128)S(1)} fusion(f32[6,17,129]{2,0,1:T(8,128)S(1)} %get-tuple-element.41, f32[6,17,129]{2,0,1:T(8,128)S(1)} %get-tuple-element.42, f32[6,17,129]{2,0,1:T(8,128)S(1)} %get-tuple-element.43, f32[6,17,129]{2,0,1:T(8,128)S(1)} %get-tuple-element.40, f32[128,24]{0,1:T(8,128)S(1)} %copy-done), kind=kOutput, calls=%fused_computation.5 | convolution fusion | flops 81000648 | bytes 1345632 | tf_op jit(solution)/shard_map/hb,bxy->hxy/dot_general | solution.py:131
  91.0 7.9 %collective-permute-start.13 = (f32[2,128]{1,0:T(2,128)S(1)}, f32[2,128]{1,0:T(2,128)S(1)}, u32[]{:S(2)}, u32[]{:S(2)}) collective-permute-start(f32[2,128]{1,0:T(2,128)S(1)} %add.317), channel_id=1, source_target_pairs={{0,2},{1,3},{2,0},{3,1},{4,6},{5,7},{6,4},{7,5},{8,10},{9,11},{10,... | collective-permute-start | bytes 3080 | tf_op jit(solution)/shard_map/ppermute | solution.py:42
  100.5 2.0 %collective-permute-done.14 = f32[2,128]{1,0:T(2,128)S(1)} collective-permute-done((f32[2,128]{1,0:T(2,128)S(1)}, f32[2,128]{1,0:T(2,128)S(1)}, u32[]{:S(2)}, u32[]{:S(2)}) %collective-permute-start.14) | collective-permute-done | bytes 1056 | tf_op jit(solution)/shard_map/ppermute | solution.py:42
  103.4 2.5 %collective-permute-start.17 = (f32[2,128]{1,0:T(2,128)S(1)}, f32[2,128]{1,0:T(2,128)S(1)}, u32[]{:S(2)}, u32[]{:S(2)}) collective-permute-start(f32[2,128]{1,0:T(2,128)S(1)} %add_add_fusion.5), channel_id=1, source_target_pairs={{0,12},{1,13},{2,14},{3,15},{4,0},{5,1},{6,2},{7,3},{8,4},{9,5},{1... | collective-permute-start | bytes 3080 | tf_op jit(solution)/shard_map/ppermute | solution.py:42
  105.9 2.0 %fusion.15 = f32[24,17,129]{2,0,1:T(8,128)S(1)} fusion(f32[17,129,24]{1,2,0:T(8,128)S(1)} %fusion.32, f32[128,17,129]{0,2,1:T(8,128)S(1)} %convolution_bitcast_fusion.2, f32[128,19,2]{0,2,1:T(2,128)S(1)} %collective-permute-done.6, f32[128,1,128]{0,2,1:T(8,128)S(1)} %collective-permute-done.5, f32[128,16,128]{0,2,1:T(8,128)S(1)} %bitcast.89, ...), kind=kOutput, calls=%fused_computation.23 | convolution fusion | flops 82070832 | bytes 2829572 | tf_op jit(solution)/shard_map/hb,hxy->bxy/dot_general | solution.py:132
  109.0 2.7 %pad_maximum_fusion.19 = f32[4]{0:T(128)S(1)} fusion(f32[1]{0:T(128)} %bitcast.20, f32[1]{0:T(128)} %bitcast.19, f32[1]{0:T(128)} %bitcast.18, f32[1]{0:T(128)} %bitcast.15), kind=kLoop, calls=%fused_computation.108 | loop fusion | flops 12 | bytes 32 | tf_op jit(solution)/shard_map/stack | solution.py:140
  111.7 2.1 %collective-permute-start.19 = (f32[4,128]{1,0:T(4,128)S(1)}, f32[4,128]{1,0:T(4,128)S(1)}, u32[]{:S(2)}, u32[]{:S(2)}) collective-permute-start(f32[4,128]{1,0:T(4,128)S(1)} %broadcast_in_dim.5), channel_id=1, source_target_pairs={{0,32},{16,48},{32,0},{48,16},{64,96},{80,112},{96,64},{112,80},{1... | collective-permute-start | bytes 6152 | tf_op jit(solution)/shard_map/ppermute | solution.py:42
  116.6 2.0 %collective-permute-start.21 = (f32[4,128]{1,0:T(4,128)S(1)}, f32[4,128]{1,0:T(4,128)S(1)}, u32[]{:S(2)}, u32[]{:S(2)}) collective-permute-start(f32[4,128]{1,0:T(4,128)S(1)} %add_add_fusion.3), channel_id=1, source_target_pairs={{0,64},{16,80},{32,96},{48,112},{64,0},{80,16},{96,32},{112,48},{1... | collective-permute-start | bytes 6152 | tf_op jit(solution)/shard_map/ppermute | solution.py:42
  118.6 3.1 %collective-permute-done.21 = f32[4,128]{1,0:T(4,128)S(1)} collective-permute-done((f32[4,128]{1,0:T(4,128)S(1)}, f32[4,128]{1,0:T(4,128)S(1)}, u32[]{:S(2)}, u32[]{:S(2)}) %collective-permute-start.21) | collective-permute-done | bytes 2080 | tf_op jit(solution)/shard_map/ppermute | solution.py:42
  121.7 2.7 %collective-permute-start.23 = (f32[4,128]{1,0:T(4,128)S(1)}, f32[4,128]{1,0:T(4,128)S(1)}, u32[]{:S(2)}, u32[]{:S(2)}) collective-permute-start(f32[4,128]{1,0:T(4,128)S(1)} %add.335), channel_id=1, source_target_pairs={{0,2},{1,3},{2,0},{3,1},{4,6},{5,7},{6,4},{7,5},{8,10},{9,11},{10,... | collective-permute-start | bytes 6152 | tf_op jit(solution)/shard_map/ppermute | solution.py:42
  127.9 2.0 %collective-permute-start.25 = (f32[4,128]{1,0:T(4,128)S(1)}, f32[4,128]{1,0:T(4,128)S(1)}, u32[]{:S(2)}, u32[]{:S(2)}) collective-permute-start(f32[4,128]{1,0:T(4,128)S(1)} %add_add_fusion.2), channel_id=1, source_target_pairs={{0,4},{1,5},{2,6},{3,7},{4,8},{5,9},{6,10},{7,11},{8,12},{9,13},{1... | collective-permute-start | bytes 6152 | tf_op jit(solution)/shard_map/ppermute | solution.py:42
  130.0 2.1 %collective-permute-start.26 = (f32[4,128]{1,0:T(4,128)S(1)}, f32[4,128]{1,0:T(4,128)S(1)}, u32[]{:S(2)}, u32[]{:S(2)}) collective-permute-start(f32[4,128]{1,0:T(4,128)S(1)} %add_add_fusion.2), channel_id=1, source_target_pairs={{0,8},{1,9},{2,10},{3,11},{4,12},{5,13},{6,14},{7,15},{8,0},{9,1},... | collective-permute-start | bytes 6152 | tf_op jit(solution)/shard_map/ppermute | solution.py:42
  (122 shorter events, 40.3 us)
Async XLA Ops:
  2.3 21.5 %collective-permute-start = (f32[12,3,128]{2,0,1:T(8,128)S(1)}, f32[12,3,128]{2,0,1:T(8,128)S(1)}, u32[]{:S(2)}, u32[]{:S(2)}) collective-permute-start(f32[12,3,128]{2,0,1:T(8,128)S(1)} %get-tuple-element.44), channel_id=1, source_target_pairs={{0,16},{16,32},{32,48},{48,64},{64,80},{80,96},{96,112},{1,17},{17... | collective-permute-start | bytes 55304 | tf_op jit(solution)/shard_map/ppermute | solution.py:22
  3.6 20.2 %collective-permute-start.1 = (f32[12,3,128]{2,0,1:T(8,128)S(1)}, f32[12,3,128]{2,0,1:T(8,128)S(1)}, u32[]{:S(2)}, u32[]{:S(2)}) collective-permute-start(f32[12,3,128]{2,0,1:T(8,128)S(1)} %get-tuple-element.45), channel_id=1, source_target_pairs={{16,0},{32,16},{48,32},{64,48},{80,64},{96,80},{112,96},{17,1},{33... | collective-permute-start | bytes 55304 | tf_op jit(solution)/shard_map/ppermute | solution.py:25
  7.3 33.2 %all-to-all-start = ((f32[128,128,9]{0,2,1:T(8,128)}), f32[128,128,9]{0,2,1:T(8,128)S(1)}, u32[]{:S(2)}, u32[]{:S(2)}) async-start(f32[128,128,9]{0,2,1:T(8,128)} %reshape.311), calls=%async_computation | async-start | bytes 2097152 | tf_op jit(solution)/shard_map/all_to_all | solution.py:98
  41.2 14.3 %collective-permute-start.2 = (f32[12,22,3]{2,0,1:T(8,128)}, f32[12,22,3]{2,0,1:T(8,128)}, u32[]{:S(2)}, u32[]{:S(2)}) collective-permute-start(f32[12,22,3]{2,0,1:T(8,128)} %get-tuple-element.34), channel_id=1, source_target_pairs={{0,1},{1,2},{2,3},{3,4},{4,5},{5,6},{6,7},{7,8},{8,9},{9,10},{10,1... | collective-permute-start | bytes 9512 | tf_op jit(solution)/shard_map/ppermute | solution.py:22
  44.4 11.1 %collective-permute-start.3 = (f32[12,22,3]{2,0,1:T(8,128)}, f32[12,22,3]{2,0,1:T(8,128)}, u32[]{:S(2)}, u32[]{:S(2)}) collective-permute-start(f32[12,22,3]{2,0,1:T(8,128)} %get-tuple-element.35), channel_id=1, source_target_pairs={{1,0},{2,1},{3,2},{4,3},{5,4},{6,5},{7,6},{8,7},{9,8},{10,9},{11,1... | collective-permute-start | bytes 9512 | tf_op jit(solution)/shard_map/ppermute | solution.py:25
  59.3 6.2 %collective-permute-start.4 = (f32[128,2,128]{0,2,1:T(8,128)S(1)}, f32[128,2,128]{0,2,1:T(8,128)S(1)}, u32[]{:S(2)}, u32[]{:S(2)}) collective-permute-start(f32[128,2,128]{0,2,1:T(8,128)S(1)} %slice.193), channel_id=1, source_target_pairs={{0,16},{16,32},{32,48},{48,64},{64,80},{80,96},{96,112},{1,17},{17... | collective-permute-start | bytes 393224 | tf_op jit(solution)/shard_map/ppermute | solution.py:22
  60.6 4.9 %collective-permute-start.5 = (f32[128,1,128]{0,2,1:T(8,128)S(1)}, f32[128,1,128]{0,2,1:T(8,128)S(1)}, u32[]{:S(2)}, u32[]{:S(2)}) collective-permute-start(f32[128,1,128]{0,2,1:T(8,128)S(1)} %slice.194), channel_id=1, source_target_pairs={{16,0},{32,16},{48,32},{64,48},{80,64},{96,80},{112,96},{17,1},{33... | collective-permute-start | bytes 196616 | tf_op jit(solution)/shard_map/ppermute | solution.py:25
  65.5 10.1 %collective-permute-start.6 = (f32[128,19,2]{0,2,1:T(2,128)S(1)}, f32[128,19,2]{0,2,1:T(2,128)S(1)}, u32[]{:S(2)}, u32[]{:S(2)}) collective-permute-start(f32[128,19,2]{0,2,1:T(2,128)S(1)} %pad_maximum_fusion.15), channel_id=1, source_target_pairs={{0,1},{1,2},{2,3},{3,4},{4,5},{5,6},{6,7},{7,8},{8,9},{9,10},{10,1... | collective-permute-start | bytes 58376 | tf_op jit(solution)/shard_map/ppermute | solution.py:22
  70.0 5.6 %collective-permute-start.7 = (f32[128,19,1]{0,2,1:T(1,128)S(1)}, f32[128,19,1]{0,2,1:T(1,128)S(1)}, u32[]{:S(2)}, u32[]{:S(2)}) collective-permute-start(f32[128,19,1]{0,2,1:T(1,128)S(1)} %pad_maximum_fusion.16), channel_id=1, source_target_pairs={{1,0},{2,1},{3,2},{4,3},{5,4},{6,5},{7,6},{8,7},{9,8},{10,9},{11,1... | collective-permute-start | bytes 29192 | tf_op jit(solution)/shard_map/ppermute | solution.py:25
  80.1 4.3 %collective-permute-start.10 = (f32[2,128]{1,0:T(2,128)S(1)}, f32[2,128]{1,0:T(2,128)S(1)}, u32[]{:S(2)}, u32[]{:S(2)}) collective-permute-start(f32[2,128]{1,0:T(2,128)S(1)} %broadcast_in_dim.4), channel_id=1, source_target_pairs={{0,48},{16,0},{32,16},{48,32},{64,112},{80,64},{96,80},{112,96},{1... | collective-permute-start | bytes 3080 | tf_op jit(solution)/shard_map/ppermute | solution.py:42
  80.7 4.4 %collective-permute-start.8 = (f32[2,128]{1,0:T(2,128)S(1)}, f32[2,128]{1,0:T(2,128)S(1)}, u32[]{:S(2)}, u32[]{:S(2)}) collective-permute-start(f32[2,128]{1,0:T(2,128)S(1)} %broadcast_in_dim.4), channel_id=1, source_target_pairs={{0,16},{16,32},{32,48},{48,0},{64,80},{80,96},{96,112},{112,64},{1... | collective-permute-start | bytes 3080 | tf_op jit(solution)/shard_map/ppermute | solution.py:42
  80.8 5.0 %collective-permute-start.9 = (f32[2,128]{1,0:T(2,128)S(1)}, f32[2,128]{1,0:T(2,128)S(1)}, u32[]{:S(2)}, u32[]{:S(2)}) collective-permute-start(f32[2,128]{1,0:T(2,128)S(1)} %broadcast_in_dim.4), channel_id=1, source_target_pairs={{0,32},{16,48},{32,0},{48,16},{64,96},{80,112},{96,64},{112,80},{1... | collective-permute-start | bytes 3080 | tf_op jit(solution)/shard_map/ppermute | solution.py:42
  85.9 5.1 %collective-permute-start.11 = (f32[2,128]{1,0:T(2,128)S(1)}, f32[2,128]{1,0:T(2,128)S(1)}, u32[]{:S(2)}, u32[]{:S(2)}) collective-permute-start(f32[2,128]{1,0:T(2,128)S(1)} %add_add_fusion.6), channel_id=1, source_target_pairs={{0,64},{16,80},{32,96},{48,112},{64,0},{80,16},{96,32},{112,48},{1... | collective-permute-start | bytes 3080 | tf_op jit(solution)/shard_map/ppermute | solution.py:42
  91.0 8.5 %collective-permute-start.12 = (f32[2,128]{1,0:T(2,128)S(1)}, f32[2,128]{1,0:T(2,128)S(1)}, u32[]{:S(2)}, u32[]{:S(2)}) collective-permute-start(f32[2,128]{1,0:T(2,128)S(1)} %add.317), channel_id=1, source_target_pairs={{0,1},{1,2},{2,3},{3,0},{4,5},{5,6},{6,7},{7,4},{8,9},{9,10},{10,1... | collective-permute-start | bytes 3080 | tf_op jit(solution)/shard_map/ppermute | solution.py:42
  91.0 9.5 %collective-permute-start.13 = (f32[2,128]{1,0:T(2,128)S(1)}, f32[2,128]{1,0:T(2,128)S(1)}, u32[]{:S(2)}, u32[]{:S(2)}) collective-permute-start(f32[2,128]{1,0:T(2,128)S(1)} %add.317), channel_id=1, source_target_pairs={{0,2},{1,3},{2,0},{3,1},{4,6},{5,7},{6,4},{7,5},{8,10},{9,11},{10,... | collective-permute-start | bytes 3080 | tf_op jit(solution)/shard_map/ppermute | solution.py:42
  102.5 5.4 %collective-permute-start.15 = (f32[2,128]{1,0:T(2,128)S(1)}, f32[2,128]{1,0:T(2,128)S(1)}, u32[]{:S(2)}, u32[]{:S(2)}) collective-permute-start(f32[2,128]{1,0:T(2,128)S(1)} %add_add_fusion.5), channel_id=1, source_target_pairs={{0,4},{1,5},{2,6},{3,7},{4,8},{5,9},{6,10},{7,11},{8,12},{9,13},{1... | collective-permute-start | bytes 3080 | tf_op jit(solution)/shard_map/ppermute | solution.py:42
  102.7 5.2 %collective-permute-start.16 = (f32[2,128]{1,0:T(2,128)S(1)}, f32[2,128]{1,0:T(2,128)S(1)}, u32[]{:S(2)}, u32[]{:S(2)}) collective-permute-start(f32[2,128]{1,0:T(2,128)S(1)} %add_add_fusion.5), channel_id=1, source_target_pairs={{0,8},{1,9},{2,10},{3,11},{4,12},{5,13},{6,14},{7,15},{8,0},{9,1},... | collective-permute-start | bytes 3080 | tf_op jit(solution)/shard_map/ppermute | solution.py:42
  103.4 4.8 %collective-permute-start.17 = (f32[2,128]{1,0:T(2,128)S(1)}, f32[2,128]{1,0:T(2,128)S(1)}, u32[]{:S(2)}, u32[]{:S(2)}) collective-permute-start(f32[2,128]{1,0:T(2,128)S(1)} %add_add_fusion.5), channel_id=1, source_target_pairs={{0,12},{1,13},{2,14},{3,15},{4,0},{5,1},{6,2},{7,3},{8,4},{9,5},{1... | collective-permute-start | bytes 3080 | tf_op jit(solution)/shard_map/ppermute | solution.py:42
  111.7 3.6 %collective-permute-start.19 = (f32[4,128]{1,0:T(4,128)S(1)}, f32[4,128]{1,0:T(4,128)S(1)}, u32[]{:S(2)}, u32[]{:S(2)}) collective-permute-start(f32[4,128]{1,0:T(4,128)S(1)} %broadcast_in_dim.5), channel_id=1, source_target_pairs={{0,32},{16,48},{32,0},{48,16},{64,96},{80,112},{96,64},{112,80},{1... | collective-permute-start | bytes 6152 | tf_op jit(solution)/shard_map/ppermute | solution.py:42
  116.6 5.1 %collective-permute-start.21 = (f32[4,128]{1,0:T(4,128)S(1)}, f32[4,128]{1,0:T(4,128)S(1)}, u32[]{:S(2)}, u32[]{:S(2)}) collective-permute-start(f32[4,128]{1,0:T(4,128)S(1)} %add_add_fusion.3), channel_id=1, source_target_pairs={{0,64},{16,80},{32,96},{48,112},{64,0},{80,16},{96,32},{112,48},{1... | collective-permute-start | bytes 6152 | tf_op jit(solution)/shard_map/ppermute | solution.py:42
  121.7 4.8 %collective-permute-start.22 = (f32[4,128]{1,0:T(4,128)S(1)}, f32[4,128]{1,0:T(4,128)S(1)}, u32[]{:S(2)}, u32[]{:S(2)}) collective-permute-start(f32[4,128]{1,0:T(4,128)S(1)} %add.335), channel_id=1, source_target_pairs={{0,1},{1,2},{2,3},{3,0},{4,5},{5,6},{6,7},{7,4},{8,9},{9,10},{10,1... | collective-permute-start | bytes 6152 | tf_op jit(solution)/shard_map/ppermute | solution.py:42
  121.7 5.1 %collective-permute-start.23 = (f32[4,128]{1,0:T(4,128)S(1)}, f32[4,128]{1,0:T(4,128)S(1)}, u32[]{:S(2)}, u32[]{:S(2)}) collective-permute-start(f32[4,128]{1,0:T(4,128)S(1)} %add.335), channel_id=1, source_target_pairs={{0,2},{1,3},{2,0},{3,1},{4,6},{5,7},{6,4},{7,5},{8,10},{9,11},{10,... | collective-permute-start | bytes 6152 | tf_op jit(solution)/shard_map/ppermute | solution.py:42
  127.9 6.6 %collective-permute-start.25 = (f32[4,128]{1,0:T(4,128)S(1)}, f32[4,128]{1,0:T(4,128)S(1)}, u32[]{:S(2)}, u32[]{:S(2)}) collective-permute-start(f32[4,128]{1,0:T(4,128)S(1)} %add_add_fusion.2), channel_id=1, source_target_pairs={{0,4},{1,5},{2,6},{3,7},{4,8},{5,9},{6,10},{7,11},{8,12},{9,13},{1... | collective-permute-start | bytes 6152 | tf_op jit(solution)/shard_map/ppermute | solution.py:42
  130.0 5.1 %collective-permute-start.26 = (f32[4,128]{1,0:T(4,128)S(1)}, f32[4,128]{1,0:T(4,128)S(1)}, u32[]{:S(2)}, u32[]{:S(2)}) collective-permute-start(f32[4,128]{1,0:T(4,128)S(1)} %add_add_fusion.2), channel_id=1, source_target_pairs={{0,8},{1,9},{2,10},{3,11},{4,12},{5,13},{6,14},{7,15},{8,0},{9,1},... | collective-permute-start | bytes 6152 | tf_op jit(solution)/shard_map/ppermute | solution.py:42
  (16 other events, 279.2 us)

commit v10 on v7

--- a/solution.py
+++ b/solution.py
@@ -94,8 +94,9 @@
     targets = slot_table.reshape(-1)
     devices = lax.axis_size("px") * lax.axis_size("py")
     width = targets.shape[0] // devices
-    held = recv_contact.reshape(hist, devices, width)
-    arrived = lax.all_to_all(held, ("px", "py"), split_axis=1, concat_axis=1, tiled=True)
+    held = recv_contact.reshape(hist, devices, width).transpose(1, 2, 0).reshape(devices, -1)
+    arrived = lax.all_to_all(held, ("px", "py"), split_axis=0, concat_axis=0, tiled=True)
+    arrived = arrived.reshape(devices * width, hist).T
 
     def with_base(shells):
         return jnp.einsum("ab,bxy->axy", stiff_base, shells, precision=HIGH)
@@ -119,7 +120,7 @@
     contact = (
         contact_home.reshape(hist, cells)
         .at[:, targets]
-        .set(arrived.reshape(hist, devices * width), mode="drop")
+        .set(arrived, mode="drop")
     )
     weights = (jax.nn.softplus(history_new) * contact).reshape(hist, rows, cols)
     weights_wide = with_halo(weights, 2, 1)

time: 135 us -> 134 us (level)
    ppermute x4, waiting for transfers between devices: 4.49 us -> 0.97 us  [with_halo(): parts.insert(0, lax.ppermute(last, axis, up))]
    ppermute x4, waiting for transfers between devices: 6.11 us -> 8.56 us  [with_halo(): parts.append(lax.ppermute(leading, axis, down))]
    reshape x2 -> x1, local copies, waits for them, and re-layouts: 1.93 us -> 0.07 us  [shards(): recv_contact.reshape(hist, devices, width).transpose(1, 2, 0)]
  transfers between devices with their start and end apart: 29 -> 29, of which waited for: 17 -> 16; matrix products, arithmetic and copies ran while one was open for 16% -> 17% of each run, Pallas kernels for 0% -> 0%
where the time goes in v10:
time: 134 us; the launch traced here: 133 us
  starting transfers between devices  62.4 us (47%)
  waiting for transfers between devices  23 us (17%)
  local copies, waits for them, and re-layouts  19.7 us (15%)
  matrix products  14.2 us (11%)
  other arithmetic  12.5 us (9%)
    ppermute x20, starting transfers between devices, all_sum(): total = total + lax.ppermute(value, axis, pairs)  33.7 us
    all_to_all x1, starting transfers between devices, shards(): lax.all_to_all(held, ('px', 'py'), split_axis=0, concat_axis=0, tiled=True)  14.6 us
    ppermute x20, waiting for transfers between devices, all_sum(): total = total + lax.ppermute(value, axis, pairs)  13.5 us
    unnamed x49, local copies, waits for them, and re-layouts  9.15 us
    ppermute x4, starting transfers between devices, with_halo(): parts.insert(0, lax.ppermute(last, axis, up))  8.76 us
    ppermute x4, waiting for transfers between devices, with_halo(): parts.append(lax.ppermute(leading, axis, down))  8.56 us
    scatter x1, local copies, waits for them, and re-layouts, shards(): contact = contact_home.reshape(hist, cells).at[:, targets].set(arrived, m...  6.76 us
    ppermute x4, starting transfers between devices, with_halo(): parts.append(lax.ppermute(leading, axis, down))  5.35 us
  transfers between devices with their start and end apart: 29, of which 16 were waited for; matrix products, arithmetic and copies ran while one was open for 17% of the time, Pallas kernels for 0%

profile of v10, /device:TPU:0, one launch (start us, length us, event | category | flops | bytes accessed | tf_op | source)
XLA Modules:
  0.0 133.0 jit_solution(3059433603133016354)
XLA Ops:
  7.8 14.6 %all-to-all-start = ((f32[128,1,1152]{2,1,0:T(1,128)}), f32[128,1,1152]{2,1,0:T(1,128)}, u32[]{:S(2)}, u32[]{:S(2)}) async-start(f32[128,1,1152]{2,1,0:T(1,128)} %copy.68), calls=%async_computation | async-start | bytes 1179648 | tf_op jit(solution)/shard_map/all_to_all | solution.py:98
  26.9 2.8 %collective-permute-start.2 = (f32[12,22,3]{2,0,1:T(8,128)}, f32[12,22,3]{2,0,1:T(8,128)S(1)}, u32[]{:S(2)}, u32[]{:S(2)}) collective-permute-start(f32[12,22,3]{2,0,1:T(8,128)} %get-tuple-element.38), channel_id=1, source_target_pairs={{0,1},{1,2},{2,3},{3,4},{4,5},{5,6},{6,7},{7,8},{8,9},{9,10},{10,1... | collective-permute-start | bytes 9512 | tf_op jit(solution)/shard_map/ppermute | solution.py:22
  34.0 4.1 %collective-permute-done.3 = f32[12,22,3]{2,0,1:T(8,128)} collective-permute-done((f32[12,22,3]{2,0,1:T(8,128)}, f32[12,22,3]{2,0,1:T(8,128)}, u32[]{:S(2)}, u32[]{:S(2)}) %collective-permute-start.3) | collective-permute-done | bytes 3200 | tf_op jit(solution)/shard_map/ppermute | solution.py:25
  42.8 6.8 %scatter_fusion = f32[128,2048]{0,1:T(8,128)S(1)} fusion(f32[128,2048]{0,1:T(8,128)S(1)} %bitcast.82, s32[1152]{0:T(1024)S(1)} %fusion.44, f32[1152,128]{1,0:T(8,128)} %bitcast.9), kind=kCustom, calls=%fused_computation | custom fusion | bytes 1774080 | tf_op jit(solution)/shard_map/scatter | solution.py:123
  49.6 3.4 %fusion.19 = (f32[128,2048]{0,1:T(8,128)S(1)}, f32[128,2048]{0,1:T(8,128)S(1)}) fusion(f32[128,2048]{0,1:T(8,128)S(1)} %scatter_fusion, f32[128,2048]{0,1:T(8,128)S(1)} %bitcast.91, f32[128,24]{0,1:T(8,128)S(1)} %copy-done, f32[6,21,133]{2,0,1:T(8,128)} %copy-done.1, f32[6,21,133]{2,0,1:T(8,128)} %copy-done.2, f32[6,21,133]{2,0,1:T(8,128)} %copy-done.3, ...), kind=kOutput, calls=%fused_computation.29 | convolution fusion | flops 77742080 | bytes 4474720 | tf_op jit(solution)/shard_map/dot_general | solution.py:117
  55.7 2.5 %convolution_bitcast_fusion.1 = f32[128,19,131]{0,2,1:T(8,128)S(1)} fusion(f32[6,19,131]{2,0,1:T(8,128)S(1)} %copy-done.5, f32[6,19,131]{2,0,1:T(8,128)S(1)} %copy-done.6, f32[6,19,131]{2,0,1:T(8,128)S(1)} %copy-done.7, f32[6,19,131]{2,0,1:T(8,128)S(1)} %copy-done.4, f32[128,24]{0,1:T(8,128)S(1)} %copy-done), kind=kOutput, calls=%fused_computation.4 | convolution fusion | flops 91933704 | bytes 1525600 | tf_op jit(solution)/shard_map/hb,bxy->hxy/dot_general | solution.py:130
  59.2 3.4 %collective-permute-start.6 = (f32[128,19,2]{0,2,1:T(2,128)S(1)}, f32[128,19,2]{0,2,1:T(2,128)S(1)}, u32[]{:S(2)}, u32[]{:S(2)}) collective-permute-start(f32[128,19,2]{0,2,1:T(2,128)S(1)} %pad_maximum_fusion.15), channel_id=1, source_target_pairs={{0,1},{1,2},{2,3},{3,4},{4,5},{5,6},{6,7},{7,8},{8,9},{9,10},{10,1... | collective-permute-start | bytes 58376 | tf_op jit(solution)/shard_map/ppermute | solution.py:22
  64.7 3.5 %collective-permute-done.7 = f32[128,19,1]{0,2,1:T(1,128)S(1)} collective-permute-done((f32[128,19,1]{0,2,1:T(1,128)S(1)}, f32[128,19,1]{0,2,1:T(1,128)S(1)}, u32[]{:S(2)}, u32[]{:S(2)}) %collective-permute-start.7) | collective-permute-done | bytes 9760 | tf_op jit(solution)/shard_map/ppermute | solution.py:25
  68.2 2.2 %fusion.13 = f32[24,19,131]{2,0,1:T(8,128)S(1)} fusion(f32[19,131,24]{1,2,0:T(8,128)S(1)} %fusion.29, f32[128,19,131]{0,2,1:T(8,128)S(1)} %convolution_bitcast_fusion.1, f32[128,19,1]{0,2,1:T(1,128)S(1)} %collective-permute-done.7, f32[128,1,128]{0,2,1:T(8,128)S(1)} %collective-permute-done.5, f32[128,16,128]{0,2,1:T(8,128)S(1)} %bitcast.87, ...), kind=kOutput, calls=%fused_computation.20 | convolution fusion | flops 93466928 | bytes 3048868 | tf_op jit(solution)/shard_map/hb,hxy->bxy/dot_general | solution.py:131
  72.7 2.6 %collective-permute-start.10 = (f32[2,128]{1,0:T(2,128)S(1)}, f32[2,128]{1,0:T(2,128)S(1)}, u32[]{:S(2)}, u32[]{:S(2)}) collective-permute-start(f32[2,128]{1,0:T(2,128)S(1)} %broadcast_in_dim.4), channel_id=1, source_target_pairs={{0,48},{16,0},{32,16},{48,32},{64,112},{80,64},{96,80},{112,96},{1... | collective-permute-start | bytes 3080 | tf_op jit(solution)/shard_map/ppermute | solution.py:42
  78.9 2.9 %collective-permute-start.11 = (f32[2,128]{1,0:T(2,128)S(1)}, f32[2,128]{1,0:T(2,128)S(1)}, u32[]{:S(2)}, u32[]{:S(2)}) collective-permute-start(f32[2,128]{1,0:T(2,128)S(1)} %add_add_fusion.6), channel_id=1, source_target_pairs={{0,64},{16,80},{32,96},{48,112},{64,0},{80,16},{96,32},{112,48},{1... | collective-permute-start | bytes 3080 | tf_op jit(solution)/shard_map/ppermute | solution.py:42
  81.9 2.2 %convolution_bitcast_fusion.2 = f32[128,17,129]{0,2,1:T(8,128)S(1)} fusion(f32[6,17,129]{2,0,1:T(8,128)S(1)} %get-tuple-element.45, f32[6,17,129]{2,0,1:T(8,128)S(1)} %get-tuple-element.46, f32[6,17,129]{2,0,1:T(8,128)S(1)} %get-tuple-element.47, f32[6,17,129]{2,0,1:T(8,128)S(1)} %get-tuple-element.44, f32[128,24]{0,1:T(8,128)S(1)} %copy-done), kind=kOutput, calls=%fused_computation.5 | convolution fusion | flops 81000648 | bytes 1345632 | tf_op jit(solution)/shard_map/hb,bxy->hxy/dot_general | solution.py:130
  84.1 3.4 %collective-permute-start.12 = (f32[2,128]{1,0:T(2,128)S(1)}, f32[2,128]{1,0:T(2,128)S(1)}, u32[]{:S(2)}, u32[]{:S(2)}) collective-permute-start(f32[2,128]{1,0:T(2,128)S(1)} %add.317), channel_id=1, source_target_pairs={{0,1},{1,2},{2,3},{3,0},{4,5},{5,6},{6,7},{7,4},{8,9},{9,10},{10,1... | collective-permute-start | bytes 3080 | tf_op jit(solution)/shard_map/ppermute | solution.py:42
  87.5 4.2 %collective-permute-start.13 = (f32[2,128]{1,0:T(2,128)S(1)}, f32[2,128]{1,0:T(2,128)S(1)}, u32[]{:S(2)}, u32[]{:S(2)}) collective-permute-start(f32[2,128]{1,0:T(2,128)S(1)} %add.317), channel_id=1, source_target_pairs={{0,2},{1,3},{2,0},{3,1},{4,6},{5,7},{6,4},{7,5},{8,10},{9,11},{10,... | collective-permute-start | bytes 3080 | tf_op jit(solution)/shard_map/ppermute | solution.py:42
  93.3 2.0 %collective-permute-done.14 = f32[2,128]{1,0:T(2,128)S(1)} collective-permute-done((f32[2,128]{1,0:T(2,128)S(1)}, f32[2,128]{1,0:T(2,128)S(1)}, u32[]{:S(2)}, u32[]{:S(2)}) %collective-permute-start.14) | collective-permute-done | bytes 1056 | tf_op jit(solution)/shard_map/ppermute | solution.py:42
  95.3 1.7 %collective-permute-start.15 = (f32[2,128]{1,0:T(2,128)S(1)}, f32[2,128]{1,0:T(2,128)S(1)}, u32[]{:S(2)}, u32[]{:S(2)}) collective-permute-start(f32[2,128]{1,0:T(2,128)S(1)} %add_add_fusion.5), channel_id=1, source_target_pairs={{0,4},{1,5},{2,6},{3,7},{4,8},{5,9},{6,10},{7,11},{8,12},{9,13},{1... | collective-permute-start | bytes 3080 | tf_op jit(solution)/shard_map/ppermute | solution.py:42
  98.6 2.5 %collective-permute-start.17 = (f32[2,128]{1,0:T(2,128)S(1)}, f32[2,128]{1,0:T(2,128)S(1)}, u32[]{:S(2)}, u32[]{:S(2)}) collective-permute-start(f32[2,128]{1,0:T(2,128)S(1)} %add_add_fusion.5), channel_id=1, source_target_pairs={{0,12},{1,13},{2,14},{3,15},{4,0},{5,1},{6,2},{7,3},{8,4},{9,5},{1... | collective-permute-start | bytes 3080 | tf_op jit(solution)/shard_map/ppermute | solution.py:42
  101.1 2.0 %fusion.15 = f32[24,17,129]{2,0,1:T(8,128)S(1)} fusion(f32[17,129,24]{1,2,0:T(8,128)S(1)} %fusion.30, f32[128,17,129]{0,2,1:T(8,128)S(1)} %convolution_bitcast_fusion.2, f32[128,19,2]{0,2,1:T(2,128)S(1)} %collective-permute-done.6, f32[128,1,128]{0,2,1:T(8,128)S(1)} %collective-permute-done.5, f32[128,16,128]{0,2,1:T(8,128)S(1)} %bitcast.88, ...), kind=kOutput, calls=%fused_computation.23 | convolution fusion | flops 82070832 | bytes 2829572 | tf_op jit(solution)/shard_map/hb,hxy->bxy/dot_general | solution.py:131
  104.0 2.7 %pad_maximum_fusion.19 = f32[4]{0:T(128)S(1)} fusion(f32[1]{0:T(128)} %bitcast.22, f32[1]{0:T(128)} %bitcast.21, f32[1]{0:T(128)} %bitcast.20, f32[1]{0:T(128)} %bitcast.17), kind=kLoop, calls=%fused_computation.106 | loop fusion | flops 12 | bytes 32 | tf_op jit(solution)/shard_map/stack | solution.py:139
  110.4 2.6 %collective-permute-start.21 = (f32[4,128]{1,0:T(4,128)S(1)}, f32[4,128]{1,0:T(4,128)S(1)}, u32[]{:S(2)}, u32[]{:S(2)}) collective-permute-start(f32[4,128]{1,0:T(4,128)S(1)} %add_add_fusion.3), channel_id=1, source_target_pairs={{0,64},{16,80},{32,96},{48,112},{64,0},{80,16},{96,32},{112,48},{1... | collective-permute-start | bytes 6152 | tf_op jit(solution)/shard_map/ppermute | solution.py:42
  113.0 2.5 %collective-permute-done.21 = f32[4,128]{1,0:T(4,128)S(1)} collective-permute-done((f32[4,128]{1,0:T(4,128)S(1)}, f32[4,128]{1,0:T(4,128)S(1)}, u32[]{:S(2)}, u32[]{:S(2)}) %collective-permute-start.21) | collective-permute-done | bytes 2080 | tf_op jit(solution)/shard_map/ppermute | solution.py:42
  115.6 3.1 %collective-permute-start.23 = (f32[4,128]{1,0:T(4,128)S(1)}, f32[4,128]{1,0:T(4,128)S(1)}, u32[]{:S(2)}, u32[]{:S(2)}) collective-permute-start(f32[4,128]{1,0:T(4,128)S(1)} %add.335), channel_id=1, source_target_pairs={{0,2},{1,3},{2,0},{3,1},{4,6},{5,7},{6,4},{7,5},{8,10},{9,11},{10,... | collective-permute-start | bytes 6152 | tf_op jit(solution)/shard_map/ppermute | solution.py:42
  122.6 3.8 %collective-permute-start.26 = (f32[4,128]{1,0:T(4,128)S(1)}, f32[4,128]{1,0:T(4,128)S(1)}, u32[]{:S(2)}, u32[]{:S(2)}) collective-permute-start(f32[4,128]{1,0:T(4,128)S(1)} %add_add_fusion.2), channel_id=1, source_target_pairs={{0,8},{1,9},{2,10},{3,11},{4,12},{5,13},{6,14},{7,15},{8,0},{9,1},... | collective-permute-start | bytes 6152 | tf_op jit(solution)/shard_map/ppermute | solution.py:42
  128.0 2.0 %collective-permute-done.27 = f32[4,128]{1,0:T(4,128)S(1)} collective-permute-done((f32[4,128]{1,0:T(4,128)S(1)}, f32[4,128]{1,0:T(4,128)S(1)}, u32[]{:S(2)}, u32[]{:S(2)}) %collective-permute-start.27) | collective-permute-done | bytes 2080 | tf_op jit(solution)/shard_map/ppermute | solution.py:42
  (141 shorter events, 48.2 us)
Async XLA Ops:
  2.3 23.7 %collective-permute-start = (f32[12,3,128]{2,0,1:T(8,128)S(1)}, f32[12,3,128]{2,0,1:T(8,128)S(1)}, u32[]{:S(2)}, u32[]{:S(2)}) collective-permute-start(f32[12,3,128]{2,0,1:T(8,128)S(1)} %get-tuple-element.48), channel_id=1, source_target_pairs={{0,16},{16,32},{32,48},{48,64},{64,80},{80,96},{96,112},{1,17},{17... | collective-permute-start | bytes 55304 | tf_op jit(solution)/shard_map/ppermute | solution.py:22
  3.6 22.4 %collective-permute-start.1 = (f32[12,3,128]{2,0,1:T(8,128)S(1)}, f32[12,3,128]{2,0,1:T(8,128)S(1)}, u32[]{:S(2)}, u32[]{:S(2)}) collective-permute-start(f32[12,3,128]{2,0,1:T(8,128)S(1)} %get-tuple-element.49), channel_id=1, source_target_pairs={{16,0},{32,16},{48,32},{64,48},{80,64},{96,80},{112,96},{17,1},{33... | collective-permute-start | bytes 55304 | tf_op jit(solution)/shard_map/ppermute | solution.py:25
  7.8 35.0 %all-to-all-start = ((f32[128,1,1152]{2,1,0:T(1,128)}), f32[128,1,1152]{2,1,0:T(1,128)}, u32[]{:S(2)}, u32[]{:S(2)}) async-start(f32[128,1,1152]{2,1,0:T(1,128)} %copy.68), calls=%async_computation | async-start | bytes 1179648 | tf_op jit(solution)/shard_map/all_to_all | solution.py:98
  26.9 7.2 %collective-permute-start.2 = (f32[12,22,3]{2,0,1:T(8,128)}, f32[12,22,3]{2,0,1:T(8,128)S(1)}, u32[]{:S(2)}, u32[]{:S(2)}) collective-permute-start(f32[12,22,3]{2,0,1:T(8,128)} %get-tuple-element.38), channel_id=1, source_target_pairs={{0,1},{1,2},{2,3},{3,4},{4,5},{5,6},{6,7},{7,8},{8,9},{9,10},{10,1... | collective-permute-start | bytes 9512 | tf_op jit(solution)/shard_map/ppermute | solution.py:22
  29.7 8.5 %collective-permute-start.3 = (f32[12,22,3]{2,0,1:T(8,128)}, f32[12,22,3]{2,0,1:T(8,128)}, u32[]{:S(2)}, u32[]{:S(2)}) collective-permute-start(f32[12,22,3]{2,0,1:T(8,128)} %get-tuple-element.39), channel_id=1, source_target_pairs={{1,0},{2,1},{3,2},{4,3},{5,4},{6,5},{7,6},{8,7},{9,8},{10,9},{11,1... | collective-permute-start | bytes 9512 | tf_op jit(solution)/shard_map/ppermute | solution.py:25
  53.0 6.1 %collective-permute-start.4 = (f32[128,2,128]{0,2,1:T(8,128)S(1)}, f32[128,2,128]{0,2,1:T(8,128)S(1)}, u32[]{:S(2)}, u32[]{:S(2)}) collective-permute-start(f32[128,2,128]{0,2,1:T(8,128)S(1)} %slice.195), channel_id=1, source_target_pairs={{0,16},{16,32},{32,48},{48,64},{64,80},{80,96},{96,112},{1,17},{17... | collective-permute-start | bytes 393224 | tf_op jit(solution)/shard_map/ppermute | solution.py:22
  54.3 4.8 %collective-permute-start.5 = (f32[128,1,128]{0,2,1:T(8,128)S(1)}, f32[128,1,128]{0,2,1:T(8,128)S(1)}, u32[]{:S(2)}, u32[]{:S(2)}) collective-permute-start(f32[128,1,128]{0,2,1:T(8,128)S(1)} %slice.196), channel_id=1, source_target_pairs={{16,0},{32,16},{48,32},{64,48},{80,64},{96,80},{112,96},{17,1},{33... | collective-permute-start | bytes 196616 | tf_op jit(solution)/shard_map/ppermute | solution.py:25
  59.2 9.0 %collective-permute-start.6 = (f32[128,19,2]{0,2,1:T(2,128)S(1)}, f32[128,19,2]{0,2,1:T(2,128)S(1)}, u32[]{:S(2)}, u32[]{:S(2)}) collective-permute-start(f32[128,19,2]{0,2,1:T(2,128)S(1)} %pad_maximum_fusion.15), channel_id=1, source_target_pairs={{0,1},{1,2},{2,3},{3,4},{4,5},{5,6},{6,7},{7,8},{8,9},{9,10},{10,1... | collective-permute-start | bytes 58376 | tf_op jit(solution)/shard_map/ppermute | solution.py:22
  62.6 5.6 %collective-permute-start.7 = (f32[128,19,1]{0,2,1:T(1,128)S(1)}, f32[128,19,1]{0,2,1:T(1,128)S(1)}, u32[]{:S(2)}, u32[]{:S(2)}) collective-permute-start(f32[128,19,1]{0,2,1:T(1,128)S(1)} %pad_maximum_fusion.16), channel_id=1, source_target_pairs={{1,0},{2,1},{3,2},{4,3},{5,4},{6,5},{7,6},{8,7},{9,8},{10,9},{11,1... | collective-permute-start | bytes 29192 | tf_op jit(solution)/shard_map/ppermute | solution.py:25
  72.7 4.1 %collective-permute-start.10 = (f32[2,128]{1,0:T(2,128)S(1)}, f32[2,128]{1,0:T(2,128)S(1)}, u32[]{:S(2)}, u32[]{:S(2)}) collective-permute-start(f32[2,128]{1,0:T(2,128)S(1)} %broadcast_in_dim.4), channel_id=1, source_target_pairs={{0,48},{16,0},{32,16},{48,32},{64,112},{80,64},{96,80},{112,96},{1... | collective-permute-start | bytes 3080 | tf_op jit(solution)/shard_map/ppermute | solution.py:42
  78.9 5.2 %collective-permute-start.11 = (f32[2,128]{1,0:T(2,128)S(1)}, f32[2,128]{1,0:T(2,128)S(1)}, u32[]{:S(2)}, u32[]{:S(2)}) collective-permute-start(f32[2,128]{1,0:T(2,128)S(1)} %add_add_fusion.6), channel_id=1, source_target_pairs={{0,64},{16,80},{32,96},{48,112},{64,0},{80,16},{96,32},{112,48},{1... | collective-permute-start | bytes 3080 | tf_op jit(solution)/shard_map/ppermute | solution.py:42
  84.1 8.2 %collective-permute-start.12 = (f32[2,128]{1,0:T(2,128)S(1)}, f32[2,128]{1,0:T(2,128)S(1)}, u32[]{:S(2)}, u32[]{:S(2)}) collective-permute-start(f32[2,128]{1,0:T(2,128)S(1)} %add.317), channel_id=1, source_target_pairs={{0,1},{1,2},{2,3},{3,0},{4,5},{5,6},{6,7},{7,4},{8,9},{9,10},{10,1... | collective-permute-start | bytes 3080 | tf_op jit(solution)/shard_map/ppermute | solution.py:42
  87.5 5.7 %collective-permute-start.13 = (f32[2,128]{1,0:T(2,128)S(1)}, f32[2,128]{1,0:T(2,128)S(1)}, u32[]{:S(2)}, u32[]{:S(2)}) collective-permute-start(f32[2,128]{1,0:T(2,128)S(1)} %add.317), channel_id=1, source_target_pairs={{0,2},{1,3},{2,0},{3,1},{4,6},{5,7},{6,4},{7,5},{8,10},{9,11},{10,... | collective-permute-start | bytes 3080 | tf_op jit(solution)/shard_map/ppermute | solution.py:42
  95.3 7.8 %collective-permute-start.15 = (f32[2,128]{1,0:T(2,128)S(1)}, f32[2,128]{1,0:T(2,128)S(1)}, u32[]{:S(2)}, u32[]{:S(2)}) collective-permute-start(f32[2,128]{1,0:T(2,128)S(1)} %add_add_fusion.5), channel_id=1, source_target_pairs={{0,4},{1,5},{2,6},{3,7},{4,8},{5,9},{6,10},{7,11},{8,12},{9,13},{1... | collective-permute-start | bytes 3080 | tf_op jit(solution)/shard_map/ppermute | solution.py:42
  97.0 6.1 %collective-permute-start.16 = (f32[2,128]{1,0:T(2,128)S(1)}, f32[2,128]{1,0:T(2,128)S(1)}, u32[]{:S(2)}, u32[]{:S(2)}) collective-permute-start(f32[2,128]{1,0:T(2,128)S(1)} %add_add_fusion.5), channel_id=1, source_target_pairs={{0,8},{1,9},{2,10},{3,11},{4,12},{5,13},{6,14},{7,15},{8,0},{9,1},... | collective-permute-start | bytes 3080 | tf_op jit(solution)/shard_map/ppermute | solution.py:42
  98.6 4.6 %collective-permute-start.17 = (f32[2,128]{1,0:T(2,128)S(1)}, f32[2,128]{1,0:T(2,128)S(1)}, u32[]{:S(2)}, u32[]{:S(2)}) collective-permute-start(f32[2,128]{1,0:T(2,128)S(1)} %add_add_fusion.5), channel_id=1, source_target_pairs={{0,12},{1,13},{2,14},{3,15},{4,0},{5,1},{6,2},{7,3},{8,4},{9,5},{1... | collective-permute-start | bytes 3080 | tf_op jit(solution)/shard_map/ppermute | solution.py:42
  106.7 3.6 %collective-permute-start.19 = (f32[4,128]{1,0:T(4,128)S(1)}, f32[4,128]{1,0:T(4,128)S(1)}, u32[]{:S(2)}, u32[]{:S(2)}) collective-permute-start(f32[4,128]{1,0:T(4,128)S(1)} %broadcast_in_dim.5), channel_id=1, source_target_pairs={{0,32},{16,48},{32,0},{48,16},{64,96},{80,112},{96,64},{112,80},{1... | collective-permute-start | bytes 6152 | tf_op jit(solution)/shard_map/ppermute | solution.py:42
  110.4 5.1 %collective-permute-start.21 = (f32[4,128]{1,0:T(4,128)S(1)}, f32[4,128]{1,0:T(4,128)S(1)}, u32[]{:S(2)}, u32[]{:S(2)}) collective-permute-start(f32[4,128]{1,0:T(4,128)S(1)} %add_add_fusion.3), channel_id=1, source_target_pairs={{0,64},{16,80},{32,96},{48,112},{64,0},{80,16},{96,32},{112,48},{1... | collective-permute-start | bytes 6152 | tf_op jit(solution)/shard_map/ppermute | solution.py:42
  115.6 4.8 %collective-permute-start.22 = (f32[4,128]{1,0:T(4,128)S(1)}, f32[4,128]{1,0:T(4,128)S(1)}, u32[]{:S(2)}, u32[]{:S(2)}) collective-permute-start(f32[4,128]{1,0:T(4,128)S(1)} %add.335), channel_id=1, source_target_pairs={{0,1},{1,2},{2,3},{3,0},{4,5},{5,6},{6,7},{7,4},{8,9},{9,10},{10,1... | collective-permute-start | bytes 6152 | tf_op jit(solution)/shard_map/ppermute | solution.py:42
  115.6 5.1 %collective-permute-start.23 = (f32[4,128]{1,0:T(4,128)S(1)}, f32[4,128]{1,0:T(4,128)S(1)}, u32[]{:S(2)}, u32[]{:S(2)}) collective-permute-start(f32[4,128]{1,0:T(4,128)S(1)} %add.335), channel_id=1, source_target_pairs={{0,2},{1,3},{2,0},{3,1},{4,6},{5,7},{6,4},{7,5},{8,10},{9,11},{10,... | collective-permute-start | bytes 6152 | tf_op jit(solution)/shard_map/ppermute | solution.py:42
  118.6 3.6 %collective-permute-start.24 = (f32[4,128]{1,0:T(4,128)S(1)}, f32[4,128]{1,0:T(4,128)S(1)}, u32[]{:S(2)}, u32[]{:S(2)}) collective-permute-start(f32[4,128]{1,0:T(4,128)S(1)} %add.335), channel_id=1, source_target_pairs={{0,3},{1,0},{2,1},{3,2},{4,7},{5,4},{6,5},{7,6},{8,11},{9,8},{10,9... | collective-permute-start | bytes 6152 | tf_op jit(solution)/shard_map/ppermute | solution.py:42
  122.2 5.6 %collective-permute-start.25 = (f32[4,128]{1,0:T(4,128)S(1)}, f32[4,128]{1,0:T(4,128)S(1)}, u32[]{:S(2)}, u32[]{:S(2)}) collective-permute-start(f32[4,128]{1,0:T(4,128)S(1)} %add_add_fusion.2), channel_id=1, source_target_pairs={{0,4},{1,5},{2,6},{3,7},{4,8},{5,9},{6,10},{7,11},{8,12},{9,13},{1... | collective-permute-start | bytes 6152 | tf_op jit(solution)/shard_map/ppermute | solution.py:42
  122.6 5.4 %collective-permute-start.26 = (f32[4,128]{1,0:T(4,128)S(1)}, f32[4,128]{1,0:T(4,128)S(1)}, u32[]{:S(2)}, u32[]{:S(2)}) collective-permute-start(f32[4,128]{1,0:T(4,128)S(1)} %add_add_fusion.2), channel_id=1, source_target_pairs={{0,8},{1,9},{2,10},{3,11},{4,12},{5,13},{6,14},{7,15},{8,0},{9,1},... | collective-permute-start | bytes 6152 | tf_op jit(solution)/shard_map/ppermute | solution.py:42
  126.4 3.6 %collective-permute-start.27 = (f32[4,128]{1,0:T(4,128)S(1)}, f32[4,128]{1,0:T(4,128)S(1)}, u32[]{:S(2)}, u32[]{:S(2)}) collective-permute-start(f32[4,128]{1,0:T(4,128)S(1)} %add_add_fusion.2), channel_id=1, source_target_pairs={{0,12},{1,13},{2,14},{3,15},{4,0},{5,1},{6,2},{7,3},{8,4},{9,5},{1... | collective-permute-start | bytes 6152 | tf_op jit(solution)/shard_map/ppermute | solution.py:42
  (25 other events, 295.1 us)

commit v11 on v8

--- a/solution.py
+++ b/solution.py
@@ -94,8 +94,9 @@
     targets = slot_table.reshape(-1)
     devices = lax.axis_size("px") * lax.axis_size("py")
     width = targets.shape[0] // devices
-    held = recv_contact.reshape(hist, devices, width)
-    arrived = lax.all_to_all(held, ("px", "py"), split_axis=1, concat_axis=1, tiled=True)
+    held = recv_contact.reshape(hist, devices, width).transpose(1, 2, 0).reshape(devices, -1)
+    arrived = lax.all_to_all(held, ("px", "py"), split_axis=0, concat_axis=0, tiled=True)
+    arrived = arrived.reshape(devices * width, hist).T
 
     def with_base(shells):
         return jnp.einsum("ab,bxy->axy", stiff_base, shells, precision=HIGH)
@@ -124,7 +125,7 @@
     contact = (
         contact_home.reshape(hist, cells)
         .at[:, targets]
-        .set(arrived.reshape(hist, devices * width), mode="drop")
+        .set(arrived, mode="drop")
     )
     weights = (jax.nn.softplus(history_new) * contact).reshape(hist, rows, cols)
     weights_wide = with_halo(weights, 2, 1)

time: 135 us -> 130 us (0.963)
  waiting for transfers between devices: 22.7 us -> 20.8 us
  starting transfers between devices: 64.1 us -> 62.7 us
    ppermute x4, waiting for transfers between devices: 3.78 us -> 0.19 us  [with_halo(): parts.insert(0, lax.ppermute(last, axis, up))]
    reshape x2 -> x1, local copies, waits for them, and re-layouts: 1.93 us -> 0.07 us  [shards(): recv_contact.reshape(hist, devices, width).transpose(1, 2, 0)]
where the time goes in v11:
time: 130 us
  starting transfers between devices  62.7 us (48%)
  local copies, waits for them, and re-layouts  21.1 us (16%)
  waiting for transfers between devices  20.8 us (16%)
  matrix products  14.2 us (11%)
  other arithmetic  9.85 us (8%)
    ppermute x20, starting transfers between devices, all_sum(): total = total + lax.ppermute(value, axis, pairs)  33.7 us
    all_to_all x1, starting transfers between devices, shards(): lax.all_to_all(held, ('px', 'py'), split_axis=0, concat_axis=0, tiled=True)  14.6 us
    ppermute x20, waiting for transfers between devices, all_sum(): total = total + lax.ppermute(value, axis, pairs)  13.2 us
    unnamed x45, local copies, waits for them, and re-layouts  9.11 us
    ppermute x4, starting transfers between devices, with_halo(): parts.insert(0, lax.ppermute(last, axis, up))  9.04 us
    ppermute x4, waiting for transfers between devices, with_halo(): parts.append(lax.ppermute(leading, axis, down))  7.33 us
    scatter x1, local copies, waits for them, and re-layouts, shards(): contact = contact_home.reshape(hist, cells).at[:, targets].set(arrived, m...  6.76 us
    ppermute x4, starting transfers between devices, with_halo(): parts.append(lax.ppermute(leading, axis, down))  5.34 us
  transfers between devices with their start and end apart: 29, of which 16 were waited for; matrix products, arithmetic and copies ran while one was open for 16% of the time, Pallas kernels for 0%

profile of v11, /device:TPU:0, one launch (start us, length us, event | category | flops | bytes accessed | tf_op | source)
XLA Modules:
  0.0 129.7 jit_solution(839469610237441607)
XLA Ops:
  7.8 14.6 %all-to-all-start = ((f32[128,1,1152]{2,1,0:T(1,128)}), f32[128,1,1152]{2,1,0:T(1,128)}, u32[]{:S(2)}, u32[]{:S(2)}) async-start(f32[128,1,1152]{2,1,0:T(1,128)} %copy.68), calls=%async_computation | async-start | bytes 1179648 | tf_op jit(solution)/shard_map/all_to_all | solution.py:98
  23.5 3.5 %collective-permute-start.2 = (f32[12,22,3]{2,0,1:T(8,128)}, f32[12,22,3]{2,0,1:T(8,128)}, u32[]{:S(2)}, u32[]{:S(2)}) collective-permute-start(f32[12,22,3]{2,0,1:T(8,128)} %get-tuple-element.38), channel_id=1, source_target_pairs={{0,1},{1,2},{2,3},{3,4},{4,5},{5,6},{6,7},{7,8},{8,9},{9,10},{10,1... | collective-permute-start | bytes 9512 | tf_op jit(solution)/shard_map/ppermute | solution.py:22
  32.6 3.1 %collective-permute-done.3 = f32[12,22,3]{2,0,1:T(8,128)} collective-permute-done((f32[12,22,3]{2,0,1:T(8,128)}, f32[12,22,3]{2,0,1:T(8,128)}, u32[]{:S(2)}, u32[]{:S(2)}) %collective-permute-start.3) | collective-permute-done | bytes 3200 | tf_op jit(solution)/shard_map/ppermute | solution.py:25
  40.4 6.8 %scatter_fusion = f32[128,2048]{0,1:T(8,128)S(1)} fusion(f32[128,2048]{0,1:T(8,128)S(1)} %bitcast.82, s32[1152]{0:T(1024)S(1)} %copy-done.16, f32[1152,128]{1,0:T(8,128)} %bitcast.9), kind=kCustom, calls=%fused_computation | custom fusion | bytes 1774080 | tf_op jit(solution)/shard_map/scatter | solution.py:128
  47.2 3.4 %fusion.19 = (f32[128,2048]{0,1:T(8,128)S(1)}, f32[128,2048]{0,1:T(8,128)S(1)}) fusion(f32[128,2048]{0,1:T(8,128)S(1)} %scatter_fusion, f32[128,2048]{0,1:T(8,128)S(1)} %bitcast.91, f32[128,24]{0,1:T(8,128)S(1)} %copy-done, f32[6,21,133]{2,0,1:T(8,128)} %copy-done.1, f32[6,21,133]{2,0,1:T(8,128)} %copy-done.2, f32[6,21,133]{2,0,1:T(8,128)} %copy-done.3, ...), kind=kOutput, calls=%fused_computation.29 | convolution fusion | flops 77742080 | bytes 4474720 | tf_op jit(solution)/shard_map/dot_general | solution.py:122
  53.2 2.5 %convolution_bitcast_fusion.1 = f32[128,19,131]{0,2,1:T(8,128)S(1)} fusion(f32[6,19,131]{2,0,1:T(8,128)S(1)} %copy-done.5, f32[6,19,131]{2,0,1:T(8,128)S(1)} %copy-done.6, f32[6,19,131]{2,0,1:T(8,128)S(1)} %copy-done.7, f32[6,19,131]{2,0,1:T(8,128)S(1)} %copy-done.4, f32[128,24]{0,1:T(8,128)S(1)} %copy-done), kind=kOutput, calls=%fused_computation.4 | convolution fusion | flops 91933704 | bytes 1525600 | tf_op jit(solution)/shard_map/hb,bxy->hxy/dot_general | solution.py:135
  56.6 3.0 %collective-permute-start.6 = (f32[128,19,2]{0,2,1:T(2,128)S(1)}, f32[128,19,2]{0,2,1:T(2,128)S(1)}, u32[]{:S(2)}, u32[]{:S(2)}) collective-permute-start(f32[128,19,2]{0,2,1:T(2,128)S(1)} %pad_maximum_fusion.15), channel_id=1, source_target_pairs={{0,1},{1,2},{2,3},{3,4},{4,5},{5,6},{6,7},{7,8},{8,9},{9,10},{10,1... | collective-permute-start | bytes 58376 | tf_op jit(solution)/shard_map/ppermute | solution.py:22
  61.7 3.5 %collective-permute-done.7 = f32[128,19,1]{0,2,1:T(1,128)S(1)} collective-permute-done((f32[128,19,1]{0,2,1:T(1,128)S(1)}, f32[128,19,1]{0,2,1:T(1,128)S(1)}, u32[]{:S(2)}, u32[]{:S(2)}) %collective-permute-start.7) | collective-permute-done | bytes 9760 | tf_op jit(solution)/shard_map/ppermute | solution.py:25
  65.2 2.2 %fusion.13 = f32[24,19,131]{2,0,1:T(8,128)S(1)} fusion(f32[19,131,24]{1,2,0:T(8,128)S(1)} %fusion.29, f32[128,19,131]{0,2,1:T(8,128)S(1)} %convolution_bitcast_fusion.1, f32[128,19,1]{0,2,1:T(1,128)S(1)} %collective-permute-done.7, f32[128,1,128]{0,2,1:T(8,128)S(1)} %collective-permute-done.5, f32[128,16,128]{0,2,1:T(8,128)S(1)} %bitcast.87, ...), kind=kOutput, calls=%fused_computation.20 | convolution fusion | flops 93466928 | bytes 3048868 | tf_op jit(solution)/shard_map/hb,hxy->bxy/dot_general | solution.py:136
  69.7 2.3 %collective-permute-start.10 = (f32[2,128]{1,0:T(2,128)S(1)}, f32[2,128]{1,0:T(2,128)S(1)}, u32[]{:S(2)}, u32[]{:S(2)}) collective-permute-start(f32[2,128]{1,0:T(2,128)S(1)} %broadcast_in_dim.4), channel_id=1, source_target_pairs={{0,48},{16,0},{32,16},{48,32},{64,112},{80,64},{96,80},{112,96},{1... | collective-permute-start | bytes 3080 | tf_op jit(solution)/shard_map/ppermute | solution.py:42
  75.7 2.9 %collective-permute-start.11 = (f32[2,128]{1,0:T(2,128)S(1)}, f32[2,128]{1,0:T(2,128)S(1)}, u32[]{:S(2)}, u32[]{:S(2)}) collective-permute-start(f32[2,128]{1,0:T(2,128)S(1)} %add_add_fusion.6), channel_id=1, source_target_pairs={{0,64},{16,80},{32,96},{48,112},{64,0},{80,16},{96,32},{112,48},{1... | collective-permute-start | bytes 3080 | tf_op jit(solution)/shard_map/ppermute | solution.py:42
  78.6 2.2 %convolution_bitcast_fusion.2 = f32[128,17,129]{0,2,1:T(8,128)S(1)} fusion(f32[6,17,129]{2,0,1:T(8,128)S(1)} %get-tuple-element.45, f32[6,17,129]{2,0,1:T(8,128)S(1)} %get-tuple-element.46, f32[6,17,129]{2,0,1:T(8,128)S(1)} %get-tuple-element.47, f32[6,17,129]{2,0,1:T(8,128)S(1)} %get-tuple-element.44, f32[128,24]{0,1:T(8,128)S(1)} %copy-done), kind=kOutput, calls=%fused_computation.5 | convolution fusion | flops 81000648 | bytes 1345632 | tf_op jit(solution)/shard_map/hb,bxy->hxy/dot_general | solution.py:135
  80.9 3.4 %collective-permute-start.12 = (f32[2,128]{1,0:T(2,128)S(1)}, f32[2,128]{1,0:T(2,128)S(1)}, u32[]{:S(2)}, u32[]{:S(2)}) collective-permute-start(f32[2,128]{1,0:T(2,128)S(1)} %add.237), channel_id=1, source_target_pairs={{0,1},{1,2},{2,3},{3,0},{4,5},{5,6},{6,7},{7,4},{8,9},{9,10},{10,1... | collective-permute-start | bytes 3080 | tf_op jit(solution)/shard_map/ppermute | solution.py:42
  84.3 4.2 %collective-permute-start.13 = (f32[2,128]{1,0:T(2,128)S(1)}, f32[2,128]{1,0:T(2,128)S(1)}, u32[]{:S(2)}, u32[]{:S(2)}) collective-permute-start(f32[2,128]{1,0:T(2,128)S(1)} %add.237), channel_id=1, source_target_pairs={{0,2},{1,3},{2,0},{3,1},{4,6},{5,7},{6,4},{7,5},{8,10},{9,11},{10,... | collective-permute-start | bytes 3080 | tf_op jit(solution)/shard_map/ppermute | solution.py:42
  90.0 2.0 %collective-permute-done.14 = f32[2,128]{1,0:T(2,128)S(1)} collective-permute-done((f32[2,128]{1,0:T(2,128)S(1)}, f32[2,128]{1,0:T(2,128)S(1)}, u32[]{:S(2)}, u32[]{:S(2)}) %collective-permute-start.14) | collective-permute-done | bytes 1056 | tf_op jit(solution)/shard_map/ppermute | solution.py:42
  92.0 1.7 %collective-permute-start.15 = (f32[2,128]{1,0:T(2,128)S(1)}, f32[2,128]{1,0:T(2,128)S(1)}, u32[]{:S(2)}, u32[]{:S(2)}) collective-permute-start(f32[2,128]{1,0:T(2,128)S(1)} %add_add_fusion.5), channel_id=1, source_target_pairs={{0,4},{1,5},{2,6},{3,7},{4,8},{5,9},{6,10},{7,11},{8,12},{9,13},{1... | collective-permute-start | bytes 3080 | tf_op jit(solution)/shard_map/ppermute | solution.py:42
  95.3 2.5 %collective-permute-start.17 = (f32[2,128]{1,0:T(2,128)S(1)}, f32[2,128]{1,0:T(2,128)S(1)}, u32[]{:S(2)}, u32[]{:S(2)}) collective-permute-start(f32[2,128]{1,0:T(2,128)S(1)} %add_add_fusion.5), channel_id=1, source_target_pairs={{0,12},{1,13},{2,14},{3,15},{4,0},{5,1},{6,2},{7,3},{8,4},{9,5},{1... | collective-permute-start | bytes 3080 | tf_op jit(solution)/shard_map/ppermute | solution.py:42
  97.9 2.0 %fusion.15 = f32[24,17,129]{2,0,1:T(8,128)S(1)} fusion(f32[17,129,24]{1,2,0:T(8,128)S(1)} %fusion.30, f32[128,17,129]{0,2,1:T(8,128)S(1)} %convolution_bitcast_fusion.2, f32[128,19,2]{0,2,1:T(2,128)S(1)} %collective-permute-done.6, f32[128,1,128]{0,2,1:T(8,128)S(1)} %collective-permute-done.5, f32[128,16,128]{0,2,1:T(8,128)S(1)} %bitcast.88, ...), kind=kOutput, calls=%fused_computation.23 | convolution fusion | flops 82070832 | bytes 2829572 | tf_op jit(solution)/shard_map/hb,hxy->bxy/dot_general | solution.py:136
  100.7 2.7 %pad_maximum_fusion.19 = f32[4]{0:T(128)S(1)} fusion(f32[1]{0:T(128)} %bitcast.22, f32[1]{0:T(128)} %bitcast.21, f32[1]{0:T(128)} %bitcast.20, f32[1]{0:T(128)} %bitcast.17), kind=kLoop, calls=%fused_computation.99 | loop fusion | flops 12 | bytes 32 | tf_op jit(solution)/shard_map/stack | solution.py:144
  107.2 2.6 %collective-permute-start.21 = (f32[4,128]{1,0:T(4,128)S(1)}, f32[4,128]{1,0:T(4,128)S(1)}, u32[]{:S(2)}, u32[]{:S(2)}) collective-permute-start(f32[4,128]{1,0:T(4,128)S(1)} %add_add_fusion.3), channel_id=1, source_target_pairs={{0,64},{16,80},{32,96},{48,112},{64,0},{80,16},{96,32},{112,48},{1... | collective-permute-start | bytes 6152 | tf_op jit(solution)/shard_map/ppermute | solution.py:42
  109.8 2.5 %collective-permute-done.21 = f32[4,128]{1,0:T(4,128)S(1)} collective-permute-done((f32[4,128]{1,0:T(4,128)S(1)}, f32[4,128]{1,0:T(4,128)S(1)}, u32[]{:S(2)}, u32[]{:S(2)}) %collective-permute-start.21) | collective-permute-done | bytes 2080 | tf_op jit(solution)/shard_map/ppermute | solution.py:42
  112.3 3.1 %collective-permute-start.23 = (f32[4,128]{1,0:T(4,128)S(1)}, f32[4,128]{1,0:T(4,128)S(1)}, u32[]{:S(2)}, u32[]{:S(2)}) collective-permute-start(f32[4,128]{1,0:T(4,128)S(1)} %add.251), channel_id=1, source_target_pairs={{0,2},{1,3},{2,0},{3,1},{4,6},{5,7},{6,4},{7,5},{8,10},{9,11},{10,... | collective-permute-start | bytes 6152 | tf_op jit(solution)/shard_map/ppermute | solution.py:42
  119.3 3.8 %collective-permute-start.26 = (f32[4,128]{1,0:T(4,128)S(1)}, f32[4,128]{1,0:T(4,128)S(1)}, u32[]{:S(2)}, u32[]{:S(2)}) collective-permute-start(f32[4,128]{1,0:T(4,128)S(1)} %add_add_fusion.2), channel_id=1, source_target_pairs={{0,8},{1,9},{2,10},{3,11},{4,12},{5,13},{6,14},{7,15},{8,0},{9,1},... | collective-permute-start | bytes 6152 | tf_op jit(solution)/shard_map/ppermute | solution.py:42
  124.7 2.0 %collective-permute-done.27 = f32[4,128]{1,0:T(4,128)S(1)} collective-permute-done((f32[4,128]{1,0:T(4,128)S(1)}, f32[4,128]{1,0:T(4,128)S(1)}, u32[]{:S(2)}, u32[]{:S(2)}) %collective-permute-start.27) | collective-permute-done | bytes 2080 | tf_op jit(solution)/shard_map/ppermute | solution.py:42
  (131 shorter events, 46.0 us)
Async XLA Ops:
  2.3 20.4 %collective-permute-start = (f32[12,3,128]{2,0,1:T(8,128)S(1)}, f32[12,3,128]{2,0,1:T(8,128)S(1)}, u32[]{:S(2)}, u32[]{:S(2)}) collective-permute-start(f32[12,3,128]{2,0,1:T(8,128)S(1)} %get-tuple-element.48), channel_id=1, source_target_pairs={{0,16},{16,32},{32,48},{48,64},{64,80},{80,96},{96,112},{1,17},{17... | collective-permute-start | bytes 55304 | tf_op jit(solution)/shard_map/ppermute | solution.py:22
  3.6 19.1 %collective-permute-start.1 = (f32[12,3,128]{2,0,1:T(8,128)S(1)}, f32[12,3,128]{2,0,1:T(8,128)S(1)}, u32[]{:S(2)}, u32[]{:S(2)}) collective-permute-start(f32[12,3,128]{2,0,1:T(8,128)S(1)} %get-tuple-element.49), channel_id=1, source_target_pairs={{16,0},{32,16},{48,32},{64,48},{80,64},{96,80},{112,96},{17,1},{33... | collective-permute-start | bytes 55304 | tf_op jit(solution)/shard_map/ppermute | solution.py:25
  7.8 32.5 %all-to-all-start = ((f32[128,1,1152]{2,1,0:T(1,128)}), f32[128,1,1152]{2,1,0:T(1,128)}, u32[]{:S(2)}, u32[]{:S(2)}) async-start(f32[128,1,1152]{2,1,0:T(1,128)} %copy.68), calls=%async_computation | async-start | bytes 1179648 | tf_op jit(solution)/shard_map/all_to_all | solution.py:98
  23.5 9.1 %collective-permute-start.2 = (f32[12,22,3]{2,0,1:T(8,128)}, f32[12,22,3]{2,0,1:T(8,128)}, u32[]{:S(2)}, u32[]{:S(2)}) collective-permute-start(f32[12,22,3]{2,0,1:T(8,128)} %get-tuple-element.38), channel_id=1, source_target_pairs={{0,1},{1,2},{2,3},{3,4},{4,5},{5,6},{6,7},{7,8},{8,9},{9,10},{10,1... | collective-permute-start | bytes 9512 | tf_op jit(solution)/shard_map/ppermute | solution.py:22
  27.0 8.7 %collective-permute-start.3 = (f32[12,22,3]{2,0,1:T(8,128)}, f32[12,22,3]{2,0,1:T(8,128)}, u32[]{:S(2)}, u32[]{:S(2)}) collective-permute-start(f32[12,22,3]{2,0,1:T(8,128)} %get-tuple-element.39), channel_id=1, source_target_pairs={{1,0},{2,1},{3,2},{4,3},{5,4},{6,5},{7,6},{8,7},{9,8},{10,9},{11,1... | collective-permute-start | bytes 9512 | tf_op jit(solution)/shard_map/ppermute | solution.py:25
  50.6 6.0 %collective-permute-start.4 = (f32[128,2,128]{0,2,1:T(8,128)S(1)}, f32[128,2,128]{0,2,1:T(8,128)S(1)}, u32[]{:S(2)}, u32[]{:S(2)}) collective-permute-start(f32[128,2,128]{0,2,1:T(8,128)S(1)} %slice.207), channel_id=1, source_target_pairs={{0,16},{16,32},{32,48},{48,64},{64,80},{80,96},{96,112},{1,17},{17... | collective-permute-start | bytes 393224 | tf_op jit(solution)/shard_map/ppermute | solution.py:22
  51.9 4.7 %collective-permute-start.5 = (f32[128,1,128]{0,2,1:T(8,128)S(1)}, f32[128,1,128]{0,2,1:T(8,128)S(1)}, u32[]{:S(2)}, u32[]{:S(2)}) collective-permute-start(f32[128,1,128]{0,2,1:T(8,128)S(1)} %slice.208), channel_id=1, source_target_pairs={{16,0},{32,16},{48,32},{64,48},{80,64},{96,80},{112,96},{17,1},{33... | collective-permute-start | bytes 196616 | tf_op jit(solution)/shard_map/ppermute | solution.py:25
  56.6 8.6 %collective-permute-start.6 = (f32[128,19,2]{0,2,1:T(2,128)S(1)}, f32[128,19,2]{0,2,1:T(2,128)S(1)}, u32[]{:S(2)}, u32[]{:S(2)}) collective-permute-start(f32[128,19,2]{0,2,1:T(2,128)S(1)} %pad_maximum_fusion.15), channel_id=1, source_target_pairs={{0,1},{1,2},{2,3},{3,4},{4,5},{5,6},{6,7},{7,8},{8,9},{9,10},{10,1... | collective-permute-start | bytes 58376 | tf_op jit(solution)/shard_map/ppermute | solution.py:22
  59.6 5.6 %collective-permute-start.7 = (f32[128,19,1]{0,2,1:T(1,128)S(1)}, f32[128,19,1]{0,2,1:T(1,128)S(1)}, u32[]{:S(2)}, u32[]{:S(2)}) collective-permute-start(f32[128,19,1]{0,2,1:T(1,128)S(1)} %pad_maximum_fusion.16), channel_id=1, source_target_pairs={{1,0},{2,1},{3,2},{4,3},{5,4},{6,5},{7,6},{8,7},{9,8},{10,9},{11,1... | collective-permute-start | bytes 29192 | tf_op jit(solution)/shard_map/ppermute | solution.py:25
  69.7 4.1 %collective-permute-start.10 = (f32[2,128]{1,0:T(2,128)S(1)}, f32[2,128]{1,0:T(2,128)S(1)}, u32[]{:S(2)}, u32[]{:S(2)}) collective-permute-start(f32[2,128]{1,0:T(2,128)S(1)} %broadcast_in_dim.4), channel_id=1, source_target_pairs={{0,48},{16,0},{32,16},{48,32},{64,112},{80,64},{96,80},{112,96},{1... | collective-permute-start | bytes 3080 | tf_op jit(solution)/shard_map/ppermute | solution.py:42
  75.7 5.2 %collective-permute-start.11 = (f32[2,128]{1,0:T(2,128)S(1)}, f32[2,128]{1,0:T(2,128)S(1)}, u32[]{:S(2)}, u32[]{:S(2)}) collective-permute-start(f32[2,128]{1,0:T(2,128)S(1)} %add_add_fusion.6), channel_id=1, source_target_pairs={{0,64},{16,80},{32,96},{48,112},{64,0},{80,16},{96,32},{112,48},{1... | collective-permute-start | bytes 3080 | tf_op jit(solution)/shard_map/ppermute | solution.py:42
  80.9 8.2 %collective-permute-start.12 = (f32[2,128]{1,0:T(2,128)S(1)}, f32[2,128]{1,0:T(2,128)S(1)}, u32[]{:S(2)}, u32[]{:S(2)}) collective-permute-start(f32[2,128]{1,0:T(2,128)S(1)} %add.237), channel_id=1, source_target_pairs={{0,1},{1,2},{2,3},{3,0},{4,5},{5,6},{6,7},{7,4},{8,9},{9,10},{10,1... | collective-permute-start | bytes 3080 | tf_op jit(solution)/shard_map/ppermute | solution.py:42
  84.3 5.7 %collective-permute-start.13 = (f32[2,128]{1,0:T(2,128)S(1)}, f32[2,128]{1,0:T(2,128)S(1)}, u32[]{:S(2)}, u32[]{:S(2)}) collective-permute-start(f32[2,128]{1,0:T(2,128)S(1)} %add.237), channel_id=1, source_target_pairs={{0,2},{1,3},{2,0},{3,1},{4,6},{5,7},{6,4},{7,5},{8,10},{9,11},{10,... | collective-permute-start | bytes 3080 | tf_op jit(solution)/shard_map/ppermute | solution.py:42
  92.0 7.8 %collective-permute-start.15 = (f32[2,128]{1,0:T(2,128)S(1)}, f32[2,128]{1,0:T(2,128)S(1)}, u32[]{:S(2)}, u32[]{:S(2)}) collective-permute-start(f32[2,128]{1,0:T(2,128)S(1)} %add_add_fusion.5), channel_id=1, source_target_pairs={{0,4},{1,5},{2,6},{3,7},{4,8},{5,9},{6,10},{7,11},{8,12},{9,13},{1... | collective-permute-start | bytes 3080 | tf_op jit(solution)/shard_map/ppermute | solution.py:42
  93.8 6.1 %collective-permute-start.16 = (f32[2,128]{1,0:T(2,128)S(1)}, f32[2,128]{1,0:T(2,128)S(1)}, u32[]{:S(2)}, u32[]{:S(2)}) collective-permute-start(f32[2,128]{1,0:T(2,128)S(1)} %add_add_fusion.5), channel_id=1, source_target_pairs={{0,8},{1,9},{2,10},{3,11},{4,12},{5,13},{6,14},{7,15},{8,0},{9,1},... | collective-permute-start | bytes 3080 | tf_op jit(solution)/shard_map/ppermute | solution.py:42
  95.3 4.6 %collective-permute-start.17 = (f32[2,128]{1,0:T(2,128)S(1)}, f32[2,128]{1,0:T(2,128)S(1)}, u32[]{:S(2)}, u32[]{:S(2)}) collective-permute-start(f32[2,128]{1,0:T(2,128)S(1)} %add_add_fusion.5), channel_id=1, source_target_pairs={{0,12},{1,13},{2,14},{3,15},{4,0},{5,1},{6,2},{7,3},{8,4},{9,5},{1... | collective-permute-start | bytes 3080 | tf_op jit(solution)/shard_map/ppermute | solution.py:42
  103.5 3.6 %collective-permute-start.19 = (f32[4,128]{1,0:T(4,128)S(1)}, f32[4,128]{1,0:T(4,128)S(1)}, u32[]{:S(2)}, u32[]{:S(2)}) collective-permute-start(f32[4,128]{1,0:T(4,128)S(1)} %broadcast_in_dim.5), channel_id=1, source_target_pairs={{0,32},{16,48},{32,0},{48,16},{64,96},{80,112},{96,64},{112,80},{1... | collective-permute-start | bytes 6152 | tf_op jit(solution)/shard_map/ppermute | solution.py:42
  107.2 5.1 %collective-permute-start.21 = (f32[4,128]{1,0:T(4,128)S(1)}, f32[4,128]{1,0:T(4,128)S(1)}, u32[]{:S(2)}, u32[]{:S(2)}) collective-permute-start(f32[4,128]{1,0:T(4,128)S(1)} %add_add_fusion.3), channel_id=1, source_target_pairs={{0,64},{16,80},{32,96},{48,112},{64,0},{80,16},{96,32},{112,48},{1... | collective-permute-start | bytes 6152 | tf_op jit(solution)/shard_map/ppermute | solution.py:42
  112.3 4.8 %collective-permute-start.22 = (f32[4,128]{1,0:T(4,128)S(1)}, f32[4,128]{1,0:T(4,128)S(1)}, u32[]{:S(2)}, u32[]{:S(2)}) collective-permute-start(f32[4,128]{1,0:T(4,128)S(1)} %add.251), channel_id=1, source_target_pairs={{0,1},{1,2},{2,3},{3,0},{4,5},{5,6},{6,7},{7,4},{8,9},{9,10},{10,1... | collective-permute-start | bytes 6152 | tf_op jit(solution)/shard_map/ppermute | solution.py:42
  112.3 5.1 %collective-permute-start.23 = (f32[4,128]{1,0:T(4,128)S(1)}, f32[4,128]{1,0:T(4,128)S(1)}, u32[]{:S(2)}, u32[]{:S(2)}) collective-permute-start(f32[4,128]{1,0:T(4,128)S(1)} %add.251), channel_id=1, source_target_pairs={{0,2},{1,3},{2,0},{3,1},{4,6},{5,7},{6,4},{7,5},{8,10},{9,11},{10,... | collective-permute-start | bytes 6152 | tf_op jit(solution)/shard_map/ppermute | solution.py:42
  115.3 3.6 %collective-permute-start.24 = (f32[4,128]{1,0:T(4,128)S(1)}, f32[4,128]{1,0:T(4,128)S(1)}, u32[]{:S(2)}, u32[]{:S(2)}) collective-permute-start(f32[4,128]{1,0:T(4,128)S(1)} %add.251), channel_id=1, source_target_pairs={{0,3},{1,0},{2,1},{3,2},{4,7},{5,4},{6,5},{7,6},{8,11},{9,8},{10,9... | collective-permute-start | bytes 6152 | tf_op jit(solution)/shard_map/ppermute | solution.py:42
  118.9 5.6 %collective-permute-start.25 = (f32[4,128]{1,0:T(4,128)S(1)}, f32[4,128]{1,0:T(4,128)S(1)}, u32[]{:S(2)}, u32[]{:S(2)}) collective-permute-start(f32[4,128]{1,0:T(4,128)S(1)} %add_add_fusion.2), channel_id=1, source_target_pairs={{0,4},{1,5},{2,6},{3,7},{4,8},{5,9},{6,10},{7,11},{8,12},{9,13},{1... | collective-permute-start | bytes 6152 | tf_op jit(solution)/shard_map/ppermute | solution.py:42
  119.3 5.4 %collective-permute-start.26 = (f32[4,128]{1,0:T(4,128)S(1)}, f32[4,128]{1,0:T(4,128)S(1)}, u32[]{:S(2)}, u32[]{:S(2)}) collective-permute-start(f32[4,128]{1,0:T(4,128)S(1)} %add_add_fusion.2), channel_id=1, source_target_pairs={{0,8},{1,9},{2,10},{3,11},{4,12},{5,13},{6,14},{7,15},{8,0},{9,1},... | collective-permute-start | bytes 6152 | tf_op jit(solution)/shard_map/ppermute | solution.py:42
  123.1 3.6 %collective-permute-start.27 = (f32[4,128]{1,0:T(4,128)S(1)}, f32[4,128]{1,0:T(4,128)S(1)}, u32[]{:S(2)}, u32[]{:S(2)}) collective-permute-start(f32[4,128]{1,0:T(4,128)S(1)} %add_add_fusion.2), channel_id=1, source_target_pairs={{0,12},{1,13},{2,14},{3,15},{4,0},{5,1},{6,2},{7,3},{8,4},{9,5},{1... | collective-permute-start | bytes 6152 | tf_op jit(solution)/shard_map/ppermute | solution.py:42
  (23 other events, 260.7 us)

commit v12 on v11

--- a/solution.py
+++ b/solution.py
@@ -141,23 +141,18 @@
     image = image_wide[:, 1 : rows + 1, 1 : cols + 1]
     again = operate(image_wide, weights_wide[:, 1 : rows + 2, 1 : cols + 2], -1)
     def lanes(values):
-        values = jnp.stack(values)
-        return jnp.broadcast_to(values[:, None], (values.shape[0], cols))
+        return jnp.stack([jnp.sum(value, axis=(0, 1)) for value in values])
 
-    first = all_sum(lanes([jnp.sum(rhs * rhs), jnp.sum(rhs * image)]))
+    def totals(values):
+        return jnp.broadcast_to(jnp.sum(values, axis=1, keepdims=True), values.shape)
+
+    first = totals(all_sum(lanes([rhs * rhs, rhs * image])))
     norm_now, curvature = first[0], first[1]
     alpha = norm_now / curvature
     residual = rhs - alpha * image
     bent = image - alpha * again
-    second = all_sum(
-        lanes(
-            [
-                jnp.sum(residual * residual),
-                jnp.sum(residual * bent),
-                jnp.sum(residual * image),
-                jnp.sum(rhs * bent),
-            ]
-        )
+    second = totals(
+        all_sum(lanes([residual * residual, residual * bent, residual * image, rhs * bent]))
     )
     norm_next = second[0]
     beta = norm_next / norm_now

time: 130 us -> 134 us (1.031)
  between operations: 1.2 us -> 7.01 us
  other arithmetic: 9.85 us -> 4.72 us
  local copies, waits for them, and re-layouts: 21.1 us -> 22.7 us
    another operation x2, other arithmetic: 4.03 us -> 0.02 us  [lanes(): return jnp.stack([jnp.sum(value, axis=(0, 1)) for value in values])]
    unnamed x45 -> x43, local copies, waits for them, and re-layouts: 9.11 us -> 8.3 us
  transfers between devices with their start and end apart: 29 -> 29, of which waited for: 16 -> 16; matrix products, arithmetic and copies ran while one was open for 16% -> 18% of each run, Pallas kernels for 0% -> 0%
where the time goes in v12:
time: 134 us; the launch traced here: 133 us
  starting transfers between devices  63.4 us (47%)
  local copies, waits for them, and re-layouts  22.7 us (17%)
  waiting for transfers between devices  19.7 us (15%)
  matrix products  15.2 us (11%)
  between operations  7.01 us (5%)
  other arithmetic  4.72 us (4%)
    ppermute x20, starting transfers between devices, all_sum(): total = total + lax.ppermute(value, axis, pairs)  34.4 us
    all_to_all x1, starting transfers between devices, shards(): lax.all_to_all(held, ('px', 'py'), split_axis=0, concat_axis=0, tiled=True)  14.6 us
    ppermute x20, waiting for transfers between devices, all_sum(): total = total + lax.ppermute(value, axis, pairs)  12.8 us
    ppermute x4, starting transfers between devices, with_halo(): parts.insert(0, lax.ppermute(last, axis, up))  9.03 us
    unnamed x43, local copies, waits for them, and re-layouts  8.3 us
    ppermute x4, waiting for transfers between devices, with_halo(): parts.append(lax.ppermute(leading, axis, down))  6.95 us
    scatter x1, local copies, waits for them, and re-layouts, shards(): contact = contact_home.reshape(hist, cells).at[:, targets].set(arrived, m...  6.76 us
    ppermute x4, starting transfers between devices, with_halo(): parts.append(lax.ppermute(leading, axis, down))  5.34 us
  transfers between devices with their start and end apart: 29, of which 16 were waited for; matrix products, arithmetic and copies ran while one was open for 18% of the time, Pallas kernels for 0%

profile of v12, /device:TPU:0, one launch (start us, length us, event | category | flops | bytes accessed | tf_op | source)
XLA Modules:
  0.0 132.7 jit_solution(7227863243126282412)
XLA Ops:
  7.8 14.6 %all-to-all-start = ((f32[128,1,1152]{2,1,0:T(1,128)}), f32[128,1,1152]{2,1,0:T(1,128)}, u32[]{:S(2)}, u32[]{:S(2)}) async-start(f32[128,1,1152]{2,1,0:T(1,128)} %copy.68), calls=%async_computation | async-start | bytes 1179648 | tf_op jit(solution)/shard_map/all_to_all | solution.py:98
  23.5 3.5 %collective-permute-start.2 = (f32[12,22,3]{2,0,1:T(8,128)}, f32[12,22,3]{2,0,1:T(8,128)}, u32[]{:S(2)}, u32[]{:S(2)}) collective-permute-start(f32[12,22,3]{2,0,1:T(8,128)} %get-tuple-element.36), channel_id=1, source_target_pairs={{0,1},{1,2},{2,3},{3,4},{4,5},{5,6},{6,7},{7,8},{8,9},{9,10},{10,1... | collective-permute-start | bytes 9512 | tf_op jit(solution)/shard_map/ppermute | solution.py:22
  33.0 2.7 %collective-permute-done.3 = f32[12,22,3]{2,0,1:T(8,128)} collective-permute-done((f32[12,22,3]{2,0,1:T(8,128)}, f32[12,22,3]{2,0,1:T(8,128)}, u32[]{:S(2)}, u32[]{:S(2)}) %collective-permute-start.3) | collective-permute-done | bytes 3200 | tf_op jit(solution)/shard_map/ppermute | solution.py:25
  37.7 1.7 %fusion.10 = f32[24,21,133]{2,0,1:T(8,128)S(1)} fusion(f32[6,21,133]{2,0,1:T(8,128)S(1)} %get-tuple-element.33, f32[6,21,133]{2,0,1:T(8,128)} %get-tuple-element.34, f32[6,21,133]{2,0,1:T(8,128)} %get-tuple-element.35, f32[6,21,133]{2,0,1:T(8,128)S(1)} %get-tuple-element.32, f32[21,133]{1,0:T(8,128)S(1)} %and_convert_fusion.1, f32[24,24]{1,0:T(8,128)S(1)} %copy-done.9), kind=kOutput, calls=%fused_computation.17 | convolution fusion | flops 19573344 | bytes 549732 | tf_op jit(solution)/shard_map/ab,bxy->axy/dot_general | solution.py:102
  41.3 6.8 %scatter_fusion = f32[128,2048]{0,1:T(8,128)S(1)} fusion(f32[128,2048]{0,1:T(8,128)S(1)} %bitcast.62, s32[1152]{0:T(1024)S(1)} %copy-done.15, f32[1152,128]{1,0:T(8,128)} %bitcast.9), kind=kCustom, calls=%fused_computation | custom fusion | bytes 1774080 | tf_op jit(solution)/shard_map/scatter | solution.py:128
  48.1 3.4 %fusion.19 = (f32[128,2048]{0,1:T(8,128)S(1)}, f32[128,2048]{0,1:T(8,128)S(1)}) fusion(f32[128,2048]{0,1:T(8,128)S(1)} %scatter_fusion, f32[128,2048]{0,1:T(8,128)S(1)} %bitcast.71, f32[128,24]{0,1:T(8,128)S(1)} %copy-done, f32[6,21,133]{2,0,1:T(8,128)} %copy-done.1, f32[6,21,133]{2,0,1:T(8,128)} %get-tuple-element.34, ...), kind=kOutput, calls=%fused_computation.29 | convolution fusion | flops 77742080 | bytes 4474720 | tf_op jit(solution)/shard_map/dot_general | solution.py:122
  54.1 2.5 %convolution_bitcast_fusion.1 = f32[128,19,131]{0,2,1:T(8,128)S(1)} fusion(f32[6,19,131]{2,0,1:T(8,128)S(1)} %copy-done.3, f32[6,19,131]{2,0,1:T(8,128)S(1)} %copy-done.4, f32[6,19,131]{2,0,1:T(8,128)S(1)} %copy-done.5, f32[6,19,131]{2,0,1:T(8,128)S(1)} %copy-done.2, f32[128,24]{0,1:T(8,128)S(1)} %copy-done), kind=kOutput, calls=%fused_computation.4 | convolution fusion | flops 91933704 | bytes 1525600 | tf_op jit(solution)/shard_map/hb,bxy->hxy/dot_general | solution.py:135
  57.5 3.0 %collective-permute-start.6 = (f32[128,19,2]{0,2,1:T(2,128)S(1)}, f32[128,19,2]{0,2,1:T(2,128)S(1)}, u32[]{:S(2)}, u32[]{:S(2)}) collective-permute-start(f32[128,19,2]{0,2,1:T(2,128)S(1)} %pad_maximum_fusion.15), channel_id=1, source_target_pairs={{0,1},{1,2},{2,3},{3,4},{4,5},{5,6},{6,7},{7,8},{8,9},{9,10},{10,1... | collective-permute-start | bytes 58376 | tf_op jit(solution)/shard_map/ppermute | solution.py:22
  62.6 3.5 %collective-permute-done.7 = f32[128,19,1]{0,2,1:T(1,128)S(1)} collective-permute-done((f32[128,19,1]{0,2,1:T(1,128)S(1)}, f32[128,19,1]{0,2,1:T(1,128)S(1)}, u32[]{:S(2)}, u32[]{:S(2)}) %collective-permute-start.7) | collective-permute-done | bytes 9760 | tf_op jit(solution)/shard_map/ppermute | solution.py:25
  66.1 2.2 %fusion.13 = f32[24,19,131]{2,0,1:T(8,128)S(1)} fusion(f32[19,131,24]{1,2,0:T(8,128)S(1)} %fusion.29, f32[128,19,131]{0,2,1:T(8,128)S(1)} %convolution_bitcast_fusion.1, f32[128,19,1]{0,2,1:T(1,128)S(1)} %collective-permute-done.7, f32[128,1,128]{0,2,1:T(8,128)S(1)} %collective-permute-done.5, f32[128,16,128]{0,2,1:T(8,128)S(1)} %bitcast.67, ...), kind=kOutput, calls=%fused_computation.20 | convolution fusion | flops 93466928 | bytes 3048868 | tf_op jit(solution)/shard_map/hb,hxy->bxy/dot_general | solution.py:136
  68.6 2.4 %collective-permute-start.10 = (f32[2,128]{1,0:T(2,128)S(1)}, f32[2,128]{1,0:T(2,128)S(1)}, u32[]{:S(2)}, u32[]{:S(2)}) collective-permute-start(f32[2,128]{1,0:T(2,128)S(1)} %pad_maximum_fusion.19), channel_id=1, source_target_pairs={{0,48},{16,0},{32,16},{48,32},{64,112},{80,64},{96,80},{112,96},{1... | collective-permute-start | bytes 3080 | tf_op jit(solution)/shard_map/ppermute | solution.py:42
  74.6 3.0 %collective-permute-start.11 = (f32[2,128]{1,0:T(2,128)S(1)}, f32[2,128]{1,0:T(2,128)S(1)}, u32[]{:S(2)}, u32[]{:S(2)}) collective-permute-start(f32[2,128]{1,0:T(2,128)S(1)} %add_add_fusion.4), channel_id=1, source_target_pairs={{0,64},{16,80},{32,96},{48,112},{64,0},{80,16},{96,32},{112,48},{1... | collective-permute-start | bytes 3080 | tf_op jit(solution)/shard_map/ppermute | solution.py:42
  77.6 2.2 %convolution_bitcast_fusion.2 = f32[128,17,129]{0,2,1:T(8,128)S(1)} fusion(f32[6,17,129]{2,0,1:T(8,128)S(1)} %get-tuple-element.43, f32[6,17,129]{2,0,1:T(8,128)S(1)} %get-tuple-element.44, f32[6,17,129]{2,0,1:T(8,128)S(1)} %get-tuple-element.45, f32[6,17,129]{2,0,1:T(8,128)S(1)} %get-tuple-element.42, f32[128,24]{0,1:T(8,128)S(1)} %copy-done), kind=kOutput, calls=%fused_computation.5 | convolution fusion | flops 81000648 | bytes 1345632 | tf_op jit(solution)/shard_map/hb,bxy->hxy/dot_general | solution.py:135
  79.8 3.5 %collective-permute-start.12 = (f32[2,128]{1,0:T(2,128)S(1)}, f32[2,128]{1,0:T(2,128)S(1)}, u32[]{:S(2)}, u32[]{:S(2)}) collective-permute-start(f32[2,128]{1,0:T(2,128)S(1)} %add.228), channel_id=1, source_target_pairs={{0,1},{1,2},{2,3},{3,0},{4,5},{5,6},{6,7},{7,4},{8,9},{9,10},{10,1... | collective-permute-start | bytes 3080 | tf_op jit(solution)/shard_map/ppermute | solution.py:42
  83.3 3.8 %collective-permute-start.13 = (f32[2,128]{1,0:T(2,128)S(1)}, f32[2,128]{1,0:T(2,128)S(1)}, u32[]{:S(2)}, u32[]{:S(2)}) collective-permute-start(f32[2,128]{1,0:T(2,128)S(1)} %add.228), channel_id=1, source_target_pairs={{0,2},{1,3},{2,0},{3,1},{4,6},{5,7},{6,4},{7,5},{8,10},{9,11},{10,... | collective-permute-start | bytes 3080 | tf_op jit(solution)/shard_map/ppermute | solution.py:42
  88.6 2.0 %collective-permute-done.14 = f32[2,128]{1,0:T(2,128)S(1)} collective-permute-done((f32[2,128]{1,0:T(2,128)S(1)}, f32[2,128]{1,0:T(2,128)S(1)}, u32[]{:S(2)}, u32[]{:S(2)}) %collective-permute-start.14) | collective-permute-done | bytes 1056 | tf_op jit(solution)/shard_map/ppermute | solution.py:42
  90.7 1.7 %collective-permute-start.15 = (f32[2,128]{1,0:T(2,128)S(1)}, f32[2,128]{1,0:T(2,128)S(1)}, u32[]{:S(2)}, u32[]{:S(2)}) collective-permute-start(f32[2,128]{1,0:T(2,128)S(1)} %add_add_fusion.3), channel_id=1, source_target_pairs={{0,4},{1,5},{2,6},{3,7},{4,8},{5,9},{6,10},{7,11},{8,12},{9,13},{1... | collective-permute-start | bytes 3080 | tf_op jit(solution)/shard_map/ppermute | solution.py:42
  93.9 2.5 %collective-permute-start.17 = (f32[2,128]{1,0:T(2,128)S(1)}, f32[2,128]{1,0:T(2,128)S(1)}, u32[]{:S(2)}, u32[]{:S(2)}) collective-permute-start(f32[2,128]{1,0:T(2,128)S(1)} %add_add_fusion.3), channel_id=1, source_target_pairs={{0,12},{1,13},{2,14},{3,15},{4,0},{5,1},{6,2},{7,3},{8,4},{9,5},{1... | collective-permute-start | bytes 3080 | tf_op jit(solution)/shard_map/ppermute | solution.py:42
  96.5 2.0 %fusion.15 = f32[24,17,129]{2,0,1:T(8,128)S(1)} fusion(f32[17,129,24]{1,2,0:T(8,128)S(1)} %fusion.30, f32[128,17,129]{0,2,1:T(8,128)S(1)} %convolution_bitcast_fusion.2, f32[128,19,2]{0,2,1:T(2,128)S(1)} %collective-permute-done.6, f32[128,1,128]{0,2,1:T(8,128)S(1)} %collective-permute-done.5, f32[128,16,128]{0,2,1:T(8,128)S(1)} %bitcast.68, ...), kind=kOutput, calls=%fused_computation.23 | convolution fusion | flops 82070832 | bytes 2829572 | tf_op jit(solution)/shard_map/hb,hxy->bxy/dot_general | solution.py:136
  104.9 2.8 %collective-permute-start.21 = (f32[4,128]{1,0:T(4,128)S(1)}, f32[4,128]{1,0:T(4,128)S(1)}, u32[]{:S(2)}, u32[]{:S(2)}) collective-permute-start(f32[4,128]{1,0:T(4,128)S(1)} %add_add_fusion.2), channel_id=1, source_target_pairs={{0,64},{16,80},{32,96},{48,112},{64,0},{80,16},{96,32},{112,48},{1... | collective-permute-start | bytes 6152 | tf_op jit(solution)/shard_map/ppermute | solution.py:42
  107.7 2.4 %collective-permute-done.21 = f32[4,128]{1,0:T(4,128)S(1)} collective-permute-done((f32[4,128]{1,0:T(4,128)S(1)}, f32[4,128]{1,0:T(4,128)S(1)}, u32[]{:S(2)}, u32[]{:S(2)}) %collective-permute-start.21) | collective-permute-done | bytes 2080 | tf_op jit(solution)/shard_map/ppermute | solution.py:42
  110.1 3.0 %collective-permute-start.23 = (f32[4,128]{1,0:T(4,128)S(1)}, f32[4,128]{1,0:T(4,128)S(1)}, u32[]{:S(2)}, u32[]{:S(2)}) collective-permute-start(f32[4,128]{1,0:T(4,128)S(1)} %add.242), channel_id=1, source_target_pairs={{0,2},{1,3},{2,0},{3,1},{4,6},{5,7},{6,4},{7,5},{8,10},{9,11},{10,... | collective-permute-start | bytes 6152 | tf_op jit(solution)/shard_map/ppermute | solution.py:42
  117.1 3.8 %collective-permute-start.26 = (f32[4,128]{1,0:T(4,128)S(1)}, f32[4,128]{1,0:T(4,128)S(1)}, u32[]{:S(2)}, u32[]{:S(2)}) collective-permute-start(f32[4,128]{1,0:T(4,128)S(1)} %add_add_fusion.1), channel_id=1, source_target_pairs={{0,8},{1,9},{2,10},{3,11},{4,12},{5,13},{6,14},{7,15},{8,0},{9,1},... | collective-permute-start | bytes 6152 | tf_op jit(solution)/shard_map/ppermute | solution.py:42
  122.5 2.0 %collective-permute-done.27 = f32[4,128]{1,0:T(4,128)S(1)} collective-permute-done((f32[4,128]{1,0:T(4,128)S(1)}, f32[4,128]{1,0:T(4,128)S(1)}, u32[]{:S(2)}, u32[]{:S(2)}) %collective-permute-start.27) | collective-permute-done | bytes 2080 | tf_op jit(solution)/shard_map/ppermute | solution.py:42
  (127 shorter events, 44.8 us)
Async XLA Ops:
  2.3 20.4 %collective-permute-start = (f32[12,3,128]{2,0,1:T(8,128)S(1)}, f32[12,3,128]{2,0,1:T(8,128)S(1)}, u32[]{:S(2)}, u32[]{:S(2)}) collective-permute-start(f32[12,3,128]{2,0,1:T(8,128)S(1)} %get-tuple-element.46), channel_id=1, source_target_pairs={{0,16},{16,32},{32,48},{48,64},{64,80},{80,96},{96,112},{1,17},{17... | collective-permute-start | bytes 55304 | tf_op jit(solution)/shard_map/ppermute | solution.py:22
  3.6 19.1 %collective-permute-start.1 = (f32[12,3,128]{2,0,1:T(8,128)S(1)}, f32[12,3,128]{2,0,1:T(8,128)S(1)}, u32[]{:S(2)}, u32[]{:S(2)}) collective-permute-start(f32[12,3,128]{2,0,1:T(8,128)S(1)} %get-tuple-element.47), channel_id=1, source_target_pairs={{16,0},{32,16},{48,32},{64,48},{80,64},{96,80},{112,96},{17,1},{33... | collective-permute-start | bytes 55304 | tf_op jit(solution)/shard_map/ppermute | solution.py:25
  7.8 33.4 %all-to-all-start = ((f32[128,1,1152]{2,1,0:T(1,128)}), f32[128,1,1152]{2,1,0:T(1,128)}, u32[]{:S(2)}, u32[]{:S(2)}) async-start(f32[128,1,1152]{2,1,0:T(1,128)} %copy.68), calls=%async_computation | async-start | bytes 1179648 | tf_op jit(solution)/shard_map/all_to_all | solution.py:98
  23.5 9.5 %collective-permute-start.2 = (f32[12,22,3]{2,0,1:T(8,128)}, f32[12,22,3]{2,0,1:T(8,128)}, u32[]{:S(2)}, u32[]{:S(2)}) collective-permute-start(f32[12,22,3]{2,0,1:T(8,128)} %get-tuple-element.36), channel_id=1, source_target_pairs={{0,1},{1,2},{2,3},{3,4},{4,5},{5,6},{6,7},{7,8},{8,9},{9,10},{10,1... | collective-permute-start | bytes 9512 | tf_op jit(solution)/shard_map/ppermute | solution.py:22
  27.0 8.7 %collective-permute-start.3 = (f32[12,22,3]{2,0,1:T(8,128)}, f32[12,22,3]{2,0,1:T(8,128)}, u32[]{:S(2)}, u32[]{:S(2)}) collective-permute-start(f32[12,22,3]{2,0,1:T(8,128)} %get-tuple-element.37), channel_id=1, source_target_pairs={{1,0},{2,1},{3,2},{4,3},{5,4},{6,5},{7,6},{8,7},{9,8},{10,9},{11,1... | collective-permute-start | bytes 9512 | tf_op jit(solution)/shard_map/ppermute | solution.py:25
  51.5 6.0 %collective-permute-start.4 = (f32[128,2,128]{0,2,1:T(8,128)S(1)}, f32[128,2,128]{0,2,1:T(8,128)S(1)}, u32[]{:S(2)}, u32[]{:S(2)}) collective-permute-start(f32[128,2,128]{0,2,1:T(8,128)S(1)} %slice.215), channel_id=1, source_target_pairs={{0,16},{16,32},{32,48},{48,64},{64,80},{80,96},{96,112},{1,17},{17... | collective-permute-start | bytes 393224 | tf_op jit(solution)/shard_map/ppermute | solution.py:22
  52.8 4.7 %collective-permute-start.5 = (f32[128,1,128]{0,2,1:T(8,128)S(1)}, f32[128,1,128]{0,2,1:T(8,128)S(1)}, u32[]{:S(2)}, u32[]{:S(2)}) collective-permute-start(f32[128,1,128]{0,2,1:T(8,128)S(1)} %slice.216), channel_id=1, source_target_pairs={{16,0},{32,16},{48,32},{64,48},{80,64},{96,80},{112,96},{17,1},{33... | collective-permute-start | bytes 196616 | tf_op jit(solution)/shard_map/ppermute | solution.py:25
  57.5 8.6 %collective-permute-start.6 = (f32[128,19,2]{0,2,1:T(2,128)S(1)}, f32[128,19,2]{0,2,1:T(2,128)S(1)}, u32[]{:S(2)}, u32[]{:S(2)}) collective-permute-start(f32[128,19,2]{0,2,1:T(2,128)S(1)} %pad_maximum_fusion.15), channel_id=1, source_target_pairs={{0,1},{1,2},{2,3},{3,4},{4,5},{5,6},{6,7},{7,8},{8,9},{9,10},{10,1... | collective-permute-start | bytes 58376 | tf_op jit(solution)/shard_map/ppermute | solution.py:22
  60.5 5.6 %collective-permute-start.7 = (f32[128,19,1]{0,2,1:T(1,128)S(1)}, f32[128,19,1]{0,2,1:T(1,128)S(1)}, u32[]{:S(2)}, u32[]{:S(2)}) collective-permute-start(f32[128,19,1]{0,2,1:T(1,128)S(1)} %pad_maximum_fusion.16), channel_id=1, source_target_pairs={{1,0},{2,1},{3,2},{4,3},{5,4},{6,5},{7,6},{8,7},{9,8},{10,9},{11,1... | collective-permute-start | bytes 29192 | tf_op jit(solution)/shard_map/ppermute | solution.py:25
  68.6 4.2 %collective-permute-start.10 = (f32[2,128]{1,0:T(2,128)S(1)}, f32[2,128]{1,0:T(2,128)S(1)}, u32[]{:S(2)}, u32[]{:S(2)}) collective-permute-start(f32[2,128]{1,0:T(2,128)S(1)} %pad_maximum_fusion.19), channel_id=1, source_target_pairs={{0,48},{16,0},{32,16},{48,32},{64,112},{80,64},{96,80},{112,96},{1... | collective-permute-start | bytes 3080 | tf_op jit(solution)/shard_map/ppermute | solution.py:42
  74.6 5.2 %collective-permute-start.11 = (f32[2,128]{1,0:T(2,128)S(1)}, f32[2,128]{1,0:T(2,128)S(1)}, u32[]{:S(2)}, u32[]{:S(2)}) collective-permute-start(f32[2,128]{1,0:T(2,128)S(1)} %add_add_fusion.4), channel_id=1, source_target_pairs={{0,64},{16,80},{32,96},{48,112},{64,0},{80,16},{96,32},{112,48},{1... | collective-permute-start | bytes 3080 | tf_op jit(solution)/shard_map/ppermute | solution.py:42
  79.8 8.2 %collective-permute-start.12 = (f32[2,128]{1,0:T(2,128)S(1)}, f32[2,128]{1,0:T(2,128)S(1)}, u32[]{:S(2)}, u32[]{:S(2)}) collective-permute-start(f32[2,128]{1,0:T(2,128)S(1)} %add.228), channel_id=1, source_target_pairs={{0,1},{1,2},{2,3},{3,0},{4,5},{5,6},{6,7},{7,4},{8,9},{9,10},{10,1... | collective-permute-start | bytes 3080 | tf_op jit(solution)/shard_map/ppermute | solution.py:42
  83.3 5.3 %collective-permute-start.13 = (f32[2,128]{1,0:T(2,128)S(1)}, f32[2,128]{1,0:T(2,128)S(1)}, u32[]{:S(2)}, u32[]{:S(2)}) collective-permute-start(f32[2,128]{1,0:T(2,128)S(1)} %add.228), channel_id=1, source_target_pairs={{0,2},{1,3},{2,0},{3,1},{4,6},{5,7},{6,4},{7,5},{8,10},{9,11},{10,... | collective-permute-start | bytes 3080 | tf_op jit(solution)/shard_map/ppermute | solution.py:42
  90.7 7.8 %collective-permute-start.15 = (f32[2,128]{1,0:T(2,128)S(1)}, f32[2,128]{1,0:T(2,128)S(1)}, u32[]{:S(2)}, u32[]{:S(2)}) collective-permute-start(f32[2,128]{1,0:T(2,128)S(1)} %add_add_fusion.3), channel_id=1, source_target_pairs={{0,4},{1,5},{2,6},{3,7},{4,8},{5,9},{6,10},{7,11},{8,12},{9,13},{1... | collective-permute-start | bytes 3080 | tf_op jit(solution)/shard_map/ppermute | solution.py:42
  92.4 6.1 %collective-permute-start.16 = (f32[2,128]{1,0:T(2,128)S(1)}, f32[2,128]{1,0:T(2,128)S(1)}, u32[]{:S(2)}, u32[]{:S(2)}) collective-permute-start(f32[2,128]{1,0:T(2,128)S(1)} %add_add_fusion.3), channel_id=1, source_target_pairs={{0,8},{1,9},{2,10},{3,11},{4,12},{5,13},{6,14},{7,15},{8,0},{9,1},... | collective-permute-start | bytes 3080 | tf_op jit(solution)/shard_map/ppermute | solution.py:42
  93.9 4.6 %collective-permute-start.17 = (f32[2,128]{1,0:T(2,128)S(1)}, f32[2,128]{1,0:T(2,128)S(1)}, u32[]{:S(2)}, u32[]{:S(2)}) collective-permute-start(f32[2,128]{1,0:T(2,128)S(1)} %add_add_fusion.3), channel_id=1, source_target_pairs={{0,12},{1,13},{2,14},{3,15},{4,0},{5,1},{6,2},{7,3},{8,4},{9,5},{1... | collective-permute-start | bytes 3080 | tf_op jit(solution)/shard_map/ppermute | solution.py:42
  100.9 3.7 %collective-permute-start.19 = (f32[4,128]{1,0:T(4,128)S(1)}, f32[4,128]{1,0:T(4,128)S(1)}, u32[]{:S(2)}, u32[]{:S(2)}) collective-permute-start(f32[4,128]{1,0:T(4,128)S(1)} %pad_maximum_fusion.18), channel_id=1, source_target_pairs={{0,32},{16,48},{32,0},{48,16},{64,96},{80,112},{96,64},{112,80},{1... | collective-permute-start | bytes 6152 | tf_op jit(solution)/shard_map/ppermute | solution.py:42
  104.9 5.2 %collective-permute-start.21 = (f32[4,128]{1,0:T(4,128)S(1)}, f32[4,128]{1,0:T(4,128)S(1)}, u32[]{:S(2)}, u32[]{:S(2)}) collective-permute-start(f32[4,128]{1,0:T(4,128)S(1)} %add_add_fusion.2), channel_id=1, source_target_pairs={{0,64},{16,80},{32,96},{48,112},{64,0},{80,16},{96,32},{112,48},{1... | collective-permute-start | bytes 6152 | tf_op jit(solution)/shard_map/ppermute | solution.py:42
  110.1 4.8 %collective-permute-start.22 = (f32[4,128]{1,0:T(4,128)S(1)}, f32[4,128]{1,0:T(4,128)S(1)}, u32[]{:S(2)}, u32[]{:S(2)}) collective-permute-start(f32[4,128]{1,0:T(4,128)S(1)} %add.242), channel_id=1, source_target_pairs={{0,1},{1,2},{2,3},{3,0},{4,5},{5,6},{6,7},{7,4},{8,9},{9,10},{10,1... | collective-permute-start | bytes 6152 | tf_op jit(solution)/shard_map/ppermute | solution.py:42
  110.1 5.1 %collective-permute-start.23 = (f32[4,128]{1,0:T(4,128)S(1)}, f32[4,128]{1,0:T(4,128)S(1)}, u32[]{:S(2)}, u32[]{:S(2)}) collective-permute-start(f32[4,128]{1,0:T(4,128)S(1)} %add.242), channel_id=1, source_target_pairs={{0,2},{1,3},{2,0},{3,1},{4,6},{5,7},{6,4},{7,5},{8,10},{9,11},{10,... | collective-permute-start | bytes 6152 | tf_op jit(solution)/shard_map/ppermute | solution.py:42
  113.1 3.6 %collective-permute-start.24 = (f32[4,128]{1,0:T(4,128)S(1)}, f32[4,128]{1,0:T(4,128)S(1)}, u32[]{:S(2)}, u32[]{:S(2)}) collective-permute-start(f32[4,128]{1,0:T(4,128)S(1)} %add.242), channel_id=1, source_target_pairs={{0,3},{1,0},{2,1},{3,2},{4,7},{5,4},{6,5},{7,6},{8,11},{9,8},{10,9... | collective-permute-start | bytes 6152 | tf_op jit(solution)/shard_map/ppermute | solution.py:42
  116.7 5.6 %collective-permute-start.25 = (f32[4,128]{1,0:T(4,128)S(1)}, f32[4,128]{1,0:T(4,128)S(1)}, u32[]{:S(2)}, u32[]{:S(2)}) collective-permute-start(f32[4,128]{1,0:T(4,128)S(1)} %add_add_fusion.1), channel_id=1, source_target_pairs={{0,4},{1,5},{2,6},{3,7},{4,8},{5,9},{6,10},{7,11},{8,12},{9,13},{1... | collective-permute-start | bytes 6152 | tf_op jit(solution)/shard_map/ppermute | solution.py:42
  117.1 5.4 %collective-permute-start.26 = (f32[4,128]{1,0:T(4,128)S(1)}, f32[4,128]{1,0:T(4,128)S(1)}, u32[]{:S(2)}, u32[]{:S(2)}) collective-permute-start(f32[4,128]{1,0:T(4,128)S(1)} %add_add_fusion.1), channel_id=1, source_target_pairs={{0,8},{1,9},{2,10},{3,11},{4,12},{5,13},{6,14},{7,15},{8,0},{9,1},... | collective-permute-start | bytes 6152 | tf_op jit(solution)/shard_map/ppermute | solution.py:42
  120.9 3.6 %collective-permute-start.27 = (f32[4,128]{1,0:T(4,128)S(1)}, f32[4,128]{1,0:T(4,128)S(1)}, u32[]{:S(2)}, u32[]{:S(2)}) collective-permute-start(f32[4,128]{1,0:T(4,128)S(1)} %add_add_fusion.1), channel_id=1, source_target_pairs={{0,12},{1,13},{2,14},{3,15},{4,0},{5,1},{6,2},{7,3},{8,4},{9,5},{1... | collective-permute-start | bytes 6152 | tf_op jit(solution)/shard_map/ppermute | solution.py:42
  (22 other events, 298.0 us)
